TPU v7x, 32 devices: a whole 2x2x4 slice. The times are simulated.
32 devices in a mesh: enc: 4 (over y, x), pool: 8 (over z, core).
Axes of the slice: x: 2, y: 2, z: 4, core: 2. Of those that a mesh axis runs over, the one named last changes fastest.
Arguments:
- encoded: bfloat16 [2048, 32, 128], P('pool', 'enc'), may hold values from -6 to 6
- slot_items: int32 [2048], replicated, may hold values from 0 to 2047, as said below
- lengths: int32 [2048], P(('enc', 'pool')), may hold values from 1 to 32
- token_mask: int32 [2048, 32], P(('enc', 'pool')), may hold values 0 or 1
Outputs:
- scores: float32 [2048, 192], P(('enc', 'pool'))
Inputs may be any that keep to these rules, and one draw needn't show every extreme that they name: `slot_items`: each item appears in exactly one slot. The slots d * 64 + p * 8 + j, for j below 8, hold items p * 256 to (p + 1) * 256 - 1, those whose encoder rows lie on pool index p.
All inputs are finite; a program needn't handle non-finite values. No bound on the sum of `token_mask` on one device may be relied on, other than what follows from the above.
Results may differ from a plain program's by a relative error of at most 0.00057.
Values may be sent and summed in bfloat16 or wider, within the bound.
No kernel may reach another device: no remote copies, remote signals or barrier semaphores. Data moves between devices by JAX's collectives and lax.ppermute only.
A program may use at most 64 MiB of HBM per device.

v0:
```python
import jax
import jax.numpy as jnp
from jax import lax
from jax.sharding import PartitionSpec as P


def from_partner(array, axis, stride):
    return lax.ppermute(array, axis, [(i, i ^ 1 << stride) for i in range(lax.axis_size(axis))])


def tile_scores(block, bias, other, other_bias, tok):
    query_items = block.shape[0] // tok
    other_items = other.shape[0] // tok
    width = block.shape[1]
    rows = min(32, query_items)
    blocks = query_items // rows
    other_tr = jnp.transpose(other.reshape(other_items, tok, width), (1, 0, 2))
    other_float = other_bias.astype(jnp.float32)
    other_add_tr = jnp.transpose(other_float.reshape(other_items, tok), (1, 0))[:, :, None]
    other_owner = (jnp.arange(other_items * tok, dtype=jnp.int32) // tok)[:, None] == jnp.arange(
        other_items, dtype=jnp.int32
    )[None, :]
    other_select = jnp.where((other_bias == 0)[:, None] & other_owner, 1.0, 0.0).astype(jnp.float32)
    query_flat = block.reshape(blocks, rows * tok, width)
    query_tr = jnp.transpose(block.reshape(blocks, rows, tok, width), (0, 2, 1, 3))
    bias_float = bias.astype(jnp.float32).reshape(blocks, rows, tok)
    query_add_tr = jnp.transpose(bias_float, (0, 2, 1))[..., None]
    query_valid = (bias == 0).reshape(blocks, rows * tok)
    query_owner = (jnp.arange(rows * tok, dtype=jnp.int32) // tok)[:, None] == jnp.arange(
        rows, dtype=jnp.int32
    )[None, :]

    def one_block(operands):
        flat, turned, adding, kept = operands
        dots_fore = jnp.einsum("ubh,qh->ubq", other_tr, flat, preferred_element_type=jnp.float32)
        fore = jnp.max(dots_fore + other_add_tr, axis=0)
        select = jnp.where(kept[:, None] & query_owner, 1.0, 0.0).astype(jnp.float32)
        fore = jnp.dot(
            fore, select, precision=lax.Precision.HIGHEST, preferred_element_type=jnp.float32
        )
        dots_back = jnp.einsum("trh,ch->trc", turned, other, preferred_element_type=jnp.float32)
        back = jnp.max(dots_back + adding, axis=0)
        back = jnp.dot(
            back, other_select, precision=lax.Precision.HIGHEST, preferred_element_type=jnp.float32
        )
        return 0.5 * (fore.T + back)

    result = lax.map(one_block, (query_flat, query_tr, query_add_tr, query_valid))
    return result.reshape(query_items, other_items)


def shards(encoded, slot_items, lengths, token_mask):
    n_enc = lax.axis_size("enc")
    n_pool = lax.axis_size("pool")
    owners = n_enc * n_pool
    group = encoded.shape[0]
    toks = encoded.shape[1]
    width = encoded.shape[2]
    items_dev = lengths.shape[0]
    per = items_dev // n_pool
    pool_index = lax.axis_index("pool")
    table = slot_items.reshape(owners, n_pool, per)
    mine = lax.dynamic_index_in_dim(table, pool_index, 1, keepdims=False) - pool_index * group
    outgoing = jnp.take(encoded, mine, axis=0)
    arrived = lax.all_to_all(outgoing, ("enc", "pool"), split_axis=0, concat_axis=0, tiled=True)
    arrived = arrived.reshape(n_enc, n_pool, per, toks, width)
    tok = n_enc * toks
    slotted = jnp.transpose(arrived, (1, 2, 0, 3, 4)).reshape(items_dev, tok, width)
    values = slotted.astype(jnp.float32)
    normed = (values / jnp.sqrt(jnp.sum(values * values, axis=-1, keepdims=True) + 1e-06)).astype(
        jnp.bfloat16
    )
    position = jnp.arange(tok, dtype=jnp.int32)[None, :]
    valid = (position < lengths[:, None]) & ((position == 0) | (token_mask == 1))
    bias = jnp.where(valid, 0.0, -4.0).astype(jnp.bfloat16).reshape(-1)
    block = normed.reshape(items_dev * tok, width)
    results = []
    for bit in range(3):
        other, other_bias = from_partner((block, bias), "pool", bit)
        results.append(tile_scores(block, bias, other, other_bias, tok))
    return jnp.concatenate(results, axis=1)


def solution(mesh):
    in_specs = (P("pool", "enc", None), P(), P(("enc", "pool")), P(("enc", "pool"), None))
    out_specs = P(("enc", "pool"), None)
    return jax.shard_map(shards, mesh=mesh, in_specs=in_specs, out_specs=out_specs, check_vma=False)
```

profile of v0, /device:TPU:0, one launch (start us, length us, event | category | flops | bytes accessed | tf_op | source)
XLA Modules:
  0.0 86.8 jit_solution(10531709045881463416)
XLA Ops:
  0.0 0.8 reshape.169
  0.9 0.1 reshape.199
  1.1 0.8 gather_fusion
  1.9 1.1 %broadcast_select_fusion = bf16[32,8,8,128]{3,2,1,0:T(8,128)(2,1)} fusion(bf16[32,8,8,128]{3,2,1,0:T(8,128)(2,1)S(1)} %bitcast.165, pred[32,8]{1,0:T(8,128)(4,1)S(1)} %compare_and_fusion), kind=kLoop, calls=%fused_computation.118 | loop fusion | flops 262144 | bytes 1048832 | tf_op jit(solution)/shard_map/jit(_take)/select_n | solution.py:64
  3.0 7.3 %all-to-all-start = ((bf16[32,8,8,128]{3,2,1,0:T(8,128)(2,1)}), bf16[32,8,8,128]{3,2,1,0:T(8,128)(2,1)S(1)}, u32[]{:S(2)}, u32[]{:S(2)}) async-start(bf16[32,8,8,128]{3,2,1,0:T(8,128)(2,1)} %broadcast_select_fusion), calls=%async_computation | async-start | bytes 1048576 | tf_op jit(solution)/shard_map/all_to_all | solution.py:65
  10.4 0.1 broadcast_compare_fusion
  10.5 0.1 copy.76
  10.5 0.1 reshape.171
  10.6 2.7 %collective-permute-start.5 = (bf16[2048]{0:T(1024)(128)(2,1)S(1)}, bf16[2048]{0:T(1024)(128)(2,1)S(1)}, u32[]{:S(2)}, u32[]{:S(2)}) collective-permute-start(bf16[2048]{0:T(1024)(128)(2,1)S(1)} %reshape.171), channel_id=1, source_target_pairs={{0,4},{1,5},{2,6},{3,7},{4,0},{5,1},{6,2},{7,3},{8,12},{9,13},{10,... | collective-permute-start | bytes 12296 | tf_op jit(solution)/shard_map/ppermute | solution.py:8
  13.3 1.5 %collective-permute-start.3 = (bf16[2048]{0:T(1024)(128)(2,1)S(1)}, bf16[2048]{0:T(1024)(128)(2,1)S(1)}, u32[]{:S(2)}, u32[]{:S(2)}) collective-permute-start(bf16[2048]{0:T(1024)(128)(2,1)S(1)} %reshape.171), channel_id=1, source_target_pairs={{0,2},{1,3},{2,0},{3,1},{4,6},{5,7},{6,4},{7,5},{8,10},{9,11},{10,... | collective-permute-start | bytes 12296 | tf_op jit(solution)/shard_map/ppermute | solution.py:8
  14.8 0.1 reshape.194
  14.9 0.1 copy.69
  15.0 0.1 eq.118
  15.2 0.8 collective-permute-done.1
  16.0 0.1 reshape.192
  16.1 3.5 %collective-permute-done.3 = bf16[2048]{0:T(1024)(128)(2,1)S(1)} collective-permute-done((bf16[2048]{0:T(1024)(128)(2,1)S(1)}, bf16[2048]{0:T(1024)(128)(2,1)S(1)}, u32[]{:S(2)}, u32[]{:S(2)}) %collective-permute-start.3) | collective-permute-done | bytes 4128 | tf_op jit(solution)/shard_map/ppermute | solution.py:8
  19.8 5.7 %collective-permute-done.5 = bf16[2048]{0:T(1024)(128)(2,1)S(1)} collective-permute-done((bf16[2048]{0:T(1024)(128)(2,1)S(1)}, bf16[2048]{0:T(1024)(128)(2,1)S(1)}, u32[]{:S(2)}, u32[]{:S(2)}) %collective-permute-start.5) | collective-permute-done | bytes 4128 | tf_op jit(solution)/shard_map/ppermute | solution.py:8
  25.7 1.1 %all-to-all-done = bf16[32,8,8,128]{3,2,1,0:T(8,128)(2,1)S(1)} async-done(((bf16[32,8,8,128]{3,2,1,0:T(8,128)(2,1)}), bf16[32,8,8,128]{3,2,1,0:T(8,128)(2,1)S(1)}, u32[]{:S(2)}, u32[]{:S(2)}) %all-to-all-start) | async-done | bytes 524320 | tf_op jit(solution)/shard_map/all_to_all | solution.py:65
  26.8 0.3 multiply_reduce_fusion
  27.1 0.1 copy.71
  27.3 0.1 reshape.189
  27.4 0.2 copy.72
  27.6 0.2 sqrt.21
  27.7 0.2 sqrt.20
  27.9 0.1 reshape.212
  28.0 0.1 convert_element_type.77
  28.1 0.1 copy.70
  28.3 0.3 fusion.99
  28.7 0.7 collective-permute-start.2
  29.4 0.3 fusion.100
  29.8 0.2 copy.81
  30.0 0.3 divide_convert_fusion.1
  30.3 23.1 %collective-permute-done.4 = bf16[2048,128]{1,0:T(8,128)(2,1)S(1)} collective-permute-done((bf16[2048,128]{1,0:T(8,128)(2,1)S(1)}, bf16[2048,128]{1,0:T(8,128)(2,1)S(1)}, u32[]{:S(2)}, u32[]{:S(2)}) %collective-permute-start.4) | collective-permute-done | bytes 524320 | tf_op jit(solution)/shard_map/ppermute | solution.py:8
  53.5 1.0 %copy.96 = bf16[64,32,128]{2,0,1:T(8,128)(2,1)} copy(bf16[64,32,128]{2,1,0:T(8,128)(2,1)S(1)} %bitcast.169) | data formatting | bytes 1048576 | tf_op jit(solution)/shard_map/reshape | solution.py:17
  54.5 11.5 %while.35 = (s32[]{:T(128)}, f32[2,32,64]{2,1,0:T(8,128)S(1)}, pred[2,1024]{1,0:T(4,128)(4,1)S(1)}, bf16[2,1024,128]{2,1,0:T(8,128)(2,1)S(1)}, bf16[32,64,128]{2...) while((s32[]{:T(128)}, f32[2,32,64]{2,1,0:T(8,128)S(1)}, ...), condition=%wide.region_12.13_spmd.clone, body=%wide.region_9.12_spmd.clone.sunk | while | flops 1157992448 | bytes 4818101 | solution.py:48
  54.5 2.4 %add_reduce_fusion.17 = f32[32,2048]{1,0:T(8,128)S(1)} fusion(f32[32,32]{1,0:T(8,128)S(1)} %dynamic-slice_bitcast_fusion.8, bf16[2048,128]{1,0:T(8,128)(2,1)} %get-tuple-element.739, bf16[2,32,32,128]{3,2,1,0:T(8,128)(2,1)S(1)} %get-tuple-element.738, s32[]{:T(128)S(6)} %copy.104), kind=kOutput, calls=%fused_computation.75.clone.1 | convolution fusion | flops 540999680 | bytes 1064964 | tf_op jit(solution)/shard_map/while/body/eval_jaxpr/trh,ch->trc/dot_general | solution.py:41
  57.0 1.3 %add_reduce_fusion.16 = f32[1024,64]{0,1:T(8,128)S(1)} fusion(f32[32,64]{1,0:T(8,128)S(1)} %bitcast.184, bf16[32,64,128]{2,1,0:T(8,128)(2,1)S(1)} %copy-done.2, bf16[2,1024,128]{2,1,0:T(8,128)(2,1)S(1)} %get-tuple-element.735, s32[]{:T(128)S(6)} %copy.104), kind=kOutput, calls=%fused_computation.76.clone.1 | convolution fusion | flops 540999680 | bytes 1064964 | tf_op jit(solution)/shard_map/while/body/eval_jaxpr/ubh,qh->ubq/dot_general | solution.py:35
  58.2 0.9 %fusion.175 = f32[32,64]{1,0:T(8,128)S(1)} fusion(f32[1024,64]{0,1:T(8,128)S(1)} %add_reduce_fusion.16, s32[1024]{0:T(1024)S(1)} %get-tuple-element.741, pred[1024]{0:T(1024)(128)(4,1)S(1)} %dynamic-slice_reduce_fusion.8), kind=kOutput, calls=%fused_computation.89.clone.1 | convolution fusion | flops 25264128 | bytes 275456 | tf_op jit(solution)/shard_map/while/body/eval_jaxpr/dot_general | solution.py:38
  59.2 1.1 %fusion.176 = f32[2,32,64]{2,1,0:T(8,128)S(1)} fusion(f32[2,32,64]{2,1,0:T(8,128)S(1)} %get-tuple-element.720, s32[]{:T(128)S(6)} %copy.104, f32[32,64]{1,0:T(8,128)S(1)} %fusion.175, f32[32,2048]{1,0:T(8,128)S(1)} %add_reduce_fusion.17, s32[2048]{0:T(1024)S(1)} %get-tuple-element.742, pred[2048]{0:T(1024)(128)(4,1)S(1)} %get-tuple-element.743), kind=kOutput, calls=%fused_computation.80.clone.1 | convolution fusion | flops 50728960 | bytes 305156 | tf_op jit(solution)/shard_map/while/body/eval_jaxpr/dot_general | solution.py:43
  60.3 2.4 %add_reduce_fusion.17 = f32[32,2048]{1,0:T(8,128)S(1)} fusion(f32[32,32]{1,0:T(8,128)S(1)} %dynamic-slice_bitcast_fusion.8, bf16[2048,128]{1,0:T(8,128)(2,1)} %get-tuple-element.739, bf16[2,32,32,128]{3,2,1,0:T(8,128)(2,1)S(1)} %get-tuple-element.738, s32[]{:T(128)S(6)} %copy.104), kind=kOutput, calls=%fused_computation.75.clone.1 | convolution fusion | flops 540999680 | bytes 1064964 | tf_op jit(solution)/shard_map/while/body/eval_jaxpr/trh,ch->trc/dot_general | solution.py:41
  62.7 1.3 %add_reduce_fusion.16 = f32[1024,64]{0,1:T(8,128)S(1)} fusion(f32[32,64]{1,0:T(8,128)S(1)} %bitcast.184, bf16[32,64,128]{2,1,0:T(8,128)(2,1)S(1)} %copy-done.2, bf16[2,1024,128]{2,1,0:T(8,128)(2,1)S(1)} %get-tuple-element.735, s32[]{:T(128)S(6)} %copy.104), kind=kOutput, calls=%fused_computation.76.clone.1 | convolution fusion | flops 540999680 | bytes 1064964 | tf_op jit(solution)/shard_map/while/body/eval_jaxpr/ubh,qh->ubq/dot_general | solution.py:35
  64.0 0.9 %fusion.175 = f32[32,64]{1,0:T(8,128)S(1)} fusion(f32[1024,64]{0,1:T(8,128)S(1)} %add_reduce_fusion.16, s32[1024]{0:T(1024)S(1)} %get-tuple-element.741, pred[1024]{0:T(1024)(128)(4,1)S(1)} %dynamic-slice_reduce_fusion.8), kind=kOutput, calls=%fused_computation.89.clone.1 | convolution fusion | flops 25264128 | bytes 275456 | tf_op jit(solution)/shard_map/while/body/eval_jaxpr/dot_general | solution.py:38
  64.9 1.1 %fusion.176 = f32[2,32,64]{2,1,0:T(8,128)S(1)} fusion(f32[2,32,64]{2,1,0:T(8,128)S(1)} %get-tuple-element.720, s32[]{:T(128)S(6)} %copy.104, f32[32,64]{1,0:T(8,128)S(1)} %fusion.175, f32[32,2048]{1,0:T(8,128)S(1)} %add_reduce_fusion.17, s32[2048]{0:T(1024)S(1)} %get-tuple-element.742, pred[2048]{0:T(1024)(128)(4,1)S(1)} %get-tuple-element.743), kind=kOutput, calls=%fused_computation.80.clone.1 | convolution fusion | flops 50728960 | bytes 305156 | tf_op jit(solution)/shard_map/while/body/eval_jaxpr/dot_general | solution.py:43
  66.0 1.0 %copy.97 = bf16[64,32,128]{2,0,1:T(8,128)(2,1)} copy(bf16[64,32,128]{2,1,0:T(8,128)(2,1)S(1)} %bitcast.168) | data formatting | bytes 1048576 | tf_op jit(solution)/shard_map/reshape | solution.py:17
  67.0 9.5 %while.34 = (s32[]{:T(128)}, f32[2,32,64]{2,1,0:T(8,128)S(1)}, pred[2,1024]{1,0:T(4,128)(4,1)S(1)}, bf16[2,1024,128]{2,1,0:T(8,128)(2,1)S(1)}, bf16[32,64,128]{2...) while((s32[]{:T(128)}, f32[2,32,64]{2,1,0:T(8,128)S(1)}, ...), condition=%wide.region_8.9_spmd.clone, body=%wide.region_5.8_spmd.clone.sunk | while | flops 1157992448 | bytes 4818101 | solution.py:48
  67.1 1.3 %add_reduce_fusion.15 = f32[32,2048]{1,0:T(8,128)S(1)} fusion(f32[32,32]{1,0:T(8,128)S(1)} %dynamic-slice_bitcast_fusion.7, bf16[2048,128]{1,0:T(8,128)(2,1)S(1)} %get-tuple-element.778, bf16[2,32,32,128]{3,2,1,0:T(8,128)(2,1)S(1)} %get-tuple-element.777, s32[]{:T(128)S(6)} %copy.110), kind=kOutput, calls=%fused_computation.41.clone.1 | convolution fusion | flops 540999680 | bytes 1064964 | tf_op jit(solution)/shard_map/while/body/eval_jaxpr/trh,ch->trc/dot_general | solution.py:41
  68.4 1.3 %add_reduce_fusion.14 = f32[1024,64]{0,1:T(8,128)S(1)} fusion(f32[32,64]{1,0:T(8,128)S(1)} %bitcast.183, bf16[32,64,128]{2,1,0:T(8,128)(2,1)S(1)} %copy-done.3, bf16[2,1024,128]{2,1,0:T(8,128)(2,1)S(1)} %get-tuple-element.774, s32[]{:T(128)S(6)} %copy.110), kind=kOutput, calls=%fused_computation.42.clone.1 | convolution fusion | flops 540999680 | bytes 1064964 | tf_op jit(solution)/shard_map/while/body/eval_jaxpr/ubh,qh->ubq/dot_general | solution.py:35
  69.7 0.9 %fusion.165 = f32[32,64]{1,0:T(8,128)S(1)} fusion(f32[1024,64]{0,1:T(8,128)S(1)} %add_reduce_fusion.14, s32[1024]{0:T(1024)S(1)} %get-tuple-element.780, pred[1024]{0:T(1024)(128)(4,1)S(1)} %dynamic-slice_reduce_fusion.7), kind=kOutput, calls=%fused_computation.55.clone.1 | convolution fusion | flops 25264128 | bytes 275456 | tf_op jit(solution)/shard_map/while/body/eval_jaxpr/dot_general | solution.py:38
  70.6 1.1 %fusion.166 = f32[2,32,64]{2,1,0:T(8,128)S(1)} fusion(f32[2,32,64]{2,1,0:T(8,128)S(1)} %get-tuple-element.759, s32[]{:T(128)S(6)} %copy.110, f32[32,64]{1,0:T(8,128)S(1)} %fusion.165, f32[32,2048]{1,0:T(8,128)S(1)} %add_reduce_fusion.15, s32[2048]{0:T(1024)S(1)} %get-tuple-element.781, pred[2048]{0:T(1024)(128)(4,1)S(1)} %get-tuple-element.782), kind=kOutput, calls=%fused_computation.46.clone.1 | convolution fusion | flops 50728960 | bytes 305156 | tf_op jit(solution)/shard_map/while/body/eval_jaxpr/dot_general | solution.py:43
  71.8 1.3 %add_reduce_fusion.15 = f32[32,2048]{1,0:T(8,128)S(1)} fusion(f32[32,32]{1,0:T(8,128)S(1)} %dynamic-slice_bitcast_fusion.7, bf16[2048,128]{1,0:T(8,128)(2,1)S(1)} %get-tuple-element.778, bf16[2,32,32,128]{3,2,1,0:T(8,128)(2,1)S(1)} %get-tuple-element.777, s32[]{:T(128)S(6)} %copy.110), kind=kOutput, calls=%fused_computation.41.clone.1 | convolution fusion | flops 540999680 | bytes 1064964 | tf_op jit(solution)/shard_map/while/body/eval_jaxpr/trh,ch->trc/dot_general | solution.py:41
  73.0 1.3 %add_reduce_fusion.14 = f32[1024,64]{0,1:T(8,128)S(1)} fusion(f32[32,64]{1,0:T(8,128)S(1)} %bitcast.183, bf16[32,64,128]{2,1,0:T(8,128)(2,1)S(1)} %copy-done.3, bf16[2,1024,128]{2,1,0:T(8,128)(2,1)S(1)} %get-tuple-element.774, s32[]{:T(128)S(6)} %copy.110), kind=kOutput, calls=%fused_computation.42.clone.1 | convolution fusion | flops 540999680 | bytes 1064964 | tf_op jit(solution)/shard_map/while/body/eval_jaxpr/ubh,qh->ubq/dot_general | solution.py:35
  74.3 0.9 %fusion.165 = f32[32,64]{1,0:T(8,128)S(1)} fusion(f32[1024,64]{0,1:T(8,128)S(1)} %add_reduce_fusion.14, s32[1024]{0:T(1024)S(1)} %get-tuple-element.780, pred[1024]{0:T(1024)(128)(4,1)S(1)} %dynamic-slice_reduce_fusion.7), kind=kOutput, calls=%fused_computation.55.clone.1 | convolution fusion | flops 25264128 | bytes 275456 | tf_op jit(solution)/shard_map/while/body/eval_jaxpr/dot_general | solution.py:38
  75.3 1.1 %fusion.166 = f32[2,32,64]{2,1,0:T(8,128)S(1)} fusion(f32[2,32,64]{2,1,0:T(8,128)S(1)} %get-tuple-element.759, s32[]{:T(128)S(6)} %copy.110, f32[32,64]{1,0:T(8,128)S(1)} %fusion.165, f32[32,2048]{1,0:T(8,128)S(1)} %add_reduce_fusion.15, s32[2048]{0:T(1024)S(1)} %get-tuple-element.781, pred[2048]{0:T(1024)(128)(4,1)S(1)} %get-tuple-element.782), kind=kOutput, calls=%fused_computation.46.clone.1 | convolution fusion | flops 50728960 | bytes 305156 | tf_op jit(solution)/shard_map/while/body/eval_jaxpr/dot_general | solution.py:43
  76.5 0.2 copy.98
  76.8 9.3 %while.33 = (s32[]{:T(128)}, f32[2,32,64]{2,1,0:T(8,128)S(1)}, pred[2,1024]{1,0:T(4,128)(4,1)S(1)}, bf16[2,1024,128]{2,1,0:T(8,128)(2,1)S(1)}, bf16[32,64,128]{2...) while((s32[]{:T(128)}, f32[2,32,64]{2,1,0:T(8,128)S(1)}, ...), condition=%wide.region_4.5_spmd.clone, body=%wide.region_1.4_spmd.clone.sunk | while | flops 1157992448 | bytes 2720921 | solution.py:48
  76.8 1.3 %add_reduce_fusion.13 = f32[32,2048]{1,0:T(8,128)S(1)} fusion(f32[32,32]{1,0:T(8,128)S(1)} %dynamic-slice_bitcast_fusion.6, bf16[2048,128]{1,0:T(8,128)(2,1)S(1)} %get-tuple-element.817, bf16[2,32,32,128]{3,2,1,0:T(8,128)(2,1)S(1)} %get-tuple-element.816, s32[]{:T(128)S(6)} %copy.116), kind=kOutput, calls=%fused_computation.7.clone.1 | convolution fusion | flops 540999680 | bytes 1064964 | tf_op jit(solution)/shard_map/while/body/eval_jaxpr/trh,ch->trc/dot_general | solution.py:41
  78.1 1.3 %add_reduce_fusion.12 = f32[1024,64]{0,1:T(8,128)S(1)} fusion(f32[32,64]{1,0:T(8,128)S(1)} %bitcast.182, bf16[32,64,128]{2,1,0:T(8,128)(2,1)S(1)} %get-tuple-element.814, bf16[2,1024,128]{2,1,0:T(8,128)(2,1)S(1)} %get-tuple-element.813, s32[]{:T(128)S(6)} %copy.116), kind=kOutput, calls=%fused_computation.8.clone.1 | convolution fusion | flops 540999680 | bytes 1064964 | tf_op jit(solution)/shard_map/while/body/eval_jaxpr/ubh,qh->ubq/dot_general | solution.py:35
  79.4 0.9 %fusion.155 = f32[32,64]{1,0:T(8,128)S(1)} fusion(f32[1024,64]{0,1:T(8,128)S(1)} %add_reduce_fusion.12, s32[1024]{0:T(1024)S(1)} %get-tuple-element.819, pred[1024]{0:T(1024)(128)(4,1)S(1)} %dynamic-slice_reduce_fusion.6), kind=kOutput, calls=%fused_computation.21.clone.1 | convolution fusion | flops 25264128 | bytes 275456 | tf_op jit(solution)/shard_map/while/body/eval_jaxpr/dot_general | solution.py:38
  80.3 1.1 %fusion.156 = f32[2,32,64]{2,1,0:T(8,128)S(1)} fusion(f32[2,32,64]{2,1,0:T(8,128)S(1)} %get-tuple-element.798, s32[]{:T(128)S(6)} %copy.116, f32[32,64]{1,0:T(8,128)S(1)} %fusion.155, f32[32,2048]{1,0:T(8,128)S(1)} %add_reduce_fusion.13, s32[2048]{0:T(1024)S(1)} %get-tuple-element.820, pred[2048]{0:T(1024)(128)(4,1)S(1)} %get-tuple-element.821), kind=kOutput, calls=%fused_computation.12.clone.1 | convolution fusion | flops 50728960 | bytes 305156 | tf_op jit(solution)/shard_map/while/body/eval_jaxpr/dot_general | solution.py:43
  81.5 1.3 %add_reduce_fusion.13 = f32[32,2048]{1,0:T(8,128)S(1)} fusion(f32[32,32]{1,0:T(8,128)S(1)} %dynamic-slice_bitcast_fusion.6, bf16[2048,128]{1,0:T(8,128)(2,1)S(1)} %get-tuple-element.817, bf16[2,32,32,128]{3,2,1,0:T(8,128)(2,1)S(1)} %get-tuple-element.816, s32[]{:T(128)S(6)} %copy.116), kind=kOutput, calls=%fused_computation.7.clone.1 | convolution fusion | flops 540999680 | bytes 1064964 | tf_op jit(solution)/shard_map/while/body/eval_jaxpr/trh,ch->trc/dot_general | solution.py:41
  82.7 1.3 %add_reduce_fusion.12 = f32[1024,64]{0,1:T(8,128)S(1)} fusion(f32[32,64]{1,0:T(8,128)S(1)} %bitcast.182, bf16[32,64,128]{2,1,0:T(8,128)(2,1)S(1)} %get-tuple-element.814, bf16[2,1024,128]{2,1,0:T(8,128)(2,1)S(1)} %get-tuple-element.813, s32[]{:T(128)S(6)} %copy.116), kind=kOutput, calls=%fused_computation.8.clone.1 | convolution fusion | flops 540999680 | bytes 1064964 | tf_op jit(solution)/shard_map/while/body/eval_jaxpr/ubh,qh->ubq/dot_general | solution.py:35
  84.0 0.9 %fusion.155 = f32[32,64]{1,0:T(8,128)S(1)} fusion(f32[1024,64]{0,1:T(8,128)S(1)} %add_reduce_fusion.12, s32[1024]{0:T(1024)S(1)} %get-tuple-element.819, pred[1024]{0:T(1024)(128)(4,1)S(1)} %dynamic-slice_reduce_fusion.6), kind=kOutput, calls=%fused_computation.21.clone.1 | convolution fusion | flops 25264128 | bytes 275456 | tf_op jit(solution)/shard_map/while/body/eval_jaxpr/dot_general | solution.py:38
  85.0 1.1 %fusion.156 = f32[2,32,64]{2,1,0:T(8,128)S(1)} fusion(f32[2,32,64]{2,1,0:T(8,128)S(1)} %get-tuple-element.798, s32[]{:T(128)S(6)} %copy.116, f32[32,64]{1,0:T(8,128)S(1)} %fusion.155, f32[32,2048]{1,0:T(8,128)S(1)} %add_reduce_fusion.13, s32[2048]{0:T(1024)S(1)} %get-tuple-element.820, pred[2048]{0:T(1024)(128)(4,1)S(1)} %get-tuple-element.821), kind=kOutput, calls=%fused_computation.12.clone.1 | convolution fusion | flops 50728960 | bytes 305156 | tf_op jit(solution)/shard_map/while/body/eval_jaxpr/dot_general | solution.py:43
  86.1 0.7 pad_maximum_fusion
  (53 shorter events, 0.8 us)
Async XLA Ops:
  0.0 1.1 %copy-start = (bf16[256,8,128]{2,1,0:T(8,128)(2,1)S(1)}, bf16[256,8,128]{2,1,0:T(8,128)(2,1)}, u32[]{:S(2)}) copy-start(bf16[256,8,128]{2,1,0:T(8,128)(2,1)} %param.10) | copy-start | bytes 1572868
  1.9 8.5 %copy-start.4 = (s32[64,32]{0,1:T(8,128)S(1)}, s32[64,32]{0,1:T(8,128)}, u32[]{:S(2)}) copy-start(s32[64,32]{0,1:T(8,128)} %param.13) | copy-start | bytes 24580
  1.9 8.5 %copy-start.5 = (s32[64]{0:T(128)S(1)}, s32[64]{0:T(128)}, u32[]{:S(2)}) copy-start(s32[64]{0:T(128)} %param.12) | copy-start | bytes 772
  3.0 23.7 %all-to-all-start = ((bf16[32,8,8,128]{3,2,1,0:T(8,128)(2,1)}), bf16[32,8,8,128]{3,2,1,0:T(8,128)(2,1)S(1)}, u32[]{:S(2)}, u32[]{:S(2)}) async-start(bf16[32,8,8,128]{3,2,1,0:T(8,128)(2,1)} %broadcast_select_fusion), calls=%async_computation | async-start | bytes 1048576 | tf_op jit(solution)/shard_map/all_to_all | solution.py:65
  10.6 14.9 %collective-permute-start.5 = (bf16[2048]{0:T(1024)(128)(2,1)S(1)}, bf16[2048]{0:T(1024)(128)(2,1)S(1)}, u32[]{:S(2)}, u32[]{:S(2)}) collective-permute-start(bf16[2048]{0:T(1024)(128)(2,1)S(1)} %reshape.171), channel_id=1, source_target_pairs={{0,4},{1,5},{2,6},{3,7},{4,0},{5,1},{6,2},{7,3},{8,12},{9,13},{10,... | collective-permute-start | bytes 12296 | tf_op jit(solution)/shard_map/ppermute | solution.py:8
  13.3 6.4 %collective-permute-start.3 = (bf16[2048]{0:T(1024)(128)(2,1)S(1)}, bf16[2048]{0:T(1024)(128)(2,1)S(1)}, u32[]{:S(2)}, u32[]{:S(2)}) collective-permute-start(bf16[2048]{0:T(1024)(128)(2,1)S(1)} %reshape.171), channel_id=1, source_target_pairs={{0,2},{1,3},{2,0},{3,1},{4,6},{5,7},{6,4},{7,5},{8,10},{9,11},{10,... | collective-permute-start | bytes 12296 | tf_op jit(solution)/shard_map/ppermute | solution.py:8
  14.8 1.2 %collective-permute-start.1 = (bf16[2048]{0:T(1024)(128)(2,1)S(1)}, bf16[2048]{0:T(1024)(128)(2,1)S(1)}, u32[]{:S(2)}, u32[]{:S(2)}) collective-permute-start(bf16[2048]{0:T(1024)(128)(2,1)S(1)} %reshape.171), channel_id=1, source_target_pairs={{0,1},{1,0},{2,3},{3,2},{4,5},{5,4},{6,7},{7,6},{8,9},{9,8},{10,11... | collective-permute-start | bytes 12296 | tf_op jit(solution)/shard_map/ppermute | solution.py:8
  28.6 24.9 %collective-permute-start.4 = (bf16[2048,128]{1,0:T(8,128)(2,1)S(1)}, bf16[2048,128]{1,0:T(8,128)(2,1)S(1)}, u32[]{:S(2)}, u32[]{:S(2)}) collective-permute-start(bf16[2048,128]{1,0:T(8,128)(2,1)S(1)} %fusion.99), channel_id=1, source_target_pairs={{0,4},{1,5},{2,6},{3,7},{4,0},{5,1},{6,2},{7,3},{8,12},{9,13},{10,... | collective-permute-start | bytes 1572872 | tf_op jit(solution)/shard_map/ppermute | solution.py:8
  28.7 37.3 %collective-permute-start.2 = (bf16[2048,128]{1,0:T(8,128)(2,1)S(1)}, bf16[2048,128]{1,0:T(8,128)(2,1)S(1)}, u32[]{:S(2)}, u32[]{:S(2)}) collective-permute-start(bf16[2048,128]{1,0:T(8,128)(2,1)S(1)} %fusion.99), channel_id=1, source_target_pairs={{0,2},{1,3},{2,0},{3,1},{4,6},{5,7},{6,4},{7,5},{8,10},{9,11},{10,... | collective-permute-start | bytes 1572872 | tf_op jit(solution)/shard_map/ppermute | solution.py:8
  29.4 47.1 %collective-permute-start = (bf16[2048,128]{1,0:T(8,128)(2,1)S(1)}, bf16[2048,128]{1,0:T(8,128)(2,1)S(1)}, u32[]{:S(2)}, u32[]{:S(2)}) collective-permute-start(bf16[2048,128]{1,0:T(8,128)(2,1)S(1)} %fusion.99), channel_id=1, source_target_pairs={{0,1},{1,0},{2,3},{3,2},{4,5},{5,4},{6,7},{7,6},{8,9},{9,8},{10,11... | collective-permute-start | bytes 1572872 | tf_op jit(solution)/shard_map/ppermute | solution.py:8
  53.5 1.0 %copy-start.1 = (bf16[2048,128]{1,0:T(8,128)(2,1)}, bf16[2048,128]{1,0:T(8,128)(2,1)S(1)}, u32[]{:S(2)}) copy-start(bf16[2048,128]{1,0:T(8,128)(2,1)S(1)} %collective-permute-done.4) | copy-start | bytes 1572868
  54.5 2.4 %copy-start.2 = (bf16[32,64,128]{2,1,0:T(8,128)(2,1)S(1)}, bf16[32,64,128]{2,1,0:T(8,128)(2,1)}, u32[]{:S(2)}) copy-start(bf16[32,64,128]{2,1,0:T(8,128)(2,1)} %get-tuple-element.736) | copy-start | bytes 1572868 | tf_op jit(solution)/shard_map/while
  60.3 2.4 %copy-start.2 = (bf16[32,64,128]{2,1,0:T(8,128)(2,1)S(1)}, bf16[32,64,128]{2,1,0:T(8,128)(2,1)}, u32[]{:S(2)}) copy-start(bf16[32,64,128]{2,1,0:T(8,128)(2,1)} %get-tuple-element.736) | copy-start | bytes 1572868 | tf_op jit(solution)/shard_map/while
  67.1 1.3 %copy-start.3 = (bf16[32,64,128]{2,1,0:T(8,128)(2,1)S(1)}, bf16[32,64,128]{2,1,0:T(8,128)(2,1)}, u32[]{:S(2)}) copy-start(bf16[32,64,128]{2,1,0:T(8,128)(2,1)} %get-tuple-element.775) | copy-start | bytes 1572868 | tf_op jit(solution)/shard_map/while
  71.8 1.3 %copy-start.3 = (bf16[32,64,128]{2,1,0:T(8,128)(2,1)S(1)}, bf16[32,64,128]{2,1,0:T(8,128)(2,1)}, u32[]{:S(2)}) copy-start(bf16[32,64,128]{2,1,0:T(8,128)(2,1)} %get-tuple-element.775) | copy-start | bytes 1572868 | tf_op jit(solution)/shard_map/while
where the time goes:
time: 87.1 us; the launch traced here: 86.8 us
  waiting for transfers between devices  34.3 us (39%)
  matrix products  29.5 us (34%)
  starting transfers between devices  12.3 us (14%)
  local copies, waits for them, and re-layouts  6.31 us (7%)
  other arithmetic  3.51 us (4%)
    ppermute x6, waiting for transfers between devices, from_partner(): lax.ppermute(array, axis, [(i, i ^ 1 << stride) for i in range(lax.axis_s...  33.2 us
    dot_general x6, matrix products, one_block(): jnp.einsum('trh,ch->trc', turned, other, preferred_element_type=jnp.float32)  9.88 us
    dot_general x6, matrix products, one_block(): jnp.einsum('ubh,qh->ubq', other_tr, flat, preferred_element_type=jnp.floa...  7.66 us
    all_to_all x1, starting transfers between devices, shards(): lax.all_to_all(outgoing, ('enc', 'pool'), split_axis=0, concat_axis=0, ti...  7.29 us
    dot_general x6, matrix products, one_block(): jnp.dot(back, other_select, precision=lax.Precision.HIGHEST, preferred_el...  6.47 us
    dot_general x6, matrix products, one_block(): jnp.dot(fore, select, precision=lax.Precision.HIGHEST, preferred_element_...  5.52 us
    ppermute x6, starting transfers between devices, from_partner(): lax.ppermute(array, axis, [(i, i ^ 1 << stride) for i in range(lax.axis_s...  5 us
    reshape x3, local copies, waits for them, and re-layouts, tile_scores(): other_tr = jnp.transpose(other.reshape(other_items, tok, width), (1, 0, 2))  2.19 us
  transfers between devices with their start and end apart: 7, of which 5 were waited for; matrix products, arithmetic and copies ran while one was open for 28% of the time, Pallas kernels for 0%

commit v1 on v0

--- a/solution.py
+++ b/solution.py
@@ -74,11 +74,45 @@
     valid = (position < lengths[:, None]) & ((position == 0) | (token_mask == 1))
     bias = jnp.where(valid, 0.0, -4.0).astype(jnp.bfloat16).reshape(-1)
     block = normed.reshape(items_dev * tok, width)
-    results = []
-    for bit in range(3):
-        other, other_bias = from_partner((block, bias), "pool", bit)
-        results.append(tile_scores(block, bias, other, other_bias, tok))
-    return jnp.concatenate(results, axis=1)
+    n_tok = items_dev * tok
+    packed = jnp.concatenate([block, bias.reshape(-1, width)], axis=0)
+
+    pool_index = lax.axis_index("pool")
+    parity = (pool_index ^ (pool_index >> 1) ^ (pool_index >> 2)) & 1
+    is_a = (pool_index & 1) == 0
+
+    def par(p):
+        return (p ^ (p >> 1) ^ (p >> 2)) & 1
+
+    send_pairs = [(p, p ^ (4 if par(p) else 2)) for p in range(n_pool)]
+    back_pairs = [(t, s) for s, t in send_pairs]
+    chip_pairs = [(p, p ^ 1) for p in range(n_pool)]
+
+    z_recv = lax.ppermute(packed, "pool", send_pairs)
+    c_recv = lax.ppermute(packed, "pool", chip_pairs)
+
+    half = n_tok // 2
+    c_blk, c_bias = c_recv[:n_tok], c_recv[n_tok:].reshape(-1)
+    query = jnp.where(is_a, block[:half], c_blk[half:])
+    query_bias = jnp.where(is_a, bias[:half], c_bias[half:])
+    other = jnp.where(is_a, c_blk, block)
+    other_bias = jnp.where(is_a, c_bias, bias)
+    part = tile_scores(query, query_bias, other, other_bias, tok)
+    part_recv = lax.ppermute(part, "pool", chip_pairs)
+    joined = jnp.where(
+        is_a,
+        jnp.concatenate([part, part_recv], axis=0),
+        jnp.concatenate([part_recv, part], axis=0),
+    )
+    tile0 = jnp.where(is_a, joined, joined.T)
+
+    z_blk, z_bias = z_recv[:n_tok], z_recv[n_tok:].reshape(-1)
+    tile_z = tile_scores(block, bias, z_blk, z_bias, tok)
+    tile_back = lax.ppermute(tile_z.T, "pool", back_pairs)
+    via_bit1 = parity == 1
+    col1 = jnp.where(via_bit1, tile_z, tile_back)
+    col2 = jnp.where(via_bit1, tile_back, tile_z)
+    return jnp.concatenate([tile0, col1, col2], axis=1)
 
 
 def solution(mesh):

time: 87.1 us -> 59.4 us (0.68)
  matrix products: 29.5 us -> 14.6 us
  waiting for transfers between devices: 34.3 us -> 21.9 us
  starting transfers between devices: 12.3 us -> 7.67 us
  other arithmetic: 3.51 us -> 7.67 us
    ppermute x6 -> x4, waiting for transfers between devices: 33.2 us -> 6.75 us  [the longest x1 3.55 us: shards(): tile_back = lax.ppermute(tile_z.T, 'pool', back_pairs)]
    all_to_all x1, waiting for transfers between devices: 1.08 us -> 15.2 us  [shards(): lax.all_to_all(outgoing, ('enc', 'pool'), split_axis=0, concat_axis=0, ti...]
    dot_general x6 -> x3, matrix products: 9.88 us -> 4.85 us  [one_block(): jnp.einsum('trh,ch->trc', turned, other, preferred_element_type=jnp.float32)]
    ppermute x6 -> x4, starting transfers between devices: 5 us -> 0.37 us  [the longest x1 0.28 us: shards(): tile_back = lax.ppermute(tile_z.T, 'pool', back_pairs)]
    dot_general x6 -> x3, matrix products: 7.66 us -> 3.79 us  [one_block(): jnp.einsum('ubh,qh->ubq', other_tr, flat, preferred_element_type=jnp.floa...]
    dot_general x6 -> x3, matrix products: 6.47 us -> 3.22 us  [one_block(): jnp.dot(back, other_select, precision=lax.Precision.HIGHEST, preferred_el...]
    dot_general x6 -> x3, matrix products: 5.52 us -> 2.77 us  [one_block(): jnp.dot(fore, select, precision=lax.Precision.HIGHEST, preferred_element_...]
    reshape x3 -> x1, local copies, waits for them, and re-layouts: 2.19 us -> 0.21 us  [tile_scores(): other_tr = jnp.transpose(other.reshape(other_items, tok, width), (1, 0, 2))]
  transfers between devices with their start and end apart: 7 -> 5, of which waited for: 5 -> 4; matrix products, arithmetic and copies ran while one was open for 28% -> 38% of each run, Pallas kernels for 0% -> 0%
where the time goes in v1:
time: 59.4 us; the launch traced here: 58.9 us
  waiting for transfers between devices  21.9 us (37%)
  matrix products  14.6 us (25%)
  other arithmetic  7.67 us (13%)
  starting transfers between devices  7.67 us (13%)
  local copies, waits for them, and re-layouts  6.51 us (11%)
    all_to_all x1, waiting for transfers between devices, shards(): lax.all_to_all(outgoing, ('enc', 'pool'), split_axis=0, concat_axis=0, ti...  15.2 us
    all_to_all x1, starting transfers between devices, shards(): lax.all_to_all(outgoing, ('enc', 'pool'), split_axis=0, concat_axis=0, ti...  7.3 us
    dot_general x3, matrix products, one_block(): jnp.einsum('trh,ch->trc', turned, other, preferred_element_type=jnp.float32)  4.85 us
    dot_general x3, matrix products, one_block(): jnp.einsum('ubh,qh->ubq', other_tr, flat, preferred_element_type=jnp.floa...  3.79 us
    ppermute x1, waiting for transfers between devices, shards(): tile_back = lax.ppermute(tile_z.T, 'pool', back_pairs)  3.55 us
    dot_general x3, matrix products, one_block(): jnp.dot(back, other_select, precision=lax.Precision.HIGHEST, preferred_el...  3.22 us
    ppermute x1, waiting for transfers between devices, shards(): z_recv = lax.ppermute(packed, 'pool', send_pairs)  3.09 us
    dot_general x3, matrix products, one_block(): jnp.dot(fore, select, precision=lax.Precision.HIGHEST, preferred_element_...  2.77 us
  transfers between devices with their start and end apart: 5, of which 4 were waited for; matrix products, arithmetic and copies ran while one was open for 38% of the time, Pallas kernels for 0%

profile of v1, /device:TPU:0, one launch (start us, length us, event | category | flops | bytes accessed | tf_op | source)
XLA Modules:
  0.0 58.9 jit_solution(9086602391619472722)
XLA Ops:
  0.0 0.8 %reshape.199 = s32[32,8,8]{2,1,0:T(8,128)S(1)} reshape(s32[2048]{0:T(1024)} %param.7) | data formatting | bytes 16384 | tf_op jit(solution)/shard_map/reshape | solution.py:62
  0.9 0.1 reshape.226
  1.0 0.0 copy-done
  1.1 0.8 %gather_fusion = bf16[256,8,128]{2,1,0:T(8,128)(2,1)S(1)} fusion(bf16[256,8,128]{2,1,0:T(8,128)(2,1)S(1)} %copy-done, s32[1024]{0:T(1024)S(1)} %pad_clamp_fusion), kind=kCustom, calls=%fused_computation | custom fusion | bytes 1049600 | tf_op jit(solution)/shard_map/jit(_take)/gather | solution.py:64
  1.9 0.0 copy-start.4
  1.9 1.1 %broadcast_select_fusion = bf16[32,8,8,128]{3,2,1,0:T(8,128)(2,1)} fusion(bf16[32,8,8,128]{3,2,1,0:T(8,128)(2,1)S(1)} %bitcast.123, pred[32,8]{1,0:T(8,128)(4,1)S(1)} %compare_and_fusion), kind=kLoop, calls=%fused_computation.65 | loop fusion | flops 262144 | bytes 1048832 | tf_op jit(solution)/shard_map/jit(_take)/select_n | solution.py:64
  3.0 7.3 %all-to-all-start = ((bf16[32,8,8,128]{3,2,1,0:T(8,128)(2,1)}), bf16[32,8,8,128]{3,2,1,0:T(8,128)(2,1)S(1)}, u32[]{:S(2)}, u32[]{:S(2)}) async-start(bf16[32,8,8,128]{3,2,1,0:T(8,128)(2,1)} %broadcast_select_fusion), calls=%async_computation | async-start | bytes 1048576 | tf_op jit(solution)/shard_map/all_to_all | solution.py:65
  10.3 0.1 copy.73
  10.4 0.1 broadcast_compare_fusion
  10.5 0.1 reshape_reshape.2
  10.6 0.1 reshape.204
  10.7 0.1 copy.98
  10.8 0.1 eq.121
  10.9 0.6 add_select_fusion.1
  11.5 15.2 %all-to-all-done = bf16[32,8,8,128]{3,2,1,0:T(8,128)(2,1)S(1)} async-done(((bf16[32,8,8,128]{3,2,1,0:T(8,128)(2,1)}), bf16[32,8,8,128]{3,2,1,0:T(8,128)(2,1)S(1)}, u32[]{:S(2)}, u32[]{:S(2)}) %all-to-all-start) | async-done | bytes 524320 | tf_op jit(solution)/shard_map/all_to_all | solution.py:65
  26.7 0.3 multiply_reduce_fusion
  27.0 0.1 copy.75
  27.2 0.1 reshape.216
  27.3 0.2 copy.76
  27.5 0.2 sqrt.24
  27.6 0.1 reshape.237
  27.7 0.1 convert_element_type.100
  27.9 0.1 copy.74
  28.0 0.3 fusion.31
  28.3 0.8 %pad_maximum_fusion = bf16[2064,128]{1,0:T(8,128)(2,1)} fusion(bf16[16,128]{1,0:T(8,128)(2,1)S(1)} %reshape_reshape.2, bf16[2048,128]{1,0:T(8,128)(2,1)S(1)} %fusion.31), kind=kLoop, calls=%fused_computation.48 | loop fusion | flops 1056768 | bytes 1056768 | tf_op jit(solution)/shard_map/concatenate | solution.py:78
  29.2 0.0 collective-permute-start
  29.2 0.1 reshape.238
  29.3 0.2 sqrt.26
  29.5 0.2 fusion.35
  29.7 1.1 %divide_convert_fusion.1 = bf16[2,1024,128]{2,1,0:T(8,128)(2,1)} fusion(f32[2,1024,128]{2,1,0:T(8,128)S(1)} %bitcast.119, f32[2,1024]{1,0:T(2,128)S(1)} %sqrt.26), kind=kLoop, calls=%fused_computation.43 | loop fusion | flops 524288 | bytes 1581056 | tf_op jit(solution)/shard_map/convert_element_type | solution.py:70
  30.8 0.3 fusion.44
  31.2 0.1 collective-permute-done
  31.3 0.1 slice.46
  31.4 0.6 %convert_bitcast_fusion.1 = (f32[32,32]{0,1:T(8,128)}, bf16[32,32]{1,0:T(8,128)(2,1)S(1)}) fusion(bf16[32,32]{1,0:T(8,128)(2,1)S(1)} %slice.46, pred[]{:T(512)S(6)} %eq.105, bf16[64,32]{1,0:T(8,128)(2,1)S(1)} %get-tuple-element.199), kind=kLoop, calls=%fused_computation.84 | loop fusion | flops 2048 | bytes 10241 | tf_op jit(solution)/shard_map/while/body/eval_jaxpr/add | solution.py:42
  32.0 0.7 %slice.38 = bf16[1024]{0:T(1024)(128)(2,1)} reshape(bf16[32,32]{1,0:T(8,128)(2,1)S(1)} %get-tuple-element.203) | data formatting | bytes 4096 | tf_op jit(solution)/shard_map/slice | solution.py:97
  32.7 0.7 %reshape.201 = bf16[64,32]{1,0:T(8,128)(2,1)} reshape(bf16[16,128]{1,0:T(8,128)(2,1)S(1)} %slice.57) | data formatting | bytes 8192 | tf_op jit(solution)/shard_map/reshape | solution.py:95
  33.4 0.7 %convert_bitcast_fusion = f32[32,64]{0,1:T(8,128)S(1)} fusion(bf16[64,32]{1,0:T(8,128)(2,1)} %reshape.201, bf16[64,32]{1,0:T(8,128)(2,1)S(1)} %get-tuple-element.199, pred[]{:T(512)S(6)} %eq.105), kind=kLoop, calls=%fused_computation.79 | loop fusion | flops 4096 | bytes 16385 | tf_op jit(solution)/shard_map/transpose | solution.py:19
  34.1 0.7 %copy.81 = f32[32,64]{1,0:T(8,128)} copy(f32[32,64]{0,1:T(8,128)S(1)} %convert_bitcast_fusion) | data formatting | bytes 16384 | tf_op jit(solution)/shard_map/transpose | solution.py:19
  34.8 0.3 slice_select_fusion
  35.2 0.3 copy-done.5
  35.5 1.3 %add_reduce_fusion.3 = f32[64,1024]{1,0:T(8,128)S(1)} fusion(f32[32,64]{1,0:T(8,128)S(1)} %copy-done.5, bf16[64,32,128]{2,1,0:T(8,128)(2,1)S(1)} %bitcast.124, bf16[1024,128]{1,0:T(8,128)(2,1)S(1)} %slice_select_fusion.1), kind=kOutput, calls=%fused_computation.37 | convolution fusion | flops 540999680 | bytes 1056768 | tf_op jit(solution)/shard_map/while/body/eval_jaxpr/ubh,qh->ubq/dot_general | solution.py:35
  36.8 0.9 %fusion.42 = f32[32,64]{1,0:T(8,128)S(1)} fusion(f32[64,1024]{1,0:T(8,128)S(1)} %add_reduce_fusion.3, s32[1024]{0:T(1024)S(1)} %copy-done.7, pred[1024]{0:T(1024)(128)(4,1)S(1)} %fusion.63), kind=kOutput, calls=%fused_computation.59 | convolution fusion | flops 25264128 | bytes 275456 | tf_op jit(solution)/shard_map/while/body/eval_jaxpr/dot_general | solution.py:38
  37.8 0.1 copy.83
  37.8 2.3 %add_reduce_fusion.2 = f32[32,2048]{1,0:T(8,128)S(1)} fusion(f32[32,32]{1,0:T(8,128)S(1)} %copy.83, bf16[2048,128]{1,0:T(8,128)(2,1)} %copy-done.2, bf16[1,32,32,128]{3,2,1,0:T(8,128)(2,1)S(1)} %bitcast.130), kind=kOutput, calls=%fused_computation.36 | convolution fusion | flops 540999680 | bytes 1052672 | tf_op jit(solution)/shard_map/while/body/eval_jaxpr/trh,ch->trc/dot_general | solution.py:41
  40.2 1.1 %fusion.30 = f32[32,64]{1,0:T(8,128)S(1)} fusion(f32[32,64]{1,0:T(8,128)S(1)} %fusion.42, f32[32,2048]{1,0:T(8,128)S(1)} %add_reduce_fusion.2, s32[2048]{0:T(1024)S(1)} %add_select_fusion, pred[2048]{0:T(1024)(128)(4,1)S(1)} %fusion.61), kind=kOutput, calls=%fused_computation.39 | convolution fusion | flops 50728960 | bytes 288768 | tf_op jit(solution)/shard_map/while/body/eval_jaxpr/dot_general | solution.py:43
  41.2 0.1 collective-permute-start.1
  41.3 3.1 %collective-permute-done.2 = bf16[2064,128]{1,0:T(8,128)(2,1)S(1)} collective-permute-done((bf16[2064,128]{1,0:T(8,128)(2,1)}, bf16[2064,128]{1,0:T(8,128)(2,1)S(1)}, u32[]{:S(2)}, u32[]{:S(2)}) %collective-permute-start.2) | collective-permute-done | bytes 528416 | tf_op jit(solution)/shard_map/ppermute | solution.py:91
  44.4 0.2 copy.113
  44.7 0.1 reshape.221
  44.7 0.1 copy.92
  44.8 9.3 %while.3 = (s32[]{:T(128)}, f32[2,32,64]{2,1,0:T(8,128)S(1)}, pred[2,1024]{1,0:T(4,128)(4,1)S(1)}, bf16[2,1024,128]{2,1,0:T(8,128)(2,1)S(1)}, bf16[32,64,128]{2,...) while((s32[]{:T(128)}, f32[2,32,64]{2,1,0:T(8,128)S(1)}, ...), condition=%wide.region_6.7_spmd.clone, body=%wide.region_3.6_spmd.clone.sunk | while | flops 1157992448 | bytes 3232913 | solution.py:48
  44.8 1.3 %add_reduce_fusion.6 = f32[1024,64]{0,1:T(8,128)S(1)} fusion(f32[32,64]{1,0:T(8,128)S(1)} %bitcast.136, bf16[32,64,128]{2,1,0:T(8,128)(2,1)S(1)} %get-tuple-element.307, bf16[2,1024,128]{2,1,0:T(8,128)(2,1)S(1)} %get-tuple-element.306, s32[]{:T(128)} %get-tuple-element.290), kind=kOutput, calls=%fused_computation.4.clone.1 | convolution fusion | flops 540999680 | bytes 1064964 | tf_op jit(solution)/shard_map/while/body/eval_jaxpr/ubh,qh->ubq/dot_general | solution.py:35
  46.2 0.9 %fusion.89 = f32[32,64]{1,0:T(8,128)S(1)} fusion(f32[1024,64]{0,1:T(8,128)S(1)} %add_reduce_fusion.6, s32[1024]{0:T(1024)S(1)} %get-tuple-element.312, pred[1024]{0:T(1024)(128)(4,1)S(1)} %dynamic-slice_reduce_fusion.2), kind=kOutput, calls=%fused_computation.17.clone.1 | convolution fusion | flops 25264128 | bytes 275456 | tf_op jit(solution)/shard_map/while/body/eval_jaxpr/dot_general | solution.py:38
  47.1 1.3 %add_reduce_fusion.7 = f32[32,2048]{1,0:T(8,128)S(1)} fusion(f32[32,32]{1,0:T(8,128)S(1)} %bitcast.128, bf16[2048,128]{1,0:T(8,128)(2,1)S(1)} %get-tuple-element.310, bf16[1,32,32,128]{3,1,2,0:T(8,128)(2,1)S(1)} %constant_dynamic-slice_fusion.5), kind=kOutput, calls=%fused_computation.3.clone.1 | convolution fusion | flops 540999680 | bytes 1052672 | tf_op jit(solution)/shard_map/while/body/eval_jaxpr/trh,ch->trc/dot_general | solution.py:41
  48.4 1.1 %fusion.90 = f32[2,32,64]{2,1,0:T(8,128)S(1)} fusion(f32[2,32,64]{2,1,0:T(8,128)S(1)} %get-tuple-element.291, s32[]{:T(128)} %get-tuple-element.290, f32[32,64]{1,0:T(8,128)S(1)} %fusion.89, f32[32,2048]{1,0:T(8,128)S(1)} %add_reduce_fusion.7, s32[2048]{0:T(1024)S(1)} %get-tuple-element.313, pred[2048]{0:T(1024)(128)(4,1)S(1)} %get-tuple-element.314), kind=kOutput, calls=%fused_computation.8.clone.1 | convolution fusion | flops 50728960 | bytes 305156 | tf_op jit(solution)/shard_map/while/body/eval_jaxpr/dot_general | solution.py:43
  49.5 1.3 %add_reduce_fusion.6 = f32[1024,64]{0,1:T(8,128)S(1)} fusion(f32[32,64]{1,0:T(8,128)S(1)} %bitcast.136, bf16[32,64,128]{2,1,0:T(8,128)(2,1)S(1)} %get-tuple-element.307, bf16[2,1024,128]{2,1,0:T(8,128)(2,1)S(1)} %get-tuple-element.306, s32[]{:T(128)} %get-tuple-element.290), kind=kOutput, calls=%fused_computation.4.clone.1 | convolution fusion | flops 540999680 | bytes 1064964 | tf_op jit(solution)/shard_map/while/body/eval_jaxpr/ubh,qh->ubq/dot_general | solution.py:35
  50.8 0.9 %fusion.89 = f32[32,64]{1,0:T(8,128)S(1)} fusion(f32[1024,64]{0,1:T(8,128)S(1)} %add_reduce_fusion.6, s32[1024]{0:T(1024)S(1)} %get-tuple-element.312, pred[1024]{0:T(1024)(128)(4,1)S(1)} %dynamic-slice_reduce_fusion.2), kind=kOutput, calls=%fused_computation.17.clone.1 | convolution fusion | flops 25264128 | bytes 275456 | tf_op jit(solution)/shard_map/while/body/eval_jaxpr/dot_general | solution.py:38
  51.8 1.3 %add_reduce_fusion.7 = f32[32,2048]{1,0:T(8,128)S(1)} fusion(f32[32,32]{1,0:T(8,128)S(1)} %bitcast.128, bf16[2048,128]{1,0:T(8,128)(2,1)S(1)} %get-tuple-element.310, bf16[1,32,32,128]{3,1,2,0:T(8,128)(2,1)S(1)} %constant_dynamic-slice_fusion.5), kind=kOutput, calls=%fused_computation.3.clone.1 | convolution fusion | flops 540999680 | bytes 1052672 | tf_op jit(solution)/shard_map/while/body/eval_jaxpr/trh,ch->trc/dot_general | solution.py:41
  53.1 1.1 %fusion.90 = f32[2,32,64]{2,1,0:T(8,128)S(1)} fusion(f32[2,32,64]{2,1,0:T(8,128)S(1)} %get-tuple-element.291, s32[]{:T(128)} %get-tuple-element.290, f32[32,64]{1,0:T(8,128)S(1)} %fusion.89, f32[32,2048]{1,0:T(8,128)S(1)} %add_reduce_fusion.7, s32[2048]{0:T(1024)S(1)} %get-tuple-element.313, pred[2048]{0:T(1024)(128)(4,1)S(1)} %get-tuple-element.314), kind=kOutput, calls=%fused_computation.8.clone.1 | convolution fusion | flops 50728960 | bytes 305156 | tf_op jit(solution)/shard_map/while/body/eval_jaxpr/dot_general | solution.py:43
  54.2 0.1 copy.95
  54.2 0.3 collective-permute-start.3
  54.5 0.1 copy.84
  54.6 3.5 %collective-permute-done.3 = f32[64,64]{1,0:T(8,128)S(1)} collective-permute-done((f32[64,64]{1,0:T(8,128)S(1)}, f32[64,64]{1,0:T(8,128)S(1)}, u32[]{:S(2)}, u32[]{:S(2)}) %collective-permute-start.3) | collective-permute-done | bytes 16416 | tf_op jit(solution)/shard_map/ppermute | solution.py:111
  58.2 0.7 %pad_maximum_fusion.1 = f32[64,192]{1,0:T(8,128)} fusion(f32[64,64]{1,0:T(8,128)S(1)} %get-tuple-element.201, f32[64,64]{1,0:T(8,128)S(1)} %get-tuple-element.200, f32[64,64]{1,0:T(8,128)S(1)} %bitcast_select_fusion), kind=kLoop, calls=%fused_computation.74 | loop fusion | flops 24576 | bytes 98304 | tf_op jit(solution)/shard_map/concatenate | solution.py:115
  (43 shorter events, 0.4 us)
Async XLA Ops:
  0.0 1.1 %copy-start = (bf16[256,8,128]{2,1,0:T(8,128)(2,1)S(1)}, bf16[256,8,128]{2,1,0:T(8,128)(2,1)}, u32[]{:S(2)}) copy-start(bf16[256,8,128]{2,1,0:T(8,128)(2,1)} %param.6) | copy-start | bytes 1572868
  1.9 8.5 %copy-start.4 = (s32[64,32]{0,1:T(8,128)S(1)}, s32[64,32]{0,1:T(8,128)}, u32[]{:S(2)}) copy-start(s32[64,32]{0,1:T(8,128)} %param.9) | copy-start | bytes 24580
  1.9 8.5 %copy-start.8 = (s32[64]{0:T(128)S(1)}, s32[64]{0:T(128)}, u32[]{:S(2)}) copy-start(s32[64]{0:T(128)} %param.8) | copy-start | bytes 772
  3.0 23.7 %all-to-all-start = ((bf16[32,8,8,128]{3,2,1,0:T(8,128)(2,1)}), bf16[32,8,8,128]{3,2,1,0:T(8,128)(2,1)S(1)}, u32[]{:S(2)}, u32[]{:S(2)}) async-start(bf16[32,8,8,128]{3,2,1,0:T(8,128)(2,1)} %broadcast_select_fusion), calls=%async_computation | async-start | bytes 1048576 | tf_op jit(solution)/shard_map/all_to_all | solution.py:65
  29.2 2.1 %collective-permute-start = (bf16[2064,128]{1,0:T(8,128)(2,1)}, bf16[2064,128]{1,0:T(8,128)(2,1)S(1)}, u32[]{:S(2)}, u32[]{:S(2)}) collective-permute-start(bf16[2064,128]{1,0:T(8,128)(2,1)} %pad_maximum_fusion), channel_id=1, source_target_pairs={{0,1},{1,0},{2,3},{3,2},{4,5},{5,4},{6,7},{7,6},{8,9},{9,8},{10,11... | collective-permute-start | bytes 1585160 | tf_op jit(solution)/shard_map/ppermute | solution.py:92
  29.2 15.2 %collective-permute-start.2 = (bf16[2064,128]{1,0:T(8,128)(2,1)}, bf16[2064,128]{1,0:T(8,128)(2,1)S(1)}, u32[]{:S(2)}, u32[]{:S(2)}) collective-permute-start(bf16[2064,128]{1,0:T(8,128)(2,1)} %pad_maximum_fusion), channel_id=1, source_target_pairs={{0,2},{1,5},{2,6},{3,1},{4,0},{5,7},{6,4},{7,3},{8,10},{9,13},{10,... | collective-permute-start | bytes 1585160 | tf_op jit(solution)/shard_map/ppermute | solution.py:91
  34.8 0.7 %copy-start.5 = (f32[32,64]{1,0:T(8,128)S(1)}, f32[32,64]{1,0:T(8,128)}, u32[]{:S(2)}) copy-start(f32[32,64]{1,0:T(8,128)} %copy.81) | copy-start | bytes 24580
  35.1 2.6 %copy-start.2 = (bf16[2048,128]{1,0:T(8,128)(2,1)}, bf16[2048,128]{1,0:T(8,128)(2,1)S(1)}, u32[]{:S(2)}) copy-start(bf16[2048,128]{1,0:T(8,128)(2,1)S(1)} %slice_select_fusion) | copy-start | bytes 1572868
  35.5 1.3 %copy-start.6 = (bf16[1024]{0:T(1024)(128)(2,1)S(1)}, bf16[1024]{0:T(1024)(128)(2,1)}, u32[]{:S(2)}) copy-start(bf16[1024]{0:T(1024)(128)(2,1)} %slice.38) | copy-start | bytes 6148
  35.5 1.3 %copy-start.7 = (s32[1024]{0:T(1024)S(1)}, s32[1024]{0:T(1024)}, u32[]{:S(2)}) copy-start(s32[1024]{0:T(1024)} %add_select_fusion.1) | copy-start | bytes 12292
  35.5 2.3 %copy-start.3 = (f32[32,32]{0,1:T(8,128)S(1)}, f32[32,32]{0,1:T(8,128)}, u32[]{:S(2)}) copy-start(f32[32,32]{0,1:T(8,128)} %get-tuple-element.202) | copy-start | bytes 12292
  41.2 3.6 %copy-start.1 = (bf16[2,1024,128]{2,1,0:T(8,128)(2,1)S(1)}, bf16[2,1024,128]{2,1,0:T(8,128)(2,1)}, u32[]{:S(2)}) copy-start(bf16[2,1024,128]{2,1,0:T(8,128)(2,1)} %divide_convert_fusion.1) | copy-start | bytes 1572868
  41.2 13.3 %collective-permute-start.1 = (f32[32,64]{1,0:T(8,128)S(1)}, f32[32,64]{1,0:T(8,128)S(1)}, u32[]{:S(2)}, u32[]{:S(2)}) collective-permute-start(f32[32,64]{1,0:T(8,128)S(1)} %fusion.30), channel_id=1, source_target_pairs={{0,1},{1,0},{2,3},{3,2},{4,5},{5,4},{6,7},{7,6},{8,9},{9,8},{10,11... | collective-permute-start | bytes 24584 | tf_op jit(solution)/shard_map/ppermute | solution.py:101
  54.2 3.9 %collective-permute-start.3 = (f32[64,64]{1,0:T(8,128)S(1)}, f32[64,64]{1,0:T(8,128)S(1)}, u32[]{:S(2)}, u32[]{:S(2)}) collective-permute-start(f32[64,64]{1,0:T(8,128)S(1)} %bitcast.135), channel_id=1, source_target_pairs={{2,0},{5,1},{6,2},{1,3},{0,4},{7,5},{4,6},{3,7},{10,8},{13,9},{14,... | collective-permute-start | bytes 49160 | tf_op jit(solution)/shard_map/ppermute | solution.py:111

commit v2 on v1

--- a/solution.py
+++ b/solution.py
@@ -59,13 +59,16 @@
     items_dev = lengths.shape[0]
     per = items_dev // n_pool
     pool_index = lax.axis_index("pool")
-    table = slot_items.reshape(owners, n_pool, per)
-    mine = lax.dynamic_index_in_dim(table, pool_index, 1, keepdims=False) - pool_index * group
-    outgoing = jnp.take(encoded, mine, axis=0)
-    arrived = lax.all_to_all(outgoing, ("enc", "pool"), split_axis=0, concat_axis=0, tiled=True)
-    arrived = arrived.reshape(n_enc, n_pool, per, toks, width)
+    enc_index = lax.axis_index("enc")
+    table = slot_items.reshape(n_enc, n_pool, n_pool, per)
+    mine = lax.dynamic_index_in_dim(table, pool_index, 2, keepdims=False) - pool_index * group
+    order = jnp.transpose(mine, (1, 2, 0))
+    outgoing = jnp.take(encoded, order, axis=0)
+    across = lax.all_to_all(outgoing, "enc", split_axis=2, concat_axis=2, tiled=True)
     tok = n_enc * toks
-    slotted = jnp.transpose(arrived, (1, 2, 0, 3, 4)).reshape(items_dev, tok, width)
+    across = across.reshape(n_pool, per, tok, width)
+    slotted = lax.all_to_all(across, "pool", split_axis=0, concat_axis=0, tiled=True)
+    slotted = slotted.reshape(items_dev, tok, width)
     values = slotted.astype(jnp.float32)
     normed = (values / jnp.sqrt(jnp.sum(values * values, axis=-1, keepdims=True) + 1e-06)).astype(
         jnp.bfloat16

time: 59.4 us -> 67.8 us (1.14)
  blocking collectives: 0 us -> 13.5 us
  starting transfers between devices: 7.67 us -> 5.29 us
  local copies, waits for them, and re-layouts: 6.51 us -> 5.35 us
  other arithmetic: 7.67 us -> 6.72 us
    all_to_all x0 -> x1, blocking collectives: none -> 13.5 us  [shards(): lax.all_to_all(outgoing, 'enc', split_axis=2, concat_axis=2, tiled=True)]
    all_to_all x1, starting transfers between devices: 7.3 us -> 4.88 us  [shards(): lax.all_to_all(across, 'pool', split_axis=0, concat_axis=0, tiled=True)]
    all_to_all x1, waiting for transfers between devices: 15.2 us -> 13.6 us  [shards(): lax.all_to_all(across, 'pool', split_axis=0, concat_axis=0, tiled=True)]
    ppermute x1, waiting for transfers between devices: 3.09 us -> 4.03 us  [shards(): z_recv = lax.ppermute(packed, 'pool', send_pairs)]
    all_to_all x0 -> x1, local copies, waits for them, and re-layouts: none -> 0.88 us  [shards(): lax.all_to_all(outgoing, 'enc', split_axis=2, concat_axis=2, tiled=True)]
    select_n x2, other arithmetic: 1.13 us -> 0.34 us  [shards(): outgoing = jnp.take(encoded, order, axis=0)]
    concatenate x1, other arithmetic: 0.81 us -> 0.04 us  [shards(): packed = jnp.concatenate([block, bias.reshape(-1, width)], axis=0)]
    sqrt x6 -> x2, local copies, waits for them, and re-layouts: 0.84 us -> 0.16 us  [shards(): jnp.sqrt(jnp.sum(values * values, axis=-1, keepdims=True) + 1e-06)]
  transfers between devices with their start and end apart: 5 -> 5, of which waited for: 4 -> 3; matrix products, arithmetic and copies ran while one was open for 38% -> 32% of each run, Pallas kernels for 0% -> 0%
where the time goes in v2:
time: 67.8 us; the launch traced here: 67.5 us
  waiting for transfers between devices  21.4 us (32%)
  matrix products  14.7 us (22%)
  blocking collectives  13.5 us (20%)
  other arithmetic  6.72 us (10%)
  local copies, waits for them, and re-layouts  5.35 us (8%)
  starting transfers between devices  5.29 us (8%)
    all_to_all x1, waiting for transfers between devices, shards(): lax.all_to_all(across, 'pool', split_axis=0, concat_axis=0, tiled=True)  13.6 us
    all_to_all x1, blocking collectives, shards(): lax.all_to_all(outgoing, 'enc', split_axis=2, concat_axis=2, tiled=True)  13.5 us
    all_to_all x1, starting transfers between devices, shards(): lax.all_to_all(across, 'pool', split_axis=0, concat_axis=0, tiled=True)  4.88 us
    dot_general x3, matrix products, one_block(): jnp.einsum('trh,ch->trc', turned, other, preferred_element_type=jnp.float32)  4.87 us
    ppermute x1, waiting for transfers between devices, shards(): z_recv = lax.ppermute(packed, 'pool', send_pairs)  4.03 us
    dot_general x3, matrix products, one_block(): jnp.einsum('ubh,qh->ubq', other_tr, flat, preferred_element_type=jnp.floa...  3.83 us
    ppermute x1, waiting for transfers between devices, shards(): tile_back = lax.ppermute(tile_z.T, 'pool', back_pairs)  3.78 us
    dot_general x3, matrix products, one_block(): jnp.dot(back, other_select, precision=lax.Precision.HIGHEST, preferred_el...  3.22 us
  transfers between devices with their start and end apart: 5, of which 3 were waited for; matrix products, arithmetic and copies ran while one was open for 32% of the time, Pallas kernels for 0%

profile of v2, /device:TPU:0, one launch (start us, length us, event | category | flops | bytes accessed | tf_op | source)
XLA Modules:
  0.0 67.5 jit_solution(10830032673529859648)
XLA Ops:
  0.0 0.0 copy-start
  0.0 0.8 %reshape.168 = s32[4,8,8,8]{3,2,1,0:T(8,128)S(1)} reshape(s32[2048]{0:T(1024)} %param.7) | data formatting | bytes 16384 | tf_op jit(solution)/shard_map/reshape | solution.py:63
  0.9 0.1 copy.57
  1.0 0.1 reshape.189
  1.2 0.1 copy.56
  1.3 0.8 %gather_fusion = bf16[256,8,128]{2,1,0:T(8,128)(2,1)S(1)} fusion(bf16[256,8,128]{2,1,0:T(8,128)(2,1)S(1)} %copy-done, s32[1024]{0:T(1024)S(1)} %pad_clamp_fusion), kind=kCustom, calls=%fused_computation | custom fusion | bytes 1049600 | tf_op jit(solution)/shard_map/jit(_take)/gather | solution.py:66
  2.1 0.3 broadcast_select_fusion
  2.5 0.1 copy.58
  2.6 13.5 %all_to_all.10 = bf16[8,8,4,8,128]{4,3,1,0,2:T(8,128)(2,1)S(1)} all-to-all(bf16[8,8,4,8,128]{4,3,1,0,2:T(8,128)(2,1)S(1)} %copy.58), channel_id=1, replica_groups=mesh['enc'=4,'pool'=8] {'enc'}, dimensions={2} | all-to-all | bytes 1048576 | tf_op jit(solution)/shard_map/all_to_all | solution.py:67
  16.1 0.9 %copy.87 = bf16[8,8,4,8,128]{4,3,2,1,0:T(8,128)(2,1)} copy(bf16[8,8,4,8,128]{4,3,1,0,2:T(8,128)(2,1)S(1)} %all_to_all.10) | data formatting | bytes 1048576 | tf_op jit(solution)/shard_map/all_to_all | solution.py:67
  17.0 4.9 %all-to-all-start.1 = ((bf16[8,8,32,128]{3,2,1,0:T(8,128)(2,1)}), bf16[8,8,32,128]{3,2,1,0:T(8,128)(2,1)S(1)}, u32[]{:S(2)}, u32[]{:S(2)}) async-start(bf16[8,8,32,128]{3,2,1,0:T(8,128)(2,1)} %bitcast.103), calls=%async_computation.1 | async-start | bytes 1048576 | tf_op jit(solution)/shard_map/all_to_all | solution.py:70
  21.9 0.1 copy.55
  22.0 0.1 broadcast_compare_fusion
  22.1 0.1 reshape_reshape.2
  22.1 0.1 reshape.174
  22.2 0.1 copy.71
  22.3 0.1 eq.121
  22.4 0.6 add_select_fusion.1
  23.0 0.6 add_select_fusion
  23.6 13.6 %all-to-all-done.1 = bf16[8,8,32,128]{3,2,1,0:T(8,128)(2,1)S(1)} async-done(((bf16[8,8,32,128]{3,2,1,0:T(8,128)(2,1)}), bf16[8,8,32,128]{3,2,1,0:T(8,128)(2,1)S(1)}, u32[]{:S(2)}, u32[]{:S(2)}) %all-to-all-start.1) | async-done | bytes 524320 | tf_op jit(solution)/shard_map/all_to_all | solution.py:70
  37.2 0.3 multiply_reduce_fusion
  37.6 0.1 sqrt.24
  37.7 0.3 fusion.32
  38.1 0.1 collective-permute-start
  38.1 0.2 collective-permute-start.2
  38.4 0.1 sqrt.26
  38.5 0.1 convert_element_type.76
  38.6 0.2 fusion.36
  38.8 1.1 %divide_convert_fusion = bf16[2,1024,128]{2,1,0:T(8,128)(2,1)} fusion(f32[2,1024,128]{2,1,0:T(8,128)S(1)} %bitcast.124, f32[2,1024]{1,0:T(2,128)S(1)} %sqrt.26), kind=kLoop, calls=%fused_computation.44 | loop fusion | flops 524288 | bytes 1581056 | tf_op jit(solution)/shard_map/convert_element_type | solution.py:73
  40.0 0.3 fusion.45
  40.3 0.0 collective-permute-done
  40.3 0.1 slice.46
  40.4 0.6 convert_bitcast_fusion.1
  41.0 0.1 slice.38
  41.1 0.7 %reshape.171 = bf16[64,32]{1,0:T(8,128)(2,1)} reshape(bf16[16,128]{1,0:T(8,128)(2,1)S(1)} %slice.57) | data formatting | bytes 8192 | tf_op jit(solution)/shard_map/reshape | solution.py:98
  41.8 0.7 %convert_bitcast_fusion = f32[32,64]{0,1:T(8,128)S(1)} fusion(bf16[64,32]{1,0:T(8,128)(2,1)} %reshape.171, bf16[64,32]{1,0:T(8,128)(2,1)S(1)} %get-tuple-element.199, pred[]{:T(512)S(6)} %eq.105), kind=kLoop, calls=%fused_computation.80 | loop fusion | flops 4096 | bytes 16385 | tf_op jit(solution)/shard_map/transpose | solution.py:19
  42.5 0.1 copy.61
  42.6 0.4 slice_select_fusion
  43.0 1.3 %add_reduce_fusion.3 = f32[64,1024]{1,0:T(8,128)S(1)} fusion(f32[32,64]{1,0:T(8,128)S(1)} %copy.61, bf16[64,32,128]{2,1,0:T(8,128)(2,1)S(1)} %bitcast.130, bf16[1024,128]{1,0:T(8,128)(2,1)S(1)} %slice_select_fusion.1), kind=kOutput, calls=%fused_computation.37 | convolution fusion | flops 540999680 | bytes 1056768 | tf_op jit(solution)/shard_map/while/body/eval_jaxpr/ubh,qh->ubq/dot_general | solution.py:35
  44.4 0.9 %fusion.43 = f32[32,64]{1,0:T(8,128)S(1)} fusion(f32[64,1024]{1,0:T(8,128)S(1)} %add_reduce_fusion.3, s32[1024]{0:T(1024)S(1)} %copy-done.6, pred[1024]{0:T(1024)(128)(4,1)S(1)} %fusion.64), kind=kOutput, calls=%fused_computation.61 | convolution fusion | flops 25264128 | bytes 275456 | tf_op jit(solution)/shard_map/while/body/eval_jaxpr/dot_general | solution.py:38
  45.3 0.1 copy.63
  45.4 2.3 %add_reduce_fusion.2 = f32[32,2048]{1,0:T(8,128)S(1)} fusion(f32[32,32]{1,0:T(8,128)S(1)} %copy.63, bf16[2048,128]{1,0:T(8,128)(2,1)} %copy-done.2, bf16[1,32,32,128]{3,2,1,0:T(8,128)(2,1)S(1)} %bitcast.134), kind=kOutput, calls=%fused_computation.36 | convolution fusion | flops 540999680 | bytes 1052672 | tf_op jit(solution)/shard_map/while/body/eval_jaxpr/trh,ch->trc/dot_general | solution.py:41
  47.8 1.1 %fusion.30 = f32[32,64]{1,0:T(8,128)S(1)} fusion(f32[32,64]{1,0:T(8,128)S(1)} %fusion.43, f32[32,2048]{1,0:T(8,128)S(1)} %add_reduce_fusion.2, s32[2048]{0:T(1024)S(1)} %copy-done.5, pred[2048]{0:T(1024)(128)(4,1)S(1)} %fusion.62), kind=kOutput, calls=%fused_computation.39 | convolution fusion | flops 50728960 | bytes 288768 | tf_op jit(solution)/shard_map/while/body/eval_jaxpr/dot_general | solution.py:43
  48.8 0.1 collective-permute-start.1
  48.9 4.0 %collective-permute-done.2 = bf16[2064,128]{1,0:T(8,128)(2,1)S(1)} collective-permute-done((bf16[2064,128]{1,0:T(8,128)(2,1)S(1)}, bf16[2064,128]{1,0:T(8,128)(2,1)S(1)}, u32[]{:S(2)}, u32[]{:S(2)}) %collective-permute-start.2) | collective-permute-done | bytes 528416 | tf_op jit(solution)/shard_map/ppermute | solution.py:94
  53.0 0.2 copy.86
  53.2 0.1 reshape.185
  53.3 0.1 copy.67
  53.4 0.0 copy-done.1
  53.4 9.4 %while.3 = (s32[]{:T(128)}, f32[2,32,64]{2,1,0:T(8,128)S(1)}, pred[2,1024]{1,0:T(4,128)(4,1)S(1)}, bf16[2,1024,128]{2,1,0:T(8,128)(2,1)S(1)}, bf16[32,64,128]{2,...) while((s32[]{:T(128)}, f32[2,32,64]{2,1,0:T(8,128)S(1)}, ...), condition=%wide.region_6.7_spmd.clone, body=%wide.region_3.6_spmd.clone.sunk | while | flops 1157992448 | bytes 3232913 | solution.py:48
  53.4 1.3 %add_reduce_fusion.6 = f32[1024,64]{0,1:T(8,128)S(1)} fusion(f32[32,64]{1,0:T(8,128)S(1)} %bitcast.140, bf16[32,64,128]{2,1,0:T(8,128)(2,1)S(1)} %get-tuple-element.309, bf16[2,1024,128]{2,1,0:T(8,128)(2,1)S(1)} %get-tuple-element.308, s32[]{:T(128)} %get-tuple-element.292), kind=kOutput, calls=%fused_computation.4.clone.1 | convolution fusion | flops 540999680 | bytes 1064964 | tf_op jit(solution)/shard_map/while/body/eval_jaxpr/ubh,qh->ubq/dot_general | solution.py:35
  54.7 0.9 %fusion.91 = f32[32,64]{1,0:T(8,128)S(1)} fusion(f32[1024,64]{0,1:T(8,128)S(1)} %add_reduce_fusion.6, s32[1024]{0:T(1024)S(1)} %get-tuple-element.314, pred[1024]{0:T(1024)(128)(4,1)S(1)} %dynamic-slice_reduce_fusion.2), kind=kOutput, calls=%fused_computation.17.clone.1 | convolution fusion | flops 25264128 | bytes 275456 | tf_op jit(solution)/shard_map/while/body/eval_jaxpr/dot_general | solution.py:38
  55.7 1.3 %add_reduce_fusion.7 = f32[32,2048]{1,0:T(8,128)S(1)} fusion(f32[32,32]{1,0:T(8,128)S(1)} %bitcast.132, bf16[2048,128]{1,0:T(8,128)(2,1)S(1)} %get-tuple-element.312, bf16[1,32,32,128]{3,1,2,0:T(8,128)(2,1)S(1)} %constant_dynamic-slice_fusion.5), kind=kOutput, calls=%fused_computation.3.clone.1 | convolution fusion | flops 540999680 | bytes 1052672 | tf_op jit(solution)/shard_map/while/body/eval_jaxpr/trh,ch->trc/dot_general | solution.py:41
  57.0 1.1 %fusion.92 = f32[2,32,64]{2,1,0:T(8,128)S(1)} fusion(f32[2,32,64]{2,1,0:T(8,128)S(1)} %get-tuple-element.293, s32[]{:T(128)} %get-tuple-element.292, f32[32,64]{1,0:T(8,128)S(1)} %fusion.91, f32[32,2048]{1,0:T(8,128)S(1)} %add_reduce_fusion.7, s32[2048]{0:T(1024)S(1)} %get-tuple-element.315, pred[2048]{0:T(1024)(128)(4,1)S(1)} %get-tuple-element.316), kind=kOutput, calls=%fused_computation.8.clone.1 | convolution fusion | flops 50728960 | bytes 305156 | tf_op jit(solution)/shard_map/while/body/eval_jaxpr/dot_general | solution.py:43
  58.1 1.3 %add_reduce_fusion.6 = f32[1024,64]{0,1:T(8,128)S(1)} fusion(f32[32,64]{1,0:T(8,128)S(1)} %bitcast.140, bf16[32,64,128]{2,1,0:T(8,128)(2,1)S(1)} %get-tuple-element.309, bf16[2,1024,128]{2,1,0:T(8,128)(2,1)S(1)} %get-tuple-element.308, s32[]{:T(128)} %get-tuple-element.292), kind=kOutput, calls=%fused_computation.4.clone.1 | convolution fusion | flops 540999680 | bytes 1064964 | tf_op jit(solution)/shard_map/while/body/eval_jaxpr/ubh,qh->ubq/dot_general | solution.py:35
  59.4 0.9 %fusion.91 = f32[32,64]{1,0:T(8,128)S(1)} fusion(f32[1024,64]{0,1:T(8,128)S(1)} %add_reduce_fusion.6, s32[1024]{0:T(1024)S(1)} %get-tuple-element.314, pred[1024]{0:T(1024)(128)(4,1)S(1)} %dynamic-slice_reduce_fusion.2), kind=kOutput, calls=%fused_computation.17.clone.1 | convolution fusion | flops 25264128 | bytes 275456 | tf_op jit(solution)/shard_map/while/body/eval_jaxpr/dot_general | solution.py:38
  60.4 1.3 %add_reduce_fusion.7 = f32[32,2048]{1,0:T(8,128)S(1)} fusion(f32[32,32]{1,0:T(8,128)S(1)} %bitcast.132, bf16[2048,128]{1,0:T(8,128)(2,1)S(1)} %get-tuple-element.312, bf16[1,32,32,128]{3,1,2,0:T(8,128)(2,1)S(1)} %constant_dynamic-slice_fusion.5), kind=kOutput, calls=%fused_computation.3.clone.1 | convolution fusion | flops 540999680 | bytes 1052672 | tf_op jit(solution)/shard_map/while/body/eval_jaxpr/trh,ch->trc/dot_general | solution.py:41
  61.6 1.1 %fusion.92 = f32[2,32,64]{2,1,0:T(8,128)S(1)} fusion(f32[2,32,64]{2,1,0:T(8,128)S(1)} %get-tuple-element.293, s32[]{:T(128)} %get-tuple-element.292, f32[32,64]{1,0:T(8,128)S(1)} %fusion.91, f32[32,2048]{1,0:T(8,128)S(1)} %add_reduce_fusion.7, s32[2048]{0:T(1024)S(1)} %get-tuple-element.315, pred[2048]{0:T(1024)(128)(4,1)S(1)} %get-tuple-element.316), kind=kOutput, calls=%fused_computation.8.clone.1 | convolution fusion | flops 50728960 | bytes 305156 | tf_op jit(solution)/shard_map/while/body/eval_jaxpr/dot_general | solution.py:43
  62.7 0.1 copy.70
  62.8 0.0 collective-permute-start.3
  62.9 0.0 collective-permute-done.1
  62.9 0.1 copy.64
  63.0 3.8 %collective-permute-done.3 = f32[64,64]{1,0:T(8,128)S(1)} collective-permute-done((f32[64,64]{1,0:T(8,128)S(1)}, f32[64,64]{1,0:T(8,128)S(1)}, u32[]{:S(2)}, u32[]{:S(2)}) %collective-permute-start.3) | collective-permute-done | bytes 16416 | tf_op jit(solution)/shard_map/ppermute | solution.py:114
  66.8 0.7 %pad_maximum_fusion.1 = f32[64,192]{1,0:T(8,128)} fusion(f32[64,64]{1,0:T(8,128)S(1)} %get-tuple-element.201, f32[64,64]{1,0:T(8,128)S(1)} %get-tuple-element.200, f32[64,64]{1,0:T(8,128)S(1)} %bitcast_select_fusion), kind=kLoop, calls=%fused_computation.76 | loop fusion | flops 24576 | bytes 98304 | tf_op jit(solution)/shard_map/concatenate | solution.py:118
  (40 shorter events, 0.4 us)
Async XLA Ops:
  0.0 1.3 %copy-start = (bf16[256,8,128]{2,1,0:T(8,128)(2,1)S(1)}, bf16[256,8,128]{2,1,0:T(8,128)(2,1)}, u32[]{:S(2)}) copy-start(bf16[256,8,128]{2,1,0:T(8,128)(2,1)} %param.6) | copy-start | bytes 1572868
  16.1 5.8 %copy-start.4 = (s32[64,32]{0,1:T(8,128)S(1)}, s32[64,32]{0,1:T(8,128)}, u32[]{:S(2)}) copy-start(s32[64,32]{0,1:T(8,128)} %param.9) | copy-start | bytes 24580
  16.1 5.9 %copy-start.7 = (s32[64]{0:T(128)S(1)}, s32[64]{0:T(128)}, u32[]{:S(2)}) copy-start(s32[64]{0:T(128)} %param.8) | copy-start | bytes 772
  17.0 20.2 %all-to-all-start.1 = ((bf16[8,8,32,128]{3,2,1,0:T(8,128)(2,1)}), bf16[8,8,32,128]{3,2,1,0:T(8,128)(2,1)S(1)}, u32[]{:S(2)}, u32[]{:S(2)}) async-start(bf16[8,8,32,128]{3,2,1,0:T(8,128)(2,1)} %bitcast.103), calls=%async_computation.1 | async-start | bytes 1048576 | tf_op jit(solution)/shard_map/all_to_all | solution.py:70
  38.1 2.3 %collective-permute-start = (bf16[2064,128]{1,0:T(8,128)(2,1)S(1)}, bf16[2064,128]{1,0:T(8,128)(2,1)S(1)}, u32[]{:S(2)}, u32[]{:S(2)}) collective-permute-start(bf16[2064,128]{1,0:T(8,128)(2,1)S(1)} %pad_maximum_fusion), channel_id=1, source_target_pairs={{0,1},{1,0},{2,3},{3,2},{4,5},{5,4},{6,7},{7,6},{8,9},{9,8},{10,11... | collective-permute-start | bytes 1585160 | tf_op jit(solution)/shard_map/ppermute | solution.py:95
  38.1 14.8 %collective-permute-start.2 = (bf16[2064,128]{1,0:T(8,128)(2,1)S(1)}, bf16[2064,128]{1,0:T(8,128)(2,1)S(1)}, u32[]{:S(2)}, u32[]{:S(2)}) collective-permute-start(bf16[2064,128]{1,0:T(8,128)(2,1)S(1)} %pad_maximum_fusion), channel_id=1, source_target_pairs={{0,2},{1,5},{2,6},{3,1},{4,0},{5,7},{6,4},{7,3},{8,10},{9,13},{10,... | collective-permute-start | bytes 1585160 | tf_op jit(solution)/shard_map/ppermute | solution.py:94
  43.0 1.4 %copy-start.2 = (bf16[2048,128]{1,0:T(8,128)(2,1)}, bf16[2048,128]{1,0:T(8,128)(2,1)S(1)}, u32[]{:S(2)}) copy-start(bf16[2048,128]{1,0:T(8,128)(2,1)S(1)} %slice_select_fusion) | copy-start | bytes 1572868
  43.0 1.4 %copy-start.6 = (s32[1024]{0:T(1024)S(1)}, s32[1024]{0:T(1024)}, u32[]{:S(2)}) copy-start(s32[1024]{0:T(1024)} %add_select_fusion.1) | copy-start | bytes 12292
  43.0 2.3 %copy-start.3 = (f32[32,32]{0,1:T(8,128)S(1)}, f32[32,32]{0,1:T(8,128)}, u32[]{:S(2)}) copy-start(f32[32,32]{0,1:T(8,128)} %get-tuple-element.204) | copy-start | bytes 12292
  45.4 2.3 %copy-start.5 = (s32[2048]{0:T(1024)S(1)}, s32[2048]{0:T(1024)}, u32[]{:S(2)}) copy-start(s32[2048]{0:T(1024)} %add_select_fusion) | copy-start | bytes 24580
  48.8 4.5 %copy-start.1 = (bf16[2,1024,128]{2,1,0:T(8,128)(2,1)S(1)}, bf16[2,1024,128]{2,1,0:T(8,128)(2,1)}, u32[]{:S(2)}) copy-start(bf16[2,1024,128]{2,1,0:T(8,128)(2,1)} %divide_convert_fusion) | copy-start | bytes 1572868
  48.8 14.0 %collective-permute-start.1 = (f32[32,64]{1,0:T(8,128)S(1)}, f32[32,64]{1,0:T(8,128)S(1)}, u32[]{:S(2)}, u32[]{:S(2)}) collective-permute-start(f32[32,64]{1,0:T(8,128)S(1)} %fusion.30), channel_id=1, source_target_pairs={{0,1},{1,0},{2,3},{3,2},{4,5},{5,4},{6,7},{7,6},{8,9},{9,8},{10,11... | collective-permute-start | bytes 24584 | tf_op jit(solution)/shard_map/ppermute | solution.py:104
  62.8 3.9 %collective-permute-start.3 = (f32[64,64]{1,0:T(8,128)S(1)}, f32[64,64]{1,0:T(8,128)S(1)}, u32[]{:S(2)}, u32[]{:S(2)}) collective-permute-start(f32[64,64]{1,0:T(8,128)S(1)} %bitcast.139), channel_id=1, source_target_pairs={{2,0},{5,1},{6,2},{1,3},{0,4},{7,5},{4,6},{3,7},{10,8},{13,9},{14,... | collective-permute-start | bytes 49160 | tf_op jit(solution)/shard_map/ppermute | solution.py:114

commit v3 on v1

--- a/solution.py
+++ b/solution.py
@@ -17,32 +17,21 @@
     other_tr = jnp.transpose(other.reshape(other_items, tok, width), (1, 0, 2))
     other_float = other_bias.astype(jnp.float32)
     other_add_tr = jnp.transpose(other_float.reshape(other_items, tok), (1, 0))[:, :, None]
-    other_owner = (jnp.arange(other_items * tok, dtype=jnp.int32) // tok)[:, None] == jnp.arange(
-        other_items, dtype=jnp.int32
-    )[None, :]
-    other_select = jnp.where((other_bias == 0)[:, None] & other_owner, 1.0, 0.0).astype(jnp.float32)
+    other_valid = (other_bias == 0).reshape(other_items, tok)
     query_flat = block.reshape(blocks, rows * tok, width)
     query_tr = jnp.transpose(block.reshape(blocks, rows, tok, width), (0, 2, 1, 3))
     bias_float = bias.astype(jnp.float32).reshape(blocks, rows, tok)
     query_add_tr = jnp.transpose(bias_float, (0, 2, 1))[..., None]
-    query_valid = (bias == 0).reshape(blocks, rows * tok)
-    query_owner = (jnp.arange(rows * tok, dtype=jnp.int32) // tok)[:, None] == jnp.arange(
-        rows, dtype=jnp.int32
-    )[None, :]
+    query_valid = (bias == 0).reshape(blocks, rows, tok)
 
     def one_block(operands):
         flat, turned, adding, kept = operands
         dots_fore = jnp.einsum("ubh,qh->ubq", other_tr, flat, preferred_element_type=jnp.float32)
-        fore = jnp.max(dots_fore + other_add_tr, axis=0)
-        select = jnp.where(kept[:, None] & query_owner, 1.0, 0.0).astype(jnp.float32)
-        fore = jnp.dot(
-            fore, select, precision=lax.Precision.HIGHEST, preferred_element_type=jnp.float32
-        )
+        fore = jnp.max(dots_fore + other_add_tr, axis=0).reshape(other_items, rows, tok)
+        fore = jnp.sum(jnp.where(kept[None], fore, 0.0), axis=2)
         dots_back = jnp.einsum("trh,ch->trc", turned, other, preferred_element_type=jnp.float32)
-        back = jnp.max(dots_back + adding, axis=0)
-        back = jnp.dot(
-            back, other_select, precision=lax.Precision.HIGHEST, preferred_element_type=jnp.float32
-        )
+        back = jnp.max(dots_back + adding, axis=0).reshape(rows, other_items, tok)
+        back = jnp.sum(jnp.where(other_valid[None], back, 0.0), axis=2)
         return 0.5 * (fore.T + back)
 
     result = lax.map(one_block, (query_flat, query_tr, query_add_tr, query_valid))

time: 59.4 us -> 60.7 us (1.022)
  matrix products: 14.6 us -> 7.6 us
  waiting for transfers between devices: 21.9 us -> 26 us
  local copies, waits for them, and re-layouts: 6.51 us -> 9.45 us
  other arithmetic: 7.67 us -> 8.85 us
    dot_general x6 -> x0, matrix products: 5.99 us -> none  [the longest x3 3.22 us: one_block(): jnp.dot(back, other_select, precision=lax.Precision.HIGHEST, preferred_el...]
    ppermute x1, waiting for transfers between devices: 3.09 us -> 6.12 us  [shards(): z_recv = lax.ppermute(packed, 'pool', send_pairs)]
    while x0 -> x13, local copies, waits for them, and re-layouts: none -> 2.17 us
    reduce_sum x0 -> x6, other arithmetic: none -> 1.71 us  [the longest x3 1.04 us: one_block(): back = jnp.sum(jnp.where(other_valid[None], back, 0.0), axis=2)]
    dot_general x3, matrix products: 4.85 us -> 3.79 us  [one_block(): jnp.einsum('trh,ch->trc', turned, other, preferred_element_type=jnp.float32)]
    reshape x1 -> x3, local copies, waits for them, and re-layouts: 0.09 us -> 1.01 us  [one_block(): back = jnp.max(dots_back + adding, axis=0).reshape(rows, other_items, tok)]
    reshape x1, local copies, waits for them, and re-layouts: 0.21 us -> 0.99 us  [tile_scores(): other_tr = jnp.transpose(other.reshape(other_items, tok, width), (1, 0, 2))]
    all_to_all x1, waiting for transfers between devices: 15.2 us -> 16 us  [shards(): lax.all_to_all(outgoing, ('enc', 'pool'), split_axis=0, concat_axis=0, ti...]
  transfers between devices with their start and end apart: 5 -> 5, of which waited for: 4 -> 4; matrix products, arithmetic and copies ran while one was open for 38% -> 30% of each run, Pallas kernels for 0% -> 0%
where the time goes in v3:
time: 60.7 us; the launch traced here: 60.2 us
  waiting for transfers between devices  26 us (43%)
  local copies, waits for them, and re-layouts  9.45 us (16%)
  other arithmetic  8.85 us (15%)
  starting transfers between devices  7.83 us (13%)
  matrix products  7.6 us (13%)
    all_to_all x1, waiting for transfers between devices, shards(): lax.all_to_all(outgoing, ('enc', 'pool'), split_axis=0, concat_axis=0, ti...  16 us
    all_to_all x1, starting transfers between devices, shards(): lax.all_to_all(outgoing, ('enc', 'pool'), split_axis=0, concat_axis=0, ti...  7.3 us
    ppermute x1, waiting for transfers between devices, shards(): z_recv = lax.ppermute(packed, 'pool', send_pairs)  6.12 us
    dot_general x3, matrix products, one_block(): jnp.einsum('ubh,qh->ubq', other_tr, flat, preferred_element_type=jnp.floa...  3.81 us
    dot_general x3, matrix products, one_block(): jnp.einsum('trh,ch->trc', turned, other, preferred_element_type=jnp.float32)  3.79 us
    ppermute x1, waiting for transfers between devices, shards(): tile_back = lax.ppermute(tile_z.T, 'pool', back_pairs)  3.78 us
    convert_element_type x3, other arithmetic, shards(): (values / jnp.sqrt(jnp.sum(values * values, axis=-1, keepdims=True) + 1e-...  1.71 us
    while x12, local copies, waits for them, and re-layouts  1.48 us
  transfers between devices with their start and end apart: 5, of which 4 were waited for; matrix products, arithmetic and copies ran while one was open for 30% of the time, Pallas kernels for 0%

profile of v3, /device:TPU:0, one launch (start us, length us, event | category | flops | bytes accessed | tf_op | source)
XLA Modules:
  0.0 60.2 jit_solution(15086335083864623060)
XLA Ops:
  0.0 0.8 %reshape.173 = s32[32,8,8]{2,1,0:T(8,128)S(1)} reshape(s32[2048]{0:T(1024)} %param.7) | data formatting | bytes 16384 | tf_op jit(solution)/shard_map/reshape | solution.py:51
  0.9 0.1 reshape.200
  1.1 0.8 %gather_fusion = bf16[256,8,128]{2,1,0:T(8,128)(2,1)S(1)} fusion(bf16[256,8,128]{2,1,0:T(8,128)(2,1)S(1)} %copy-done, s32[1024]{0:T(1024)S(1)} %pad_clamp_fusion), kind=kCustom, calls=%fused_computation | custom fusion | bytes 1049600 | tf_op jit(solution)/shard_map/jit(_take)/gather | solution.py:53
  1.9 1.1 %broadcast_select_fusion = bf16[32,8,8,128]{3,2,1,0:T(8,128)(2,1)} fusion(bf16[32,8,8,128]{3,2,1,0:T(8,128)(2,1)S(1)} %bitcast.132, pred[32,8]{1,0:T(8,128)(4,1)S(1)} %compare_and_fusion), kind=kLoop, calls=%fused_computation.34 | loop fusion | flops 262144 | bytes 1048832 | tf_op jit(solution)/shard_map/jit(_take)/select_n | solution.py:53
  3.0 7.3 %all-to-all-start = ((bf16[32,8,8,128]{3,2,1,0:T(8,128)(2,1)}), bf16[32,8,8,128]{3,2,1,0:T(8,128)(2,1)S(1)}, u32[]{:S(2)}, u32[]{:S(2)}) async-start(bf16[32,8,8,128]{3,2,1,0:T(8,128)(2,1)} %broadcast_select_fusion), calls=%async_computation | async-start | bytes 1048576 | tf_op jit(solution)/shard_map/all_to_all | solution.py:54
  10.4 0.1 copy.85
  10.5 0.1 broadcast_compare_fusion
  10.5 0.1 reshape_reshape.2
  10.6 0.1 copy.111
  10.7 16.0 %all-to-all-done = bf16[32,8,8,128]{3,2,1,0:T(8,128)(2,1)S(1)} async-done(((bf16[32,8,8,128]{3,2,1,0:T(8,128)(2,1)}), bf16[32,8,8,128]{3,2,1,0:T(8,128)(2,1)S(1)}, u32[]{:S(2)}, u32[]{:S(2)}) %all-to-all-start) | async-done | bytes 524320 | tf_op jit(solution)/shard_map/all_to_all | solution.py:54
  26.7 0.3 multiply_reduce_fusion
  27.0 0.1 copy.87
  27.2 0.1 reshape.190
  27.3 0.2 copy.88
  27.5 0.2 sqrt.24
  27.6 0.1 reshape.211
  27.8 0.1 convert_element_type.100
  27.9 0.1 copy.86
  28.0 0.3 fusion.5
  28.4 0.8 %pad_maximum_fusion = bf16[2064,128]{1,0:T(8,128)(2,1)} fusion(bf16[16,128]{1,0:T(8,128)(2,1)S(1)} %reshape_reshape.2, bf16[2048,128]{1,0:T(8,128)(2,1)S(1)} %fusion.5), kind=kLoop, calls=%fused_computation.24 | loop fusion | flops 1056768 | bytes 1056768 | tf_op jit(solution)/shard_map/concatenate | solution.py:67
  29.2 0.1 reshape.212
  29.3 0.2 sqrt.26
  29.5 0.2 fusion.6
  29.7 1.2 %divide_convert_fusion.1 = bf16[2,1024,128]{2,1,0:T(8,128)(2,1)} fusion(f32[2,1024,128]{2,1,0:T(8,128)S(1)} %bitcast.127, f32[2,1024]{1,0:T(2,128)S(1)} %sqrt.26), kind=kLoop, calls=%fused_computation.21 | loop fusion | flops 524288 | bytes 1581056 | tf_op jit(solution)/shard_map/convert_element_type | solution.py:59
  30.9 0.3 fusion.10
  31.2 0.1 collective-permute-done
  31.3 0.1 reshape.175
  31.4 0.6 %broadcast_compare_fusion.1 = pred[64,32]{1,0:T(8,128)(4,1)} fusion(bf16[64,32]{1,0:T(8,128)(2,1)S(1)} %reshape.175, bf16[64,32]{1,0:T(8,128)(2,1)S(1)} %get-tuple-element.149, pred[]{:T(512)S(6)} %eq.49), kind=kLoop, calls=%fused_computation.59 | loop fusion | flops 4096 | bytes 10241 | tf_op jit(solution)/shard_map/eq | solution.py:20
  32.0 0.7 %copy.93 = f32[32,64]{1,0:T(8,128)} copy(f32[32,64]{0,1:T(8,128)S(1)} %convert_bitcast_fusion) | data formatting | bytes 16384 | tf_op jit(solution)/shard_map/transpose | solution.py:19
  32.7 0.1 slice.35
  32.9 1.1 %slice_select_fusion = bf16[2048,128]{1,0:T(8,128)(2,1)S(1)} fusion(bf16[2064,128]{1,0:T(8,128)(2,1)S(1)} %collective-permute-done, pred[]{:T(512)S(6)} %eq.49, f32[2048]{0:T(1024)} %copy-done.3, f32[8,8,4,8,128]{4,3,2,1,0:T(8,128)S(1)} %copy.86), kind=kLoop, calls=%fused_computation.27 | loop fusion | flops 786432 | bytes 2105345 | tf_op jit(solution)/shard_map/jit(_where)/select_n | solution.py:87
  34.0 1.3 %add_reduce_fusion.3 = f32[64,1024]{1,0:T(8,128)S(1)} fusion(f32[32,64]{1,0:T(8,128)S(1)} %copy-done.7, bf16[64,32,128]{2,1,0:T(8,128)(2,1)S(1)} %bitcast.134, bf16[1024,128]{1,0:T(8,128)(2,1)S(1)} %slice_select_fusion.1), kind=kOutput, calls=%fused_computation.17 | convolution fusion | flops 540999680 | bytes 1056768 | tf_op jit(solution)/shard_map/while/body/eval_jaxpr/ubh,qh->ubq/dot_general | solution.py:29
  35.3 1.3 %add_reduce_fusion.2 = f32[32,2048]{1,0:T(8,128)S(1)} fusion(f32[32,32]{1,0:T(8,128)S(1)} %copy.96, bf16[2048,128]{1,0:T(8,128)(2,1)S(1)} %slice_select_fusion, bf16[1,32,32,128]{3,2,1,0:T(8,128)(2,1)S(1)} %bitcast.139), kind=kOutput, calls=%fused_computation.16 | convolution fusion | flops 540999680 | bytes 1052672 | tf_op jit(solution)/shard_map/while/body/eval_jaxpr/trh,ch->trc/dot_general | solution.py:32
  36.6 0.2 copy.94
  36.8 0.3 reshape.178
  37.1 0.2 select_reduce_fusion.3
  37.4 0.1 copy-done.4
  37.5 0.3 select_reduce_fusion.2
  37.8 0.5 collective-permute-start.1
  38.3 6.1 %collective-permute-done.2 = bf16[2064,128]{1,0:T(8,128)(2,1)S(1)} collective-permute-done((bf16[2064,128]{1,0:T(8,128)(2,1)}, bf16[2064,128]{1,0:T(8,128)(2,1)S(1)}, u32[]{:S(2)}, u32[]{:S(2)}) %collective-permute-start.2) | collective-permute-done | bytes 528416 | tf_op jit(solution)/shard_map/ppermute | solution.py:80
  44.5 1.0 %copy.126 = bf16[64,32,128]{2,0,1:T(8,128)(2,1)} copy(bf16[64,32,128]{2,1,0:T(8,128)(2,1)S(1)} %bitcast.131) | data formatting | bytes 1048576 | tf_op jit(solution)/shard_map/reshape | solution.py:17
  45.5 0.7 %copy.105 = f32[32,64,1]{1,0,2:T(8,128)} copy(f32[32,64,1]{0,1,2:T(8,128)S(1)} %bitcast.142) | data formatting | bytes 16384 | tf_op jit(solution)/shard_map/while | solution.py:37
  46.2 9.2 %while.2 = (s32[]{:T(128)}, f32[2,32,64]{2,1,0:T(8,128)S(1)}, pred[2,32,32]{2,1,0:T(8,128)(4,1)S(1)}, bf16[2,1024,128]{2,1,0:T(8,128)(2,1)}, bf16[32,64,128]{2,1...) while((s32[]{:T(128)}, f32[2,32,64]{2,1,0:T(8,128)S(1)}, ...), condition=%wide.region_10.11_spmd, body=%wide.region_5.10_spmd.sunk | while | flops 1082261504 | bytes 8525013 | solution.py:37
  46.3 1.3 %add_reduce_fusion.6 = f32[32,2048]{1,0:T(8,128)S(1)} fusion(f32[32,32]{1,0:T(8,128)S(1)} %bitcast.137, bf16[2048,128]{1,0:T(8,128)(2,1)S(1)} %get-tuple-element.243, bf16[1,32,32,128]{3,1,2,0:T(8,128)(2,1)S(1)} %constant_dynamic-slice_fusion.5), kind=kOutput, calls=%fused_computation.1.clone.1 | convolution fusion | flops 540999680 | bytes 1052672 | tf_op jit(solution)/shard_map/while/body/eval_jaxpr/trh,ch->trc/dot_general | solution.py:32
  47.6 0.3 reshape.214
  47.9 0.1 broadcast_in_dim.143
  48.0 0.3 select_reduce_fusion.6
  48.4 0.2 copy-done.1
  48.6 0.5 copy-done.2
  49.1 1.3 %add_reduce_fusion.7 = f32[1024,64]{0,1:T(8,128)S(1)} fusion(f32[32,64]{1,0:T(8,128)S(1)} %bitcast.146, bf16[32,64,128]{2,1,0:T(8,128)(2,1)S(1)} %copy-done.2, bf16[2,1024,128]{2,1,0:T(8,128)(2,1)S(1)} %copy-done.1, s32[]{:T(128)} %get-tuple-element.224), kind=kOutput, calls=%fused_computation.2.clone.1 | convolution fusion | flops 540999680 | bytes 1064964 | tf_op jit(solution)/shard_map/while/body/eval_jaxpr/ubh,qh->ubq/dot_general | solution.py:29
  50.4 0.2 copy.130
  50.6 0.2 select_reduce_fusion.7
  50.9 1.3 %add_reduce_fusion.6 = f32[32,2048]{1,0:T(8,128)S(1)} fusion(f32[32,32]{1,0:T(8,128)S(1)} %bitcast.137, bf16[2048,128]{1,0:T(8,128)(2,1)S(1)} %get-tuple-element.243, bf16[1,32,32,128]{3,1,2,0:T(8,128)(2,1)S(1)} %constant_dynamic-slice_fusion.5), kind=kOutput, calls=%fused_computation.1.clone.1 | convolution fusion | flops 540999680 | bytes 1052672 | tf_op jit(solution)/shard_map/while/body/eval_jaxpr/trh,ch->trc/dot_general | solution.py:32
  52.2 0.3 reshape.214
  52.6 0.1 broadcast_in_dim.143
  52.6 0.3 select_reduce_fusion.6
  53.0 0.2 copy-done.1
  53.2 0.5 copy-done.2
  53.7 1.3 %add_reduce_fusion.7 = f32[1024,64]{0,1:T(8,128)S(1)} fusion(f32[32,64]{1,0:T(8,128)S(1)} %bitcast.146, bf16[32,64,128]{2,1,0:T(8,128)(2,1)S(1)} %copy-done.2, bf16[2,1024,128]{2,1,0:T(8,128)(2,1)S(1)} %copy-done.1, s32[]{:T(128)} %get-tuple-element.224), kind=kOutput, calls=%fused_computation.2.clone.1 | convolution fusion | flops 540999680 | bytes 1064964 | tf_op jit(solution)/shard_map/while/body/eval_jaxpr/ubh,qh->ubq/dot_general | solution.py:29
  55.0 0.2 copy.130
  55.2 0.2 select_reduce_fusion.7
  55.6 0.1 copy.97
  55.7 3.8 %collective-permute-done.3 = f32[64,64]{1,0:T(8,128)S(1)} collective-permute-done((f32[64,64]{1,0:T(8,128)S(1)}, f32[64,64]{1,0:T(8,128)S(1)}, u32[]{:S(2)}, u32[]{:S(2)}) %collective-permute-start.3) | collective-permute-done | bytes 16416 | tf_op jit(solution)/shard_map/ppermute | solution.py:100
  59.5 0.7 %pad_maximum_fusion.1 = f32[64,192]{1,0:T(8,128)} fusion(f32[64,64]{1,0:T(8,128)S(1)} %get-tuple-element.151, f32[64,64]{1,0:T(8,128)S(1)} %get-tuple-element.150, f32[64,64]{1,0:T(8,128)S(1)} %bitcast_select_fusion), kind=kLoop, calls=%fused_computation.39 | loop fusion | flops 24576 | bytes 98304 | tf_op jit(solution)/shard_map/concatenate | solution.py:104
  (55 shorter events, 0.7 us)
Async XLA Ops:
  0.0 1.1 %copy-start = (bf16[256,8,128]{2,1,0:T(8,128)(2,1)S(1)}, bf16[256,8,128]{2,1,0:T(8,128)(2,1)}, u32[]{:S(2)}) copy-start(bf16[256,8,128]{2,1,0:T(8,128)(2,1)} %param.6) | copy-start | bytes 1572868
  1.9 8.5 %copy-start.5 = (s32[64,32]{0,1:T(8,128)S(1)}, s32[64,32]{0,1:T(8,128)}, u32[]{:S(2)}) copy-start(s32[64,32]{0,1:T(8,128)} %param.9) | copy-start | bytes 24580
  1.9 8.6 %copy-start.8 = (s32[64]{0:T(128)S(1)}, s32[64]{0:T(128)}, u32[]{:S(2)}) copy-start(s32[64]{0:T(128)} %param.8) | copy-start | bytes 772
  3.0 23.7 %all-to-all-start = ((bf16[32,8,8,128]{3,2,1,0:T(8,128)(2,1)}), bf16[32,8,8,128]{3,2,1,0:T(8,128)(2,1)S(1)}, u32[]{:S(2)}, u32[]{:S(2)}) async-start(bf16[32,8,8,128]{3,2,1,0:T(8,128)(2,1)} %broadcast_select_fusion), calls=%async_computation | async-start | bytes 1048576 | tf_op jit(solution)/shard_map/all_to_all | solution.py:54
  27.6 1.6 %copy-start.3 = (f32[2048]{0:T(1024)}, f32[2048]{0:T(1024)S(1)}, u32[]{:S(2)}) copy-start(f32[2048]{0:T(1024)S(1)} %sqrt.24) | copy-start | bytes 24580
  29.2 2.1 %collective-permute-start = (bf16[2064,128]{1,0:T(8,128)(2,1)}, bf16[2064,128]{1,0:T(8,128)(2,1)S(1)}, u32[]{:S(2)}, u32[]{:S(2)}) collective-permute-start(bf16[2064,128]{1,0:T(8,128)(2,1)} %pad_maximum_fusion), channel_id=1, source_target_pairs={{0,1},{1,0},{2,3},{3,2},{4,5},{5,4},{6,7},{7,6},{8,9},{9,8},{10,11... | collective-permute-start | bytes 1585160 | tf_op jit(solution)/shard_map/ppermute | solution.py:81
  29.2 15.2 %collective-permute-start.2 = (bf16[2064,128]{1,0:T(8,128)(2,1)}, bf16[2064,128]{1,0:T(8,128)(2,1)S(1)}, u32[]{:S(2)}, u32[]{:S(2)}) collective-permute-start(bf16[2064,128]{1,0:T(8,128)(2,1)} %pad_maximum_fusion), channel_id=1, source_target_pairs={{0,2},{1,5},{2,6},{3,1},{4,0},{5,7},{6,4},{7,3},{8,10},{9,13},{10,... | collective-permute-start | bytes 1585160 | tf_op jit(solution)/shard_map/ppermute | solution.py:80
  32.9 1.1 %copy-start.7 = (f32[32,64]{1,0:T(8,128)S(1)}, f32[32,64]{1,0:T(8,128)}, u32[]{:S(2)}) copy-start(f32[32,64]{1,0:T(8,128)} %copy.93) | copy-start | bytes 24580
  36.8 0.7 %copy-start.4 = (pred[64,32]{1,0:T(8,128)(4,1)S(1)}, pred[64,32]{1,0:T(8,128)(4,1)}, u32[]{:S(2)}) copy-start(pred[64,32]{1,0:T(8,128)(4,1)} %broadcast_compare_fusion.1) | copy-start | bytes 6148
  37.8 17.8 %collective-permute-start.1 = (f32[32,64]{1,0:T(8,128)S(1)}, f32[32,64]{1,0:T(8,128)S(1)}, u32[]{:S(2)}, u32[]{:S(2)}) collective-permute-start(f32[32,64]{1,0:T(8,128)S(1)} %fusion.15), channel_id=1, source_target_pairs={{0,1},{1,0},{2,3},{3,2},{4,5},{5,4},{6,7},{7,6},{8,9},{9,8},{10,11... | collective-permute-start | bytes 24584 | tf_op jit(solution)/shard_map/ppermute | solution.py:90
  47.6 1.0 %copy-start.1 = (bf16[2,1024,128]{2,1,0:T(8,128)(2,1)S(1)}, bf16[2,1024,128]{2,1,0:T(8,128)(2,1)}, u32[]{:S(2)}) copy-start(bf16[2,1024,128]{2,1,0:T(8,128)(2,1)} %get-tuple-element.238) | copy-start | bytes 1572868 | tf_op jit(solution)/shard_map/while
  47.6 1.0 %copy-start.6 = (f32[32,64,1]{1,0,2:T(8,128)S(1)}, f32[32,64,1]{1,0,2:T(8,128)}, u32[]{:S(2)}) copy-start(f32[32,64,1]{1,0,2:T(8,128)} %get-tuple-element.240) | copy-start | bytes 24580 | tf_op jit(solution)/shard_map/while
  48.0 1.1 %copy-start.2 = (bf16[32,64,128]{2,1,0:T(8,128)(2,1)S(1)}, bf16[32,64,128]{2,1,0:T(8,128)(2,1)}, u32[]{:S(2)}) copy-start(bf16[32,64,128]{2,1,0:T(8,128)(2,1)} %get-tuple-element.239) | copy-start | bytes 1572868 | tf_op jit(solution)/shard_map/while
  52.2 1.0 %copy-start.1 = (bf16[2,1024,128]{2,1,0:T(8,128)(2,1)S(1)}, bf16[2,1024,128]{2,1,0:T(8,128)(2,1)}, u32[]{:S(2)}) copy-start(bf16[2,1024,128]{2,1,0:T(8,128)(2,1)} %get-tuple-element.238) | copy-start | bytes 1572868 | tf_op jit(solution)/shard_map/while
  52.2 1.0 %copy-start.6 = (f32[32,64,1]{1,0,2:T(8,128)S(1)}, f32[32,64,1]{1,0,2:T(8,128)}, u32[]{:S(2)}) copy-start(f32[32,64,1]{1,0,2:T(8,128)} %get-tuple-element.240) | copy-start | bytes 24580 | tf_op jit(solution)/shard_map/while
  52.6 1.1 %copy-start.2 = (bf16[32,64,128]{2,1,0:T(8,128)(2,1)S(1)}, bf16[32,64,128]{2,1,0:T(8,128)(2,1)}, u32[]{:S(2)}) copy-start(bf16[32,64,128]{2,1,0:T(8,128)(2,1)} %get-tuple-element.239) | copy-start | bytes 1572868 | tf_op jit(solution)/shard_map/while
  55.6 3.9 %collective-permute-start.3 = (f32[64,64]{1,0:T(8,128)S(1)}, f32[64,64]{1,0:T(8,128)S(1)}, u32[]{:S(2)}, u32[]{:S(2)}) collective-permute-start(f32[64,64]{1,0:T(8,128)S(1)} %bitcast.145), channel_id=1, source_target_pairs={{2,0},{5,1},{6,2},{1,3},{0,4},{7,5},{4,6},{3,7},{10,8},{13,9},{14,... | collective-permute-start | bytes 49160 | tf_op jit(solution)/shard_map/ppermute | solution.py:100

commit v4 on v3

--- a/solution.py
+++ b/solution.py
@@ -77,16 +77,19 @@
     back_pairs = [(t, s) for s, t in send_pairs]
     chip_pairs = [(p, p ^ 1) for p in range(n_pool)]
 
-    z_recv = lax.ppermute(packed, "pool", send_pairs)
+    half = n_tok // 2
+    first = jnp.concatenate([block[:half], bias.reshape(-1, width)], axis=0)
+    z_first = lax.ppermute(first, "pool", send_pairs)
+    z_second = lax.ppermute(block[half:], "pool", send_pairs)
     c_recv = lax.ppermute(packed, "pool", chip_pairs)
 
-    half = n_tok // 2
     c_blk, c_bias = c_recv[:n_tok], c_recv[n_tok:].reshape(-1)
     query = jnp.where(is_a, block[:half], c_blk[half:])
     query_bias = jnp.where(is_a, bias[:half], c_bias[half:])
     other = jnp.where(is_a, c_blk, block)
     other_bias = jnp.where(is_a, c_bias, bias)
     part = tile_scores(query, query_bias, other, other_bias, tok)
+    part, z_first = lax.optimization_barrier((part, z_first))
     part_recv = lax.ppermute(part, "pool", chip_pairs)
     joined = jnp.where(
         is_a,
@@ -95,9 +98,14 @@
     )
     tile0 = jnp.where(is_a, joined, joined.T)
 
-    z_blk, z_bias = z_recv[:n_tok], z_recv[n_tok:].reshape(-1)
-    tile_z = tile_scores(block, bias, z_blk, z_bias, tok)
-    tile_back = lax.ppermute(tile_z.T, "pool", back_pairs)
+    z_bias = z_first[half:].reshape(-1)
+    tile_a = tile_scores(block, bias, z_first[:half], z_bias[:half], tok)
+    tile_a, z_second = lax.optimization_barrier((tile_a, z_second))
+    back_a = lax.ppermute(tile_a.T, "pool", back_pairs)
+    tile_b = tile_scores(block, bias, z_second, z_bias[half:], tok)
+    back_b = lax.ppermute(tile_b.T, "pool", back_pairs)
+    tile_z = jnp.concatenate([tile_a, tile_b], axis=1)
+    tile_back = jnp.concatenate([back_a, back_b], axis=0)
     via_bit1 = parity == 1
     col1 = jnp.where(via_bit1, tile_z, tile_back)
     col2 = jnp.where(via_bit1, tile_back, tile_z)

time: 60.7 us -> 62.5 us (1.030)
  waiting for transfers between devices: 26 us -> 21.3 us
  matrix products: 7.6 us -> 10.3 us
  starting transfers between devices: 7.83 us -> 10.1 us
  local copies, waits for them, and re-layouts: 9.45 us -> 11 us
    ppermute x2 -> x4, waiting for transfers between devices: 9.9 us -> 5.34 us  [the longest x1 2.97 us: shards(): z_first = lax.ppermute(first, 'pool', send_pairs)]
    ppermute x2 -> x4, starting transfers between devices: 0.03 us -> 2.72 us  [the longest x1 1.44 us: shards(): back_a = lax.ppermute(tile_a.T, 'pool', back_pairs)]
    dot_general x3 -> x5, matrix products: 3.79 us -> 6.07 us  [one_block(): jnp.einsum('trh,ch->trc', turned, other, preferred_element_type=jnp.float32)]
    slice x2, local copies, waits for them, and re-layouts: 0.04 us -> 1.72 us  [the longest x1 0.97 us: shards(): tile_a = tile_scores(block, bias, z_first[:half], z_bias[:half], tok)]
    while x12 -> x0, local copies, waits for them, and re-layouts: 1.48 us -> none
    concatenate x1, other arithmetic: 0.82 us -> 0.04 us  [shards(): packed = jnp.concatenate([block, bias.reshape(-1, width)], axis=0)]
    concatenate x0 -> x1, other arithmetic: none -> 0.72 us  [shards(): first = jnp.concatenate([block[:half], bias.reshape(-1, width)], axis=0)]
    select_n x1, other arithmetic: 1.06 us -> 0.34 us  [shards(): other = jnp.where(is_a, c_blk, block)]
  transfers between devices with their start and end apart: 5 -> 7, of which waited for: 4 -> 3; matrix products, arithmetic and copies ran while one was open for 30% -> 39% of each run, Pallas kernels for 0% -> 0%
where the time goes in v4:
time: 62.5 us; the launch traced here: 62.1 us
  waiting for transfers between devices  21.3 us (34%)
  local copies, waits for them, and re-layouts  11 us (18%)
  matrix products  10.3 us (16%)
  starting transfers between devices  10.1 us (16%)
  other arithmetic  8.85 us (14%)
    all_to_all x1, waiting for transfers between devices, shards(): lax.all_to_all(outgoing, ('enc', 'pool'), split_axis=0, concat_axis=0, ti...  16 us
    all_to_all x1, starting transfers between devices, shards(): lax.all_to_all(outgoing, ('enc', 'pool'), split_axis=0, concat_axis=0, ti...  7.3 us
    dot_general x5, matrix products, one_block(): jnp.einsum('trh,ch->trc', turned, other, preferred_element_type=jnp.float32)  6.07 us
    dot_general x5, matrix products, one_block(): jnp.einsum('ubh,qh->ubq', other_tr, flat, preferred_element_type=jnp.floa...  4.19 us
    ppermute x1, waiting for transfers between devices, shards(): z_first = lax.ppermute(first, 'pool', send_pairs)  2.97 us
    ppermute x1, waiting for transfers between devices, shards(): back_a = lax.ppermute(tile_a.T, 'pool', back_pairs)  2.37 us
    ppermute x1, starting transfers between devices, shards(): back_a = lax.ppermute(tile_a.T, 'pool', back_pairs)  1.44 us
    ppermute x1, starting transfers between devices, shards(): z_second = lax.ppermute(block[half:], 'pool', send_pairs)  1.26 us
  transfers between devices with their start and end apart: 7, of which 3 were waited for; matrix products, arithmetic and copies ran while one was open for 39% of the time, Pallas kernels for 0%

profile of v4, /device:TPU:0, one launch (start us, length us, event | category | flops | bytes accessed | tf_op | source)
XLA Modules:
  0.0 62.1 jit_solution(13340608032462832074)
XLA Ops:
  0.0 0.8 %reshape.198 = s32[32,8,8]{2,1,0:T(8,128)S(1)} reshape(s32[2048]{0:T(1024)} %param.9) | data formatting | bytes 16384 | tf_op jit(solution)/shard_map/reshape | solution.py:51
  1.1 0.8 %gather_fusion = bf16[256,8,128]{2,1,0:T(8,128)(2,1)S(1)} fusion(bf16[256,8,128]{2,1,0:T(8,128)(2,1)S(1)} %copy-done, s32[1024]{0:T(1024)S(1)} %pad_clamp_fusion), kind=kCustom, calls=%fused_computation | custom fusion | bytes 1049600 | tf_op jit(solution)/shard_map/jit(_take)/gather | solution.py:53
  1.9 1.1 %broadcast_select_fusion = bf16[32,8,8,128]{3,2,1,0:T(8,128)(2,1)} fusion(bf16[32,8,8,128]{3,2,1,0:T(8,128)(2,1)S(1)} %bitcast.183, pred[32,8]{1,0:T(8,128)(4,1)S(1)} %compare_and_fusion), kind=kLoop, calls=%fused_computation.47 | loop fusion | flops 262144 | bytes 1048832 | tf_op jit(solution)/shard_map/jit(_take)/select_n | solution.py:53
  3.0 7.3 %all-to-all-start = ((bf16[32,8,8,128]{3,2,1,0:T(8,128)(2,1)}), bf16[32,8,8,128]{3,2,1,0:T(8,128)(2,1)S(1)}, u32[]{:S(2)}, u32[]{:S(2)}) async-start(bf16[32,8,8,128]{3,2,1,0:T(8,128)(2,1)} %broadcast_select_fusion), calls=%async_computation | async-start | bytes 1048576 | tf_op jit(solution)/shard_map/all_to_all | solution.py:54
  10.7 16.0 %all-to-all-done = bf16[32,8,8,128]{3,2,1,0:T(8,128)(2,1)S(1)} async-done(((bf16[32,8,8,128]{3,2,1,0:T(8,128)(2,1)}), bf16[32,8,8,128]{3,2,1,0:T(8,128)(2,1)S(1)}, u32[]{:S(2)}, u32[]{:S(2)}) %all-to-all-start) | async-done | bytes 524320 | tf_op jit(solution)/shard_map/all_to_all | solution.py:54
  26.7 0.3 multiply_reduce_fusion
  27.2 0.1 reshape.218
  27.3 0.2 copy.146
  27.5 0.2 sqrt.24
  27.6 0.1 reshape.242
  27.8 0.1 reshape.243
  27.9 0.2 sqrt.26
  28.0 0.1 convert_element_type.107
  28.2 0.1 copy.144
  28.3 0.3 fusion.16
  28.8 0.3 divide_convert_fusion.2
  29.1 0.8 %fusion.26 = (bf16[32,32,128]{2,1,0:T(8,128)(2,1)}, bf16[32,32,128]{2,1,0:T(8,128)(2,1)S(1)}) fusion(bf16[64,32,128]{2,1,0:T(8,128)(2,1)S(1)} %divide_convert_fusion.2), kind=kLoop, calls=%fused_computation.86 | loop fusion | bytes 1048576 | tf_op jit(solution)/shard_map/slice | solution.py:83
  29.9 0.7 %pad_maximum_fusion.1 = bf16[1040,128]{1,0:T(8,128)(2,1)} fusion(bf16[16,128]{1,0:T(8,128)(2,1)S(1)} %reshape_reshape.2, bf16[1024,128]{1,0:T(8,128)(2,1)S(1)} %bitcast.182), kind=kLoop, calls=%fused_computation.48 | loop fusion | flops 532480 | bytes 532480 | tf_op jit(solution)/shard_map/concatenate | solution.py:81
  30.6 0.3 fusion.20
  31.0 1.0 %copy.164 = bf16[2,32,32,128]{3,2,1,0:T(8,128)(2,1)} copy(bf16[2,32,32,128]{3,1,2,0:T(8,128)(2,1)S(1)} %fusion.20) | data formatting | bytes 1048576 | tf_op jit(solution)/shard_map/while | solution.py:37
  32.0 1.3 %collective-permute-start.3 = (bf16[1024,128]{1,0:T(8,128)(2,1)}, bf16[1024,128]{1,0:T(8,128)(2,1)}, u32[]{:S(2)}, u32[]{:S(2)}) collective-permute-start(bf16[1024,128]{1,0:T(8,128)(2,1)} %bitcast.56), channel_id=1, source_target_pairs={{0,2},{1,5},{2,6},{3,1},{4,0},{5,7},{6,4},{7,3},{8,10},{9,13},{10,... | collective-permute-start | bytes 786440 | tf_op jit(solution)/shard_map/ppermute | solution.py:83
  33.2 0.3 divide_convert_fusion.1
  34.0 0.3 slice_select_fusion
  34.3 1.3 %add_reduce_fusion.5 = f32[64,1024]{1,0:T(8,128)S(1)} fusion(f32[32,64]{1,0:T(8,128)S(1)} %copy.151, bf16[64,32,128]{2,1,0:T(8,128)(2,1)S(1)} %bitcast.188, bf16[1024,128]{1,0:T(8,128)(2,1)S(1)} %slice_select_fusion.1), kind=kOutput, calls=%fused_computation.32 | convolution fusion | flops 540999680 | bytes 1056768 | tf_op jit(solution)/shard_map/while/body/eval_jaxpr/ubh,qh->ubq/dot_general | solution.py:29
  35.6 0.2 copy.152
  35.9 1.3 %add_reduce_fusion.4 = f32[32,2048]{1,0:T(8,128)S(1)} fusion(f32[32,32]{1,0:T(8,128)S(1)} %copy.154, bf16[2048,128]{1,0:T(8,128)(2,1)S(1)} %slice_select_fusion, bf16[1,32,32,128]{3,2,1,0:T(8,128)(2,1)S(1)} %bitcast.193), kind=kOutput, calls=%fused_computation.31 | convolution fusion | flops 540999680 | bytes 1052672 | tf_op jit(solution)/shard_map/while/body/eval_jaxpr/trh,ch->trc/dot_general | solution.py:32
  37.2 0.3 reshape.203
  37.5 0.4 select_reduce_fusion.4
  37.9 0.2 select_reduce_fusion.5
  38.1 3.0 %collective-permute-done.1 = bf16[1040,128]{1,0:T(8,128)(2,1)} collective-permute-done((bf16[1040,128]{1,0:T(8,128)(2,1)}, bf16[1040,128]{1,0:T(8,128)(2,1)}, u32[]{:S(2)}, u32[]{:S(2)}) %collective-permute-start.1) | collective-permute-done | bytes 266272 | tf_op jit(solution)/shard_map/ppermute | solution.py:82
  41.1 1.0 %slice.56 = bf16[1024,128]{1,0:T(8,128)(2,1)S(1)} slice(bf16[1040,128]{1,0:T(8,128)(2,1)} %collective-permute-done.1), slice={[0:1024], [0:128]} | slice | bytes 524288 | tf_op jit(solution)/shard_map/slice | solution.py:102
  42.1 0.7 %slice_convert_fusion = (f32[8,128]{1,0:T(8,128)S(1)}, f32[8,128]{1,0:T(8,128)S(1)}) fusion(bf16[1040,128]{1,0:T(8,128)(2,1)} %collective-permute-done.1), kind=kLoop, calls=%fused_computation.83 | loop fusion | flops 2048 | bytes 12288 | tf_op jit(solution)/shard_map/broadcast_in_dim | solution.py:19
  42.7 0.7 %compare_bitcast_fusion = (pred[1024]{0:T(1024)(128)(4,1)S(1)}, pred[1024]{0:T(1024)(128)(4,1)S(1)}) fusion(bf16[1040,128]{1,0:T(8,128)(2,1)} %collective-permute-done.1), kind=kLoop, calls=%fused_computation.81 | loop fusion | flops 2048 | bytes 6144 | tf_op jit(solution)/shard_map/eq | solution.py:20
  43.4 0.1 copy.196
  43.7 5.1 %while.24 = (s32[]{:T(128)}, f32[2,32,32]{1,0,2:T(2,128)S(1)}, pred[2,32,32]{2,1,0:T(8,128)(4,1)S(1)}, bf16[2,1024,128]{2,1,0:T(8,128)(2,1)S(1)}, bf16[32,32,128...) while((s32[]{:T(128)}, f32[2,32,32]{1,0,2:T(2,128)S(1)}, ...), condition=%wide.region_10.11_spmd, body=%wide.region_5.10_spmd.sunk | while | flops 541130752 | bytes 2181257 | solution.py:37
  43.7 0.7 %add_reduce_fusion.10 = f32[32,1024]{1,0:T(8,128)S(1)} fusion(f32[32,32]{1,0:T(8,128)S(1)} %dynamic-slice_bitcast_fusion.8, bf16[1024,128]{1,0:T(8,128)(2,1)S(1)} %get-tuple-element.453, bf16[2,32,32,128]{3,2,1,0:T(8,128)(2,1)S(1)} %get-tuple-element.452, s32[]{:T(128)} %get-tuple-element.433), kind=kOutput, calls=%fused_computation.1.clone.1 | convolution fusion | flops 270499840 | bytes 671748 | tf_op jit(solution)/shard_map/while/body/eval_jaxpr/trh,ch->trc/dot_general | solution.py:32
  44.5 0.2 reshape.248
  44.7 0.2 select_reduce_fusion.10
  45.0 0.7 %add_reduce_fusion.11 = f32[1024,32]{0,1:T(8,128)S(1)} fusion(bf16[32,32,128]{2,1,0:T(8,128)(2,1)S(1)} %get-tuple-element.449, f32[32,32]{1,0:T(8,128)S(1)} %bitcast.202, bf16[2,1024,128]{2,1,0:T(8,128)(2,1)S(1)} %get-tuple-element.448, s32[]{:T(128)} %get-tuple-element.433), kind=kOutput, calls=%fused_computation.2.clone.1 | convolution fusion | flops 270499840 | bytes 671748 | tf_op jit(solution)/shard_map/while/body/eval_jaxpr/ubh,qh->ubq/dot_general | solution.py:29
  45.7 0.2 reshape.249
  45.9 0.2 select_reduce_fusion.11
  46.3 0.7 %add_reduce_fusion.10 = f32[32,1024]{1,0:T(8,128)S(1)} fusion(f32[32,32]{1,0:T(8,128)S(1)} %dynamic-slice_bitcast_fusion.8, bf16[1024,128]{1,0:T(8,128)(2,1)S(1)} %get-tuple-element.453, bf16[2,32,32,128]{3,2,1,0:T(8,128)(2,1)S(1)} %get-tuple-element.452, s32[]{:T(128)} %get-tuple-element.433), kind=kOutput, calls=%fused_computation.1.clone.1 | convolution fusion | flops 270499840 | bytes 671748 | tf_op jit(solution)/shard_map/while/body/eval_jaxpr/trh,ch->trc/dot_general | solution.py:32
  47.0 0.2 reshape.248
  47.3 0.2 select_reduce_fusion.10
  47.5 0.7 %add_reduce_fusion.11 = f32[1024,32]{0,1:T(8,128)S(1)} fusion(bf16[32,32,128]{2,1,0:T(8,128)(2,1)S(1)} %get-tuple-element.449, f32[32,32]{1,0:T(8,128)S(1)} %bitcast.202, bf16[2,1024,128]{2,1,0:T(8,128)(2,1)S(1)} %get-tuple-element.448, s32[]{:T(128)} %get-tuple-element.433), kind=kOutput, calls=%fused_computation.2.clone.1 | convolution fusion | flops 270499840 | bytes 671748 | tf_op jit(solution)/shard_map/while/body/eval_jaxpr/ubh,qh->ubq/dot_general | solution.py:29
  48.3 0.2 reshape.249
  48.5 0.2 select_reduce_fusion.11
  48.9 1.1 %copy.195 = bf16[32,32,128]{2,0,1:T(8,128)(2,1)S(1)} copy(bf16[32,32,128]{2,1,0:T(8,128)(2,1)} %bitcast.57) | data formatting | bytes 524288 | tf_op jit(solution)/shard_map/reshape | solution.py:17
  50.1 7.0 %while.25 = (s32[]{:T(128)}, f32[2,32,32]{1,0,2:T(2,128)S(1)}, pred[2,32,32]{2,1,0:T(8,128)(4,1)S(1)}, bf16[2,1024,128]{2,1,0:T(8,128)(2,1)S(1)}, bf16[32,32,128...) while((s32[]{:T(128)}, f32[2,32,32]{1,0,2:T(2,128)S(1)}, ...), condition=%wide.region_16.17_spmd, body=%wide.region_11.16_spmd.sunk | while | flops 541130752 | bytes 2181257 | solution.py:37
  50.1 1.7 %add_reduce_fusion.12 = f32[32,1024]{1,0:T(8,128)S(1)} fusion(f32[32,32]{1,0:T(8,128)S(1)} %dynamic-slice_bitcast_fusion.10, bf16[1024,128]{1,0:T(8,128)(2,1)} %get-tuple-element.489, bf16[2,32,32,128]{3,2,1,0:T(8,128)(2,1)S(1)} %get-tuple-element.488, s32[]{:T(128)} %get-tuple-element.469), kind=kOutput, calls=%fused_computation.16.clone.1 | convolution fusion | flops 270499840 | bytes 671748 | tf_op jit(solution)/shard_map/while/body/eval_jaxpr/trh,ch->trc/dot_general | solution.py:32
  51.8 0.2 reshape.250
  52.1 0.2 select_reduce_fusion.12
  52.4 0.7 %add_reduce_fusion.13 = f32[1024,32]{0,1:T(8,128)S(1)} fusion(bf16[32,32,128]{2,1,0:T(8,128)(2,1)S(1)} %get-tuple-element.485, f32[32,32]{1,0:T(8,128)S(1)} %bitcast.200, bf16[2,1024,128]{2,1,0:T(8,128)(2,1)S(1)} %get-tuple-element.484, s32[]{:T(128)} %get-tuple-element.469), kind=kOutput, calls=%fused_computation.17.clone.1 | convolution fusion | flops 270499840 | bytes 671748 | tf_op jit(solution)/shard_map/while/body/eval_jaxpr/ubh,qh->ubq/dot_general | solution.py:29
  53.1 0.2 reshape.251
  53.3 0.2 select_reduce_fusion.13
  53.6 1.7 %add_reduce_fusion.12 = f32[32,1024]{1,0:T(8,128)S(1)} fusion(f32[32,32]{1,0:T(8,128)S(1)} %dynamic-slice_bitcast_fusion.10, bf16[1024,128]{1,0:T(8,128)(2,1)} %get-tuple-element.489, bf16[2,32,32,128]{3,2,1,0:T(8,128)(2,1)S(1)} %get-tuple-element.488, s32[]{:T(128)} %get-tuple-element.469), kind=kOutput, calls=%fused_computation.16.clone.1 | convolution fusion | flops 270499840 | bytes 671748 | tf_op jit(solution)/shard_map/while/body/eval_jaxpr/trh,ch->trc/dot_general | solution.py:32
  55.3 0.2 reshape.250
  55.6 0.2 select_reduce_fusion.12
  55.9 0.7 %add_reduce_fusion.13 = f32[1024,32]{0,1:T(8,128)S(1)} fusion(bf16[32,32,128]{2,1,0:T(8,128)(2,1)S(1)} %get-tuple-element.485, f32[32,32]{1,0:T(8,128)S(1)} %bitcast.200, bf16[2,1024,128]{2,1,0:T(8,128)(2,1)S(1)} %get-tuple-element.484, s32[]{:T(128)} %get-tuple-element.469), kind=kOutput, calls=%fused_computation.17.clone.1 | convolution fusion | flops 270499840 | bytes 671748 | tf_op jit(solution)/shard_map/while/body/eval_jaxpr/ubh,qh->ubq/dot_general | solution.py:29
  56.6 0.2 reshape.251
  56.8 0.2 select_reduce_fusion.13
  57.4 1.4 %collective-permute-start.4 = (f32[32,64]{1,0:T(8,128)S(1)}, f32[32,64]{1,0:T(8,128)S(1)}, u32[]{:S(2)}, u32[]{:S(2)}) collective-permute-start(f32[32,64]{1,0:T(8,128)S(1)} %bitcast.197), channel_id=1, source_target_pairs={{2,0},{5,1},{6,2},{1,3},{0,4},{7,5},{4,6},{3,7},{10,8},{13,9},{14,... | collective-permute-start | bytes 24584 | tf_op jit(solution)/shard_map/ppermute | solution.py:104
  58.9 2.4 %collective-permute-done.4 = f32[32,64]{1,0:T(8,128)S(1)} collective-permute-done((f32[32,64]{1,0:T(8,128)S(1)}, f32[32,64]{1,0:T(8,128)S(1)}, u32[]{:S(2)}, u32[]{:S(2)}) %collective-permute-start.4) | collective-permute-done | bytes 8224 | tf_op jit(solution)/shard_map/ppermute | solution.py:104
  61.4 0.7 %pad_maximum_fusion.2 = f32[64,192]{1,0:T(8,128)} fusion(f32[64,64]{1,0:T(8,128)S(1)} %get-tuple-element.298, f32[64,64]{1,0:T(8,128)S(1)} %get-tuple-element.297, f32[64,64]{1,0:T(8,128)S(1)} %bitcast_select_fusion), kind=kLoop, calls=%fused_computation.55 | loop fusion | flops 24576 | bytes 98304 | tf_op jit(solution)/shard_map/concatenate | solution.py:112
  (82 shorter events, 3.1 us)
Async XLA Ops:
  0.0 1.1 %copy-start = (bf16[256,8,128]{2,1,0:T(8,128)(2,1)S(1)}, bf16[256,8,128]{2,1,0:T(8,128)(2,1)}, u32[]{:S(2)}) copy-start(bf16[256,8,128]{2,1,0:T(8,128)(2,1)} %param.8) | copy-start | bytes 1572868
  1.9 8.5 %copy-start.2 = (s32[64,32]{0,1:T(8,128)S(1)}, s32[64,32]{0,1:T(8,128)}, u32[]{:S(2)}) copy-start(s32[64,32]{0,1:T(8,128)} %param.11) | copy-start | bytes 24580
  1.9 8.5 %copy-start.3 = (s32[64]{0:T(128)S(1)}, s32[64]{0:T(128)}, u32[]{:S(2)}) copy-start(s32[64]{0:T(128)} %param.10) | copy-start | bytes 772
  3.0 23.7 %all-to-all-start = ((bf16[32,8,8,128]{3,2,1,0:T(8,128)(2,1)}), bf16[32,8,8,128]{3,2,1,0:T(8,128)(2,1)S(1)}, u32[]{:S(2)}, u32[]{:S(2)}) async-start(bf16[32,8,8,128]{3,2,1,0:T(8,128)(2,1)} %broadcast_select_fusion), calls=%async_computation | async-start | bytes 1048576 | tf_op jit(solution)/shard_map/all_to_all | solution.py:54
  28.7 4.9 %collective-permute-start = (bf16[2064,128]{1,0:T(8,128)(2,1)S(1)}, bf16[2064,128]{1,0:T(8,128)(2,1)S(1)}, u32[]{:S(2)}, u32[]{:S(2)}) collective-permute-start(bf16[2064,128]{1,0:T(8,128)(2,1)S(1)} %pad_maximum_fusion), channel_id=1, source_target_pairs={{0,1},{1,0},{2,3},{3,2},{4,5},{5,4},{6,7},{7,6},{8,9},{9,8},{10,11... | collective-permute-start | bytes 1585160 | tf_op jit(solution)/shard_map/ppermute | solution.py:84
  30.6 10.5 %collective-permute-start.1 = (bf16[1040,128]{1,0:T(8,128)(2,1)}, bf16[1040,128]{1,0:T(8,128)(2,1)}, u32[]{:S(2)}, u32[]{:S(2)}) collective-permute-start(bf16[1040,128]{1,0:T(8,128)(2,1)} %pad_maximum_fusion.1), channel_id=1, source_target_pairs={{0,2},{1,5},{2,6},{3,1},{4,0},{5,7},{6,4},{7,3},{8,10},{9,13},{10,... | collective-permute-start | bytes 798728 | tf_op jit(solution)/shard_map/ppermute | solution.py:82
  32.0 16.9 %collective-permute-start.3 = (bf16[1024,128]{1,0:T(8,128)(2,1)}, bf16[1024,128]{1,0:T(8,128)(2,1)}, u32[]{:S(2)}, u32[]{:S(2)}) collective-permute-start(bf16[1024,128]{1,0:T(8,128)(2,1)} %bitcast.56), channel_id=1, source_target_pairs={{0,2},{1,5},{2,6},{3,1},{4,0},{5,7},{6,4},{7,3},{8,10},{9,13},{10,... | collective-permute-start | bytes 786440 | tf_op jit(solution)/shard_map/ppermute | solution.py:83
  37.9 5.8 %copy-start.1 = (bf16[2,32,32,128]{3,2,1,0:T(8,128)(2,1)S(1)}, bf16[2,32,32,128]{3,2,1,0:T(8,128)(2,1)}, u32[]{:S(2)}) copy-start(bf16[2,32,32,128]{3,2,1,0:T(8,128)(2,1)} %copy.164) | copy-start | bytes 1572868
  43.4 15.4 %collective-permute-start.2 = (f32[32,64]{1,0:T(8,128)S(1)}, f32[32,64]{1,0:T(8,128)S(1)}, u32[]{:S(2)}, u32[]{:S(2)}) collective-permute-start(f32[32,64]{1,0:T(8,128)S(1)} %fusion.25), channel_id=1, source_target_pairs={{0,1},{1,0},{2,3},{3,2},{4,5},{5,4},{6,7},{7,6},{8,9},{9,8},{10,11... | collective-permute-start | bytes 24584 | tf_op jit(solution)/shard_map/ppermute | solution.py:93
  57.3 4.0 %collective-permute-start.5 = (f32[32,64]{1,0:T(8,128)S(1)}, f32[32,64]{1,0:T(8,128)S(1)}, u32[]{:S(2)}, u32[]{:S(2)}) collective-permute-start(f32[32,64]{1,0:T(8,128)S(1)} %bitcast.198), channel_id=1, source_target_pairs={{2,0},{5,1},{6,2},{1,3},{0,4},{7,5},{4,6},{3,7},{10,8},{13,9},{14,... | collective-permute-start | bytes 24584 | tf_op jit(solution)/shard_map/ppermute | solution.py:106
  57.4 3.8 %collective-permute-start.4 = (f32[32,64]{1,0:T(8,128)S(1)}, f32[32,64]{1,0:T(8,128)S(1)}, u32[]{:S(2)}, u32[]{:S(2)}) collective-permute-start(f32[32,64]{1,0:T(8,128)S(1)} %bitcast.197), channel_id=1, source_target_pairs={{2,0},{5,1},{6,2},{1,3},{0,4},{7,5},{4,6},{3,7},{10,8},{13,9},{14,... | collective-permute-start | bytes 24584 | tf_op jit(solution)/shard_map/ppermute | solution.py:104

commit v5 on v4

--- a/solution.py
+++ b/solution.py
@@ -78,9 +78,12 @@
     chip_pairs = [(p, p ^ 1) for p in range(n_pool)]
 
     half = n_tok // 2
-    first = jnp.concatenate([block[:half], bias.reshape(-1, width)], axis=0)
+    bias_rows = half // width
+    pad_rows = -bias_rows % 16
+    pad = jnp.zeros((pad_rows, width), jnp.bfloat16)
+    first = jnp.concatenate([block[:half], bias[:half].reshape(bias_rows, width), pad], axis=0)
+    second = jnp.concatenate([block[half:], bias[half:].reshape(bias_rows, width), pad], axis=0)
     z_first = lax.ppermute(first, "pool", send_pairs)
-    z_second = lax.ppermute(block[half:], "pool", send_pairs)
     c_recv = lax.ppermute(packed, "pool", chip_pairs)
 
     c_blk, c_bias = c_recv[:n_tok], c_recv[n_tok:].reshape(-1)
@@ -98,11 +101,12 @@
     )
     tile0 = jnp.where(is_a, joined, joined.T)
 
-    z_bias = z_first[half:].reshape(-1)
-    tile_a = tile_scores(block, bias, z_first[:half], z_bias[:half], tok)
+    second, z_first = lax.optimization_barrier((second, z_first))
+    z_second = lax.ppermute(second, "pool", send_pairs)
+    tile_a = tile_scores(block, bias, z_first[:half], z_first[half:half + bias_rows].reshape(-1), tok)
     tile_a, z_second = lax.optimization_barrier((tile_a, z_second))
     back_a = lax.ppermute(tile_a.T, "pool", back_pairs)
-    tile_b = tile_scores(block, bias, z_second, z_bias[half:], tok)
+    tile_b = tile_scores(block, bias, z_second[:half], z_second[half:half + bias_rows].reshape(-1), tok)
     back_b = lax.ppermute(tile_b.T, "pool", back_pairs)
     tile_z = jnp.concatenate([tile_a, tile_b], axis=1)
     tile_back = jnp.concatenate([back_a, back_b], axis=0)

time: 62.5 us -> 74 us (1.18)
  waiting for transfers between devices: 21.3 us -> 34.2 us
  matrix products: 10.3 us -> 8.27 us
  other arithmetic: 8.85 us -> 10.5 us
  local copies, waits for them, and re-layouts: 11 us -> 10.2 us
    ppermute x1, waiting for transfers between devices: 0.01 us -> 9.31 us  [shards(): z_second = lax.ppermute(second, 'pool', send_pairs)]
    ppermute x1, waiting for transfers between devices: 2.97 us -> 7.49 us  [shards(): z_first = lax.ppermute(first, 'pool', send_pairs)]
    ppermute x1, waiting for transfers between devices: 2.37 us -> 0.01 us  [shards(): back_a = lax.ppermute(tile_a.T, 'pool', back_pairs)]
    ppermute x1, starting transfers between devices: 0.02 us -> 2.29 us  [shards(): back_b = lax.ppermute(tile_b.T, 'pool', back_pairs)]
    dot_general x5, matrix products: 6.07 us -> 4.12 us  [one_block(): jnp.einsum('trh,ch->trc', turned, other, preferred_element_type=jnp.float32)]
    ppermute x1, waiting for transfers between devices: 0.01 us -> 1.46 us  [shards(): back_b = lax.ppermute(tile_b.T, 'pool', back_pairs)]
    ppermute x1, starting transfers between devices: 1.44 us -> 0.18 us  [shards(): back_a = lax.ppermute(tile_a.T, 'pool', back_pairs)]
    ppermute x1, starting transfers between devices: 1.26 us -> 0.01 us  [shards(): z_second = lax.ppermute(second, 'pool', send_pairs)]
  transfers between devices with their start and end apart: 7 -> 7, of which waited for: 3 -> 4; matrix products, arithmetic and copies ran while one was open for 39% -> 22% of each run, Pallas kernels for 0% -> 0%
where the time goes in v5:
time: 74 us; the launch traced here: 73.7 us
  waiting for transfers between devices  34.2 us (46%)
  other arithmetic  10.5 us (14%)
  local copies, waits for them, and re-layouts  10.2 us (14%)
  starting transfers between devices  9.8 us (13%)
  matrix products  8.27 us (11%)
    all_to_all x1, waiting for transfers between devices, shards(): lax.all_to_all(outgoing, ('enc', 'pool'), split_axis=0, concat_axis=0, ti...  16 us
    ppermute x1, waiting for transfers between devices, shards(): z_second = lax.ppermute(second, 'pool', send_pairs)  9.31 us
    ppermute x1, waiting for transfers between devices, shards(): z_first = lax.ppermute(first, 'pool', send_pairs)  7.49 us
    all_to_all x1, starting transfers between devices, shards(): lax.all_to_all(outgoing, ('enc', 'pool'), split_axis=0, concat_axis=0, ti...  7.3 us
    dot_general x5, matrix products, one_block(): jnp.einsum('ubh,qh->ubq', other_tr, flat, preferred_element_type=jnp.floa...  4.14 us
    dot_general x5, matrix products, one_block(): jnp.einsum('trh,ch->trc', turned, other, preferred_element_type=jnp.float32)  4.12 us
    ppermute x1, starting transfers between devices, shards(): back_b = lax.ppermute(tile_b.T, 'pool', back_pairs)  2.29 us
    convert_element_type x3, other arithmetic, shards(): (values / jnp.sqrt(jnp.sum(values * values, axis=-1, keepdims=True) + 1e-...  1.84 us
  transfers between devices with their start and end apart: 7, of which 4 were waited for; matrix products, arithmetic and copies ran while one was open for 22% of the time, Pallas kernels for 0%

profile of v5, /device:TPU:0, one launch (start us, length us, event | category | flops | bytes accessed | tf_op | source)
XLA Modules:
  0.0 73.7 jit_solution(2478734355230029004)
XLA Ops:
  0.0 0.8 %reshape.206 = s32[32,8,8]{2,1,0:T(8,128)S(1)} reshape(s32[2048]{0:T(1024)} %param.9) | data formatting | bytes 16384 | tf_op jit(solution)/shard_map/reshape | solution.py:51
  1.1 0.8 %gather_fusion = bf16[256,8,128]{2,1,0:T(8,128)(2,1)S(1)} fusion(bf16[256,8,128]{2,1,0:T(8,128)(2,1)S(1)} %copy-done, s32[1024]{0:T(1024)S(1)} %pad_clamp_fusion), kind=kCustom, calls=%fused_computation | custom fusion | bytes 1049600 | tf_op jit(solution)/shard_map/jit(_take)/gather | solution.py:53
  1.9 1.1 %broadcast_select_fusion = bf16[32,8,8,128]{3,2,1,0:T(8,128)(2,1)} fusion(bf16[32,8,8,128]{3,2,1,0:T(8,128)(2,1)S(1)} %bitcast.183, pred[32,8]{1,0:T(8,128)(4,1)S(1)} %compare_and_fusion), kind=kLoop, calls=%fused_computation.47 | loop fusion | flops 262144 | bytes 1048832 | tf_op jit(solution)/shard_map/jit(_take)/select_n | solution.py:53
  3.0 7.3 %all-to-all-start = ((bf16[32,8,8,128]{3,2,1,0:T(8,128)(2,1)}), bf16[32,8,8,128]{3,2,1,0:T(8,128)(2,1)S(1)}, u32[]{:S(2)}, u32[]{:S(2)}) async-start(bf16[32,8,8,128]{3,2,1,0:T(8,128)(2,1)} %broadcast_select_fusion), calls=%async_computation | async-start | bytes 1048576 | tf_op jit(solution)/shard_map/all_to_all | solution.py:54
  10.7 16.0 %all-to-all-done = bf16[32,8,8,128]{3,2,1,0:T(8,128)(2,1)S(1)} async-done(((bf16[32,8,8,128]{3,2,1,0:T(8,128)(2,1)}), bf16[32,8,8,128]{3,2,1,0:T(8,128)(2,1)S(1)}, u32[]{:S(2)}, u32[]{:S(2)}) %all-to-all-start) | async-done | bytes 524320 | tf_op jit(solution)/shard_map/all_to_all | solution.py:54
  26.7 0.3 multiply_reduce_fusion
  27.2 0.1 reshape.228
  27.3 0.2 copy.149
  27.5 0.2 sqrt.24
  27.6 0.1 reshape.253
  27.8 0.1 reshape.252
  27.9 0.1 convert_element_type.107
  28.0 0.1 copy.147
  28.1 0.3 fusion.16
  28.5 0.9 %pad_maximum_fusion = bf16[2064,128]{1,0:T(8,128)(2,1)} fusion(bf16[16,128]{1,0:T(8,128)(2,1)S(1)} %reshape_reshape.2, bf16[2048,128]{1,0:T(8,128)(2,1)S(1)} %fusion.16), kind=kLoop, calls=%fused_computation.40 | loop fusion | flops 1056768 | bytes 1056768 | tf_op jit(solution)/shard_map/concatenate | solution.py:67
  29.3 0.3 divide_convert_fusion.2
  29.7 0.3 fusion.20
  30.0 0.2 sqrt.26
  30.2 1.0 %copy.167 = bf16[2,32,32,128]{3,2,1,0:T(8,128)(2,1)} copy(bf16[2,32,32,128]{3,1,2,0:T(8,128)(2,1)S(1)} %fusion.20) | data formatting | bytes 1048576 | tf_op jit(solution)/shard_map/while | solution.py:37
  31.2 1.2 %divide_convert_fusion.1 = bf16[2,1024,128]{2,1,0:T(8,128)(2,1)} fusion(f32[2,1024,128]{2,1,0:T(8,128)S(1)} %bitcast.178, f32[2,1024]{1,0:T(2,128)S(1)} %sqrt.26), kind=kLoop, calls=%fused_computation.36 | loop fusion | flops 524288 | bytes 1581056 | tf_op jit(solution)/shard_map/convert_element_type | solution.py:59
  32.9 0.4 slice_select_fusion
  33.4 0.8 %copy-done.2 = bf16[2048,128]{1,0:T(8,128)(2,1)} copy-done((bf16[2048,128]{1,0:T(8,128)(2,1)}, bf16[2048,128]{1,0:T(8,128)(2,1)S(1)}, u32[]{:S(2)}) %copy-start.2) | copy-done | bytes 524312
  34.1 1.3 %add_reduce_fusion.5 = f32[64,1024]{1,0:T(8,128)S(1)} fusion(f32[32,64]{1,0:T(8,128)S(1)} %copy.154, bf16[64,32,128]{2,1,0:T(8,128)(2,1)S(1)} %bitcast.190, bf16[1024,128]{1,0:T(8,128)(2,1)S(1)} %slice_select_fusion.1), kind=kOutput, calls=%fused_computation.32 | convolution fusion | flops 540999680 | bytes 1056768 | tf_op jit(solution)/shard_map/while/body/eval_jaxpr/ubh,qh->ubq/dot_general | solution.py:29
  35.4 0.2 copy.155
  35.6 0.8 %pad_maximum_fusion.2 = (bf16[1040,128]{1,0:T(8,128)(2,1)}, bf16[1040,128]{1,0:T(8,128)(2,1)}) fusion(bf16[8,128]{1,0:T(8,128)(2,1)S(1)} %broadcast_in_dim.139, bf16[8,128]{1,0:T(8,128)(2,1)S(1)} %reshape.212, bf16[1024,128]{1,0:T(8,128)(2,1)S(1)} %bitcast.182, bf16[8,128]{1,0:T(8,128)(2,1)S(1)} %reshape.213, bf16[1024,128]{1,0:T(8,128)(2,1)S(1)} %bitcast.188), kind=kLoop, calls=%fused_computation.49 | loop fusion | flops 1464320 | bytes 1062912 | tf_op jit(solution)/shard_map/concatenate | solution.py:84
  36.5 1.3 %add_reduce_fusion.4 = f32[32,2048]{1,0:T(8,128)S(1)} fusion(f32[32,32]{1,0:T(8,128)S(1)} %copy.157, bf16[2048,128]{1,0:T(8,128)(2,1)S(1)} %copy-done.3, bf16[1,32,32,128]{3,2,1,0:T(8,128)(2,1)S(1)} %bitcast.195), kind=kOutput, calls=%fused_computation.31 | convolution fusion | flops 540999680 | bytes 1052672 | tf_op jit(solution)/shard_map/while/body/eval_jaxpr/trh,ch->trc/dot_general | solution.py:32
  37.7 0.3 reshape.211
  38.1 0.3 select_reduce_fusion.4
  38.4 0.2 select_reduce_fusion.5
  38.7 7.5 %collective-permute-done.1 = bf16[1040,128]{1,0:T(8,128)(2,1)} collective-permute-done((bf16[1040,128]{1,0:T(8,128)(2,1)}, bf16[1040,128]{1,0:T(8,128)(2,1)}, u32[]{:S(2)}, u32[]{:S(2)}) %collective-permute-start.1) | collective-permute-done | bytes 266272 | tf_op jit(solution)/shard_map/ppermute | solution.py:86
  46.2 0.7 compare_bitcast_fusion.1
  46.8 0.7 slice_convert_fusion.1
  47.5 1.0 %slice.62 = bf16[1024,128]{1,0:T(8,128)(2,1)S(1)} slice(bf16[1040,128]{1,0:T(8,128)(2,1)} %collective-permute-done.1), slice={[0:1024], [0:128]} | slice | bytes 524288 | tf_op jit(solution)/shard_map/slice | solution.py:106
  48.8 5.0 %while.24 = (s32[]{:T(128)}, f32[2,32,32]{1,0,2:T(2,128)S(1)}, pred[2,32,32]{2,1,0:T(8,128)(4,1)S(1)}, bf16[2,1024,128]{2,1,0:T(8,128)(2,1)S(1)}, bf16[32,32,128...) while((s32[]{:T(128)}, f32[2,32,32]{1,0,2:T(2,128)S(1)}, ...), condition=%wide.region_10.11_spmd, body=%wide.region_5.10_spmd.sunk | while | flops 541130752 | bytes 2181265 | solution.py:37
  48.9 0.7 add_reduce_fusion.10
  49.6 0.7 add_reduce_fusion.11
  50.4 0.2 reshape.259
  50.5 0.2 select_reduce_fusion.11
  50.7 0.2 reshape.258
  50.9 0.2 select_reduce_fusion.10
  51.4 0.7 add_reduce_fusion.10
  52.1 0.7 add_reduce_fusion.11
  52.9 0.2 reshape.259
  53.0 0.2 select_reduce_fusion.11
  53.2 0.2 reshape.258
  53.4 0.2 select_reduce_fusion.10
  54.0 9.3 %collective-permute-done.3 = bf16[1040,128]{1,0:T(8,128)(2,1)S(1)} collective-permute-done((bf16[1040,128]{1,0:T(8,128)(2,1)S(1)}, bf16[1040,128]{1,0:T(8,128)(2,1)S(1)}, u32[]{:S(2)}, u32[]{:S(2)}) %collective-permute-start.3) | collective-permute-done | bytes 266272 | tf_op jit(solution)/shard_map/ppermute | solution.py:105
  63.5 0.2 collective-permute-start.4
  63.9 5.0 %while.25 = (s32[]{:T(128)}, f32[2,32,32]{1,0,2:T(2,128)S(1)}, pred[2,32,32]{2,1,0:T(8,128)(4,1)S(1)}, bf16[2,1024,128]{2,1,0:T(8,128)(2,1)S(1)}, bf16[32,32,128...) while((s32[]{:T(128)}, f32[2,32,32]{1,0,2:T(2,128)S(1)}, ...), condition=%wide.region_16.17_spmd, body=%wide.region_11.16_spmd.sunk | while | flops 541130752 | bytes 2181265 | solution.py:37
  64.0 0.7 add_reduce_fusion.12
  64.7 0.7 add_reduce_fusion.13
  65.4 0.2 reshape.261
  65.6 0.2 select_reduce_fusion.13
  65.8 0.2 reshape.260
  66.0 0.2 select_reduce_fusion.12
  66.4 0.7 add_reduce_fusion.12
  67.2 0.7 add_reduce_fusion.13
  67.9 0.2 reshape.261
  68.1 0.2 select_reduce_fusion.13
  68.3 0.2 reshape.260
  68.5 0.2 select_reduce_fusion.12
  69.1 2.3 %collective-permute-start.5 = (f32[32,64]{1,0:T(8,128)S(1)}, f32[32,64]{1,0:T(8,128)S(1)}, u32[]{:S(2)}, u32[]{:S(2)}) collective-permute-start(f32[32,64]{1,0:T(8,128)S(1)} %bitcast.200), channel_id=1, source_target_pairs={{2,0},{5,1},{6,2},{1,3},{0,4},{7,5},{4,6},{3,7},{10,8},{13,9},{14,... | collective-permute-start | bytes 24584 | tf_op jit(solution)/shard_map/ppermute | solution.py:110
  71.4 1.5 %collective-permute-done.5 = f32[32,64]{1,0:T(8,128)S(1)} collective-permute-done((f32[32,64]{1,0:T(8,128)S(1)}, f32[32,64]{1,0:T(8,128)S(1)}, u32[]{:S(2)}, u32[]{:S(2)}) %collective-permute-start.5) | collective-permute-done | bytes 8224 | tf_op jit(solution)/shard_map/ppermute | solution.py:110
  72.9 0.7 pad_maximum_fusion.3
  (96 shorter events, 3.4 us)
Async XLA Ops:
  0.0 1.1 %copy-start = (bf16[256,8,128]{2,1,0:T(8,128)(2,1)S(1)}, bf16[256,8,128]{2,1,0:T(8,128)(2,1)}, u32[]{:S(2)}) copy-start(bf16[256,8,128]{2,1,0:T(8,128)(2,1)} %param.8) | copy-start | bytes 1572868
  1.9 8.5 %copy-start.6 = (s32[64,32]{0,1:T(8,128)S(1)}, s32[64,32]{0,1:T(8,128)}, u32[]{:S(2)}) copy-start(s32[64,32]{0,1:T(8,128)} %param.11) | copy-start | bytes 24580
  1.9 8.6 %copy-start.7 = (s32[64]{0:T(128)S(1)}, s32[64]{0:T(128)}, u32[]{:S(2)}) copy-start(s32[64]{0:T(128)} %param.10) | copy-start | bytes 772
  3.0 23.7 %all-to-all-start = ((bf16[32,8,8,128]{3,2,1,0:T(8,128)(2,1)}), bf16[32,8,8,128]{3,2,1,0:T(8,128)(2,1)S(1)}, u32[]{:S(2)}, u32[]{:S(2)}) async-start(bf16[32,8,8,128]{3,2,1,0:T(8,128)(2,1)} %broadcast_select_fusion), calls=%async_computation | async-start | bytes 1048576 | tf_op jit(solution)/shard_map/all_to_all | solution.py:54
  29.3 3.1 %collective-permute-start = (bf16[2064,128]{1,0:T(8,128)(2,1)}, bf16[2064,128]{1,0:T(8,128)(2,1)S(1)}, u32[]{:S(2)}, u32[]{:S(2)}) collective-permute-start(bf16[2064,128]{1,0:T(8,128)(2,1)} %pad_maximum_fusion), channel_id=1, source_target_pairs={{0,1},{1,0},{2,3},{3,2},{4,5},{5,4},{6,7},{7,6},{8,9},{9,8},{10,11... | collective-permute-start | bytes 1585160 | tf_op jit(solution)/shard_map/ppermute | solution.py:87
  33.3 0.8 %copy-start.2 = (bf16[2048,128]{1,0:T(8,128)(2,1)}, bf16[2048,128]{1,0:T(8,128)(2,1)S(1)}, u32[]{:S(2)}) copy-start(bf16[2048,128]{1,0:T(8,128)(2,1)S(1)} %slice_select_fusion) | copy-start | bytes 1572868
  35.4 1.1 %copy-start.3 = (bf16[2048,128]{1,0:T(8,128)(2,1)S(1)}, bf16[2048,128]{1,0:T(8,128)(2,1)}, u32[]{:S(2)}) copy-start(bf16[2048,128]{1,0:T(8,128)(2,1)} %copy-done.2) | copy-start | bytes 1572868
  36.5 9.7 %collective-permute-start.1 = (bf16[1040,128]{1,0:T(8,128)(2,1)}, bf16[1040,128]{1,0:T(8,128)(2,1)}, u32[]{:S(2)}, u32[]{:S(2)}) collective-permute-start(bf16[1040,128]{1,0:T(8,128)(2,1)} %get-tuple-element.302), channel_id=1, source_target_pairs={{0,2},{1,5},{2,6},{3,1},{4,0},{5,7},{6,4},{7,3},{8,10},{9,13},{10,... | collective-permute-start | bytes 798728 | tf_op jit(solution)/shard_map/ppermute | solution.py:86
  38.4 10.3 %copy-start.1 = (bf16[2,1024,128]{2,1,0:T(8,128)(2,1)S(1)}, bf16[2,1024,128]{2,1,0:T(8,128)(2,1)}, u32[]{:S(2)}) copy-start(bf16[2,1024,128]{2,1,0:T(8,128)(2,1)} %divide_convert_fusion.1) | copy-start | bytes 1572868
  38.4 10.3 %copy-start.4 = (bf16[2,32,32,128]{3,2,1,0:T(8,128)(2,1)S(1)}, bf16[2,32,32,128]{3,2,1,0:T(8,128)(2,1)}, u32[]{:S(2)}) copy-start(bf16[2,32,32,128]{3,2,1,0:T(8,128)(2,1)} %copy.167) | copy-start | bytes 1572868
  48.6 5.3 %collective-permute-start.2 = (f32[32,64]{1,0:T(8,128)S(1)}, f32[32,64]{1,0:T(8,128)S(1)}, u32[]{:S(2)}, u32[]{:S(2)}) collective-permute-start(f32[32,64]{1,0:T(8,128)S(1)} %fusion.25), channel_id=1, source_target_pairs={{0,1},{1,0},{2,3},{3,2},{4,5},{5,4},{6,7},{7,6},{8,9},{9,8},{10,11... | collective-permute-start | bytes 24584 | tf_op jit(solution)/shard_map/ppermute | solution.py:96
  48.8 5.1 %copy-start.5 = (bf16[1040,128]{1,0:T(8,128)(2,1)S(1)}, bf16[1040,128]{1,0:T(8,128)(2,1)}, u32[]{:S(2)}) copy-start(bf16[1040,128]{1,0:T(8,128)(2,1)} %get-tuple-element.149) | copy-start | bytes 798724
  53.9 9.5 %collective-permute-start.3 = (bf16[1040,128]{1,0:T(8,128)(2,1)S(1)}, bf16[1040,128]{1,0:T(8,128)(2,1)S(1)}, u32[]{:S(2)}, u32[]{:S(2)}) collective-permute-start(bf16[1040,128]{1,0:T(8,128)(2,1)S(1)} %copy-done.5), channel_id=1, source_target_pairs={{0,2},{1,5},{2,6},{3,1},{4,0},{5,7},{6,4},{7,3},{8,10},{9,13},{10,... | collective-permute-start | bytes 798728 | tf_op jit(solution)/shard_map/ppermute | solution.py:105
  63.5 7.9 %collective-permute-start.4 = (f32[32,64]{1,0:T(8,128)S(1)}, f32[32,64]{1,0:T(8,128)S(1)}, u32[]{:S(2)}, u32[]{:S(2)}) collective-permute-start(f32[32,64]{1,0:T(8,128)S(1)} %bitcast.199), channel_id=1, source_target_pairs={{2,0},{5,1},{6,2},{1,3},{0,4},{7,5},{4,6},{3,7},{10,8},{13,9},{14,... | collective-permute-start | bytes 24584 | tf_op jit(solution)/shard_map/ppermute | solution.py:108
  69.1 3.8 %collective-permute-start.5 = (f32[32,64]{1,0:T(8,128)S(1)}, f32[32,64]{1,0:T(8,128)S(1)}, u32[]{:S(2)}, u32[]{:S(2)}) collective-permute-start(f32[32,64]{1,0:T(8,128)S(1)} %bitcast.200), channel_id=1, source_target_pairs={{2,0},{5,1},{6,2},{1,3},{0,4},{7,5},{4,6},{3,7},{10,8},{13,9},{14,... | collective-permute-start | bytes 24584 | tf_op jit(solution)/shard_map/ppermute | solution.py:110

commit v6 on v3

--- a/solution.py
+++ b/solution.py
@@ -48,9 +48,11 @@
     items_dev = lengths.shape[0]
     per = items_dev // n_pool
     pool_index = lax.axis_index("pool")
-    table = slot_items.reshape(owners, n_pool, per)
-    mine = lax.dynamic_index_in_dim(table, pool_index, 1, keepdims=False) - pool_index * group
-    outgoing = jnp.take(encoded, mine, axis=0)
+    slot_of = (jnp.arange(owners, dtype=jnp.int32) * items_dev + pool_index * per)[:, None] + jnp.arange(
+        per, dtype=jnp.int32
+    )[None, :]
+    mine = jnp.take(slot_items, slot_of, mode="clip") - pool_index * group
+    outgoing = jnp.take(encoded, mine, axis=0, mode="clip")
     arrived = lax.all_to_all(outgoing, ("enc", "pool"), split_axis=0, concat_axis=0, tiled=True)
     arrived = arrived.reshape(n_enc, n_pool, per, toks, width)
     tok = n_enc * toks
@@ -62,9 +64,9 @@
     position = jnp.arange(tok, dtype=jnp.int32)[None, :]
     valid = (position < lengths[:, None]) & ((position == 0) | (token_mask == 1))
     bias = jnp.where(valid, 0.0, -4.0).astype(jnp.bfloat16).reshape(-1)
-    block = normed.reshape(items_dev * tok, width)
     n_tok = items_dev * tok
-    packed = jnp.concatenate([block, bias.reshape(-1, width)], axis=0)
+    packed = jnp.concatenate([normed.reshape(n_tok, width), bias.reshape(-1, width)], axis=0)
+    block = packed[:n_tok]
 
     pool_index = lax.axis_index("pool")
     parity = (pool_index ^ (pool_index >> 1) ^ (pool_index >> 2)) & 1

time: 60.7 us -> 61.8 us (1.018)
  local copies, waits for them, and re-layouts: 9.45 us -> 11.6 us
  other arithmetic: 8.85 us -> 7.78 us
    gather x1 -> x2, local copies, waits for them, and re-layouts: 0.81 us -> 3.3 us  [the longest x1 1.72 us: shards(): mine = jnp.take(slot_items, slot_of, mode='clip') - pool_index * group]
    select_n x2 -> x0, other arithmetic: 1.14 us -> none  [shards(): outgoing = jnp.take(encoded, mine, axis=0)]
    reshape x1 -> x0, local copies, waits for them, and re-layouts: 0.85 us -> none  [shards(): table = slot_items.reshape(owners, n_pool, per)]
where the time goes in v6:
time: 61.8 us; the launch traced here: 61.3 us
  waiting for transfers between devices  26 us (42%)
  local copies, waits for them, and re-layouts  11.6 us (19%)
  starting transfers between devices  7.83 us (13%)
  other arithmetic  7.78 us (13%)
  matrix products  7.6 us (12%)
    all_to_all x1, waiting for transfers between devices, shards(): lax.all_to_all(outgoing, ('enc', 'pool'), split_axis=0, concat_axis=0, ti...  16 us
    all_to_all x1, starting transfers between devices, shards(): lax.all_to_all(outgoing, ('enc', 'pool'), split_axis=0, concat_axis=0, ti...  7.3 us
    ppermute x1, waiting for transfers between devices, shards(): z_recv = lax.ppermute(packed, 'pool', send_pairs)  6.12 us
    dot_general x3, matrix products, one_block(): jnp.einsum('ubh,qh->ubq', other_tr, flat, preferred_element_type=jnp.floa...  3.81 us
    dot_general x3, matrix products, one_block(): jnp.einsum('trh,ch->trc', turned, other, preferred_element_type=jnp.float32)  3.79 us
    ppermute x1, waiting for transfers between devices, shards(): tile_back = lax.ppermute(tile_z.T, 'pool', back_pairs)  3.78 us
    gather x1, local copies, waits for them, and re-layouts, shards(): mine = jnp.take(slot_items, slot_of, mode='clip') - pool_index * group  1.72 us
    convert_element_type x3, other arithmetic, shards(): (values / jnp.sqrt(jnp.sum(values * values, axis=-1, keepdims=True) + 1e-...  1.71 us
  transfers between devices with their start and end apart: 5, of which 4 were waited for; matrix products, arithmetic and copies ran while one was open for 30% of the time, Pallas kernels for 0%

profile of v6, /device:TPU:0, one launch (start us, length us, event | category | flops | bytes accessed | tf_op | source)
XLA Modules:
  0.0 61.3 jit_solution(4632002085271300873)
XLA Ops:
  0.1 0.1 reshape.211
  0.2 0.6 copy-done.1
  0.8 1.7 %gather_fusion = s32[256]{0:T(256)S(1)} fusion(s32[2048]{0:T(1024)S(1)} %copy-done.1, s32[1024]{0:T(1024)S(1)} %pad_clamp_fusion.1), kind=kCustom, calls=%fused_computation | custom fusion | bytes 3072 | tf_op jit(solution)/shard_map/jit(_take)/gather | solution.py:54
  2.5 1.6 %gather_fusion.1 = bf16[256,8,128]{2,1,0:T(8,128)(2,1)} fusion(bf16[256,8,128]{2,1,0:T(8,128)(2,1)S(1)} %copy-done, s32[1024]{0:T(1024)S(1)} %pad_clamp_fusion), kind=kCustom, calls=%fused_computation.1 | custom fusion | bytes 1049600 | tf_op jit(solution)/shard_map/jit(_take)/gather | solution.py:55
  4.1 7.3 %all-to-all-start = ((bf16[32,8,8,128]{3,2,1,0:T(8,128)(2,1)}), bf16[32,8,8,128]{3,2,1,0:T(8,128)(2,1)S(1)}, u32[]{:S(2)}, u32[]{:S(2)}) async-start(bf16[32,8,8,128]{3,2,1,0:T(8,128)(2,1)} %bitcast.11), calls=%async_computation | async-start | bytes 1048576 | tf_op jit(solution)/shard_map/all_to_all | solution.py:56
  11.4 0.1 copy.85
  11.5 0.1 broadcast_compare_fusion
  11.6 0.1 reshape_reshape.2
  11.7 0.1 copy.111
  11.8 16.0 %all-to-all-done = bf16[32,8,8,128]{3,2,1,0:T(8,128)(2,1)S(1)} async-done(((bf16[32,8,8,128]{3,2,1,0:T(8,128)(2,1)}), bf16[32,8,8,128]{3,2,1,0:T(8,128)(2,1)S(1)}, u32[]{:S(2)}, u32[]{:S(2)}) %all-to-all-start) | async-done | bytes 524320 | tf_op jit(solution)/shard_map/all_to_all | solution.py:56
  27.8 0.3 multiply_reduce_fusion
  28.1 0.1 copy.87
  28.3 0.1 reshape.201
  28.4 0.2 copy.88
  28.6 0.2 sqrt.24
  28.7 0.1 reshape.235
  28.8 0.1 convert_element_type.100
  29.0 0.1 copy.86
  29.1 0.3 fusion.5
  29.5 0.8 %pad_maximum_fusion = bf16[2064,128]{1,0:T(8,128)(2,1)} fusion(bf16[16,128]{1,0:T(8,128)(2,1)S(1)} %reshape_reshape.2, bf16[2048,128]{1,0:T(8,128)(2,1)S(1)} %fusion.5), kind=kLoop, calls=%fused_computation.25 | loop fusion | flops 1056768 | bytes 1056768 | tf_op jit(solution)/shard_map/concatenate | solution.py:68
  30.3 0.1 reshape.236
  30.4 0.2 sqrt.26
  30.6 0.2 fusion.6
  30.8 1.2 %divide_convert_fusion.1 = bf16[2,1024,128]{2,1,0:T(8,128)(2,1)} fusion(f32[2,1024,128]{2,1,0:T(8,128)S(1)} %bitcast.125, f32[2,1024]{1,0:T(2,128)S(1)} %sqrt.26), kind=kLoop, calls=%fused_computation.22 | loop fusion | flops 524288 | bytes 1581056 | tf_op jit(solution)/shard_map/convert_element_type | solution.py:61
  32.0 0.3 fusion.10
  32.3 0.1 collective-permute-done
  32.4 0.1 reshape.186
  32.5 0.6 broadcast_compare_fusion.1
  33.1 0.7 %copy.93 = f32[32,64]{1,0:T(8,128)} copy(f32[32,64]{0,1:T(8,128)S(1)} %convert_bitcast_fusion) | data formatting | bytes 16384 | tf_op jit(solution)/shard_map/transpose | solution.py:19
  33.8 0.1 slice.35
  33.9 0.1 copy.96
  34.0 1.1 %slice_select_fusion = bf16[2048,128]{1,0:T(8,128)(2,1)S(1)} fusion(bf16[2064,128]{1,0:T(8,128)(2,1)S(1)} %collective-permute-done, pred[]{:T(512)S(6)} %eq.49, f32[2048]{0:T(1024)} %copy-done.4, f32[8,8,4,8,128]{4,3,2,1,0:T(8,128)S(1)} %copy.86), kind=kLoop, calls=%fused_computation.28 | loop fusion | flops 786432 | bytes 2105345 | tf_op jit(solution)/shard_map/jit(_where)/select_n | solution.py:89
  35.1 1.3 %add_reduce_fusion.3 = f32[64,1024]{1,0:T(8,128)S(1)} fusion(f32[32,64]{1,0:T(8,128)S(1)} %copy-done.8, bf16[64,32,128]{2,1,0:T(8,128)(2,1)S(1)} %bitcast.131, bf16[1024,128]{1,0:T(8,128)(2,1)S(1)} %slice_select_fusion.1), kind=kOutput, calls=%fused_computation.18 | convolution fusion | flops 540999680 | bytes 1056768 | tf_op jit(solution)/shard_map/while/body/eval_jaxpr/ubh,qh->ubq/dot_general | solution.py:29
  36.4 1.3 %add_reduce_fusion.2 = f32[32,2048]{1,0:T(8,128)S(1)} fusion(f32[32,32]{1,0:T(8,128)S(1)} %copy.96, bf16[2048,128]{1,0:T(8,128)(2,1)S(1)} %slice_select_fusion, bf16[1,32,32,128]{3,2,1,0:T(8,128)(2,1)S(1)} %bitcast.136), kind=kOutput, calls=%fused_computation.17 | convolution fusion | flops 540999680 | bytes 1052672 | tf_op jit(solution)/shard_map/while/body/eval_jaxpr/trh,ch->trc/dot_general | solution.py:32
  37.7 0.2 copy.94
  37.9 0.3 reshape.189
  38.2 0.2 select_reduce_fusion.3
  38.4 0.1 copy-done.5
  38.6 0.3 select_reduce_fusion.2
  38.9 0.5 collective-permute-start.1
  39.4 6.1 %collective-permute-done.2 = bf16[2064,128]{1,0:T(8,128)(2,1)S(1)} collective-permute-done((bf16[2064,128]{1,0:T(8,128)(2,1)}, bf16[2064,128]{1,0:T(8,128)(2,1)S(1)}, u32[]{:S(2)}, u32[]{:S(2)}) %collective-permute-start.2) | collective-permute-done | bytes 528416 | tf_op jit(solution)/shard_map/ppermute | solution.py:82
  45.6 1.0 %copy.126 = bf16[64,32,128]{2,0,1:T(8,128)(2,1)} copy(bf16[64,32,128]{2,1,0:T(8,128)(2,1)S(1)} %bitcast.129) | data formatting | bytes 1048576 | tf_op jit(solution)/shard_map/reshape | solution.py:17
  46.6 0.7 %copy.105 = f32[32,64,1]{1,0,2:T(8,128)} copy(f32[32,64,1]{0,1,2:T(8,128)S(1)} %bitcast.137) | data formatting | bytes 16384 | tf_op jit(solution)/shard_map/while | solution.py:37
  47.3 9.2 %while.2 = (s32[]{:T(128)}, f32[2,32,64]{2,1,0:T(8,128)S(1)}, pred[2,32,32]{2,1,0:T(8,128)(4,1)S(1)}, bf16[2,1024,128]{2,1,0:T(8,128)(2,1)}, bf16[32,64,128]{2,1...) while((s32[]{:T(128)}, f32[2,32,64]{2,1,0:T(8,128)S(1)}, ...), condition=%wide.region_10.11_spmd, body=%wide.region_5.10_spmd.sunk | while | flops 1082261504 | bytes 8525013 | solution.py:37
  47.4 1.3 %add_reduce_fusion.6 = f32[32,2048]{1,0:T(8,128)S(1)} fusion(f32[32,32]{1,0:T(8,128)S(1)} %bitcast.134, bf16[2048,128]{1,0:T(8,128)(2,1)S(1)} %get-tuple-element.243, bf16[1,32,32,128]{3,1,2,0:T(8,128)(2,1)S(1)} %constant_dynamic-slice_fusion.5), kind=kOutput, calls=%fused_computation.2.clone.1 | convolution fusion | flops 540999680 | bytes 1052672 | tf_op jit(solution)/shard_map/while/body/eval_jaxpr/trh,ch->trc/dot_general | solution.py:32
  48.7 0.3 reshape.238
  49.0 0.1 broadcast_in_dim.135
  49.1 0.3 select_reduce_fusion.6
  49.5 0.2 copy-done.2
  49.7 0.5 copy-done.3
  50.2 1.3 %add_reduce_fusion.7 = f32[1024,64]{0,1:T(8,128)S(1)} fusion(f32[32,64]{1,0:T(8,128)S(1)} %bitcast.141, bf16[32,64,128]{2,1,0:T(8,128)(2,1)S(1)} %copy-done.3, bf16[2,1024,128]{2,1,0:T(8,128)(2,1)S(1)} %copy-done.2, s32[]{:T(128)} %get-tuple-element.224), kind=kOutput, calls=%fused_computation.3.clone.1 | convolution fusion | flops 540999680 | bytes 1064964 | tf_op jit(solution)/shard_map/while/body/eval_jaxpr/ubh,qh->ubq/dot_general | solution.py:29
  51.5 0.2 copy.130
  51.7 0.2 select_reduce_fusion.7
  52.0 1.3 %add_reduce_fusion.6 = f32[32,2048]{1,0:T(8,128)S(1)} fusion(f32[32,32]{1,0:T(8,128)S(1)} %bitcast.134, bf16[2048,128]{1,0:T(8,128)(2,1)S(1)} %get-tuple-element.243, bf16[1,32,32,128]{3,1,2,0:T(8,128)(2,1)S(1)} %constant_dynamic-slice_fusion.5), kind=kOutput, calls=%fused_computation.2.clone.1 | convolution fusion | flops 540999680 | bytes 1052672 | tf_op jit(solution)/shard_map/while/body/eval_jaxpr/trh,ch->trc/dot_general | solution.py:32
  53.3 0.3 reshape.238
  53.6 0.1 broadcast_in_dim.135
  53.7 0.3 select_reduce_fusion.6
  54.1 0.2 copy-done.2
  54.3 0.5 copy-done.3
  54.8 1.3 %add_reduce_fusion.7 = f32[1024,64]{0,1:T(8,128)S(1)} fusion(f32[32,64]{1,0:T(8,128)S(1)} %bitcast.141, bf16[32,64,128]{2,1,0:T(8,128)(2,1)S(1)} %copy-done.3, bf16[2,1024,128]{2,1,0:T(8,128)(2,1)S(1)} %copy-done.2, s32[]{:T(128)} %get-tuple-element.224), kind=kOutput, calls=%fused_computation.3.clone.1 | convolution fusion | flops 540999680 | bytes 1064964 | tf_op jit(solution)/shard_map/while/body/eval_jaxpr/ubh,qh->ubq/dot_general | solution.py:29
  56.1 0.2 copy.130
  56.3 0.2 select_reduce_fusion.7
  56.8 3.8 %collective-permute-done.3 = f32[64,64]{1,0:T(8,128)S(1)} collective-permute-done((f32[64,64]{1,0:T(8,128)S(1)}, f32[64,64]{1,0:T(8,128)S(1)}, u32[]{:S(2)}, u32[]{:S(2)}) %collective-permute-start.3) | collective-permute-done | bytes 16416 | tf_op jit(solution)/shard_map/ppermute | solution.py:102
  60.6 0.7 %pad_maximum_fusion.1 = f32[64,192]{1,0:T(8,128)} fusion(f32[64,64]{1,0:T(8,128)S(1)} %get-tuple-element.151, f32[64,64]{1,0:T(8,128)S(1)} %get-tuple-element.150, f32[64,64]{1,0:T(8,128)S(1)} %bitcast_select_fusion), kind=kLoop, calls=%fused_computation.39 | loop fusion | flops 24576 | bytes 98304 | tf_op jit(solution)/shard_map/concatenate | solution.py:106
  (57 shorter events, 0.7 us)
Async XLA Ops:
  0.0 2.5 %copy-start = (bf16[256,8,128]{2,1,0:T(8,128)(2,1)S(1)}, bf16[256,8,128]{2,1,0:T(8,128)(2,1)}, u32[]{:S(2)}) copy-start(bf16[256,8,128]{2,1,0:T(8,128)(2,1)} %param.6) | copy-start | bytes 1572868
  0.0 0.8 %copy-start.1 = (s32[2048]{0:T(1024)S(1)}, s32[2048]{0:T(1024)}, u32[]{:S(2)}) copy-start(s32[2048]{0:T(1024)} %param.7) | copy-start | bytes 24580
  2.5 8.9 %copy-start.6 = (s32[64,32]{0,1:T(8,128)S(1)}, s32[64,32]{0,1:T(8,128)}, u32[]{:S(2)}) copy-start(s32[64,32]{0,1:T(8,128)} %param.9) | copy-start | bytes 24580
  2.5 9.0 %copy-start.9 = (s32[64]{0:T(128)S(1)}, s32[64]{0:T(128)}, u32[]{:S(2)}) copy-start(s32[64]{0:T(128)} %param.8) | copy-start | bytes 772
  4.1 23.7 %all-to-all-start = ((bf16[32,8,8,128]{3,2,1,0:T(8,128)(2,1)}), bf16[32,8,8,128]{3,2,1,0:T(8,128)(2,1)S(1)}, u32[]{:S(2)}, u32[]{:S(2)}) async-start(bf16[32,8,8,128]{3,2,1,0:T(8,128)(2,1)} %bitcast.11), calls=%async_computation | async-start | bytes 1048576 | tf_op jit(solution)/shard_map/all_to_all | solution.py:56
  28.7 1.6 %copy-start.4 = (f32[2048]{0:T(1024)}, f32[2048]{0:T(1024)S(1)}, u32[]{:S(2)}) copy-start(f32[2048]{0:T(1024)S(1)} %sqrt.24) | copy-start | bytes 24580
  30.3 2.1 %collective-permute-start = (bf16[2064,128]{1,0:T(8,128)(2,1)}, bf16[2064,128]{1,0:T(8,128)(2,1)S(1)}, u32[]{:S(2)}, u32[]{:S(2)}) collective-permute-start(bf16[2064,128]{1,0:T(8,128)(2,1)} %pad_maximum_fusion), channel_id=1, source_target_pairs={{0,1},{1,0},{2,3},{3,2},{4,5},{5,4},{6,7},{7,6},{8,9},{9,8},{10,11... | collective-permute-start | bytes 1585160 | tf_op jit(solution)/shard_map/ppermute | solution.py:83
  30.3 15.2 %collective-permute-start.2 = (bf16[2064,128]{1,0:T(8,128)(2,1)}, bf16[2064,128]{1,0:T(8,128)(2,1)S(1)}, u32[]{:S(2)}, u32[]{:S(2)}) collective-permute-start(bf16[2064,128]{1,0:T(8,128)(2,1)} %pad_maximum_fusion), channel_id=1, source_target_pairs={{0,2},{1,5},{2,6},{3,1},{4,0},{5,7},{6,4},{7,3},{8,10},{9,13},{10,... | collective-permute-start | bytes 1585160 | tf_op jit(solution)/shard_map/ppermute | solution.py:82
  34.0 1.1 %copy-start.8 = (f32[32,64]{1,0:T(8,128)S(1)}, f32[32,64]{1,0:T(8,128)}, u32[]{:S(2)}) copy-start(f32[32,64]{1,0:T(8,128)} %copy.93) | copy-start | bytes 24580
  37.9 0.7 %copy-start.5 = (pred[64,32]{1,0:T(8,128)(4,1)S(1)}, pred[64,32]{1,0:T(8,128)(4,1)}, u32[]{:S(2)}) copy-start(pred[64,32]{1,0:T(8,128)(4,1)} %broadcast_compare_fusion.1) | copy-start | bytes 6148
  38.9 17.8 %collective-permute-start.1 = (f32[32,64]{1,0:T(8,128)S(1)}, f32[32,64]{1,0:T(8,128)S(1)}, u32[]{:S(2)}, u32[]{:S(2)}) collective-permute-start(f32[32,64]{1,0:T(8,128)S(1)} %fusion.15), channel_id=1, source_target_pairs={{0,1},{1,0},{2,3},{3,2},{4,5},{5,4},{6,7},{7,6},{8,9},{9,8},{10,11... | collective-permute-start | bytes 24584 | tf_op jit(solution)/shard_map/ppermute | solution.py:92
  48.6 1.0 %copy-start.2 = (bf16[2,1024,128]{2,1,0:T(8,128)(2,1)S(1)}, bf16[2,1024,128]{2,1,0:T(8,128)(2,1)}, u32[]{:S(2)}) copy-start(bf16[2,1024,128]{2,1,0:T(8,128)(2,1)} %get-tuple-element.238) | copy-start | bytes 1572868 | tf_op jit(solution)/shard_map/while
  48.7 1.0 %copy-start.7 = (f32[32,64,1]{1,0,2:T(8,128)S(1)}, f32[32,64,1]{1,0,2:T(8,128)}, u32[]{:S(2)}) copy-start(f32[32,64,1]{1,0,2:T(8,128)} %get-tuple-element.240) | copy-start | bytes 24580 | tf_op jit(solution)/shard_map/while
  49.1 1.1 %copy-start.3 = (bf16[32,64,128]{2,1,0:T(8,128)(2,1)S(1)}, bf16[32,64,128]{2,1,0:T(8,128)(2,1)}, u32[]{:S(2)}) copy-start(bf16[32,64,128]{2,1,0:T(8,128)(2,1)} %get-tuple-element.239) | copy-start | bytes 1572868 | tf_op jit(solution)/shard_map/while
  53.3 1.0 %copy-start.2 = (bf16[2,1024,128]{2,1,0:T(8,128)(2,1)S(1)}, bf16[2,1024,128]{2,1,0:T(8,128)(2,1)}, u32[]{:S(2)}) copy-start(bf16[2,1024,128]{2,1,0:T(8,128)(2,1)} %get-tuple-element.238) | copy-start | bytes 1572868 | tf_op jit(solution)/shard_map/while
  53.3 1.0 %copy-start.7 = (f32[32,64,1]{1,0,2:T(8,128)S(1)}, f32[32,64,1]{1,0,2:T(8,128)}, u32[]{:S(2)}) copy-start(f32[32,64,1]{1,0,2:T(8,128)} %get-tuple-element.240) | copy-start | bytes 24580 | tf_op jit(solution)/shard_map/while
  53.7 1.1 %copy-start.3 = (bf16[32,64,128]{2,1,0:T(8,128)(2,1)S(1)}, bf16[32,64,128]{2,1,0:T(8,128)(2,1)}, u32[]{:S(2)}) copy-start(bf16[32,64,128]{2,1,0:T(8,128)(2,1)} %get-tuple-element.239) | copy-start | bytes 1572868 | tf_op jit(solution)/shard_map/while
  56.6 3.9 %collective-permute-start.3 = (f32[64,64]{1,0:T(8,128)S(1)}, f32[64,64]{1,0:T(8,128)S(1)}, u32[]{:S(2)}, u32[]{:S(2)}) collective-permute-start(f32[64,64]{1,0:T(8,128)S(1)} %bitcast.140), channel_id=1, source_target_pairs={{2,0},{5,1},{6,2},{1,3},{0,4},{7,5},{4,6},{3,7},{10,8},{13,9},{14,... | collective-permute-start | bytes 49160 | tf_op jit(solution)/shard_map/ppermute | solution.py:102

commit v7 on v3

v7 whole, which is shorter than its diff:
```python
import jax
import jax.numpy as jnp
from jax import lax
from jax.sharding import PartitionSpec as P


def tile_scores(query, query_bias, other, other_bias):
    tok, query_items, width = query.shape
    other_items = other.shape[1]
    rows = min(32, query_items)
    blocks = query_items // rows
    other_flat = other.reshape(tok * other_items, width)
    other_add = other_bias.astype(jnp.float32)[:, :, None]
    other_valid = other_bias == 0
    turned_all = jnp.transpose(query.reshape(tok, blocks, rows, width), (1, 0, 2, 3))
    adding_all = jnp.transpose(query_bias.astype(jnp.float32).reshape(tok, blocks, rows), (1, 0, 2))[..., None]
    kept_all = jnp.transpose((query_bias == 0).reshape(tok, blocks, rows), (1, 0, 2))

    def one_block(operands):
        turned, adding, kept = operands
        flat = turned.reshape(tok * rows, width)
        dots_fore = jnp.einsum("ubh,qh->ubq", other, flat, preferred_element_type=jnp.float32)
        fore = jnp.max(dots_fore + other_add, axis=0).reshape(other_items, tok, rows)
        fore = jnp.sum(jnp.where(kept[None], fore, 0.0), axis=1)
        dots_back = jnp.einsum("trh,ch->trc", turned, other_flat, preferred_element_type=jnp.float32)
        back = jnp.max(dots_back + adding, axis=0).reshape(rows, tok, other_items)
        back = jnp.sum(jnp.where(other_valid[None], back, 0.0), axis=1)
        return 0.5 * (fore.T + back)

    result = lax.map(one_block, (turned_all, adding_all, kept_all))
    return result.reshape(query_items, other_items)


def shards(encoded, slot_items, lengths, token_mask):
    n_enc = lax.axis_size("enc")
    n_pool = lax.axis_size("pool")
    owners = n_enc * n_pool
    group = encoded.shape[0]
    toks = encoded.shape[1]
    width = encoded.shape[2]
    items_dev = lengths.shape[0]
    per = items_dev // n_pool
    tok = n_enc * toks
    n_tok = items_dev * tok
    pool_index = lax.axis_index("pool")

    table = slot_items.reshape(owners, n_pool, per)
    mine = lax.dynamic_index_in_dim(table, pool_index, 1, keepdims=False) - pool_index * group
    outgoing = jnp.take(encoded, mine, axis=0, mode="clip")
    outgoing = jnp.transpose(outgoing, (2, 0, 1, 3))
    arrived = lax.all_to_all(outgoing, ("enc", "pool"), split_axis=1, concat_axis=1, tiled=True)
    slotted = arrived.reshape(tok, items_dev, width)
    values = slotted.astype(jnp.float32)
    normed = (values / jnp.sqrt(jnp.sum(values * values, axis=-1, keepdims=True) + 1e-06)).astype(
        jnp.bfloat16
    )
    position = jnp.arange(tok, dtype=jnp.int32)[None, :]
    valid = (position < lengths[:, None]) & ((position == 0) | (token_mask == 1))
    valid_tm = jnp.transpose(valid.reshape(items_dev, n_enc, toks), (2, 1, 0)).reshape(tok, items_dev)
    bias = jnp.where(valid_tm, 0.0, -4.0).astype(jnp.bfloat16)
    packed = jnp.concatenate([normed.reshape(n_tok, width), bias.reshape(-1, width)], axis=0)
    block = packed[:n_tok].reshape(tok, items_dev, width)

    parity = (pool_index ^ (pool_index >> 1) ^ (pool_index >> 2)) & 1
    is_a = (pool_index & 1) == 0

    def par(p):
        return (p ^ (p >> 1) ^ (p >> 2)) & 1

    send_pairs = [(p, p ^ (4 if par(p) else 2)) for p in range(n_pool)]
    back_pairs = [(t, s) for s, t in send_pairs]
    chip_pairs = [(p, p ^ 1) for p in range(n_pool)]

    z_recv = lax.ppermute(packed, "pool", send_pairs)
    c_recv = lax.ppermute(packed, "pool", chip_pairs)

    def unpack(received):
        return received[:n_tok].reshape(tok, items_dev, width), received[n_tok:].reshape(tok, items_dev)

    half = items_dev // 2
    c_blk, c_bias = unpack(c_recv)
    query = jnp.where(is_a, block[:, :half], c_blk[:, half:])
    query_bias = jnp.where(is_a, bias[:, :half], c_bias[:, half:])
    other = jnp.where(is_a, c_blk, block)
    other_bias = jnp.where(is_a, c_bias, bias)
    part = tile_scores(query, query_bias, other, other_bias)
    part_recv = lax.ppermute(part, "pool", chip_pairs)
    joined = jnp.where(
        is_a,
        jnp.concatenate([part, part_recv], axis=0),
        jnp.concatenate([part_recv, part], axis=0),
    )
    tile0 = jnp.where(is_a, joined, joined.T)

    z_blk, z_bias = unpack(z_recv)
    tile_z = tile_scores(block, bias, z_blk, z_bias)
    tile_back = lax.ppermute(tile_z.T, "pool", back_pairs)
    via_bit1 = parity == 1
    col1 = jnp.where(via_bit1, tile_z, tile_back)
    col2 = jnp.where(via_bit1, tile_back, tile_z)
    return jnp.concatenate([tile0, col1, col2], axis=1)


def solution(mesh):
    in_specs = (P("pool", "enc", None), P(), P(("enc", "pool")), P(("enc", "pool"), None))
    out_specs = P(("enc", "pool"), None)
    return jax.shard_map(shards, mesh=mesh, in_specs=in_specs, out_specs=out_specs, check_vma=False)
```

time: 60.7 us -> 55 us (0.906)
  other arithmetic: 8.85 us -> 4.81 us
  local copies, waits for them, and re-layouts: 9.45 us -> 5.7 us
  waiting for transfers between devices: 26 us -> 28.4 us
    while x13 -> x1, local copies, waits for them, and re-layouts: 2.17 us -> 0.01 us  [tile_scores(): result = lax.map(one_block, (turned_all, adding_all, kept_all))]
    convert_element_type x3 -> x1, other arithmetic: 1.71 us -> 0.34 us  [shards(): (values / jnp.sqrt(jnp.sum(values * values, axis=-1, keepdims=True) + 1e-...]
    reshape x5 -> x4, local copies, waits for them, and re-layouts: 2.09 us -> 0.73 us  [the longest x3 0.65 us: one_block(): back = jnp.max(dots_back + adding, axis=0).reshape(rows, tok, other_items)]
    ppermute x1, waiting for transfers between devices: 6.12 us -> 7.28 us  [shards(): z_recv = lax.ppermute(packed, 'pool', send_pairs)]
    ppermute x1, waiting for transfers between devices: 0.09 us -> 1.17 us  [shards(): c_recv = lax.ppermute(packed, 'pool', chip_pairs)]
    select_n x3 -> x1, other arithmetic: 1.18 us -> 0.22 us  [shards(): query = jnp.where(is_a, block[:, :half], c_blk[:, half:])]
    reduce_sum x6, other arithmetic: 1.71 us -> 0.87 us  [the longest x3 0.61 us: one_block(): fore = jnp.sum(jnp.where(kept[None], fore, 0.0), axis=1)]
    concatenate x1, other arithmetic: 0.82 us -> 0.04 us  [shards(): jnp.concatenate([normed.reshape(n_tok, width), bias.reshape(-1, width)],...]
  transfers between devices with their start and end apart: 5 -> 5, of which waited for: 4 -> 4; matrix products, arithmetic and copies ran while one was open for 30% -> 25% of each run, Pallas kernels for 0% -> 0%
where the time goes in v7:
time: 55 us; the launch traced here: 54.6 us
  waiting for transfers between devices  28.4 us (52%)
  starting transfers between devices  7.67 us (14%)
  matrix products  7.59 us (14%)
  local copies, waits for them, and re-layouts  5.7 us (10%)
  other arithmetic  4.81 us (9%)
    all_to_all x1, waiting for transfers between devices, shards(): lax.all_to_all(outgoing, ('enc', 'pool'), split_axis=1, concat_axis=1, ti...  16.1 us
    all_to_all x1, starting transfers between devices, shards(): lax.all_to_all(outgoing, ('enc', 'pool'), split_axis=1, concat_axis=1, ti...  7.3 us
    ppermute x1, waiting for transfers between devices, shards(): z_recv = lax.ppermute(packed, 'pool', send_pairs)  7.28 us
    dot_general x3, matrix products, one_block(): jnp.einsum('ubh,qh->ubq', other, flat, preferred_element_type=jnp.float32)  3.8 us
    dot_general x3, matrix products, one_block(): jnp.einsum('trh,ch->trc', turned, other_flat, preferred_element_type=jnp....  3.79 us
    ppermute x1, waiting for transfers between devices, shards(): tile_back = lax.ppermute(tile_z.T, 'pool', back_pairs)  3.78 us
    select_n x1, other arithmetic, shards(): other = jnp.where(is_a, c_blk, block)  1.4 us
    ppermute x1, waiting for transfers between devices, shards(): c_recv = lax.ppermute(packed, 'pool', chip_pairs)  1.17 us
  transfers between devices with their start and end apart: 5, of which 4 were waited for; matrix products, arithmetic and copies ran while one was open for 25% of the time, Pallas kernels for 0%

profile of v7, /device:TPU:0, one launch (start us, length us, event | category | flops | bytes accessed | tf_op | source)
XLA Modules:
  0.0 54.6 jit_solution(1600819310395637438)
XLA Ops:
  0.0 0.0 copy-start
  0.0 0.8 %reshape.184 = s32[32,8,8]{2,1,0:T(8,128)S(1)} reshape(s32[2048]{0:T(1024)} %param.7) | data formatting | bytes 16384 | tf_op jit(solution)/shard_map/reshape | solution.py:47
  0.9 0.1 subtract_reduce_fusion
  0.9 0.1 reshape.200
  1.0 0.0 copy-done
  1.1 0.8 %gather_fusion = bf16[256,8,128]{2,1,0:T(8,128)(2,1)S(1)} fusion(bf16[256,8,128]{2,1,0:T(8,128)(2,1)S(1)} %copy-done, s32[1024]{0:T(1024)S(1)} %pad_clamp_fusion), kind=kCustom, calls=%fused_computation | custom fusion | bytes 1049600 | tf_op jit(solution)/shard_map/jit(_take)/gather | solution.py:49
  1.9 0.0 copy-start.1
  1.9 0.0 copy-start.2
  1.9 0.9 %copy.42 = bf16[8,32,8,128]{3,2,0,1:T(8,128)(2,1)} copy(bf16[8,32,8,128]{3,0,2,1:T(8,128)(2,1)S(1)} %bitcast.110) | data formatting | bytes 1048576 | tf_op jit(solution)/shard_map/transpose | solution.py:50
  2.8 7.3 %all-to-all-start = ((bf16[8,32,8,128]{3,2,0,1:T(8,128)(2,1)}), bf16[8,32,8,128]{3,2,0,1:T(8,128)(2,1)S(1)}, u32[]{:S(2)}, u32[]{:S(2)}) async-start(bf16[8,32,8,128]{3,2,0,1:T(8,128)(2,1)} %copy.42), calls=%async_computation | async-start | bytes 1048576 | tf_op jit(solution)/shard_map/all_to_all | solution.py:51
  10.1 0.0 copy-done.1
  10.1 0.0 copy-done.2
  10.1 0.1 fusion.10
  10.2 0.1 convert_element_type.102
  10.3 16.1 %all-to-all-done = bf16[8,32,8,128]{3,2,0,1:T(8,128)(2,1)S(1)} async-done(((bf16[8,32,8,128]{3,2,0,1:T(8,128)(2,1)}), bf16[8,32,8,128]{3,2,0,1:T(8,128)(2,1)S(1)}, u32[]{:S(2)}, u32[]{:S(2)}) %all-to-all-start) | async-done | bytes 524320 | tf_op jit(solution)/shard_map/all_to_all | solution.py:51
  26.4 0.3 multiply_reduce_fusion
  26.8 0.1 sqrt.20
  27.0 0.1 copy_convert_fusion
  27.0 0.3 fusion.3
  27.4 0.1 collective-permute-start
  27.5 0.1 reshape.197
  27.6 0.1 eq.63
  27.7 0.1 sqrt.21
  27.8 0.1 collective-permute-start.2
  27.9 0.1 sqrt.22
  28.0 0.3 fusion.6
  28.4 1.2 %collective-permute-done = bf16[2064,128]{1,0:T(8,128)(2,1)} collective-permute-done((bf16[2064,128]{1,0:T(8,128)(2,1)S(1)}, bf16[2064,128]{1,0:T(8,128)(2,1)}, u32[]{:S(2)}, u32[]{:S(2)}) %collective-permute-start) | collective-permute-done | bytes 528416 | tf_op jit(solution)/shard_map/ppermute | solution.py:75
  29.5 0.7 %slice.35 = bf16[16,128]{1,0:T(8,128)(2,1)S(1)} slice(bf16[2064,128]{1,0:T(8,128)(2,1)} %collective-permute-done), slice={[2048:2064], [0:128]} | slice | bytes 8192 | tf_op jit(solution)/shard_map/slice | solution.py:78
  30.2 0.1 reshape.185
  30.3 0.1 broadcast_compare_fusion.1
  30.4 0.1 fusion.12
  30.5 1.4 %broadcast_select_fusion = (bf16[2048,128]{1,0:T(8,128)(2,1)S(1)}, bf16[2048,128]{1,0:T(8,128)(2,1)S(1)}) fusion(pred[]{:T(512)S(6)} %eq.52, bf16[2064,128]{1,0:T(8,128)(2,1)} %collective-permute-done, f32[2048]{0:T(1024)S(1)} %sqrt.20, f32[8,32,8,128]{3,2,1,0:T(8,128)S(1)} %copy_convert_fusion), kind=kLoop, calls=%fused_computation.27 | loop fusion | flops 786432 | bytes 2629633 | tf_op jit(solution)/shard_map/jit(_where)/select_n | solution.py:84
  31.9 0.2 fusion.7
  32.1 1.3 %add_reduce_fusion.2 = f32[32,2048]{1,0:T(8,128)S(1)} fusion(bf16[32,32,128]{2,1,0:T(8,128)(2,1)S(1)} %fusion.7, f32[32,32]{1,0:T(8,128)S(1)} %fusion.12, bf16[2048,128]{1,0:T(8,128)(2,1)S(1)} %get-tuple-element.134), kind=kOutput, calls=%fused_computation.13 | convolution fusion | flops 540999680 | bytes 1052672 | tf_op jit(solution)/shard_map/while/body/eval_jaxpr/trh,ch->trc/dot_general | solution.py:25
  33.4 1.3 %add_reduce_fusion.3 = f32[64,1024]{1,0:T(8,128)S(1)} fusion(f32[32,64]{1,0:T(8,128)S(1)} %fusion.11, bf16[32,64,128]{2,1,0:T(8,128)(2,1)S(1)} %bitcast.115, bf16[1024,128,1]{1,0,2:T(8,128)(2,1)S(1)} %bitcast.118), kind=kOutput, calls=%fused_computation.14 | convolution fusion | flops 540999680 | bytes 1056768 | tf_op jit(solution)/shard_map/while/body/eval_jaxpr/ubh,qh->ubq/dot_general | solution.py:22
  34.7 0.2 copy.44
  34.9 0.2 reshape.189
  35.1 0.1 select_reduce_fusion.2
  35.2 0.2 select_reduce_fusion.3
  35.4 0.2 collective-permute-start.1
  35.6 7.3 %collective-permute-done.2 = bf16[2064,128]{1,0:T(8,128)(2,1)S(1)} collective-permute-done((bf16[2064,128]{1,0:T(8,128)(2,1)S(1)}, bf16[2064,128]{1,0:T(8,128)(2,1)S(1)}, u32[]{:S(2)}, u32[]{:S(2)}) %collective-permute-start.2) | collective-permute-done | bytes 528416 | tf_op jit(solution)/shard_map/ppermute | solution.py:74
  42.9 0.1 reshape.195
  43.0 0.1 eq.65
  43.1 6.8 %while.2 = (s32[]{:T(128)}, f32[2,32,64]{2,1,0:T(8,128)S(1)}, pred[2,32,32]{2,1,0:T(8,128)(4,1)S(1)}, bf16[2,32,32,128]{3,2,0,1:T(8,128)(2,1)S(1)}, bf16[32,64,1...) while((s32[]{:T(128)}, f32[2,32,64]{2,1,0:T(8,128)S(1)}, ...), condition=%wide.region_10.11_spmd, body=%wide.region_5.10_spmd.sunk | while | flops 1082261504 | bytes 4285557 | solution.py:30
  43.2 1.3 %add_reduce_fusion.6 = f32[32,2048]{1,0:T(8,128)S(1)} fusion(f32[32,32]{1,0:T(8,128)S(1)} %bitcast.116, bf16[2048,128]{1,0:T(8,128)(2,1)S(1)} %get-tuple-element.223, bf16[1,32,32,128]{3,2,0,1:T(8,128)(2,1)S(1)} %constant_dynamic-slice_fusion.5), kind=kOutput, calls=%fused_computation.1.clone.1 | convolution fusion | flops 540999680 | bytes 1052672 | tf_op jit(solution)/shard_map/while/body/eval_jaxpr/trh,ch->trc/dot_general | solution.py:25
  44.5 0.2 reshape.220
  44.7 0.1 select_reduce_fusion.6
  44.8 1.3 %add_reduce_fusion.7 = f32[1024,64]{0,1:T(8,128)S(1)} fusion(f32[32,64]{1,0:T(8,128)S(1)} %bitcast.127, bf16[1024,128,1]{1,0,2:T(8,128)(2,1)S(1)} %bitcast.108, bf16[32,64,128]{2,1,0:T(8,128)(2,1)S(1)} %bitcast.113), kind=kOutput, calls=%fused_computation.2.clone.1 | convolution fusion | flops 540999680 | bytes 1056768 | tf_op jit(solution)/shard_map/while/body/eval_jaxpr/ubh,qh->ubq/dot_general | solution.py:22
  46.0 0.2 copy.61
  46.3 0.2 select_reduce_fusion.7
  46.6 1.3 %add_reduce_fusion.6 = f32[32,2048]{1,0:T(8,128)S(1)} fusion(f32[32,32]{1,0:T(8,128)S(1)} %bitcast.116, bf16[2048,128]{1,0:T(8,128)(2,1)S(1)} %get-tuple-element.223, bf16[1,32,32,128]{3,2,0,1:T(8,128)(2,1)S(1)} %constant_dynamic-slice_fusion.5), kind=kOutput, calls=%fused_computation.1.clone.1 | convolution fusion | flops 540999680 | bytes 1052672 | tf_op jit(solution)/shard_map/while/body/eval_jaxpr/trh,ch->trc/dot_general | solution.py:25
  47.8 0.2 reshape.220
  48.1 0.1 select_reduce_fusion.6
  48.2 1.3 %add_reduce_fusion.7 = f32[1024,64]{0,1:T(8,128)S(1)} fusion(f32[32,64]{1,0:T(8,128)S(1)} %bitcast.127, bf16[1024,128,1]{1,0,2:T(8,128)(2,1)S(1)} %bitcast.108, bf16[32,64,128]{2,1,0:T(8,128)(2,1)S(1)} %bitcast.113), kind=kOutput, calls=%fused_computation.2.clone.1 | convolution fusion | flops 540999680 | bytes 1056768 | tf_op jit(solution)/shard_map/while/body/eval_jaxpr/ubh,qh->ubq/dot_general | solution.py:22
  49.4 0.2 copy.61
  49.7 0.2 select_reduce_fusion.7
  49.9 0.1 copy.50
  50.0 0.0 collective-permute-start.3
  50.0 0.0 collective-permute-done.1
  50.0 0.1 copy.45
  50.1 3.8 %collective-permute-done.3 = f32[64,64]{1,0:T(8,128)S(1)} collective-permute-done((f32[64,64]{1,0:T(8,128)S(1)}, f32[64,64]{1,0:T(8,128)S(1)}, u32[]{:S(2)}, u32[]{:S(2)}) %collective-permute-start.3) | collective-permute-done | bytes 16416 | tf_op jit(solution)/shard_map/ppermute | solution.py:97
  53.9 0.7 %pad_maximum_fusion.1 = f32[64,192]{1,0:T(8,128)} fusion(f32[64,64]{1,0:T(8,128)S(1)} %get-tuple-element.137, f32[64,64]{1,0:T(8,128)S(1)} %get-tuple-element.136, f32[64,64]{1,0:T(8,128)S(1)} %bitcast_select_fusion), kind=kLoop, calls=%fused_computation.30 | loop fusion | flops 24576 | bytes 98304 | tf_op jit(solution)/shard_map/concatenate | solution.py:101
  (25 shorter events, 0.4 us)
Async XLA Ops:
  0.0 1.1 %copy-start = (bf16[256,8,128]{2,1,0:T(8,128)(2,1)S(1)}, bf16[256,8,128]{2,1,0:T(8,128)(2,1)}, u32[]{:S(2)}) copy-start(bf16[256,8,128]{2,1,0:T(8,128)(2,1)} %param.6) | copy-start | bytes 1572868
  1.9 8.2 %copy-start.1 = (s32[64,32]{0,1:T(8,128)S(1)}, s32[64,32]{0,1:T(8,128)}, u32[]{:S(2)}) copy-start(s32[64,32]{0,1:T(8,128)} %param.9) | copy-start | bytes 24580
  1.9 8.2 %copy-start.2 = (s32[64]{0:T(128)S(1)}, s32[64]{0:T(128)}, u32[]{:S(2)}) copy-start(s32[64]{0:T(128)} %param.8) | copy-start | bytes 772
  2.8 23.7 %all-to-all-start = ((bf16[8,32,8,128]{3,2,0,1:T(8,128)(2,1)}), bf16[8,32,8,128]{3,2,0,1:T(8,128)(2,1)S(1)}, u32[]{:S(2)}, u32[]{:S(2)}) async-start(bf16[8,32,8,128]{3,2,0,1:T(8,128)(2,1)} %copy.42), calls=%async_computation | async-start | bytes 1048576 | tf_op jit(solution)/shard_map/all_to_all | solution.py:51
  27.4 2.1 %collective-permute-start = (bf16[2064,128]{1,0:T(8,128)(2,1)S(1)}, bf16[2064,128]{1,0:T(8,128)(2,1)}, u32[]{:S(2)}, u32[]{:S(2)}) collective-permute-start(bf16[2064,128]{1,0:T(8,128)(2,1)S(1)} %pad_maximum_fusion), channel_id=1, source_target_pairs={{0,1},{1,0},{2,3},{3,2},{4,5},{5,4},{6,7},{7,6},{8,9},{9,8},{10,11... | collective-permute-start | bytes 1585160 | tf_op jit(solution)/shard_map/ppermute | solution.py:75
  27.8 15.1 %collective-permute-start.2 = (bf16[2064,128]{1,0:T(8,128)(2,1)S(1)}, bf16[2064,128]{1,0:T(8,128)(2,1)S(1)}, u32[]{:S(2)}, u32[]{:S(2)}) collective-permute-start(bf16[2064,128]{1,0:T(8,128)(2,1)S(1)} %pad_maximum_fusion), channel_id=1, source_target_pairs={{0,2},{1,5},{2,6},{3,1},{4,0},{5,7},{6,4},{7,3},{8,10},{9,13},{10,... | collective-permute-start | bytes 1585160 | tf_op jit(solution)/shard_map/ppermute | solution.py:74
  35.4 14.6 %collective-permute-start.1 = (f32[32,64]{1,0:T(8,128)S(1)}, f32[32,64]{1,0:T(8,128)S(1)}, u32[]{:S(2)}, u32[]{:S(2)}) collective-permute-start(f32[32,64]{1,0:T(8,128)S(1)} %fusion.8), channel_id=1, source_target_pairs={{0,1},{1,0},{2,3},{3,2},{4,5},{5,4},{6,7},{7,6},{8,9},{9,8},{10,11... | collective-permute-start | bytes 24584 | tf_op jit(solution)/shard_map/ppermute | solution.py:87
  50.0 3.9 %collective-permute-start.3 = (f32[64,64]{1,0:T(8,128)S(1)}, f32[64,64]{1,0:T(8,128)S(1)}, u32[]{:S(2)}, u32[]{:S(2)}) collective-permute-start(f32[64,64]{1,0:T(8,128)S(1)} %bitcast.126), channel_id=1, source_target_pairs={{2,0},{5,1},{6,2},{1,3},{0,4},{7,5},{4,6},{3,7},{10,8},{13,9},{14,... | collective-permute-start | bytes 49160 | tf_op jit(solution)/shard_map/ppermute | solution.py:97

commit v8 on v7

--- a/solution.py
+++ b/solution.py
@@ -10,24 +10,22 @@
     rows = min(32, query_items)
     blocks = query_items // rows
     other_flat = other.reshape(tok * other_items, width)
-    other_add = other_bias.astype(jnp.float32)[:, :, None]
     other_valid = other_bias == 0
     turned_all = jnp.transpose(query.reshape(tok, blocks, rows, width), (1, 0, 2, 3))
-    adding_all = jnp.transpose(query_bias.astype(jnp.float32).reshape(tok, blocks, rows), (1, 0, 2))[..., None]
     kept_all = jnp.transpose((query_bias == 0).reshape(tok, blocks, rows), (1, 0, 2))
 
     def one_block(operands):
-        turned, adding, kept = operands
+        turned, kept = operands
         flat = turned.reshape(tok * rows, width)
         dots_fore = jnp.einsum("ubh,qh->ubq", other, flat, preferred_element_type=jnp.float32)
-        fore = jnp.max(dots_fore + other_add, axis=0).reshape(other_items, tok, rows)
+        fore = jnp.max(dots_fore, axis=0).reshape(other_items, tok, rows)
         fore = jnp.sum(jnp.where(kept[None], fore, 0.0), axis=1)
         dots_back = jnp.einsum("trh,ch->trc", turned, other_flat, preferred_element_type=jnp.float32)
-        back = jnp.max(dots_back + adding, axis=0).reshape(rows, tok, other_items)
+        back = jnp.max(dots_back, axis=0).reshape(rows, tok, other_items)
         back = jnp.sum(jnp.where(other_valid[None], back, 0.0), axis=1)
         return 0.5 * (fore.T + back)
 
-    result = lax.map(one_block, (turned_all, adding_all, kept_all))
+    result = lax.map(one_block, (turned_all, kept_all))
     return result.reshape(query_items, other_items)
 
 
@@ -46,18 +44,21 @@
 
     table = slot_items.reshape(owners, n_pool, per)
     mine = lax.dynamic_index_in_dim(table, pool_index, 1, keepdims=False) - pool_index * group
-    outgoing = jnp.take(encoded, mine, axis=0, mode="clip")
-    outgoing = jnp.transpose(outgoing, (2, 0, 1, 3))
+    dnums = lax.GatherDimensionNumbers(offset_dims=(0, 3), collapsed_slice_dims=(0,), start_index_map=(0,))
+    outgoing = lax.gather(
+        encoded, mine[..., None], dnums, (1, toks, width), mode=lax.GatherScatterMode.CLIP
+    )
     arrived = lax.all_to_all(outgoing, ("enc", "pool"), split_axis=1, concat_axis=1, tiled=True)
     slotted = arrived.reshape(tok, items_dev, width)
+    position = jnp.arange(tok, dtype=jnp.int32)[None, :]
+    valid = (position < lengths[:, None]) & ((position == 0) | (token_mask == 1))
+    valid_tm = jnp.transpose(valid.reshape(items_dev, n_enc, toks), (2, 1, 0)).reshape(tok, items_dev)
+    bias = jnp.where(valid_tm, 0.0, -4.0).astype(jnp.bfloat16)
     values = slotted.astype(jnp.float32)
     normed = (values / jnp.sqrt(jnp.sum(values * values, axis=-1, keepdims=True) + 1e-06)).astype(
         jnp.bfloat16
     )
-    position = jnp.arange(tok, dtype=jnp.int32)[None, :]
-    valid = (position < lengths[:, None]) & ((position == 0) | (token_mask == 1))
-    valid_tm = jnp.transpose(valid.reshape(items_dev, n_enc, toks), (2, 1, 0)).reshape(tok, items_dev)
-    bias = jnp.where(valid_tm, 0.0, -4.0).astype(jnp.bfloat16)
+    normed = jnp.where(valid_tm[:, :, None], normed, normed[0][None])
     packed = jnp.concatenate([normed.reshape(n_tok, width), bias.reshape(-1, width)], axis=0)
     block = packed[:n_tok].reshape(tok, items_dev, width)
 

time: 55 us -> 63.3 us (1.15)
  waiting for transfers between devices: 28.4 us -> 33.6 us
  other arithmetic: 4.81 us -> 7.11 us
  local copies, waits for them, and re-layouts: 5.7 us -> 6.63 us
    ppermute x1, waiting for transfers between devices: 7.28 us -> 13.9 us  [shards(): z_recv = lax.ppermute(packed, 'pool', send_pairs)]
    ppermute x1, waiting for transfers between devices: 1.17 us -> 0.01 us  [shards(): c_recv = lax.ppermute(packed, 'pool', chip_pairs)]
    slice x1, local copies, waits for them, and re-layouts: 0.03 us -> 1.08 us  [unpack(): received[:n_tok].reshape(tok, items_dev, width)]
    gather x1 -> x2, local copies, waits for them, and re-layouts: 0.82 us -> 1.71 us  [shards(): lax.gather(encoded, mine[..., None], dnums, (1, toks, width), mode=lax.Ga...]
    transpose x1 -> x0, local copies, waits for them, and re-layouts: 0.89 us -> none  [shards(): outgoing = jnp.transpose(outgoing, (2, 0, 1, 3))]
    concatenate x1, other arithmetic: 0.04 us -> 0.85 us  [shards(): jnp.concatenate([normed.reshape(n_tok, width), bias.reshape(-1, width)],...]
    select_n x0 -> x1, other arithmetic: none -> 0.8 us  [shards(): normed = jnp.where(valid_tm[:, :, None], normed, normed[0][None])]
    eq x2, other arithmetic: 0.02 us -> 0.7 us  [tile_scores(): other_valid = other_bias == 0]
  transfers between devices with their start and end apart: 5 -> 5, of which waited for: 4 -> 3; matrix products, arithmetic and copies ran while one was open for 25% -> 16% of each run, Pallas kernels for 0% -> 0%
where the time goes in v8:
time: 63.3 us; the launch traced here: 62.9 us
  waiting for transfers between devices  33.6 us (53%)
  matrix products  7.61 us (12%)
  starting transfers between devices  7.48 us (12%)
  other arithmetic  7.11 us (11%)
  local copies, waits for them, and re-layouts  6.63 us (10%)
    all_to_all x1, waiting for transfers between devices, shards(): lax.all_to_all(outgoing, ('enc', 'pool'), split_axis=1, concat_axis=1, ti...  16 us
    ppermute x1, waiting for transfers between devices, shards(): z_recv = lax.ppermute(packed, 'pool', send_pairs)  13.9 us
    all_to_all x1, starting transfers between devices, shards(): lax.all_to_all(outgoing, ('enc', 'pool'), split_axis=1, concat_axis=1, ti...  7.3 us
    dot_general x3, matrix products, one_block(): jnp.einsum('ubh,qh->ubq', other, flat, preferred_element_type=jnp.float32)  3.84 us
    ppermute x1, waiting for transfers between devices, shards(): tile_back = lax.ppermute(tile_z.T, 'pool', back_pairs)  3.78 us
    dot_general x3, matrix products, one_block(): jnp.einsum('trh,ch->trc', turned, other_flat, preferred_element_type=jnp....  3.76 us
    gather x2, local copies, waits for them, and re-layouts, shards(): lax.gather(encoded, mine[..., None], dnums, (1, toks, width), mode=lax.Ga...  1.71 us
  transfers between devices with their start and end apart: 5, of which 3 were waited for; matrix products, arithmetic and copies ran while one was open for 16% of the time, Pallas kernels for 0%

profile of v8, /device:TPU:0, one launch (start us, length us, event | category | flops | bytes accessed | tf_op | source)
XLA Modules:
  0.0 62.9 jit_solution(15746382197442514996)
XLA Ops:
  0.0 0.0 copy-start
  0.0 0.8 %reshape.151 = s32[32,8,8]{2,1,0:T(8,128)S(1)} reshape(s32[2048]{0:T(1024)} %param.7) | data formatting | bytes 16384 | tf_op jit(solution)/shard_map/reshape | solution.py:45
  0.9 0.1 subtract_reduce_fusion
  0.9 0.1 reshape.164
  1.0 0.0 copy-done
  1.1 0.8 %gather_fusion = bf16[256,8,128]{2,1,0:T(8,128)(2,1)S(1)} fusion(bf16[256,8,128]{2,1,0:T(8,128)(2,1)S(1)} %copy-done, s32[1024]{0:T(1024)S(1)} %pad_clamp_fusion), kind=kCustom, calls=%fused_computation | custom fusion | bytes 1049600 | tf_op jit(solution)/shard_map/gather | solution.py:48
  1.9 0.0 copy-start.1
  1.9 0.0 copy-start.2
  1.9 0.9 %copy.36 = bf16[8,32,8,128]{3,2,0,1:T(8,128)(2,1)} copy(bf16[8,32,8,128]{3,0,2,1:T(8,128)(2,1)S(1)} %bitcast.103) | data formatting | bytes 1048576 | tf_op jit(solution)/shard_map/gather | solution.py:48
  2.8 7.3 %all-to-all-start = ((bf16[8,32,8,128]{3,2,0,1:T(8,128)(2,1)}), bf16[8,32,8,128]{3,2,0,1:T(8,128)(2,1)S(1)}, u32[]{:S(2)}, u32[]{:S(2)}) async-start(bf16[8,32,8,128]{3,2,0,1:T(8,128)(2,1)} %copy.36), calls=%async_computation | async-start | bytes 1048576 | tf_op jit(solution)/shard_map/all_to_all | solution.py:51
  10.1 0.0 copy-done.1
  10.1 0.0 copy-done.2
  10.1 0.1 fusion.8
  10.2 0.1 broadcast_in_dim.133
  10.3 0.1 broadcast_in_dim.120
  10.4 0.1 convert_element_type.59
  10.5 16.0 %all-to-all-done = bf16[8,32,8,128]{3,2,0,1:T(8,128)(2,1)S(1)} async-done(((bf16[8,32,8,128]{3,2,0,1:T(8,128)(2,1)}), bf16[8,32,8,128]{3,2,0,1:T(8,128)(2,1)S(1)}, u32[]{:S(2)}, u32[]{:S(2)}) %all-to-all-start) | async-done | bytes 524320 | tf_op jit(solution)/shard_map/all_to_all | solution.py:51
  26.5 0.3 multiply_reduce_fusion
  26.8 0.1 sqrt.21
  27.0 0.1 sqrt.20
  27.1 0.1 copy_convert_fusion
  27.1 0.3 divide_convert_fusion.1
  27.5 0.8 %fusion.4 = bf16[2048,128]{1,0:T(8,128)(2,1)S(1)} fusion(f32[8,32,8,128]{3,2,1,0:T(8,128)S(1)} %copy_convert_fusion, f32[2048]{0:T(1024)S(1)} %sqrt.20, pred[2048]{0:T(1024)(128)(4,1)S(1)} %broadcast_in_dim.120, bf16[64,128]{1,0:T(8,128)(2,1)S(1)} %get-tuple-element.108), kind=kLoop, calls=%fused_computation.20 | loop fusion | flops 786432 | bytes 1599488 | tf_op jit(solution)/shard_map/jit(_where)/select_n | solution.py:61
  28.3 0.8 %pad_maximum_fusion = bf16[2064,128]{1,0:T(8,128)(2,1)} fusion(bf16[16,128]{1,0:T(8,128)(2,1)S(1)} %convert_element_type.59, bf16[2048,128]{1,0:T(8,128)(2,1)S(1)} %fusion.4), kind=kLoop, calls=%fused_computation.19 | loop fusion | flops 1056768 | bytes 1056768 | tf_op jit(solution)/shard_map/concatenate | solution.py:62
  29.2 0.0 collective-permute-start.2
  29.2 0.1 collective-permute-start
  29.3 0.1 sqrt.22
  29.4 0.7 %select_bitcast_fusion = bf16[2,32,32,128]{3,2,0,1:T(8,128)(2,1)S(1)} fusion(f32[32,2,32,128]{3,2,1,0:T(8,128)S(1)} %bitcast.99, f32[32,2,32]{2,1,0:T(2,128)S(1)} %sqrt.22, pred[32,2,32]{2,1,0:T(4,128)(4,1)S(1)} %broadcast_in_dim.133, bf16[2,32,128]{2,1,0:T(8,128)(2,1)S(1)} %bitcast.116), kind=kLoop, calls=%fused_computation.23 | loop fusion | flops 786432 | bytes 1599488 | tf_op jit(solution)/shard_map/transpose | solution.py:14
  30.2 13.9 %collective-permute-done.2 = bf16[2064,128]{1,0:T(8,128)(2,1)} collective-permute-done((bf16[2064,128]{1,0:T(8,128)(2,1)}, bf16[2064,128]{1,0:T(8,128)(2,1)}, u32[]{:S(2)}, u32[]{:S(2)}) %collective-permute-start.2) | collective-permute-done | bytes 528416 | tf_op jit(solution)/shard_map/ppermute | solution.py:75
  44.0 0.7 %slice_compare_fusion = pred[16,128]{1,0:T(8,128)(4,1)S(1)} fusion(bf16[2064,128]{1,0:T(8,128)(2,1)} %collective-permute-done.2), kind=kLoop, calls=%fused_computation.48 | loop fusion | flops 2048 | bytes 6144 | tf_op jit(solution)/shard_map/eq | solution.py:13
  44.7 0.1 eq.57
  44.8 0.0 collective-permute-done
  44.8 1.1 %broadcast_select_fusion = (bf16[2048,128]{1,0:T(8,128)(2,1)S(1)}, bf16[2048,128]{1,0:T(8,128)(2,1)S(1)}) fusion(bf16[2048,128]{1,0:T(8,128)(2,1)S(1)} %fusion.4, pred[]{:T(512)S(6)} %eq.46, bf16[2064,128]{1,0:T(8,128)(2,1)} %collective-permute-done), kind=kLoop, calls=%fused_computation.26 | loop fusion | flops 262144 | bytes 2097153 | tf_op jit(solution)/shard_map/jit(_where)/select_n | solution.py:85
  45.9 0.2 slice_select_fusion
  46.1 1.3 %convolution_reduce_fusion.2 = f32[32,2048]{1,0:T(8,128)S(1)} fusion(bf16[32,32,128]{2,1,0:T(8,128)(2,1)S(1)} %slice_select_fusion, bf16[2048,128]{1,0:T(8,128)(2,1)S(1)} %get-tuple-element.106), kind=kOutput, calls=%fused_computation.12 | convolution fusion | flops 538902528 | bytes 1048576 | tf_op jit(solution)/shard_map/while/body/eval_jaxpr/trh,ch->trc/dot_general | solution.py:23
  47.4 0.2 reshape.156
  47.6 0.7 %slice.40 = bf16[16,128]{1,0:T(8,128)(2,1)S(1)} slice(bf16[2064,128]{1,0:T(8,128)(2,1)} %collective-permute-done), slice={[2048:2064], [0:128]} | slice | bytes 8192 | tf_op jit(solution)/shard_map/slice | solution.py:79
  48.3 0.1 reshape.152
  48.4 1.3 %convolution_reduce_fusion.3 = f32[64,1024]{1,0:T(8,128)S(1)} fusion(bf16[32,64,128]{2,1,0:T(8,128)(2,1)S(1)} %bitcast.105, bf16[1024,128,1]{1,0,2:T(8,128)(2,1)S(1)} %bitcast.109), kind=kOutput, calls=%fused_computation.13 | convolution fusion | flops 538902528 | bytes 1048576 | tf_op jit(solution)/shard_map/while/body/eval_jaxpr/ubh,qh->ubq/dot_general | solution.py:20
  49.7 0.2 copy.38
  49.9 0.1 fusion.9
  50.0 0.1 select_reduce_fusion.2
  50.1 0.2 select_reduce_fusion.3
  50.3 0.1 collective-permute-start.1
  50.4 1.1 %slice.47 = bf16[2048,128]{1,0:T(8,128)(2,1)S(1)} slice(bf16[2064,128]{1,0:T(8,128)(2,1)} %collective-permute-done.2), slice={[0:2048], [0:128]} | slice | bytes 1048576 | tf_op jit(solution)/shard_map/slice | solution.py:79
  51.4 6.7 %while.2 = (s32[]{:T(128)}, f32[2,32,64]{2,1,0:T(8,128)S(1)}, pred[2,32,32]{2,1,0:T(8,128)(4,1)S(1)}, bf16[2,32,32,128]{3,2,0,1:T(8,128)(2,1)S(1)}, bf16[32,64,1...) while((s32[]{:T(128)}, f32[2,32,64]{2,1,0:T(8,128)S(1)}, ...), condition=%wide.region_10.11_spmd, body=%wide.region_5.10_spmd.sunk | while | flops 1078067200 | bytes 4265065 | solution.py:28
  51.5 1.3 %convolution_reduce_fusion.6 = f32[32,2048]{1,0:T(8,128)S(1)} fusion(bf16[2048,128]{1,0:T(8,128)(2,1)S(1)} %get-tuple-element.179, bf16[1,32,32,128]{3,2,0,1:T(8,128)(2,1)S(1)} %constant_dynamic-slice_fusion.2), kind=kOutput, calls=%fused_computation.1.clone.1 | convolution fusion | flops 538902528 | bytes 1048576 | tf_op jit(solution)/shard_map/while/body/eval_jaxpr/trh,ch->trc/dot_general | solution.py:23
  52.7 0.2 reshape.184
  53.0 0.1 select_reduce_fusion.6
  53.1 1.3 %convolution_reduce_fusion.7 = f32[1024,64]{0,1:T(8,128)S(1)} fusion(bf16[1024,128,1]{1,0,2:T(8,128)(2,1)S(1)} %bitcast.101, bf16[32,64,128]{2,1,0:T(8,128)(2,1)S(1)} %bitcast.107), kind=kOutput, calls=%fused_computation.2.clone.1 | convolution fusion | flops 538902528 | bytes 1048576 | tf_op jit(solution)/shard_map/while/body/eval_jaxpr/ubh,qh->ubq/dot_general | solution.py:20
  54.4 0.2 copy.52
  54.6 0.2 select_reduce_fusion.7
  54.8 1.3 %convolution_reduce_fusion.6 = f32[32,2048]{1,0:T(8,128)S(1)} fusion(bf16[2048,128]{1,0:T(8,128)(2,1)S(1)} %get-tuple-element.179, bf16[1,32,32,128]{3,2,0,1:T(8,128)(2,1)S(1)} %constant_dynamic-slice_fusion.2), kind=kOutput, calls=%fused_computation.1.clone.1 | convolution fusion | flops 538902528 | bytes 1048576 | tf_op jit(solution)/shard_map/while/body/eval_jaxpr/trh,ch->trc/dot_general | solution.py:23
  56.1 0.2 reshape.184
  56.3 0.1 select_reduce_fusion.6
  56.4 1.3 %convolution_reduce_fusion.7 = f32[1024,64]{0,1:T(8,128)S(1)} fusion(bf16[1024,128,1]{1,0,2:T(8,128)(2,1)S(1)} %bitcast.101, bf16[32,64,128]{2,1,0:T(8,128)(2,1)S(1)} %bitcast.107), kind=kOutput, calls=%fused_computation.2.clone.1 | convolution fusion | flops 538902528 | bytes 1048576 | tf_op jit(solution)/shard_map/while/body/eval_jaxpr/ubh,qh->ubq/dot_general | solution.py:20
  57.7 0.2 copy.52
  57.9 0.2 select_reduce_fusion.7
  58.2 0.1 copy.42
  58.2 0.0 collective-permute-start.3
  58.3 0.0 collective-permute-done.1
  58.3 0.1 copy.39
  58.4 3.8 %collective-permute-done.3 = f32[64,64]{1,0:T(8,128)S(1)} collective-permute-done((f32[64,64]{1,0:T(8,128)S(1)}, f32[64,64]{1,0:T(8,128)S(1)}, u32[]{:S(2)}, u32[]{:S(2)}) %collective-permute-start.3) | collective-permute-done | bytes 16416 | tf_op jit(solution)/shard_map/ppermute | solution.py:98
  62.2 0.7 %pad_maximum_fusion.1 = f32[64,192]{1,0:T(8,128)} fusion(f32[64,64]{1,0:T(8,128)S(1)} %get-tuple-element.111, f32[64,64]{1,0:T(8,128)S(1)} %get-tuple-element.110, f32[64,64]{1,0:T(8,128)S(1)} %bitcast_select_fusion), kind=kLoop, calls=%fused_computation.30 | loop fusion | flops 24576 | bytes 98304 | tf_op jit(solution)/shard_map/concatenate | solution.py:102
  (22 shorter events, 0.3 us)
Async XLA Ops:
  0.0 1.1 %copy-start = (bf16[256,8,128]{2,1,0:T(8,128)(2,1)S(1)}, bf16[256,8,128]{2,1,0:T(8,128)(2,1)}, u32[]{:S(2)}) copy-start(bf16[256,8,128]{2,1,0:T(8,128)(2,1)} %param.6) | copy-start | bytes 1572868
  1.9 8.2 %copy-start.1 = (s32[64,32]{0,1:T(8,128)S(1)}, s32[64,32]{0,1:T(8,128)}, u32[]{:S(2)}) copy-start(s32[64,32]{0,1:T(8,128)} %param.9) | copy-start | bytes 24580
  1.9 8.2 %copy-start.2 = (s32[64]{0:T(128)S(1)}, s32[64]{0:T(128)}, u32[]{:S(2)}) copy-start(s32[64]{0:T(128)} %param.8) | copy-start | bytes 772
  2.8 23.7 %all-to-all-start = ((bf16[8,32,8,128]{3,2,0,1:T(8,128)(2,1)}), bf16[8,32,8,128]{3,2,0,1:T(8,128)(2,1)S(1)}, u32[]{:S(2)}, u32[]{:S(2)}) async-start(bf16[8,32,8,128]{3,2,0,1:T(8,128)(2,1)} %copy.36), calls=%async_computation | async-start | bytes 1048576 | tf_op jit(solution)/shard_map/all_to_all | solution.py:51
  29.2 14.9 %collective-permute-start.2 = (bf16[2064,128]{1,0:T(8,128)(2,1)}, bf16[2064,128]{1,0:T(8,128)(2,1)}, u32[]{:S(2)}, u32[]{:S(2)}) collective-permute-start(bf16[2064,128]{1,0:T(8,128)(2,1)} %pad_maximum_fusion), channel_id=1, source_target_pairs={{0,2},{1,5},{2,6},{3,1},{4,0},{5,7},{6,4},{7,3},{8,10},{9,13},{10,... | collective-permute-start | bytes 1585160 | tf_op jit(solution)/shard_map/ppermute | solution.py:75
  29.2 15.6 %collective-permute-start = (bf16[2064,128]{1,0:T(8,128)(2,1)}, bf16[2064,128]{1,0:T(8,128)(2,1)}, u32[]{:S(2)}, u32[]{:S(2)}) collective-permute-start(bf16[2064,128]{1,0:T(8,128)(2,1)} %pad_maximum_fusion), channel_id=1, source_target_pairs={{0,1},{1,0},{2,3},{3,2},{4,5},{5,4},{6,7},{7,6},{8,9},{9,8},{10,11... | collective-permute-start | bytes 1585160 | tf_op jit(solution)/shard_map/ppermute | solution.py:76
  50.3 8.0 %collective-permute-start.1 = (f32[32,64]{1,0:T(8,128)S(1)}, f32[32,64]{1,0:T(8,128)S(1)}, u32[]{:S(2)}, u32[]{:S(2)}) collective-permute-start(f32[32,64]{1,0:T(8,128)S(1)} %fusion.6), channel_id=1, source_target_pairs={{0,1},{1,0},{2,3},{3,2},{4,5},{5,4},{6,7},{7,6},{8,9},{9,8},{10,11... | collective-permute-start | bytes 24584 | tf_op jit(solution)/shard_map/ppermute | solution.py:88
  58.2 3.9 %collective-permute-start.3 = (f32[64,64]{1,0:T(8,128)S(1)}, f32[64,64]{1,0:T(8,128)S(1)}, u32[]{:S(2)}, u32[]{:S(2)}) collective-permute-start(f32[64,64]{1,0:T(8,128)S(1)} %bitcast.117), channel_id=1, source_target_pairs={{2,0},{5,1},{6,2},{1,3},{0,4},{7,5},{4,6},{3,7},{10,8},{13,9},{14,... | collective-permute-start | bytes 49160 | tf_op jit(solution)/shard_map/ppermute | solution.py:98

commit v9 on v7

--- a/solution.py
+++ b/solution.py
@@ -44,8 +44,17 @@
     n_tok = items_dev * tok
     pool_index = lax.axis_index("pool")
 
-    table = slot_items.reshape(owners, n_pool, per)
-    mine = lax.dynamic_index_in_dim(table, pool_index, 1, keepdims=False) - pool_index * group
+    lanes = 128
+    if lanes % items_dev == 0 and slot_items.shape[0] % lanes == 0:
+        per_row = lanes // items_dev
+        view = slot_items.reshape(-1, lanes)
+        pieces = [
+            lax.dynamic_slice_in_dim(view, h * items_dev + pool_index * per, per, axis=1) for h in range(per_row)
+        ]
+        table = jnp.concatenate(pieces, axis=1).reshape(owners, per)
+    else:
+        table = lax.dynamic_index_in_dim(slot_items.reshape(owners, n_pool, per), pool_index, 1, keepdims=False)
+    mine = table - pool_index * group
     outgoing = jnp.take(encoded, mine, axis=0, mode="clip")
     outgoing = jnp.transpose(outgoing, (2, 0, 1, 3))
     arrived = lax.all_to_all(outgoing, ("enc", "pool"), split_axis=1, concat_axis=1, tiled=True)

time: 55 us -> 55 us (level)
    reshape x1 -> x0, local copies, waits for them, and re-layouts: 0.85 us -> none  [shards(): table = slot_items.reshape(owners, n_pool, per)]
    dynamic_slice x0 -> x1, local copies, waits for them, and re-layouts: none -> 0.84 us  [shards(): lax.dynamic_slice_in_dim(view, h * items_dev + pool_index * per, per, axi...]
where the time goes in v9:
time: 55 us; the launch traced here: 54.7 us
  waiting for transfers between devices  28.4 us (52%)
  starting transfers between devices  7.65 us (14%)
  matrix products  7.6 us (14%)
  local copies, waits for them, and re-layouts  5.72 us (10%)
  other arithmetic  4.82 us (9%)
    all_to_all x1, waiting for transfers between devices, shards(): lax.all_to_all(outgoing, ('enc', 'pool'), split_axis=1, concat_axis=1, ti...  16.1 us
    all_to_all x1, starting transfers between devices, shards(): lax.all_to_all(outgoing, ('enc', 'pool'), split_axis=1, concat_axis=1, ti...  7.3 us
    ppermute x1, waiting for transfers between devices, shards(): z_recv = lax.ppermute(packed, 'pool', send_pairs)  7.28 us
    dot_general x3, matrix products, one_block(): jnp.einsum('trh,ch->trc', turned, other_flat, preferred_element_type=jnp....  3.81 us
    dot_general x3, matrix products, one_block(): jnp.einsum('ubh,qh->ubq', other, flat, preferred_element_type=jnp.float32)  3.8 us
    ppermute x1, waiting for transfers between devices, shards(): tile_back = lax.ppermute(tile_z.T, 'pool', back_pairs)  3.78 us
    select_n x1, other arithmetic, shards(): other = jnp.where(is_a, c_blk, block)  1.4 us
    ppermute x1, waiting for transfers between devices, shards(): c_recv = lax.ppermute(packed, 'pool', chip_pairs)  1.17 us
  transfers between devices with their start and end apart: 5, of which 4 were waited for; matrix products, arithmetic and copies ran while one was open for 25% of the time, Pallas kernels for 0%

profile of v9, /device:TPU:0, one launch (start us, length us, event | category | flops | bytes accessed | tf_op | source)
XLA Modules:
  0.0 54.7 jit_solution(4618065417370844875)
XLA Ops:
  0.0 0.0 copy-start
  0.0 0.8 %constant_dynamic-slice_fusion.3 = (s32[16,8]{1,0:T(8,128)S(1)}, s32[16,8]{1,0:T(8,128)S(1)}) fusion(s32[16,128]{1,0:T(8,128)} %bitcast.128, s32[]{:T(128)S(6)} %select_n.115, s32[]{:T(128)S(6)} %select_n.116), kind=kLoop, calls=%fused_computation.54 | loop fusion | bytes 2056 | tf_op jit(solution)/shard_map/dynamic_slice | solution.py:52
  0.8 0.1 add_subtract_fusion
  0.9 0.1 reshape.201
  1.0 0.1 copy-done
  1.1 0.8 %gather_fusion = bf16[256,8,128]{2,1,0:T(8,128)(2,1)S(1)} fusion(bf16[256,8,128]{2,1,0:T(8,128)(2,1)S(1)} %copy-done, s32[1024]{0:T(1024)S(1)} %pad_clamp_fusion), kind=kCustom, calls=%fused_computation | custom fusion | bytes 1049600 | tf_op jit(solution)/shard_map/jit(_take)/gather | solution.py:58
  1.9 0.0 copy-start.1
  1.9 0.0 copy-start.2
  1.9 0.9 %copy.42 = bf16[8,32,8,128]{3,2,0,1:T(8,128)(2,1)} copy(bf16[8,32,8,128]{3,0,2,1:T(8,128)(2,1)S(1)} %bitcast.111) | data formatting | bytes 1048576 | tf_op jit(solution)/shard_map/transpose | solution.py:59
  2.8 7.3 %all-to-all-start = ((bf16[8,32,8,128]{3,2,0,1:T(8,128)(2,1)}), bf16[8,32,8,128]{3,2,0,1:T(8,128)(2,1)S(1)}, u32[]{:S(2)}, u32[]{:S(2)}) async-start(bf16[8,32,8,128]{3,2,0,1:T(8,128)(2,1)} %copy.42), calls=%async_computation | async-start | bytes 1048576 | tf_op jit(solution)/shard_map/all_to_all | solution.py:60
  10.1 0.0 copy-done.1
  10.1 0.0 copy-done.2
  10.1 0.1 fusion.10
  10.2 0.1 convert_element_type.102
  10.3 16.1 %all-to-all-done = bf16[8,32,8,128]{3,2,0,1:T(8,128)(2,1)S(1)} async-done(((bf16[8,32,8,128]{3,2,0,1:T(8,128)(2,1)}), bf16[8,32,8,128]{3,2,0,1:T(8,128)(2,1)S(1)}, u32[]{:S(2)}, u32[]{:S(2)}) %all-to-all-start) | async-done | bytes 524320 | tf_op jit(solution)/shard_map/all_to_all | solution.py:60
  26.5 0.3 multiply_reduce_fusion
  26.9 0.1 sqrt.20
  27.0 0.1 copy_convert_fusion
  27.1 0.3 fusion.3
  27.4 0.1 collective-permute-start
  27.5 0.1 reshape.198
  27.7 0.1 eq.63
  27.8 0.1 sqrt.21
  27.9 0.1 collective-permute-start.2
  27.9 0.1 sqrt.22
  28.0 0.3 fusion.6
  28.4 1.2 %collective-permute-done = bf16[2064,128]{1,0:T(8,128)(2,1)} collective-permute-done((bf16[2064,128]{1,0:T(8,128)(2,1)S(1)}, bf16[2064,128]{1,0:T(8,128)(2,1)}, u32[]{:S(2)}, u32[]{:S(2)}) %collective-permute-start) | collective-permute-done | bytes 528416 | tf_op jit(solution)/shard_map/ppermute | solution.py:84
  29.6 0.7 %slice.35 = bf16[16,128]{1,0:T(8,128)(2,1)S(1)} slice(bf16[2064,128]{1,0:T(8,128)(2,1)} %collective-permute-done), slice={[2048:2064], [0:128]} | slice | bytes 8192 | tf_op jit(solution)/shard_map/slice | solution.py:87
  30.2 0.1 reshape.186
  30.3 0.1 broadcast_compare_fusion.1
  30.4 0.1 fusion.12
  30.5 1.4 %broadcast_select_fusion = (bf16[2048,128]{1,0:T(8,128)(2,1)S(1)}, bf16[2048,128]{1,0:T(8,128)(2,1)S(1)}) fusion(pred[]{:T(512)S(6)} %eq.52, bf16[2064,128]{1,0:T(8,128)(2,1)} %collective-permute-done, f32[2048]{0:T(1024)S(1)} %sqrt.20, f32[8,32,8,128]{3,2,1,0:T(8,128)S(1)} %copy_convert_fusion), kind=kLoop, calls=%fused_computation.27 | loop fusion | flops 786432 | bytes 2629633 | tf_op jit(solution)/shard_map/jit(_where)/select_n | solution.py:93
  31.9 0.2 fusion.7
  32.1 1.3 %add_reduce_fusion.2 = f32[32,2048]{1,0:T(8,128)S(1)} fusion(bf16[32,32,128]{2,1,0:T(8,128)(2,1)S(1)} %fusion.7, f32[32,32]{1,0:T(8,128)S(1)} %fusion.12, bf16[2048,128]{1,0:T(8,128)(2,1)S(1)} %get-tuple-element.134), kind=kOutput, calls=%fused_computation.13 | convolution fusion | flops 540999680 | bytes 1052672 | tf_op jit(solution)/shard_map/while/body/eval_jaxpr/trh,ch->trc/dot_general | solution.py:25
  33.4 1.3 %add_reduce_fusion.3 = f32[64,1024]{1,0:T(8,128)S(1)} fusion(f32[32,64]{1,0:T(8,128)S(1)} %fusion.11, bf16[32,64,128]{2,1,0:T(8,128)(2,1)S(1)} %bitcast.116, bf16[1024,128,1]{1,0,2:T(8,128)(2,1)S(1)} %bitcast.119), kind=kOutput, calls=%fused_computation.14 | convolution fusion | flops 540999680 | bytes 1056768 | tf_op jit(solution)/shard_map/while/body/eval_jaxpr/ubh,qh->ubq/dot_general | solution.py:22
  34.7 0.2 copy.44
  34.9 0.2 reshape.190
  35.1 0.1 select_reduce_fusion.2
  35.2 0.2 select_reduce_fusion.3
  35.5 0.2 collective-permute-start.1
  35.6 7.3 %collective-permute-done.2 = bf16[2064,128]{1,0:T(8,128)(2,1)S(1)} collective-permute-done((bf16[2064,128]{1,0:T(8,128)(2,1)S(1)}, bf16[2064,128]{1,0:T(8,128)(2,1)S(1)}, u32[]{:S(2)}, u32[]{:S(2)}) %collective-permute-start.2) | collective-permute-done | bytes 528416 | tf_op jit(solution)/shard_map/ppermute | solution.py:83
  42.9 0.1 reshape.196
  43.0 0.1 eq.65
  43.1 6.8 %while.2 = (s32[]{:T(128)}, f32[2,32,64]{2,1,0:T(8,128)S(1)}, pred[2,32,32]{2,1,0:T(8,128)(4,1)S(1)}, bf16[2,32,32,128]{3,2,0,1:T(8,128)(2,1)S(1)}, bf16[32,64,1...) while((s32[]{:T(128)}, f32[2,32,64]{2,1,0:T(8,128)S(1)}, ...), condition=%wide.region_10.11_spmd, body=%wide.region_5.10_spmd.sunk | while | flops 1082261504 | bytes 4285557 | solution.py:30
  43.2 1.3 %add_reduce_fusion.6 = f32[32,2048]{1,0:T(8,128)S(1)} fusion(f32[32,32]{1,0:T(8,128)S(1)} %bitcast.117, bf16[2048,128]{1,0:T(8,128)(2,1)S(1)} %get-tuple-element.225, bf16[1,32,32,128]{3,2,0,1:T(8,128)(2,1)S(1)} %constant_dynamic-slice_fusion.7), kind=kOutput, calls=%fused_computation.1.clone.1 | convolution fusion | flops 540999680 | bytes 1052672 | tf_op jit(solution)/shard_map/while/body/eval_jaxpr/trh,ch->trc/dot_general | solution.py:25
  44.5 0.2 reshape.214
  44.7 0.1 select_reduce_fusion.6
  44.8 1.3 %add_reduce_fusion.7 = f32[1024,64]{0,1:T(8,128)S(1)} fusion(f32[32,64]{1,0:T(8,128)S(1)} %bitcast.129, bf16[1024,128,1]{1,0,2:T(8,128)(2,1)S(1)} %bitcast.109, bf16[32,64,128]{2,1,0:T(8,128)(2,1)S(1)} %bitcast.114), kind=kOutput, calls=%fused_computation.2.clone.1 | convolution fusion | flops 540999680 | bytes 1056768 | tf_op jit(solution)/shard_map/while/body/eval_jaxpr/ubh,qh->ubq/dot_general | solution.py:22
  46.1 0.2 copy.61
  46.3 0.2 select_reduce_fusion.7
  46.6 1.3 %add_reduce_fusion.6 = f32[32,2048]{1,0:T(8,128)S(1)} fusion(f32[32,32]{1,0:T(8,128)S(1)} %bitcast.117, bf16[2048,128]{1,0:T(8,128)(2,1)S(1)} %get-tuple-element.225, bf16[1,32,32,128]{3,2,0,1:T(8,128)(2,1)S(1)} %constant_dynamic-slice_fusion.7), kind=kOutput, calls=%fused_computation.1.clone.1 | convolution fusion | flops 540999680 | bytes 1052672 | tf_op jit(solution)/shard_map/while/body/eval_jaxpr/trh,ch->trc/dot_general | solution.py:25
  47.9 0.2 reshape.214
  48.1 0.1 select_reduce_fusion.6
  48.2 1.3 %add_reduce_fusion.7 = f32[1024,64]{0,1:T(8,128)S(1)} fusion(f32[32,64]{1,0:T(8,128)S(1)} %bitcast.129, bf16[1024,128,1]{1,0,2:T(8,128)(2,1)S(1)} %bitcast.109, bf16[32,64,128]{2,1,0:T(8,128)(2,1)S(1)} %bitcast.114), kind=kOutput, calls=%fused_computation.2.clone.1 | convolution fusion | flops 540999680 | bytes 1056768 | tf_op jit(solution)/shard_map/while/body/eval_jaxpr/ubh,qh->ubq/dot_general | solution.py:22
  49.4 0.2 copy.61
  49.7 0.2 select_reduce_fusion.7
  49.9 0.1 copy.50
  50.0 0.0 collective-permute-start.3
  50.0 0.0 collective-permute-done.1
  50.0 0.1 copy.45
  50.1 3.8 %collective-permute-done.3 = f32[64,64]{1,0:T(8,128)S(1)} collective-permute-done((f32[64,64]{1,0:T(8,128)S(1)}, f32[64,64]{1,0:T(8,128)S(1)}, u32[]{:S(2)}, u32[]{:S(2)}) %collective-permute-start.3) | collective-permute-done | bytes 16416 | tf_op jit(solution)/shard_map/ppermute | solution.py:106
  53.9 0.7 %pad_maximum_fusion.1 = f32[64,192]{1,0:T(8,128)} fusion(f32[64,64]{1,0:T(8,128)S(1)} %get-tuple-element.137, f32[64,64]{1,0:T(8,128)S(1)} %get-tuple-element.136, f32[64,64]{1,0:T(8,128)S(1)} %bitcast_select_fusion), kind=kLoop, calls=%fused_computation.30 | loop fusion | flops 24576 | bytes 98304 | tf_op jit(solution)/shard_map/concatenate | solution.py:110
  (25 shorter events, 0.4 us)
Async XLA Ops:
  0.0 1.1 %copy-start = (bf16[256,8,128]{2,1,0:T(8,128)(2,1)S(1)}, bf16[256,8,128]{2,1,0:T(8,128)(2,1)}, u32[]{:S(2)}) copy-start(bf16[256,8,128]{2,1,0:T(8,128)(2,1)} %param.6) | copy-start | bytes 1572868
  1.9 8.2 %copy-start.1 = (s32[64,32]{0,1:T(8,128)S(1)}, s32[64,32]{0,1:T(8,128)}, u32[]{:S(2)}) copy-start(s32[64,32]{0,1:T(8,128)} %param.9) | copy-start | bytes 24580
  1.9 8.2 %copy-start.2 = (s32[64]{0:T(128)S(1)}, s32[64]{0:T(128)}, u32[]{:S(2)}) copy-start(s32[64]{0:T(128)} %param.8) | copy-start | bytes 772
  2.8 23.7 %all-to-all-start = ((bf16[8,32,8,128]{3,2,0,1:T(8,128)(2,1)}), bf16[8,32,8,128]{3,2,0,1:T(8,128)(2,1)S(1)}, u32[]{:S(2)}, u32[]{:S(2)}) async-start(bf16[8,32,8,128]{3,2,0,1:T(8,128)(2,1)} %copy.42), calls=%async_computation | async-start | bytes 1048576 | tf_op jit(solution)/shard_map/all_to_all | solution.py:60
  27.4 2.1 %collective-permute-start = (bf16[2064,128]{1,0:T(8,128)(2,1)S(1)}, bf16[2064,128]{1,0:T(8,128)(2,1)}, u32[]{:S(2)}, u32[]{:S(2)}) collective-permute-start(bf16[2064,128]{1,0:T(8,128)(2,1)S(1)} %pad_maximum_fusion), channel_id=1, source_target_pairs={{0,1},{1,0},{2,3},{3,2},{4,5},{5,4},{6,7},{7,6},{8,9},{9,8},{10,11... | collective-permute-start | bytes 1585160 | tf_op jit(solution)/shard_map/ppermute | solution.py:84
  27.9 15.1 %collective-permute-start.2 = (bf16[2064,128]{1,0:T(8,128)(2,1)S(1)}, bf16[2064,128]{1,0:T(8,128)(2,1)S(1)}, u32[]{:S(2)}, u32[]{:S(2)}) collective-permute-start(bf16[2064,128]{1,0:T(8,128)(2,1)S(1)} %pad_maximum_fusion), channel_id=1, source_target_pairs={{0,2},{1,5},{2,6},{3,1},{4,0},{5,7},{6,4},{7,3},{8,10},{9,13},{10,... | collective-permute-start | bytes 1585160 | tf_op jit(solution)/shard_map/ppermute | solution.py:83
  35.5 14.6 %collective-permute-start.1 = (f32[32,64]{1,0:T(8,128)S(1)}, f32[32,64]{1,0:T(8,128)S(1)}, u32[]{:S(2)}, u32[]{:S(2)}) collective-permute-start(f32[32,64]{1,0:T(8,128)S(1)} %fusion.8), channel_id=1, source_target_pairs={{0,1},{1,0},{2,3},{3,2},{4,5},{5,4},{6,7},{7,6},{8,9},{9,8},{10,11... | collective-permute-start | bytes 24584 | tf_op jit(solution)/shard_map/ppermute | solution.py:96
  50.0 3.9 %collective-permute-start.3 = (f32[64,64]{1,0:T(8,128)S(1)}, f32[64,64]{1,0:T(8,128)S(1)}, u32[]{:S(2)}, u32[]{:S(2)}) collective-permute-start(f32[64,64]{1,0:T(8,128)S(1)} %bitcast.127), channel_id=1, source_target_pairs={{2,0},{5,1},{6,2},{1,3},{0,4},{7,5},{4,6},{3,7},{10,8},{13,9},{14,... | collective-permute-start | bytes 49160 | tf_op jit(solution)/shard_map/ppermute | solution.py:106

commit v10 on v7

--- a/solution.py
+++ b/solution.py
@@ -7,7 +7,7 @@
 def tile_scores(query, query_bias, other, other_bias):
     tok, query_items, width = query.shape
     other_items = other.shape[1]
-    rows = min(32, query_items)
+    rows = min(64, query_items)
     blocks = query_items // rows
     other_flat = other.reshape(tok * other_items, width)
     other_add = other_bias.astype(jnp.float32)[:, :, None]

time: 55 us -> 71.6 us (1.30)
  local copies, waits for them, and re-layouts: 5.7 us -> 10.2 us
  waiting for transfers between devices: 28.4 us -> 32.6 us
  other arithmetic: 4.81 us -> 8.92 us
  matrix products: 7.59 us -> 11.4 us
    ppermute x1, waiting for transfers between devices: 7.28 us -> 12.2 us  [shards(): z_recv = lax.ppermute(packed, 'pool', send_pairs)]
    reshape x3 -> x2, local copies, waits for them, and re-layouts: 0.65 us -> 2.67 us  [one_block(): back = jnp.max(dots_back + adding, axis=0).reshape(rows, tok, other_items)]
    dot_general x3 -> x2, matrix products: 3.8 us -> 5.69 us  [one_block(): jnp.einsum('ubh,qh->ubq', other, flat, preferred_element_type=jnp.float32)]
    dot_general x3 -> x2, matrix products: 3.79 us -> 5.68 us  [one_block(): jnp.einsum('trh,ch->trc', turned, other_flat, preferred_element_type=jnp....]
    convert_element_type x1 -> x3, other arithmetic: 0.34 us -> 1.82 us  [shards(): (values / jnp.sqrt(jnp.sum(values * values, axis=-1, keepdims=True) + 1e-...]
    reshape x1, local copies, waits for them, and re-layouts: 0.07 us -> 1.45 us  [one_block(): jnp.max(dots_fore + other_add, axis=0).reshape(other_items, tok, rows)]
    reduce_sum x3 -> x2, other arithmetic: 0.26 us -> 1.51 us  [one_block(): back = jnp.sum(jnp.where(other_valid[None], back, 0.0), axis=1)]
    slice x1, local copies, waits for them, and re-layouts: 0.03 us -> 1.08 us  [unpack(): received[:n_tok].reshape(tok, items_dev, width)]
  transfers between devices with their start and end apart: 5 -> 5, of which waited for: 4 -> 5; matrix products, arithmetic and copies ran while one was open for 25% -> 4% of each run, Pallas kernels for 0% -> 0%
where the time goes in v10:
time: 71.6 us; the launch traced here: 71 us
  waiting for transfers between devices  32.6 us (46%)
  matrix products  11.4 us (16%)
  local copies, waits for them, and re-layouts  10.2 us (14%)
  other arithmetic  8.92 us (12%)
  starting transfers between devices  7.59 us (11%)
    all_to_all x1, waiting for transfers between devices, shards(): lax.all_to_all(outgoing, ('enc', 'pool'), split_axis=1, concat_axis=1, ti...  16.1 us
    ppermute x1, waiting for transfers between devices, shards(): z_recv = lax.ppermute(packed, 'pool', send_pairs)  12.2 us
    all_to_all x1, starting transfers between devices, shards(): lax.all_to_all(outgoing, ('enc', 'pool'), split_axis=1, concat_axis=1, ti...  7.3 us
    dot_general x2, matrix products, one_block(): jnp.einsum('ubh,qh->ubq', other, flat, preferred_element_type=jnp.float32)  5.69 us
    dot_general x2, matrix products, one_block(): jnp.einsum('trh,ch->trc', turned, other_flat, preferred_element_type=jnp....  5.68 us
    ppermute x1, waiting for transfers between devices, shards(): tile_back = lax.ppermute(tile_z.T, 'pool', back_pairs)  2.97 us
    reshape x2, local copies, waits for them, and re-layouts, one_block(): back = jnp.max(dots_back + adding, axis=0).reshape(rows, tok, other_items)  2.67 us
    convert_element_type x3, other arithmetic, shards(): (values / jnp.sqrt(jnp.sum(values * values, axis=-1, keepdims=True) + 1e-...  1.82 us
  transfers between devices with their start and end apart: 5, of which 5 were waited for; matrix products, arithmetic and copies ran while one was open for 4% of the time, Pallas kernels for 0%

profile of v10, /device:TPU:0, one launch (start us, length us, event | category | flops | bytes accessed | tf_op | source)
XLA Modules:
  0.0 71.0 jit_solution(5710720355632084069)
XLA Ops:
  0.0 0.0 copy-start
  0.0 0.8 %reshape.175 = s32[32,8,8]{2,1,0:T(8,128)S(1)} reshape(s32[2048]{0:T(1024)} %param.5) | data formatting | bytes 16384 | tf_op jit(solution)/shard_map/reshape | solution.py:47
  0.9 0.1 subtract_reduce_fusion
  0.9 0.1 reshape.189
  1.0 0.0 copy-done
  1.1 0.8 %gather_fusion = bf16[256,8,128]{2,1,0:T(8,128)(2,1)S(1)} fusion(bf16[256,8,128]{2,1,0:T(8,128)(2,1)S(1)} %copy-done, s32[1024]{0:T(1024)S(1)} %pad_clamp_fusion), kind=kCustom, calls=%fused_computation | custom fusion | bytes 1049600 | tf_op jit(solution)/shard_map/jit(_take)/gather | solution.py:49
  1.9 0.0 copy-start.3
  1.9 0.0 copy-start.4
  1.9 0.9 %copy.28 = bf16[8,32,8,128]{3,2,0,1:T(8,128)(2,1)} copy(bf16[8,32,8,128]{3,0,2,1:T(8,128)(2,1)S(1)} %bitcast.58) | data formatting | bytes 1048576 | tf_op jit(solution)/shard_map/transpose | solution.py:50
  2.8 7.3 %all-to-all-start = ((bf16[8,32,8,128]{3,2,0,1:T(8,128)(2,1)}), bf16[8,32,8,128]{3,2,0,1:T(8,128)(2,1)S(1)}, u32[]{:S(2)}, u32[]{:S(2)}) async-start(bf16[8,32,8,128]{3,2,0,1:T(8,128)(2,1)} %copy.28), calls=%async_computation | async-start | bytes 1048576 | tf_op jit(solution)/shard_map/all_to_all | solution.py:51
  10.1 0.0 copy-done.3
  10.1 0.0 copy-done.4
  10.1 0.1 fusion.7
  10.2 0.1 convert_element_type.97
  10.3 16.1 %all-to-all-done = bf16[8,32,8,128]{3,2,0,1:T(8,128)(2,1)S(1)} async-done(((bf16[8,32,8,128]{3,2,0,1:T(8,128)(2,1)}), bf16[8,32,8,128]{3,2,0,1:T(8,128)(2,1)S(1)}, u32[]{:S(2)}, u32[]{:S(2)}) %all-to-all-start) | async-done | bytes 524320 | tf_op jit(solution)/shard_map/all_to_all | solution.py:51
  26.4 0.3 multiply_reduce_fusion
  26.8 0.1 sqrt.17
  27.0 0.1 copy_convert_fusion
  27.0 0.3 fusion
  27.4 0.8 %pad_maximum_fusion = bf16[2064,128]{1,0:T(8,128)(2,1)} fusion(bf16[16,128]{1,0:T(8,128)(2,1)S(1)} %convert_element_type.97, bf16[2048,128]{1,0:T(8,128)(2,1)S(1)} %fusion), kind=kLoop, calls=%fused_computation.12 | loop fusion | flops 1056768 | bytes 1056768 | tf_op jit(solution)/shard_map/concatenate | solution.py:61
  28.2 0.0 collective-permute-start
  28.2 0.0 collective-permute-start.2
  28.2 0.1 sqrt.18
  28.3 1.1 %divide_convert_fusion = bf16[8,32,8,128]{3,2,1,0:T(8,128)(2,1)} fusion(f32[8,32,8]{2,1,0:T(8,128)S(1)} %add_sqrt_fusion, bf16[8,32,8,128]{3,2,0,1:T(8,128)(2,1)S(1)} %all-to-all-done), kind=kLoop, calls=%fused_computation.9 | loop fusion | flops 786432 | bytes 1056768 | tf_op jit(solution)/shard_map/convert_element_type | solution.py:54
  29.5 0.0 copy-start.1
  29.5 0.3 divide_convert_fusion.1
  29.8 0.7 collective-permute-done
  30.5 0.7 slice.35
  31.1 0.1 reshape.176
  31.2 0.1 broadcast_compare_fusion.2
  31.3 0.1 fusion.9
  31.4 12.2 %collective-permute-done.2 = bf16[2064,128]{1,0:T(8,128)(2,1)} collective-permute-done((bf16[2064,128]{1,0:T(8,128)(2,1)}, bf16[2064,128]{1,0:T(8,128)(2,1)}, u32[]{:S(2)}, u32[]{:S(2)}) %collective-permute-start.2) | collective-permute-done | bytes 528416 | tf_op jit(solution)/shard_map/ppermute | solution.py:74
  43.6 0.7 slice_convert_fusion
  44.2 0.1 reshape.186
  44.3 1.1 %slice.40 = bf16[2048,128]{1,0:T(8,128)(2,1)S(1)} slice(bf16[2064,128]{1,0:T(8,128)(2,1)} %collective-permute-done.2), slice={[0:2048], [0:128]} | slice | bytes 1048576 | tf_op jit(solution)/shard_map/slice | solution.py:78
  45.4 0.0 copy-done.1
  45.4 3.4 %add_reduce_fusion.1 = f32[64,2048]{1,0:T(8,128)} fusion(f32[32,64]{1,0:T(8,128)S(1)} %reshape.186, bf16[32,64,128]{2,1,0:T(8,128)(2,1)S(1)} %bitcast.61, bf16[2048,128,1]{1,0,2:T(8,128)(2,1)S(1)} %bitcast.60), kind=kOutput, calls=%fused_computation.2 | convolution fusion | flops 1081999360 | bytes 1581056 | tf_op jit(solution)/shard_map/while/body/eval_jaxpr/ubh,qh->ubq/dot_general | solution.py:22
  48.8 1.5 %reshape.182 = f32[64,32,64]{2,1,0:T(8,128)S(1)} reshape(f32[64,2048]{1,0:T(8,128)} %add_reduce_fusion.1) | data formatting | bytes 1048576 | tf_op jit(solution)/shard_map/while/body/eval_jaxpr/reshape | solution.py:23
  50.2 4.4 %add_reduce_fusion = f32[64,2048]{1,0:T(8,128)} fusion(f32[32,64]{1,0:T(8,128)S(1)} %convert_element_type.107, bf16[32,64,128]{2,1,0:T(8,128)(2,1)S(1)} %divide_convert_fusion.1, bf16[2064,128]{1,0:T(8,128)(2,1)} %collective-permute-done.2), kind=kOutput, calls=%fused_computation.1 | convolution fusion | flops 1081999360 | bytes 1581056 | tf_op jit(solution)/shard_map/while/body/eval_jaxpr/trh,ch->trc/dot_general | solution.py:25
  54.6 2.5 %reshape.183 = f32[64,32,64]{2,1,0:T(8,128)} reshape(f32[64,2048]{1,0:T(8,128)} %add_reduce_fusion) | data formatting | bytes 1048576 | tf_op jit(solution)/shard_map/while/body/eval_jaxpr/reshape | solution.py:26
  57.1 0.7 slice_compare_fusion
  57.8 0.1 eq.60
  57.9 1.4 %select_reduce_fusion = f32[64,64]{1,0:T(8,128)S(1)} fusion(f32[64,32,64]{2,1,0:T(8,128)} %reshape.183, pred[32,64]{1,0:T(8,128)(4,1)S(1)} %eq.60), kind=kLoop, calls=%fused_computation.7 | loop fusion | flops 258048 | bytes 542720 | tf_op jit(solution)/shard_map/while/body/eval_jaxpr/reduce_sum | solution.py:27
  59.3 0.1 copy.33
  59.4 1.4 %broadcast_select_fusion = (bf16[2048,128]{1,0:T(8,128)(2,1)S(1)}, bf16[2048,128]{1,0:T(8,128)(2,1)S(1)}) fusion(pred[]{:T(512)S(6)} %eq.49, bf16[2064,128]{1,0:T(8,128)(2,1)} %collective-permute-done, f32[2048]{0:T(1024)S(1)} %sqrt.17, f32[8,32,8,128]{3,2,1,0:T(8,128)S(1)} %copy_convert_fusion), kind=kLoop, calls=%fused_computation.18 | loop fusion | flops 786432 | bytes 2629633 | tf_op jit(solution)/shard_map/jit(_where)/select_n | solution.py:84
  60.8 0.0 copy-start.2
  60.8 0.7 %copy-done.2 = bf16[2048,128]{1,0:T(8,128)(2,1)} copy-done((bf16[2048,128]{1,0:T(8,128)(2,1)}, bf16[2048,128]{1,0:T(8,128)(2,1)S(1)}, u32[]{:S(2)}) %copy-start.2) | copy-done | bytes 524312
  61.6 1.3 %add_reduce_fusion.2 = f32[32,2048]{1,0:T(8,128)S(1)} fusion(bf16[32,32,128]{2,1,0:T(8,128)(2,1)S(1)} %slice_select_fusion, f32[32,32]{1,0:T(8,128)S(1)} %fusion.9, bf16[2048,128]{1,0:T(8,128)(2,1)S(1)} %get-tuple-element.39), kind=kOutput, calls=%fused_computation.3 | convolution fusion | flops 540999680 | bytes 1052672 | tf_op jit(solution)/shard_map/while/body/eval_jaxpr/trh,ch->trc/dot_general | solution.py:25
  62.8 0.2 reshape.180
  63.1 2.3 %add_reduce_fusion.3 = f32[64,1024]{1,0:T(8,128)S(1)} fusion(f32[32,64]{1,0:T(8,128)S(1)} %fusion.8, bf16[32,64,128]{2,1,0:T(8,128)(2,1)} %bitcast.62, bf16[1024,128,1]{1,0,2:T(8,128)(2,1)S(1)} %bitcast.69), kind=kOutput, calls=%fused_computation.4 | convolution fusion | flops 540999680 | bytes 1056768 | tf_op jit(solution)/shard_map/while/body/eval_jaxpr/ubh,qh->ubq/dot_general | solution.py:22
  65.4 0.2 copy.30
  65.6 0.1 select_reduce_fusion.2
  65.7 0.2 select_reduce_fusion.3
  65.9 0.1 collective-permute-start.1
  66.0 0.2 select_reduce_fusion.1
  66.2 0.1 copy.32
  66.3 0.2 collective-permute-start.3
  66.5 0.7 collective-permute-done.1
  67.2 0.1 copy.31
  67.3 3.0 %collective-permute-done.3 = f32[64,64]{1,0:T(8,128)S(1)} collective-permute-done((f32[64,64]{1,0:T(8,128)S(1)}, f32[64,64]{1,0:T(8,128)S(1)}, u32[]{:S(2)}, u32[]{:S(2)}) %collective-permute-start.3) | collective-permute-done | bytes 16416 | tf_op jit(solution)/shard_map/ppermute | solution.py:97
  70.2 0.7 %pad_maximum_fusion.1 = f32[64,192]{1,0:T(8,128)} fusion(f32[64,64]{1,0:T(8,128)S(1)} %get-tuple-element.42, f32[64,64]{1,0:T(8,128)S(1)} %get-tuple-element.41, f32[64,64]{1,0:T(8,128)S(1)} %bitcast_select_fusion), kind=kLoop, calls=%fused_computation.21 | loop fusion | flops 24576 | bytes 98304 | tf_op jit(solution)/shard_map/concatenate | solution.py:101
  (13 shorter events, 0.2 us)
Async XLA Ops:
  0.0 1.1 %copy-start = (bf16[256,8,128]{2,1,0:T(8,128)(2,1)S(1)}, bf16[256,8,128]{2,1,0:T(8,128)(2,1)}, u32[]{:S(2)}) copy-start(bf16[256,8,128]{2,1,0:T(8,128)(2,1)} %param.4) | copy-start | bytes 1572868
  1.9 8.2 %copy-start.3 = (s32[64,32]{0,1:T(8,128)S(1)}, s32[64,32]{0,1:T(8,128)}, u32[]{:S(2)}) copy-start(s32[64,32]{0,1:T(8,128)} %param.7) | copy-start | bytes 24580
  1.9 8.2 %copy-start.4 = (s32[64]{0:T(128)S(1)}, s32[64]{0:T(128)}, u32[]{:S(2)}) copy-start(s32[64]{0:T(128)} %param.6) | copy-start | bytes 772
  2.8 23.7 %all-to-all-start = ((bf16[8,32,8,128]{3,2,0,1:T(8,128)(2,1)}), bf16[8,32,8,128]{3,2,0,1:T(8,128)(2,1)S(1)}, u32[]{:S(2)}, u32[]{:S(2)}) async-start(bf16[8,32,8,128]{3,2,0,1:T(8,128)(2,1)} %copy.28), calls=%async_computation | async-start | bytes 1048576 | tf_op jit(solution)/shard_map/all_to_all | solution.py:51
  28.2 2.3 %collective-permute-start = (bf16[2064,128]{1,0:T(8,128)(2,1)}, bf16[2064,128]{1,0:T(8,128)(2,1)}, u32[]{:S(2)}, u32[]{:S(2)}) collective-permute-start(bf16[2064,128]{1,0:T(8,128)(2,1)} %pad_maximum_fusion), channel_id=1, source_target_pairs={{0,1},{1,0},{2,3},{3,2},{4,5},{5,4},{6,7},{7,6},{8,9},{9,8},{10,11... | collective-permute-start | bytes 1585160 | tf_op jit(solution)/shard_map/ppermute | solution.py:75
  28.2 15.3 %collective-permute-start.2 = (bf16[2064,128]{1,0:T(8,128)(2,1)}, bf16[2064,128]{1,0:T(8,128)(2,1)}, u32[]{:S(2)}, u32[]{:S(2)}) collective-permute-start(bf16[2064,128]{1,0:T(8,128)(2,1)} %pad_maximum_fusion), channel_id=1, source_target_pairs={{0,2},{1,5},{2,6},{3,1},{4,0},{5,7},{6,4},{7,3},{8,10},{9,13},{10,... | collective-permute-start | bytes 1585160 | tf_op jit(solution)/shard_map/ppermute | solution.py:74
  29.5 15.9 %copy-start.1 = (bf16[8,32,8,128]{3,2,1,0:T(8,128)(2,1)S(1)}, bf16[8,32,8,128]{3,2,1,0:T(8,128)(2,1)}, u32[]{:S(2)}) copy-start(bf16[8,32,8,128]{3,2,1,0:T(8,128)(2,1)} %divide_convert_fusion) | copy-start | bytes 1572868
  60.8 0.8 %copy-start.2 = (bf16[2048,128]{1,0:T(8,128)(2,1)}, bf16[2048,128]{1,0:T(8,128)(2,1)S(1)}, u32[]{:S(2)}) copy-start(bf16[2048,128]{1,0:T(8,128)(2,1)S(1)} %get-tuple-element.39) | copy-start | bytes 1572868
  65.9 1.2 %collective-permute-start.1 = (f32[32,64]{1,0:T(8,128)S(1)}, f32[32,64]{1,0:T(8,128)S(1)}, u32[]{:S(2)}, u32[]{:S(2)}) collective-permute-start(f32[32,64]{1,0:T(8,128)S(1)} %fusion.5), channel_id=1, source_target_pairs={{0,1},{1,0},{2,3},{3,2},{4,5},{5,4},{6,7},{7,6},{8,9},{9,8},{10,11... | collective-permute-start | bytes 24584 | tf_op jit(solution)/shard_map/ppermute | solution.py:87
  66.3 3.9 %collective-permute-start.3 = (f32[64,64]{1,0:T(8,128)S(1)}, f32[64,64]{1,0:T(8,128)S(1)}, u32[]{:S(2)}, u32[]{:S(2)}) collective-permute-start(f32[64,64]{1,0:T(8,128)S(1)} %fusion.3), channel_id=1, source_target_pairs={{2,0},{5,1},{6,2},{1,3},{0,4},{7,5},{4,6},{3,7},{10,8},{13,9},{14,... | collective-permute-start | bytes 49160 | tf_op jit(solution)/shard_map/ppermute | solution.py:97

commit v11 on v7

--- a/solution.py
+++ b/solution.py
@@ -95,10 +95,13 @@
     z_blk, z_bias = unpack(z_recv)
     tile_z = tile_scores(block, bias, z_blk, z_bias)
     tile_back = lax.ppermute(tile_z.T, "pool", back_pairs)
-    via_bit1 = parity == 1
-    col1 = jnp.where(via_bit1, tile_z, tile_back)
-    col2 = jnp.where(via_bit1, tile_back, tile_z)
-    return jnp.concatenate([tile0, col1, col2], axis=1)
+    other_items = tile_z.shape[1]
+    z_col = (2 - parity) * other_items
+    back_col = (1 + parity) * other_items
+    scores = jnp.zeros((items_dev, 3 * other_items), jnp.float32)
+    scores = lax.dynamic_update_slice_in_dim(scores, tile0, 0, axis=1)
+    scores = lax.dynamic_update_slice_in_dim(scores, tile_z, z_col, axis=1)
+    return lax.dynamic_update_slice_in_dim(scores, tile_back, back_col, axis=1)
 
 
 def solution(mesh):

time: 55 us -> 55.9 us (1.016)
  local copies, waits for them, and re-layouts: 5.7 us -> 7.59 us
  other arithmetic: 4.81 us -> 4.07 us
    dynamic_update_slice x0 -> x3, local copies, waits for them, and re-layouts: none -> 1.89 us  [the longest x1 1.57 us: shards(): return lax.dynamic_update_slice_in_dim(scores, tile_back, back_col, axis=1)]
    concatenate x1 -> x0, other arithmetic: 0.72 us -> none  [shards(): return jnp.concatenate([tile0, col1, col2], axis=1)]
where the time goes in v11:
time: 55.9 us; the launch traced here: 55.6 us
  waiting for transfers between devices  28.1 us (50%)
  starting transfers between devices  7.67 us (14%)
  matrix products  7.6 us (14%)
  local copies, waits for them, and re-layouts  7.59 us (14%)
  other arithmetic  4.07 us (7%)
    all_to_all x1, waiting for transfers between devices, shards(): lax.all_to_all(outgoing, ('enc', 'pool'), split_axis=1, concat_axis=1, ti...  16.1 us
    ppermute x1, waiting for transfers between devices, shards(): z_recv = lax.ppermute(packed, 'pool', send_pairs)  7.38 us
    all_to_all x1, starting transfers between devices, shards(): lax.all_to_all(outgoing, ('enc', 'pool'), split_axis=1, concat_axis=1, ti...  7.29 us
    dot_general x3, matrix products, one_block(): jnp.einsum('ubh,qh->ubq', other, flat, preferred_element_type=jnp.float32)  3.8 us
    dot_general x3, matrix products, one_block(): jnp.einsum('trh,ch->trc', turned, other_flat, preferred_element_type=jnp....  3.8 us
    ppermute x1, waiting for transfers between devices, shards(): tile_back = lax.ppermute(tile_z.T, 'pool', back_pairs)  3.44 us
    dynamic_update_slice x1, local copies, waits for them, and re-layouts, shards(): return lax.dynamic_update_slice_in_dim(scores, tile_back, back_col, axis=1)  1.57 us
    select_n x1, other arithmetic, shards(): other = jnp.where(is_a, c_blk, block)  1.4 us
  transfers between devices with their start and end apart: 5, of which 4 were waited for; matrix products, arithmetic and copies ran while one was open for 25% of the time, Pallas kernels for 0%

profile of v11, /device:TPU:0, one launch (start us, length us, event | category | flops | bytes accessed | tf_op | source)
XLA Modules:
  0.0 55.6 jit_solution(8312121919566242447)
XLA Ops:
  0.0 0.0 copy-start
  0.0 0.8 %reshape.184 = s32[32,8,8]{2,1,0:T(8,128)S(1)} reshape(s32[2048]{0:T(1024)} %param.7) | data formatting | bytes 16384 | tf_op jit(solution)/shard_map/reshape | solution.py:47
  0.9 0.1 subtract_reduce_fusion
  0.9 0.1 reshape.200
  1.0 0.0 copy-done
  1.1 0.8 %gather_fusion = bf16[256,8,128]{2,1,0:T(8,128)(2,1)S(1)} fusion(bf16[256,8,128]{2,1,0:T(8,128)(2,1)S(1)} %copy-done, s32[1024]{0:T(1024)S(1)} %pad_clamp_fusion), kind=kCustom, calls=%fused_computation | custom fusion | bytes 1049600 | tf_op jit(solution)/shard_map/jit(_take)/gather | solution.py:49
  1.9 0.0 copy-start.2
  1.9 0.0 copy-start.3
  1.9 0.9 %copy.43 = bf16[8,32,8,128]{3,2,0,1:T(8,128)(2,1)} copy(bf16[8,32,8,128]{3,0,2,1:T(8,128)(2,1)S(1)} %bitcast.108) | data formatting | bytes 1048576 | tf_op jit(solution)/shard_map/transpose | solution.py:50
  2.8 7.3 %all-to-all-start = ((bf16[8,32,8,128]{3,2,0,1:T(8,128)(2,1)}), bf16[8,32,8,128]{3,2,0,1:T(8,128)(2,1)S(1)}, u32[]{:S(2)}, u32[]{:S(2)}) async-start(bf16[8,32,8,128]{3,2,0,1:T(8,128)(2,1)} %copy.43), calls=%async_computation | async-start | bytes 1048576 | tf_op jit(solution)/shard_map/all_to_all | solution.py:51
  10.1 0.0 copy-done.2
  10.1 0.0 copy-done.3
  10.1 0.1 fusion.10
  10.2 0.1 convert_element_type.102
  10.3 16.1 %all-to-all-done = bf16[8,32,8,128]{3,2,0,1:T(8,128)(2,1)S(1)} async-done(((bf16[8,32,8,128]{3,2,0,1:T(8,128)(2,1)}), bf16[8,32,8,128]{3,2,0,1:T(8,128)(2,1)S(1)}, u32[]{:S(2)}, u32[]{:S(2)}) %all-to-all-start) | async-done | bytes 524320 | tf_op jit(solution)/shard_map/all_to_all | solution.py:51
  26.4 0.3 multiply_reduce_fusion
  26.8 0.1 sqrt.20
  27.0 0.1 copy_convert_fusion
  27.0 0.3 fusion.3
  27.4 0.1 collective-permute-start
  27.5 0.1 eq.59
  27.6 0.1 reshape.197
  27.7 0.1 sqrt.21
  27.8 0.1 sqrt.22
  28.0 0.1 collective-permute-start.2
  28.0 0.3 fusion.6
  28.4 1.2 %collective-permute-done = bf16[2064,128]{1,0:T(8,128)(2,1)} collective-permute-done((bf16[2064,128]{1,0:T(8,128)(2,1)S(1)}, bf16[2064,128]{1,0:T(8,128)(2,1)}, u32[]{:S(2)}, u32[]{:S(2)}) %collective-permute-start) | collective-permute-done | bytes 528416 | tf_op jit(solution)/shard_map/ppermute | solution.py:75
  29.5 0.7 %slice.35 = bf16[16,128]{1,0:T(8,128)(2,1)S(1)} slice(bf16[2064,128]{1,0:T(8,128)(2,1)} %collective-permute-done), slice={[2048:2064], [0:128]} | slice | bytes 8192 | tf_op jit(solution)/shard_map/slice | solution.py:78
  30.2 0.1 reshape.185
  30.3 0.1 fusion.12
  30.4 1.4 %broadcast_select_fusion = (bf16[2048,128]{1,0:T(8,128)(2,1)S(1)}, bf16[2048,128]{1,0:T(8,128)(2,1)S(1)}) fusion(pred[]{:T(512)S(6)} %eq.49, bf16[2064,128]{1,0:T(8,128)(2,1)} %collective-permute-done, f32[2048]{0:T(1024)S(1)} %sqrt.20, f32[8,32,8,128]{3,2,1,0:T(8,128)S(1)} %copy_convert_fusion), kind=kLoop, calls=%fused_computation.27 | loop fusion | flops 786432 | bytes 2629633 | tf_op jit(solution)/shard_map/jit(_where)/select_n | solution.py:84
  31.8 0.2 fusion.7
  32.0 1.3 %add_reduce_fusion.2 = f32[32,2048]{1,0:T(8,128)S(1)} fusion(bf16[32,32,128]{2,1,0:T(8,128)(2,1)S(1)} %fusion.7, f32[32,32]{1,0:T(8,128)S(1)} %fusion.12, bf16[2048,128]{1,0:T(8,128)(2,1)S(1)} %get-tuple-element.134), kind=kOutput, calls=%fused_computation.13 | convolution fusion | flops 540999680 | bytes 1052672 | tf_op jit(solution)/shard_map/while/body/eval_jaxpr/trh,ch->trc/dot_general | solution.py:25
  33.3 1.3 %add_reduce_fusion.3 = f32[64,1024]{1,0:T(8,128)S(1)} fusion(f32[32,64]{1,0:T(8,128)S(1)} %fusion.11, bf16[32,64,128]{2,1,0:T(8,128)(2,1)S(1)} %bitcast.113, bf16[1024,128,1]{1,0,2:T(8,128)(2,1)S(1)} %bitcast.116), kind=kOutput, calls=%fused_computation.14 | convolution fusion | flops 540999680 | bytes 1056768 | tf_op jit(solution)/shard_map/while/body/eval_jaxpr/ubh,qh->ubq/dot_general | solution.py:22
  34.6 0.1 broadcast_compare_fusion.1
  34.7 0.2 reshape.189
  34.9 0.2 copy.45
  35.1 0.1 select_reduce_fusion.2
  35.2 0.2 select_reduce_fusion.3
  35.4 0.2 collective-permute-start.1
  35.6 7.4 %collective-permute-done.2 = bf16[2064,128]{1,0:T(8,128)(2,1)S(1)} collective-permute-done((bf16[2064,128]{1,0:T(8,128)(2,1)S(1)}, bf16[2064,128]{1,0:T(8,128)(2,1)S(1)}, u32[]{:S(2)}, u32[]{:S(2)}) %collective-permute-start.2) | collective-permute-done | bytes 528416 | tf_op jit(solution)/shard_map/ppermute | solution.py:74
  43.0 0.1 reshape.195
  43.1 0.1 eq.61
  43.2 6.8 %while.2 = (s32[]{:T(128)}, f32[2,32,64]{2,1,0:T(8,128)S(1)}, pred[2,32,32]{2,1,0:T(8,128)(4,1)S(1)}, bf16[2,32,32,128]{3,2,0,1:T(8,128)(2,1)S(1)}, bf16[32,64,1...) while((s32[]{:T(128)}, f32[2,32,64]{2,1,0:T(8,128)S(1)}, ...), condition=%wide.region_10.11_spmd, body=%wide.region_5.10_spmd.sunk | while | flops 1082261504 | bytes 4285565 | solution.py:30
  43.3 1.3 %add_reduce_fusion.6 = f32[32,2048]{1,0:T(8,128)S(1)} fusion(f32[32,32]{1,0:T(8,128)S(1)} %bitcast.114, bf16[2048,128]{1,0:T(8,128)(2,1)S(1)} %get-tuple-element.221, bf16[1,32,32,128]{3,2,0,1:T(8,128)(2,1)S(1)} %constant_dynamic-slice_fusion.5), kind=kOutput, calls=%fused_computation.1.clone.1 | convolution fusion | flops 540999680 | bytes 1052672 | tf_op jit(solution)/shard_map/while/body/eval_jaxpr/trh,ch->trc/dot_general | solution.py:25
  44.6 0.2 reshape.220
  44.8 0.1 select_reduce_fusion.6
  44.9 1.3 %add_reduce_fusion.7 = f32[1024,64]{0,1:T(8,128)S(1)} fusion(f32[32,64]{1,0:T(8,128)S(1)} %bitcast.126, bf16[1024,128,1]{1,0,2:T(8,128)(2,1)S(1)} %bitcast.106, bf16[32,64,128]{2,1,0:T(8,128)(2,1)S(1)} %bitcast.111), kind=kOutput, calls=%fused_computation.2.clone.1 | convolution fusion | flops 540999680 | bytes 1056768 | tf_op jit(solution)/shard_map/while/body/eval_jaxpr/ubh,qh->ubq/dot_general | solution.py:22
  46.2 0.2 copy.62
  46.4 0.2 select_reduce_fusion.7
  46.7 1.3 %add_reduce_fusion.6 = f32[32,2048]{1,0:T(8,128)S(1)} fusion(f32[32,32]{1,0:T(8,128)S(1)} %bitcast.114, bf16[2048,128]{1,0:T(8,128)(2,1)S(1)} %get-tuple-element.221, bf16[1,32,32,128]{3,2,0,1:T(8,128)(2,1)S(1)} %constant_dynamic-slice_fusion.5), kind=kOutput, calls=%fused_computation.1.clone.1 | convolution fusion | flops 540999680 | bytes 1052672 | tf_op jit(solution)/shard_map/while/body/eval_jaxpr/trh,ch->trc/dot_general | solution.py:25
  48.0 0.2 reshape.220
  48.2 0.1 select_reduce_fusion.6
  48.3 1.3 %add_reduce_fusion.7 = f32[1024,64]{0,1:T(8,128)S(1)} fusion(f32[32,64]{1,0:T(8,128)S(1)} %bitcast.126, bf16[1024,128,1]{1,0,2:T(8,128)(2,1)S(1)} %bitcast.106, bf16[32,64,128]{2,1,0:T(8,128)(2,1)S(1)} %bitcast.111), kind=kOutput, calls=%fused_computation.2.clone.1 | convolution fusion | flops 540999680 | bytes 1056768 | tf_op jit(solution)/shard_map/while/body/eval_jaxpr/ubh,qh->ubq/dot_general | solution.py:22
  49.5 0.2 copy.62
  49.8 0.2 select_reduce_fusion.7
  50.0 0.1 copy.51
  50.1 0.0 collective-permute-start.3
  50.1 0.0 collective-permute-done.1
  50.1 0.1 copy.46
  50.3 0.3 dynamic_update_slice.17
  50.6 0.0 copy-start.1
  50.6 3.4 %collective-permute-done.3 = f32[64,64]{1,0:T(8,128)S(1)} collective-permute-done((f32[64,64]{1,0:T(8,128)S(1)}, f32[64,64]{1,0:T(8,128)S(1)}, u32[]{:S(2)}, u32[]{:S(2)}) %collective-permute-start.3) | collective-permute-done | bytes 16416 | tf_op jit(solution)/shard_map/ppermute | solution.py:97
  54.0 1.6 %dynamic_update_slice.18 = f32[64,192]{1,0:T(8,128)} dynamic-update-slice(f32[64,192]{1,0:T(8,128)} %copy-done.1, f32[64,64]{1,0:T(8,128)S(1)} %collective-permute-done.3, s32[]{:T(128)} %constant.28.clone.1, s32[]{:T(128)S(6)} %select_n.123) | dynamic-update-slice | bytes 32772 | tf_op jit(solution)/shard_map/dynamic_update_slice | solution.py:104
  (26 shorter events, 0.3 us)
Async XLA Ops:
  0.0 1.1 %copy-start = (bf16[256,8,128]{2,1,0:T(8,128)(2,1)S(1)}, bf16[256,8,128]{2,1,0:T(8,128)(2,1)}, u32[]{:S(2)}) copy-start(bf16[256,8,128]{2,1,0:T(8,128)(2,1)} %param.6) | copy-start | bytes 1572868
  1.9 8.2 %copy-start.2 = (s32[64,32]{0,1:T(8,128)S(1)}, s32[64,32]{0,1:T(8,128)}, u32[]{:S(2)}) copy-start(s32[64,32]{0,1:T(8,128)} %param.9) | copy-start | bytes 24580
  1.9 8.2 %copy-start.3 = (s32[64]{0:T(128)S(1)}, s32[64]{0:T(128)}, u32[]{:S(2)}) copy-start(s32[64]{0:T(128)} %param.8) | copy-start | bytes 772
  2.8 23.7 %all-to-all-start = ((bf16[8,32,8,128]{3,2,0,1:T(8,128)(2,1)}), bf16[8,32,8,128]{3,2,0,1:T(8,128)(2,1)S(1)}, u32[]{:S(2)}, u32[]{:S(2)}) async-start(bf16[8,32,8,128]{3,2,0,1:T(8,128)(2,1)} %copy.43), calls=%async_computation | async-start | bytes 1048576 | tf_op jit(solution)/shard_map/all_to_all | solution.py:51
  27.4 2.1 %collective-permute-start = (bf16[2064,128]{1,0:T(8,128)(2,1)S(1)}, bf16[2064,128]{1,0:T(8,128)(2,1)}, u32[]{:S(2)}, u32[]{:S(2)}) collective-permute-start(bf16[2064,128]{1,0:T(8,128)(2,1)S(1)} %pad_maximum_fusion), channel_id=1, source_target_pairs={{0,1},{1,0},{2,3},{3,2},{4,5},{5,4},{6,7},{7,6},{8,9},{9,8},{10,11... | collective-permute-start | bytes 1585160 | tf_op jit(solution)/shard_map/ppermute | solution.py:75
  28.0 15.1 %collective-permute-start.2 = (bf16[2064,128]{1,0:T(8,128)(2,1)S(1)}, bf16[2064,128]{1,0:T(8,128)(2,1)S(1)}, u32[]{:S(2)}, u32[]{:S(2)}) collective-permute-start(bf16[2064,128]{1,0:T(8,128)(2,1)S(1)} %pad_maximum_fusion), channel_id=1, source_target_pairs={{0,2},{1,5},{2,6},{3,1},{4,0},{5,7},{6,4},{7,3},{8,10},{9,13},{10,... | collective-permute-start | bytes 1585160 | tf_op jit(solution)/shard_map/ppermute | solution.py:74
  35.4 14.7 %collective-permute-start.1 = (f32[32,64]{1,0:T(8,128)S(1)}, f32[32,64]{1,0:T(8,128)S(1)}, u32[]{:S(2)}, u32[]{:S(2)}) collective-permute-start(f32[32,64]{1,0:T(8,128)S(1)} %fusion.8), channel_id=1, source_target_pairs={{0,1},{1,0},{2,3},{3,2},{4,5},{5,4},{6,7},{7,6},{8,9},{9,8},{10,11... | collective-permute-start | bytes 24584 | tf_op jit(solution)/shard_map/ppermute | solution.py:87
  50.1 3.9 %collective-permute-start.3 = (f32[64,64]{1,0:T(8,128)S(1)}, f32[64,64]{1,0:T(8,128)S(1)}, u32[]{:S(2)}, u32[]{:S(2)}) collective-permute-start(f32[64,64]{1,0:T(8,128)S(1)} %bitcast.125), channel_id=1, source_target_pairs={{2,0},{5,1},{6,2},{1,3},{0,4},{7,5},{4,6},{3,7},{10,8},{13,9},{14,... | collective-permute-start | bytes 49160 | tf_op jit(solution)/shard_map/ppermute | solution.py:97
  50.6 3.5 %copy-start.1 = (f32[64,192]{1,0:T(8,128)}, f32[64,192]{1,0:T(8,128)S(1)}, u32[]{:S(2)}) copy-start(f32[64,192]{1,0:T(8,128)S(1)} %dynamic_update_slice.17) | copy-start | bytes 147460

commit v12 on v7

--- a/solution.py
+++ b/solution.py
@@ -2,6 +2,19 @@
 import jax.numpy as jnp
 from jax import lax
 from jax.sharding import PartitionSpec as P
+
+
+def lane_group_sum(x, group):
+    n = x.shape[1]
+    if 128 % group or n % 128:
+        return x.reshape(x.shape[0], n // group, group).sum(axis=1)
+    partial = x[:, :128]
+    for k in range(1, n // 128):
+        partial = partial + x[:, k * 128:(k + 1) * 128]
+    total = partial[:, :group]
+    for g in range(1, 128 // group):
+        total = total + partial[:, g * group:(g + 1) * group]
+    return total
 
 
 def tile_scores(query, query_bias, other, other_bias):
@@ -20,11 +33,11 @@
         turned, adding, kept = operands
         flat = turned.reshape(tok * rows, width)
         dots_fore = jnp.einsum("ubh,qh->ubq", other, flat, preferred_element_type=jnp.float32)
-        fore = jnp.max(dots_fore + other_add, axis=0).reshape(other_items, tok, rows)
-        fore = jnp.sum(jnp.where(kept[None], fore, 0.0), axis=1)
+        fore = jnp.max(dots_fore + other_add, axis=0)
+        fore = lane_group_sum(jnp.where(kept.reshape(1, tok * rows), fore, 0.0), rows)
         dots_back = jnp.einsum("trh,ch->trc", turned, other_flat, preferred_element_type=jnp.float32)
-        back = jnp.max(dots_back + adding, axis=0).reshape(rows, tok, other_items)
-        back = jnp.sum(jnp.where(other_valid[None], back, 0.0), axis=1)
+        back = jnp.max(dots_back + adding, axis=0)
+        back = lane_group_sum(jnp.where(other_valid.reshape(1, -1), back, 0.0), other_items)
         return 0.5 * (fore.T + back)
 
     result = lax.map(one_block, (turned_all, adding_all, kept_all))

time: 55 us -> 61.9 us (1.13)
  matrix products: 7.59 us -> 12.8 us
  waiting for transfers between devices: 28.4 us -> 25.1 us
  local copies, waits for them, and re-layouts: 5.7 us -> 8.93 us
  other arithmetic: 4.81 us -> 6.33 us
    ppermute x1, waiting for transfers between devices: 7.28 us -> 4.06 us  [shards(): z_recv = lax.ppermute(packed, 'pool', send_pairs)]
    dot_general x3, matrix products: 3.8 us -> 6.87 us  [one_block(): jnp.einsum('ubh,qh->ubq', other, flat, preferred_element_type=jnp.float32)]
    dot_general x3, matrix products: 3.79 us -> 5.91 us  [one_block(): jnp.einsum('trh,ch->trc', turned, other_flat, preferred_element_type=jnp....]
    unnamed x6 -> x14, local copies, waits for them, and re-layouts: 0.04 us -> 1.44 us
    select_n x0 -> x6, other arithmetic: none -> 1.09 us  [the longest x3 1.02 us: one_block(): jnp.where(other_valid.reshape(1, -1), back, 0.0)]
    reduce_sum x6 -> x0, other arithmetic: 0.87 us -> none  [the longest x3 0.61 us: one_block(): fore = jnp.sum(jnp.where(kept[None], fore, 0.0), axis=1)]
    slice x1, local copies, waits for them, and re-layouts: 0.03 us -> 0.83 us  [unpack(): received[:n_tok].reshape(tok, items_dev, width)]
    concatenate x1, other arithmetic: 0.04 us -> 0.82 us  [shards(): jnp.concatenate([normed.reshape(n_tok, width), bias.reshape(-1, width)],...]
  transfers between devices with their start and end apart: 5 -> 5, of which waited for: 4 -> 4; matrix products, arithmetic and copies ran while one was open for 25% -> 35% of each run, Pallas kernels for 0% -> 0%
where the time goes in v12:
time: 61.9 us; the launch traced here: 61.3 us
  waiting for transfers between devices  25.1 us (41%)
  matrix products  12.8 us (21%)
  local copies, waits for them, and re-layouts  8.93 us (14%)
  starting transfers between devices  7.6 us (12%)
  other arithmetic  6.33 us (10%)
    all_to_all x1, waiting for transfers between devices, shards(): lax.all_to_all(outgoing, ('enc', 'pool'), split_axis=1, concat_axis=1, ti...  16.1 us
    all_to_all x1, starting transfers between devices, shards(): lax.all_to_all(outgoing, ('enc', 'pool'), split_axis=1, concat_axis=1, ti...  7.3 us
    dot_general x3, matrix products, one_block(): jnp.einsum('ubh,qh->ubq', other, flat, preferred_element_type=jnp.float32)  6.87 us
    dot_general x3, matrix products, one_block(): jnp.einsum('trh,ch->trc', turned, other_flat, preferred_element_type=jnp....  5.91 us
    ppermute x1, waiting for transfers between devices, shards(): z_recv = lax.ppermute(packed, 'pool', send_pairs)  4.06 us
    ppermute x1, waiting for transfers between devices, shards(): tile_back = lax.ppermute(tile_z.T, 'pool', back_pairs)  3.63 us
    unnamed x14, local copies, waits for them, and re-layouts  1.44 us
    select_n x1, other arithmetic, shards(): other = jnp.where(is_a, c_blk, block)  1.4 us
  transfers between devices with their start and end apart: 5, of which 4 were waited for; matrix products, arithmetic and copies ran while one was open for 35% of the time, Pallas kernels for 0%

profile of v12, /device:TPU:0, one launch (start us, length us, event | category | flops | bytes accessed | tf_op | source)
XLA Modules:
  0.0 61.3 jit_solution(2600473987399819095)
XLA Ops:
  0.0 0.8 %reshape.190 = s32[32,8,8]{2,1,0:T(8,128)S(1)} reshape(s32[2048]{0:T(1024)} %param.7) | data formatting | bytes 16384 | tf_op jit(solution)/shard_map/reshape | solution.py:60
  0.9 0.1 subtract_reduce_fusion
  0.9 0.1 reshape.205
  1.1 0.8 %gather_fusion = bf16[256,8,128]{2,1,0:T(8,128)(2,1)S(1)} fusion(bf16[256,8,128]{2,1,0:T(8,128)(2,1)S(1)} %copy-done, s32[1024]{0:T(1024)S(1)} %pad_clamp_fusion), kind=kCustom, calls=%fused_computation | custom fusion | bytes 1049600 | tf_op jit(solution)/shard_map/jit(_take)/gather | solution.py:62
  1.9 0.9 %copy.53 = bf16[8,32,8,128]{3,2,0,1:T(8,128)(2,1)} copy(bf16[8,32,8,128]{3,0,2,1:T(8,128)(2,1)S(1)} %bitcast.111) | data formatting | bytes 1048576 | tf_op jit(solution)/shard_map/transpose | solution.py:63
  2.8 7.3 %all-to-all-start = ((bf16[8,32,8,128]{3,2,0,1:T(8,128)(2,1)}), bf16[8,32,8,128]{3,2,0,1:T(8,128)(2,1)S(1)}, u32[]{:S(2)}, u32[]{:S(2)}) async-start(bf16[8,32,8,128]{3,2,0,1:T(8,128)(2,1)} %copy.53), calls=%async_computation | async-start | bytes 1048576 | tf_op jit(solution)/shard_map/all_to_all | solution.py:64
  10.1 0.1 fusion.15
  10.2 0.1 convert_element_type.107
  10.3 16.1 %all-to-all-done = bf16[8,32,8,128]{3,2,0,1:T(8,128)(2,1)S(1)} async-done(((bf16[8,32,8,128]{3,2,0,1:T(8,128)(2,1)}), bf16[8,32,8,128]{3,2,0,1:T(8,128)(2,1)S(1)}, u32[]{:S(2)}, u32[]{:S(2)}) %all-to-all-start) | async-done | bytes 524320 | tf_op jit(solution)/shard_map/all_to_all | solution.py:64
  26.4 0.3 multiply_reduce_fusion
  26.8 0.1 sqrt.20
  27.0 0.1 copy_convert_fusion
  27.0 0.3 fusion.6
  27.4 0.8 %pad_maximum_fusion = bf16[2064,128]{1,0:T(8,128)(2,1)} fusion(bf16[16,128]{1,0:T(8,128)(2,1)S(1)} %convert_element_type.107, bf16[2048,128]{1,0:T(8,128)(2,1)S(1)} %fusion.6), kind=kLoop, calls=%fused_computation.47 | loop fusion | flops 1056768 | bytes 1056768 | tf_op jit(solution)/shard_map/concatenate | solution.py:74
  28.2 0.1 convert_element_type.112
  28.3 0.1 reshape.202
  28.4 0.1 eq.63
  28.5 0.1 sqrt.21
  28.6 0.1 collective-permute-start.2
  28.7 0.1 sqrt.22
  28.8 0.3 fusion.9
  29.2 1.3 %collective-permute-done = bf16[2064,128]{1,0:T(8,128)(2,1)} collective-permute-done((bf16[2064,128]{1,0:T(8,128)(2,1)}, bf16[2064,128]{1,0:T(8,128)(2,1)}, u32[]{:S(2)}, u32[]{:S(2)}) %collective-permute-start) | collective-permute-done | bytes 528416 | tf_op jit(solution)/shard_map/ppermute | solution.py:88
  30.5 0.7 %slice.305 = bf16[16,128]{1,0:T(8,128)(2,1)S(1)} slice(bf16[2064,128]{1,0:T(8,128)(2,1)} %collective-permute-done), slice={[2048:2064], [0:128]} | slice | bytes 8192 | tf_op jit(solution)/shard_map/slice | solution.py:91
  31.1 0.1 reshape.191
  31.2 0.1 broadcast_compare_fusion
  31.3 0.1 fusion.17
  31.4 0.1 broadcast_in_dim.88
  31.5 1.4 %broadcast_select_fusion.2 = (bf16[2048,128]{1,0:T(8,128)(2,1)S(1)}, bf16[2048,128]{1,0:T(8,128)(2,1)S(1)}) fusion(pred[]{:T(512)S(6)} %eq.52, bf16[2064,128]{1,0:T(8,128)(2,1)} %collective-permute-done, f32[2048]{0:T(1024)S(1)} %sqrt.20, f32[8,32,8,128]{3,2,1,0:T(8,128)S(1)} %copy_convert_fusion), kind=kLoop, calls=%fused_computation.54 | loop fusion | flops 786432 | bytes 2629633 | tf_op jit(solution)/shard_map/jit(_where)/select_n | solution.py:97
  32.9 0.2 fusion.10
  33.1 0.6 copy-done.1
  33.7 0.1 copy-done.3
  33.8 1.3 %add_reduce_fusion.2 = f32[32,2048]{1,0:T(8,128)S(1)} fusion(bf16[32,32,128]{2,1,0:T(8,128)(2,1)S(1)} %fusion.10, f32[32,32]{1,0:T(8,128)S(1)} %fusion.17, bf16[2048,128]{1,0:T(8,128)(2,1)S(1)} %get-tuple-element.143), kind=kOutput, calls=%fused_computation.41 | convolution fusion | flops 540999680 | bytes 1052672 | tf_op jit(solution)/shard_map/while/body/eval_jaxpr/trh,ch->trc/dot_general | solution.py:38
  35.1 0.3 copy.55
  35.5 0.7 %copy-done.2 = bf16[2048,128]{1,0:T(8,128)(2,1)S(1)} copy-done((bf16[2048,128]{1,0:T(8,128)(2,1)S(1)}, bf16[2048,128]{1,0:T(8,128)(2,1)}, u32[]{:S(2)}) %copy-start.2) | copy-done | bytes 524312
  36.2 2.2 %add_reduce_fusion.3 = f32[64,1024]{1,0:T(8,128)S(1)} fusion(f32[32,64]{1,0:T(8,128)S(1)} %select_convert_fusion.1, bf16[32,64,128]{2,1,0:T(8,128)(2,1)S(1)} %bitcast.113, bf16[1024,128,1]{1,0,2:T(8,128)(2,1)} %bitcast.116), kind=kOutput, calls=%fused_computation.42 | convolution fusion | flops 540999680 | bytes 1056768 | tf_op jit(solution)/shard_map/while/body/eval_jaxpr/ubh,qh->ubq/dot_general | solution.py:35
  38.4 0.7 %fusion.16 = pred[2048]{0:T(1024)(128)(4,1)S(1)} fusion(bf16[2048]{0:T(1024)(128)(2,1)S(1)} %convert_element_type.112, pred[]{:T(512)S(6)} %eq.52, bf16[2064,128]{1,0:T(8,128)(2,1)} %collective-permute-done), kind=kLoop, calls=%fused_computation.102 | loop fusion | flops 4096 | bytes 10241 | tf_op jit(solution)/shard_map/eq | solution.py:27
  39.1 0.3 broadcast_select_fusion.1
  39.6 0.1 fusion.12
  39.6 0.2 collective-permute-start.1
  39.9 4.1 %collective-permute-done.2 = bf16[2064,128]{1,0:T(8,128)(2,1)S(1)} collective-permute-done((bf16[2064,128]{1,0:T(8,128)(2,1)}, bf16[2064,128]{1,0:T(8,128)(2,1)S(1)}, u32[]{:S(2)}, u32[]{:S(2)}) %collective-permute-start.2) | collective-permute-done | bytes 528416 | tf_op jit(solution)/shard_map/ppermute | solution.py:87
  43.9 0.1 eq.65
  44.0 0.1 broadcast_in_dim.110
  44.1 0.1 reshape.200
  44.2 0.8 %slice.341 = bf16[2048,128]{1,0:T(8,128)(2,1)} slice(bf16[2064,128]{1,0:T(8,128)(2,1)S(1)} %collective-permute-done.2), slice={[0:2048], [0:128]} | slice | bytes 1048576 | tf_op jit(solution)/shard_map/slice | solution.py:91
  45.0 11.6 %while.3 = (s32[]{:T(128)}, f32[2,32,64]{2,1,0:T(8,128)S(1)}, pred[2,32,32]{2,1,0:T(8,128)(4,1)S(1)}, bf16[2,32,32,128]{3,2,0,1:T(8,128)(2,1)S(1)}, bf16[32,64,1...) while((s32[]{:T(128)}, f32[2,32,64]{2,1,0:T(8,128)S(1)}, ...), condition=%wide.wide.region_6.7_spmd, body=%wide.wide.region_3.6_spmd.sunk | while | flops 1082261504 | bytes 4902013 | solution.py:43
  45.0 2.3 %add_reduce_fusion.8 = f32[32,2048]{1,0:T(8,128)S(1)} fusion(f32[32,32]{1,0:T(8,128)S(1)} %bitcast.114, bf16[2048,128]{1,0:T(8,128)(2,1)} %get-tuple-element.276, bf16[1,32,32,128]{3,2,0,1:T(8,128)(2,1)S(1)} %constant_dynamic-slice_fusion.10), kind=kOutput, calls=%fused_computation.1.clone.clone.1 | convolution fusion | flops 540999680 | bytes 1052672 | tf_op jit(solution)/shard_map/while/body/eval_jaxpr/trh,ch->trc/dot_general | solution.py:38
  47.4 0.3 copy.81
  47.7 0.3 broadcast_select_fusion.8
  48.1 2.3 %add_reduce_fusion.9 = f32[1024,64]{0,1:T(8,128)S(1)} fusion(f32[32,64]{1,0:T(8,128)S(1)} %bitcast.124, bf16[1024,128,1]{1,0,2:T(8,128)(2,1)S(1)} %bitcast.110, bf16[32,64,128]{2,1,0:T(8,128)(2,1)} %get-tuple-element.273), kind=kOutput, calls=%fused_computation.2.clone.clone.1 | convolution fusion | flops 540999680 | bytes 1056768 | tf_op jit(solution)/shard_map/while/body/eval_jaxpr/ubh,qh->ubq/dot_general | solution.py:35
  50.5 0.1 broadcast_in_dim.126
  50.6 0.1 fusion.38
  50.7 0.1 copy.82
  50.8 2.3 %add_reduce_fusion.8 = f32[32,2048]{1,0:T(8,128)S(1)} fusion(f32[32,32]{1,0:T(8,128)S(1)} %bitcast.114, bf16[2048,128]{1,0:T(8,128)(2,1)} %get-tuple-element.276, bf16[1,32,32,128]{3,2,0,1:T(8,128)(2,1)S(1)} %constant_dynamic-slice_fusion.10), kind=kOutput, calls=%fused_computation.1.clone.clone.1 | convolution fusion | flops 540999680 | bytes 1052672 | tf_op jit(solution)/shard_map/while/body/eval_jaxpr/trh,ch->trc/dot_general | solution.py:38
  53.2 0.3 copy.81
  53.5 0.3 broadcast_select_fusion.8
  53.9 2.3 %add_reduce_fusion.9 = f32[1024,64]{0,1:T(8,128)S(1)} fusion(f32[32,64]{1,0:T(8,128)S(1)} %bitcast.124, bf16[1024,128,1]{1,0,2:T(8,128)(2,1)S(1)} %bitcast.110, bf16[32,64,128]{2,1,0:T(8,128)(2,1)} %get-tuple-element.273), kind=kOutput, calls=%fused_computation.2.clone.clone.1 | convolution fusion | flops 540999680 | bytes 1056768 | tf_op jit(solution)/shard_map/while/body/eval_jaxpr/ubh,qh->ubq/dot_general | solution.py:35
  56.3 0.1 broadcast_in_dim.126
  56.4 0.1 fusion.38
  56.5 0.1 copy.82
  56.6 0.1 copy.62
  56.7 0.1 maximum_select_fusion
  56.8 0.1 copy.56
  56.9 3.6 %collective-permute-done.3 = f32[64,64]{0,1:T(8,128)S(1)} collective-permute-done((f32[64,64]{0,1:T(8,128)S(1)}, f32[64,64]{0,1:T(8,128)S(1)}, u32[]{:S(2)}, u32[]{:S(2)}) %collective-permute-start.3) | collective-permute-done | bytes 16416 | tf_op jit(solution)/shard_map/ppermute | solution.py:110
  60.6 0.7 %copy.64 = f32[64,192]{1,0:T(8,128)} copy(f32[64,192]{0,1:T(8,128)S(1)} %pad_maximum_fusion.1) | data formatting | bytes 98304 | tf_op jit(solution)/shard_map/concatenate | solution.py:114
  (44 shorter events, 0.7 us)
Async XLA Ops:
  0.0 1.1 %copy-start = (bf16[256,8,128]{2,1,0:T(8,128)(2,1)S(1)}, bf16[256,8,128]{2,1,0:T(8,128)(2,1)}, u32[]{:S(2)}) copy-start(bf16[256,8,128]{2,1,0:T(8,128)(2,1)} %param.6) | copy-start | bytes 1572868
  1.9 8.2 %copy-start.5 = (s32[64,32]{0,1:T(8,128)S(1)}, s32[64,32]{0,1:T(8,128)}, u32[]{:S(2)}) copy-start(s32[64,32]{0,1:T(8,128)} %param.9) | copy-start | bytes 24580
  1.9 8.2 %copy-start.6 = (s32[64]{0:T(128)S(1)}, s32[64]{0:T(128)}, u32[]{:S(2)}) copy-start(s32[64]{0:T(128)} %param.8) | copy-start | bytes 772
  2.8 23.7 %all-to-all-start = ((bf16[8,32,8,128]{3,2,0,1:T(8,128)(2,1)}), bf16[8,32,8,128]{3,2,0,1:T(8,128)(2,1)S(1)}, u32[]{:S(2)}, u32[]{:S(2)}) async-start(bf16[8,32,8,128]{3,2,0,1:T(8,128)(2,1)} %copy.53), calls=%async_computation | async-start | bytes 1048576 | tf_op jit(solution)/shard_map/all_to_all | solution.py:64
  28.2 2.3 %collective-permute-start = (bf16[2064,128]{1,0:T(8,128)(2,1)}, bf16[2064,128]{1,0:T(8,128)(2,1)}, u32[]{:S(2)}, u32[]{:S(2)}) collective-permute-start(bf16[2064,128]{1,0:T(8,128)(2,1)} %pad_maximum_fusion), channel_id=1, source_target_pairs={{0,1},{1,0},{2,3},{3,2},{4,5},{5,4},{6,7},{7,6},{8,9},{9,8},{10,11... | collective-permute-start | bytes 1585160 | tf_op jit(solution)/shard_map/ppermute | solution.py:88
  28.6 15.3 %collective-permute-start.2 = (bf16[2064,128]{1,0:T(8,128)(2,1)}, bf16[2064,128]{1,0:T(8,128)(2,1)S(1)}, u32[]{:S(2)}, u32[]{:S(2)}) collective-permute-start(bf16[2064,128]{1,0:T(8,128)(2,1)} %pad_maximum_fusion), channel_id=1, source_target_pairs={{0,2},{1,5},{2,6},{3,1},{4,0},{5,7},{6,4},{7,3},{8,10},{9,13},{10,... | collective-permute-start | bytes 1585160 | tf_op jit(solution)/shard_map/ppermute | solution.py:87
  32.9 0.8 %copy-start.1 = (bf16[2048,128]{1,0:T(8,128)(2,1)}, bf16[2048,128]{1,0:T(8,128)(2,1)S(1)}, u32[]{:S(2)}) copy-start(bf16[2048,128]{1,0:T(8,128)(2,1)S(1)} %get-tuple-element.143) | copy-start | bytes 1572868
  33.1 0.7 %copy-start.3 = (bf16[32,32,128]{2,1,0:T(8,128)(2,1)}, bf16[32,32,128]{2,1,0:T(8,128)(2,1)S(1)}, u32[]{:S(2)}) copy-start(bf16[32,32,128]{2,1,0:T(8,128)(2,1)S(1)} %fusion.10) | copy-start | bytes 786436
  35.1 1.0 %copy-start.2 = (bf16[2048,128]{1,0:T(8,128)(2,1)S(1)}, bf16[2048,128]{1,0:T(8,128)(2,1)}, u32[]{:S(2)}) copy-start(bf16[2048,128]{1,0:T(8,128)(2,1)} %copy-done.1) | copy-start | bytes 1572868
  39.6 17.1 %collective-permute-start.1 = (f32[32,64]{0,1:T(8,128)S(1)}, f32[32,64]{0,1:T(8,128)S(1)}, u32[]{:S(2)}, u32[]{:S(2)}) collective-permute-start(f32[32,64]{0,1:T(8,128)S(1)} %fusion.12), channel_id=1, source_target_pairs={{0,1},{1,0},{2,3},{3,2},{4,5},{5,4},{6,7},{7,6},{8,9},{9,8},{10,11... | collective-permute-start | bytes 24584 | tf_op jit(solution)/shard_map/ppermute | solution.py:100
  44.0 1.0 %copy-start.4 = (pred[32,64]{1,0:T(8,128)(4,1)}, pred[32,64]{1,0:T(8,128)(4,1)S(1)}, u32[]{:S(2)}) copy-start(pred[32,64]{1,0:T(8,128)(4,1)S(1)} %eq.65) | copy-start | bytes 6148
  56.6 3.9 %collective-permute-start.3 = (f32[64,64]{0,1:T(8,128)S(1)}, f32[64,64]{0,1:T(8,128)S(1)}, u32[]{:S(2)}, u32[]{:S(2)}) collective-permute-start(f32[64,64]{0,1:T(8,128)S(1)} %bitcast.122), channel_id=1, source_target_pairs={{2,0},{5,1},{6,2},{1,3},{0,4},{7,5},{4,6},{3,7},{10,8},{13,9},{14,... | collective-permute-start | bytes 49160 | tf_op jit(solution)/shard_map/ppermute | solution.py:110

commit v13 on v7

--- a/solution.py
+++ b/solution.py
@@ -95,10 +95,11 @@
     z_blk, z_bias = unpack(z_recv)
     tile_z = tile_scores(block, bias, z_blk, z_bias)
     tile_back = lax.ppermute(tile_z.T, "pool", back_pairs)
-    via_bit1 = parity == 1
-    col1 = jnp.where(via_bit1, tile_z, tile_back)
-    col2 = jnp.where(via_bit1, tile_back, tile_z)
-    return jnp.concatenate([tile0, col1, col2], axis=1)
+    other_items = tile_z.shape[1]
+    ready = lax.optimization_barrier(jnp.concatenate([tile0, tile_z, tile_z], axis=1))
+    column = jnp.arange(3 * other_items, dtype=jnp.int32)[None, :] // other_items
+    back_here = column == 1 + parity
+    return jnp.where(back_here, jnp.tile(tile_back, (1, 3)), ready)
 
 
 def solution(mesh):

time: 55 us -> 54.8 us (level)
    concatenate x1, other arithmetic: 0.72 us -> 0.08 us  [shards(): jnp.concatenate([tile0, tile_z, tile_z], axis=1)]
    select_n x1, other arithmetic: 0.01 us -> 0.64 us  [shards(): return jnp.where(back_here, jnp.tile(tile_back, (1, 3)), ready)]
where the time goes in v13:
time: 54.8 us; the launch traced here: 54.5 us
  waiting for transfers between devices  28.2 us (51%)
  starting transfers between devices  7.69 us (14%)
  matrix products  7.58 us (14%)
  local copies, waits for them, and re-layouts  5.71 us (10%)
  other arithmetic  4.8 us (9%)
    all_to_all x1, waiting for transfers between devices, shards(): lax.all_to_all(outgoing, ('enc', 'pool'), split_axis=1, concat_axis=1, ti...  16 us
    all_to_all x1, starting transfers between devices, shards(): lax.all_to_all(outgoing, ('enc', 'pool'), split_axis=1, concat_axis=1, ti...  7.3 us
    ppermute x1, waiting for transfers between devices, shards(): z_recv = lax.ppermute(packed, 'pool', send_pairs)  7.19 us
    dot_general x3, matrix products, one_block(): jnp.einsum('ubh,qh->ubq', other, flat, preferred_element_type=jnp.float32)  3.79 us
    dot_general x3, matrix products, one_block(): jnp.einsum('trh,ch->trc', turned, other_flat, preferred_element_type=jnp....  3.79 us
    ppermute x1, waiting for transfers between devices, shards(): tile_back = lax.ppermute(tile_z.T, 'pool', back_pairs)  3.69 us
    select_n x1, other arithmetic, shards(): other = jnp.where(is_a, c_blk, block)  1.4 us
    ppermute x1, waiting for transfers between devices, shards(): c_recv = lax.ppermute(packed, 'pool', chip_pairs)  1.27 us
  transfers between devices with their start and end apart: 5, of which 4 were waited for; matrix products, arithmetic and copies ran while one was open for 25% of the time, Pallas kernels for 0%

profile of v13, /device:TPU:0, one launch (start us, length us, event | category | flops | bytes accessed | tf_op | source)
XLA Modules:
  0.0 54.5 jit_solution(16466838070889059354)
XLA Ops:
  0.0 0.0 copy-start
  0.0 0.8 %reshape.227 = s32[32,8,8]{2,1,0:T(8,128)S(1)} reshape(s32[2048]{0:T(1024)} %param.7) | data formatting | bytes 16384 | tf_op jit(solution)/shard_map/reshape | solution.py:47
  0.9 0.1 subtract_reduce_fusion
  0.9 0.1 reshape.243
  1.0 0.0 copy-done
  1.1 0.8 %gather_fusion = bf16[256,8,128]{2,1,0:T(8,128)(2,1)S(1)} fusion(bf16[256,8,128]{2,1,0:T(8,128)(2,1)S(1)} %copy-done, s32[1024]{0:T(1024)S(1)} %pad_clamp_fusion), kind=kCustom, calls=%fused_computation | custom fusion | bytes 1049600 | tf_op jit(solution)/shard_map/jit(_take)/gather | solution.py:49
  1.9 0.0 copy-start.1
  1.9 0.0 copy-start.2
  1.9 0.9 %copy.53 = bf16[8,32,8,128]{3,2,0,1:T(8,128)(2,1)} copy(bf16[8,32,8,128]{3,0,2,1:T(8,128)(2,1)S(1)} %bitcast.110) | data formatting | bytes 1048576 | tf_op jit(solution)/shard_map/transpose | solution.py:50
  2.8 7.3 %all-to-all-start = ((bf16[8,32,8,128]{3,2,0,1:T(8,128)(2,1)}), bf16[8,32,8,128]{3,2,0,1:T(8,128)(2,1)S(1)}, u32[]{:S(2)}, u32[]{:S(2)}) async-start(bf16[8,32,8,128]{3,2,0,1:T(8,128)(2,1)} %copy.53), calls=%async_computation | async-start | bytes 1048576 | tf_op jit(solution)/shard_map/all_to_all | solution.py:51
  10.1 0.0 copy-done.1
  10.1 0.0 copy-done.2
  10.1 0.1 fusion.10
  10.2 0.1 convert_element_type.104
  10.3 0.1 reshape.240
  10.4 16.0 %all-to-all-done = bf16[8,32,8,128]{3,2,0,1:T(8,128)(2,1)S(1)} async-done(((bf16[8,32,8,128]{3,2,0,1:T(8,128)(2,1)}), bf16[8,32,8,128]{3,2,0,1:T(8,128)(2,1)S(1)}, u32[]{:S(2)}, u32[]{:S(2)}) %all-to-all-start) | async-done | bytes 524320 | tf_op jit(solution)/shard_map/all_to_all | solution.py:51
  26.4 0.3 multiply_reduce_fusion
  26.8 0.1 sqrt.21
  27.0 0.1 copy_convert_fusion
  27.0 0.3 fusion.3
  27.4 0.1 collective-permute-start.2
  27.5 0.1 eq.68
  27.6 0.1 sqrt.22
  27.7 0.1 collective-permute-start
  27.8 0.1 sqrt.20
  27.9 0.3 fusion.6
  28.3 1.3 %collective-permute-done.2 = bf16[2064,128]{1,0:T(8,128)(2,1)} collective-permute-done((bf16[2064,128]{1,0:T(8,128)(2,1)S(1)}, bf16[2064,128]{1,0:T(8,128)(2,1)}, u32[]{:S(2)}, u32[]{:S(2)}) %collective-permute-start.2) | collective-permute-done | bytes 528416 | tf_op jit(solution)/shard_map/ppermute | solution.py:75
  29.5 0.7 %slice.37 = bf16[16,128]{1,0:T(8,128)(2,1)S(1)} slice(bf16[2064,128]{1,0:T(8,128)(2,1)} %collective-permute-done.2), slice={[2048:2064], [0:128]} | slice | bytes 8192 | tf_op jit(solution)/shard_map/slice | solution.py:78
  30.2 0.1 reshape.230
  30.3 0.1 broadcast_compare_fusion.1
  30.4 0.1 fusion.13
  30.5 1.4 %broadcast_select_fusion = (bf16[2048,128]{1,0:T(8,128)(2,1)S(1)}, bf16[2048,128]{1,0:T(8,128)(2,1)S(1)}) fusion(pred[]{:T(512)S(6)} %eq.71, bf16[2064,128]{1,0:T(8,128)(2,1)} %collective-permute-done.2, f32[2048]{0:T(1024)S(1)} %sqrt.21, f32[8,32,8,128]{3,2,1,0:T(8,128)S(1)} %copy_convert_fusion), kind=kLoop, calls=%fused_computation.27 | loop fusion | flops 786432 | bytes 2629633 | tf_op jit(solution)/shard_map/jit(_where)/select_n | solution.py:84
  31.9 0.2 fusion.7
  32.1 1.3 %add_reduce_fusion.2 = f32[32,2048]{1,0:T(8,128)S(1)} fusion(bf16[32,32,128]{2,1,0:T(8,128)(2,1)S(1)} %fusion.7, f32[32,32]{1,0:T(8,128)S(1)} %fusion.13, bf16[2048,128]{1,0:T(8,128)(2,1)S(1)} %get-tuple-element.143), kind=kOutput, calls=%fused_computation.13 | convolution fusion | flops 540999680 | bytes 1052672 | tf_op jit(solution)/shard_map/while/body/eval_jaxpr/trh,ch->trc/dot_general | solution.py:25
  33.4 1.3 %add_reduce_fusion.3 = f32[64,1024]{1,0:T(8,128)S(1)} fusion(f32[32,64]{1,0:T(8,128)S(1)} %fusion.11, bf16[32,64,128]{2,1,0:T(8,128)(2,1)S(1)} %bitcast.115, bf16[1024,128,1]{1,0,2:T(8,128)(2,1)S(1)} %bitcast.119), kind=kOutput, calls=%fused_computation.14 | convolution fusion | flops 540999680 | bytes 1056768 | tf_op jit(solution)/shard_map/while/body/eval_jaxpr/ubh,qh->ubq/dot_general | solution.py:22
  34.7 0.2 copy.59
  34.9 0.2 reshape.234
  35.1 0.1 select_reduce_fusion.2
  35.2 0.2 select_reduce_fusion.3
  35.4 0.2 collective-permute-start.3
  35.6 7.2 %collective-permute-done = bf16[2064,128]{1,0:T(8,128)(2,1)S(1)} collective-permute-done((bf16[2064,128]{1,0:T(8,128)(2,1)S(1)}, bf16[2064,128]{1,0:T(8,128)(2,1)S(1)}, u32[]{:S(2)}, u32[]{:S(2)}) %collective-permute-start) | collective-permute-done | bytes 528416 | tf_op jit(solution)/shard_map/ppermute | solution.py:74
  42.8 0.1 reshape.237
  42.9 0.1 eq.70
  43.0 6.7 %while.2 = (s32[]{:T(128)}, f32[2,32,64]{2,1,0:T(8,128)S(1)}, pred[2,32,32]{2,1,0:T(8,128)(4,1)S(1)}, bf16[2,32,32,128]{3,2,0,1:T(8,128)(2,1)S(1)}, bf16[32,64,1...) while((s32[]{:T(128)}, f32[2,32,64]{2,1,0:T(8,128)S(1)}, ...), condition=%wide.region_6.7_spmd, body=%wide.region_1.6_spmd.sunk | while | flops 1082261504 | bytes 4285557 | solution.py:30
  43.1 1.3 %add_reduce_fusion.6 = f32[32,2048]{1,0:T(8,128)S(1)} fusion(f32[32,32]{1,0:T(8,128)S(1)} %bitcast.116, bf16[2048,128]{1,0:T(8,128)(2,1)S(1)} %get-tuple-element.230, bf16[1,32,32,128]{3,2,0,1:T(8,128)(2,1)S(1)} %constant_dynamic-slice_fusion.5), kind=kOutput, calls=%fused_computation.1.clone.1 | convolution fusion | flops 540999680 | bytes 1052672 | tf_op jit(solution)/shard_map/while/body/eval_jaxpr/trh,ch->trc/dot_general | solution.py:25
  44.4 0.2 reshape.263
  44.6 0.1 select_reduce_fusion.6
  44.7 1.3 %add_reduce_fusion.7 = f32[1024,64]{0,1:T(8,128)S(1)} fusion(f32[32,64]{1,0:T(8,128)S(1)} %bitcast.128, bf16[1024,128,1]{1,0,2:T(8,128)(2,1)S(1)} %bitcast.108, bf16[32,64,128]{2,1,0:T(8,128)(2,1)S(1)} %bitcast.113), kind=kOutput, calls=%fused_computation.2.clone.1 | convolution fusion | flops 540999680 | bytes 1056768 | tf_op jit(solution)/shard_map/while/body/eval_jaxpr/ubh,qh->ubq/dot_general | solution.py:22
  46.0 0.2 copy.72
  46.2 0.2 select_reduce_fusion.7
  46.5 1.3 %add_reduce_fusion.6 = f32[32,2048]{1,0:T(8,128)S(1)} fusion(f32[32,32]{1,0:T(8,128)S(1)} %bitcast.116, bf16[2048,128]{1,0:T(8,128)(2,1)S(1)} %get-tuple-element.230, bf16[1,32,32,128]{3,2,0,1:T(8,128)(2,1)S(1)} %constant_dynamic-slice_fusion.5), kind=kOutput, calls=%fused_computation.1.clone.1 | convolution fusion | flops 540999680 | bytes 1052672 | tf_op jit(solution)/shard_map/while/body/eval_jaxpr/trh,ch->trc/dot_general | solution.py:25
  47.7 0.2 reshape.263
  48.0 0.1 select_reduce_fusion.6
  48.1 1.3 %add_reduce_fusion.7 = f32[1024,64]{0,1:T(8,128)S(1)} fusion(f32[32,64]{1,0:T(8,128)S(1)} %bitcast.128, bf16[1024,128,1]{1,0,2:T(8,128)(2,1)S(1)} %bitcast.108, bf16[32,64,128]{2,1,0:T(8,128)(2,1)S(1)} %bitcast.113), kind=kOutput, calls=%fused_computation.2.clone.1 | convolution fusion | flops 540999680 | bytes 1056768 | tf_op jit(solution)/shard_map/while/body/eval_jaxpr/ubh,qh->ubq/dot_general | solution.py:22
  49.3 0.2 copy.72
  49.5 0.2 select_reduce_fusion.7
  49.8 0.1 collective-permute-start.1
  49.8 0.0 collective-permute-done.3
  49.9 0.1 copy.60
  50.0 0.1 pad_maximum_fusion.1
  50.1 3.7 %collective-permute-done.1 = f32[64,64]{0,1:T(8,128)S(1)} collective-permute-done((f32[64,64]{0,1:T(8,128)S(1)}, f32[64,64]{0,1:T(8,128)S(1)}, u32[]{:S(2)}, u32[]{:S(2)}) %collective-permute-start.1) | collective-permute-done | bytes 16416 | tf_op jit(solution)/shard_map/ppermute | solution.py:97
  53.8 0.1 copy.61
  53.8 0.6 %broadcast_select_fusion.1 = f32[64,192]{1,0:T(8,128)} fusion(f32[64,192]{1,0:T(8,128)S(1)} %copy.61, f32[64,192]{1,0:T(8,128)S(1)} %pad_maximum_fusion.1, pred[192]{0:T(512)(128)(4,1)S(1)} %fusion.12), kind=kLoop, calls=%fused_computation.33 | loop fusion | flops 12288 | bytes 147648 | tf_op jit(solution)/shard_map/jit(_where)/select_n | solution.py:102
  (26 shorter events, 0.4 us)
Async XLA Ops:
  0.0 1.1 %copy-start = (bf16[256,8,128]{2,1,0:T(8,128)(2,1)S(1)}, bf16[256,8,128]{2,1,0:T(8,128)(2,1)}, u32[]{:S(2)}) copy-start(bf16[256,8,128]{2,1,0:T(8,128)(2,1)} %param.6) | copy-start | bytes 1572868
  1.9 8.2 %copy-start.1 = (s32[64,32]{0,1:T(8,128)S(1)}, s32[64,32]{0,1:T(8,128)}, u32[]{:S(2)}) copy-start(s32[64,32]{0,1:T(8,128)} %param.9) | copy-start | bytes 24580
  1.9 8.2 %copy-start.2 = (s32[64]{0:T(128)S(1)}, s32[64]{0:T(128)}, u32[]{:S(2)}) copy-start(s32[64]{0:T(128)} %param.8) | copy-start | bytes 772
  2.8 23.7 %all-to-all-start = ((bf16[8,32,8,128]{3,2,0,1:T(8,128)(2,1)}), bf16[8,32,8,128]{3,2,0,1:T(8,128)(2,1)S(1)}, u32[]{:S(2)}, u32[]{:S(2)}) async-start(bf16[8,32,8,128]{3,2,0,1:T(8,128)(2,1)} %copy.53), calls=%async_computation | async-start | bytes 1048576 | tf_op jit(solution)/shard_map/all_to_all | solution.py:51
  27.4 2.1 %collective-permute-start.2 = (bf16[2064,128]{1,0:T(8,128)(2,1)S(1)}, bf16[2064,128]{1,0:T(8,128)(2,1)}, u32[]{:S(2)}, u32[]{:S(2)}) collective-permute-start(bf16[2064,128]{1,0:T(8,128)(2,1)S(1)} %pad_maximum_fusion), channel_id=1, source_target_pairs={{0,1},{1,0},{2,3},{3,2},{4,5},{5,4},{6,7},{7,6},{8,9},{9,8},{10,11... | collective-permute-start | bytes 1585160 | tf_op jit(solution)/shard_map/ppermute | solution.py:75
  27.7 15.1 %collective-permute-start = (bf16[2064,128]{1,0:T(8,128)(2,1)S(1)}, bf16[2064,128]{1,0:T(8,128)(2,1)S(1)}, u32[]{:S(2)}, u32[]{:S(2)}) collective-permute-start(bf16[2064,128]{1,0:T(8,128)(2,1)S(1)} %pad_maximum_fusion), channel_id=1, source_target_pairs={{0,2},{1,5},{2,6},{3,1},{4,0},{5,7},{6,4},{7,3},{8,10},{9,13},{10,... | collective-permute-start | bytes 1585160 | tf_op jit(solution)/shard_map/ppermute | solution.py:74
  35.4 14.4 %collective-permute-start.3 = (f32[32,64]{1,0:T(8,128)S(1)}, f32[32,64]{1,0:T(8,128)S(1)}, u32[]{:S(2)}, u32[]{:S(2)}) collective-permute-start(f32[32,64]{1,0:T(8,128)S(1)} %fusion.8), channel_id=1, source_target_pairs={{0,1},{1,0},{2,3},{3,2},{4,5},{5,4},{6,7},{7,6},{8,9},{9,8},{10,11... | collective-permute-start | bytes 24584 | tf_op jit(solution)/shard_map/ppermute | solution.py:87
  49.8 4.0 %collective-permute-start.1 = (f32[64,64]{0,1:T(8,128)S(1)}, f32[64,64]{0,1:T(8,128)S(1)}, u32[]{:S(2)}, u32[]{:S(2)}) collective-permute-start(f32[64,64]{0,1:T(8,128)S(1)} %bitcast.126), channel_id=1, source_target_pairs={{2,0},{5,1},{6,2},{1,3},{0,4},{7,5},{4,6},{3,7},{10,8},{13,9},{14,... | collective-permute-start | bytes 49160 | tf_op jit(solution)/shard_map/ppermute | solution.py:97

commit v14 on v7

--- a/solution.py
+++ b/solution.py
@@ -1,6 +1,10 @@
+import functools
+
 import jax
 import jax.numpy as jnp
 from jax import lax
+from jax.experimental import pallas as pl
+from jax.experimental.pallas import tpu as pltpu
 from jax.sharding import PartitionSpec as P
 
 
@@ -31,6 +35,57 @@
     return result.reshape(query_items, other_items)
 
 
+def _chamfer_kernel(tok, nq, no, cw, q_ref, o_ref, qv_ref, ov_ref, out_ref, fm_ref):
+    q = q_ref[...]
+    acc_b = jnp.zeros((nq, 128), jnp.float32)
+    for c in range(tok * no // cw):
+        o_c = o_ref[c * cw:(c + 1) * cw, :]
+        d = lax.dot_general(q, o_c, (((1,), (1,)), ((), ())), preferred_element_type=jnp.float32)
+        m = d[:, 0:128]
+        for k in range(1, cw // 128):
+            m = jnp.maximum(m, d[:, k * 128:(k + 1) * 128])
+        if c == 0:
+            fm_ref[...] = m
+        else:
+            fm_ref[...] = jnp.maximum(fm_ref[...], m)
+        mb = jnp.max(d.reshape(tok, nq, cw), axis=0)
+        mbm = jnp.where(ov_ref[:, c * cw:(c + 1) * cw] > 0, mb, 0.0)
+        s = mbm[:, 0:128]
+        for k in range(1, cw // 128):
+            s = s + mbm[:, k * 128:(k + 1) * 128]
+        acc_b = acc_b + s
+    fm = fm_ref[...]
+    fm = jnp.maximum(fm, pltpu.roll(fm, 64, 1))
+    fsum = jnp.sum(jnp.where(qv_ref[...] > 0, fm, 0.0).reshape(tok, nq, 128), axis=0)
+    bsum = acc_b + pltpu.roll(acc_b, 64, 1)
+    out_ref[...] = (0.5 * (fsum + bsum))[:, :no]
+
+
+def chamfer_tile(query, query_valid, other, other_valid):
+    tok, nq, width = query.shape
+    no = other.shape[1]
+    if no != 64 or (tok * no) % 512 or nq % 8:
+        return tile_scores(
+            query, jnp.where(query_valid, 0.0, -4.0), other, jnp.where(other_valid, 0.0, -4.0)
+        )
+    tok_nq, tok_no, cw = tok * nq, tok * no, 512
+    q = query.reshape(tok_nq, width)
+    o = other.reshape(tok_no, width)
+    qv = jnp.broadcast_to(query_valid.astype(jnp.float32).reshape(tok_nq, 1), (tok_nq, 128))
+    ov = other_valid.astype(jnp.float32).reshape(1, tok_no)
+    kernel = functools.partial(_chamfer_kernel, tok, nq, no, cw)
+    return pl.pallas_call(
+        kernel,
+        out_shape=jax.ShapeDtypeStruct((nq, no), jnp.float32),
+        in_specs=[pl.BlockSpec(memory_space=pltpu.VMEM)] * 4,
+        out_specs=pl.BlockSpec(memory_space=pltpu.VMEM),
+        scratch_shapes=[pltpu.VMEM((tok_nq, 128), jnp.float32)],
+        cost_estimate=pl.CostEstimate(
+            flops=2 * tok_nq * tok_no * width, transcendentals=0, bytes_accessed=(tok_nq + tok_no) * width * 2
+        ),
+    )(q, o, qv, ov)
+
+
 def shards(encoded, slot_items, lengths, token_mask):
     n_enc = lax.axis_size("enc")
     n_pool = lax.axis_size("pool")
@@ -58,6 +113,7 @@
     valid = (position < lengths[:, None]) & ((position == 0) | (token_mask == 1))
     valid_tm = jnp.transpose(valid.reshape(items_dev, n_enc, toks), (2, 1, 0)).reshape(tok, items_dev)
     bias = jnp.where(valid_tm, 0.0, -4.0).astype(jnp.bfloat16)
+    normed = jnp.where(valid_tm[:, :, None], normed, normed[0][None])
     packed = jnp.concatenate([normed.reshape(n_tok, width), bias.reshape(-1, width)], axis=0)
     block = packed[:n_tok].reshape(tok, items_dev, width)
 
@@ -83,7 +139,7 @@
     query_bias = jnp.where(is_a, bias[:, :half], c_bias[:, half:])
     other = jnp.where(is_a, c_blk, block)
     other_bias = jnp.where(is_a, c_bias, bias)
-    part = tile_scores(query, query_bias, other, other_bias)
+    part = chamfer_tile(query, query_bias == 0, other, other_bias == 0)
     part_recv = lax.ppermute(part, "pool", chip_pairs)
     joined = jnp.where(
         is_a,
@@ -93,7 +149,7 @@
     tile0 = jnp.where(is_a, joined, joined.T)
 
     z_blk, z_bias = unpack(z_recv)
-    tile_z = tile_scores(block, bias, z_blk, z_bias)
+    tile_z = chamfer_tile(block, valid_tm, z_blk, z_bias == 0)
     tile_back = lax.ppermute(tile_z.T, "pool", back_pairs)
     via_bit1 = parity == 1
     col1 = jnp.where(via_bit1, tile_z, tile_back)

time: 55 us -> 57.7 us (1.049)
  Pallas kernels: 0 us -> 7.84 us
  matrix products: 7.59 us -> 0 us
  local copies, waits for them, and re-layouts: 5.7 us -> 8.15 us
  other arithmetic: 4.81 us -> 6.43 us
  waiting for transfers between devices: 28.4 us -> 27 us
    pallas_call x0 -> x2, Pallas kernels: none -> 7.84 us  [chamfer_tile(): pl.pallas_call(kernel, out_shape=jax.ShapeDtypeStruct((nq, no), jnp.float...]
    dot_general x6 -> x0, matrix products: 7.59 us -> none  [the longest x3 3.8 us: one_block(): jnp.einsum('ubh,qh->ubq', other, flat, preferred_element_type=jnp.float32)]
    broadcast_in_dim x3 -> x5, local copies, waits for them, and re-layouts: 0.11 us -> 2.45 us  [the longest x3 2.36 us: chamfer_tile(): jnp.broadcast_to(query_valid.astype(jnp.float32).reshape(tok_nq, 1), (tok...]
    ppermute x1, waiting for transfers between devices: 7.28 us -> 5.46 us  [shards(): z_recv = lax.ppermute(packed, 'pool', send_pairs)]
    pallas_call x0 -> x2, local copies, waits for them, and re-layouts: none -> 1.63 us  [chamfer_tile(): pl.pallas_call(kernel, out_shape=jax.ShapeDtypeStruct((nq, no), jnp.float...]
    convert_element_type x3, other arithmetic: 0.09 us -> 1.21 us  [the longest x2 1.2 us: chamfer_tile(): ov = other_valid.astype(jnp.float32).reshape(1, tok_no)]
    reduce_sum x6 -> x0, other arithmetic: 0.87 us -> none  [the longest x3 0.61 us: one_block(): fore = jnp.sum(jnp.where(kept[None], fore, 0.0), axis=1)]
    select_n x0 -> x1, other arithmetic: none -> 0.8 us  [shards(): normed = jnp.where(valid_tm[:, :, None], normed, normed[0][None])]
  transfers between devices with their start and end apart: 5 -> 5, of which waited for: 4 -> 4; matrix products, arithmetic and copies ran while one was open for 25% -> 15% of each run, Pallas kernels for 0% -> 14%
where the time goes in v14:
time: 57.7 us; the launch traced here: 57.2 us
  waiting for transfers between devices  27 us (47%)
  local copies, waits for them, and re-layouts  8.15 us (14%)
  Pallas kernels  7.84 us (14%)
  starting transfers between devices  7.65 us (13%)
  other arithmetic  6.43 us (11%)
    all_to_all x1, waiting for transfers between devices, shards(): lax.all_to_all(outgoing, ('enc', 'pool'), split_axis=1, concat_axis=1, ti...  16 us
    pallas_call x2, Pallas kernels, chamfer_tile(): pl.pallas_call(kernel, out_shape=jax.ShapeDtypeStruct((nq, no), jnp.float...  7.84 us
    all_to_all x1, starting transfers between devices, shards(): lax.all_to_all(outgoing, ('enc', 'pool'), split_axis=1, concat_axis=1, ti...  7.3 us
    ppermute x1, waiting for transfers between devices, shards(): z_recv = lax.ppermute(packed, 'pool', send_pairs)  5.46 us
    ppermute x1, waiting for transfers between devices, shards(): tile_back = lax.ppermute(tile_z.T, 'pool', back_pairs)  3.71 us
    broadcast_in_dim x3, local copies, waits for them, and re-layouts, chamfer_tile(): jnp.broadcast_to(query_valid.astype(jnp.float32).reshape(tok_nq, 1), (tok...  2.36 us
    ppermute x1, waiting for transfers between devices, shards(): c_recv = lax.ppermute(packed, 'pool', chip_pairs)  1.75 us
    pallas_call x2, local copies, waits for them, and re-layouts, chamfer_tile(): pl.pallas_call(kernel, out_shape=jax.ShapeDtypeStruct((nq, no), jnp.float...  1.63 us
  transfers between devices with their start and end apart: 5, of which 4 were waited for; matrix products, arithmetic and copies ran while one was open for 15% of the time, Pallas kernels for 14%

profile of v14, /device:TPU:0, one launch (start us, length us, event | category | flops | bytes accessed | tf_op | source)
XLA Modules:
  0.0 57.2 jit_solution(5493233181570778562)
XLA Ops:
  0.0 0.0 copy-start
  0.0 0.8 %reshape.141 = s32[32,8,8]{2,1,0:T(8,128)S(1)} reshape(s32[2048]{0:T(1024)} %param.5) | data formatting | bytes 16384 | tf_op jit(solution)/shard_map/reshape | solution.py:102
  0.9 0.1 subtract_reduce_fusion
  0.9 0.1 reshape.152
  1.0 0.0 copy-done
  1.1 0.8 %gather_fusion = bf16[256,8,128]{2,1,0:T(8,128)(2,1)S(1)} fusion(bf16[256,8,128]{2,1,0:T(8,128)(2,1)S(1)} %copy-done, s32[1024]{0:T(1024)S(1)} %pad_clamp_fusion), kind=kCustom, calls=%fused_computation | custom fusion | bytes 1049600 | tf_op jit(solution)/shard_map/jit(_take)/gather | solution.py:104
  1.9 0.0 copy-start.3
  1.9 0.0 copy-start.4
  1.9 0.9 %copy.30 = bf16[8,32,8,128]{3,2,0,1:T(8,128)(2,1)} copy(bf16[8,32,8,128]{3,0,2,1:T(8,128)(2,1)S(1)} %bitcast.33) | data formatting | bytes 1048576 | tf_op jit(solution)/shard_map/transpose | solution.py:105
  2.8 7.3 %all-to-all-start = ((bf16[8,32,8,128]{3,2,0,1:T(8,128)(2,1)}), bf16[8,32,8,128]{3,2,0,1:T(8,128)(2,1)S(1)}, u32[]{:S(2)}, u32[]{:S(2)}) async-start(bf16[8,32,8,128]{3,2,0,1:T(8,128)(2,1)} %copy.30), calls=%async_computation | async-start | bytes 1048576 | tf_op jit(solution)/shard_map/all_to_all | solution.py:106
  10.1 0.0 copy-done.3
  10.1 0.0 copy-done.4
  10.1 0.1 fusion.3
  10.2 0.1 broadcast_in_dim.62
  10.3 0.1 convert_element_type.81
  10.4 16.0 %all-to-all-done = bf16[8,32,8,128]{3,2,0,1:T(8,128)(2,1)S(1)} async-done(((bf16[8,32,8,128]{3,2,0,1:T(8,128)(2,1)}), bf16[8,32,8,128]{3,2,0,1:T(8,128)(2,1)S(1)}, u32[]{:S(2)}, u32[]{:S(2)}) %all-to-all-start) | async-done | bytes 524320 | tf_op jit(solution)/shard_map/all_to_all | solution.py:106
  26.4 0.3 multiply_reduce_fusion
  26.8 0.1 sqrt.16
  27.0 0.1 sqrt.17
  27.1 0.1 copy_convert_fusion
  27.1 0.3 divide_convert_fusion
  27.5 0.0 copy-start.2
  27.5 0.8 %fusion.1.q_ref = bf16[2048,128]{1,0:T(8,128)(2,1)S(1)} fusion(f32[8,32,8,128]{3,2,1,0:T(8,128)S(1)} %copy_convert_fusion, f32[2048]{0:T(1024)S(1)} %sqrt.17, pred[2048]{0:T(1024)(128)(4,1)S(1)} %broadcast_in_dim.62, bf16[64,128]{1,0:T(8,128)(2,1)S(1)} %slice_bitcast_fusion), kind=kLoop, calls=%fused_computation.6 | loop fusion | flops 786432 | bytes 1599488 | tf_op jit(solution)/shard_map/jit(_where)/select_n | solution.py:116
  28.3 0.0 copy-start.1
  28.4 0.1 collective-permute-start
  28.5 0.1 convert_element_type.83
  28.6 0.0 copy-done.2
  28.6 0.1 collective-permute-start.2
  28.6 1.7 %collective-permute-done = bf16[2064,128]{1,0:T(8,128)(2,1)S(1)} collective-permute-done((bf16[2064,128]{1,0:T(8,128)(2,1)S(1)}, bf16[2064,128]{1,0:T(8,128)(2,1)S(1)}, u32[]{:S(2)}, u32[]{:S(2)}) %collective-permute-start) | collective-permute-done | bytes 528416 | tf_op jit(solution)/shard_map/ppermute | solution.py:131
  30.4 0.1 reshape.144
  30.4 0.1 compare_convert_fusion.1
  30.5 0.0 slice-start
  30.5 0.9 %broadcast_select_fusion = (bf16[2048,128]{1,0:T(8,128)(2,1)}, bf16[2048,128]{1,0:T(8,128)(2,1)S(1)}) fusion(bf16[2048,128]{1,0:T(8,128)(2,1)S(1)} %fusion.1.q_ref, pred[]{:T(512)S(6)} %eq.50, bf16[2064,128]{1,0:T(8,128)(2,1)S(1)} %collective-permute-done), kind=kLoop, calls=%fused_computation.8 | loop fusion | flops 262144 | bytes 2097153 | tf_op jit(solution)/shard_map/jit(_where)/select_n | solution.py:140
  31.4 0.0 copy-done.1
  31.4 0.0 slice-done
  31.4 0.9 %slice_select_fusion = bf16[32,32,128]{2,1,0:T(8,128)(2,1)} fusion(bf16[32,64,128]{2,1,0:T(8,128)(2,1)S(1)} %bitcast.34, bf16[32,64,128]{2,1,0:T(8,128)(2,1)S(1)} %divide_convert_fusion, pred[32,32]{1,0:T(8,128)(4,1)S(1)} %get-tuple-element.12, pred[]{:T(512)S(6)} %eq.50, bf16[32,128]{1,0:T(8,128)(2,1)S(1)} %slice-done), kind=kLoop, calls=%fused_computation.9 | loop fusion | flops 262144 | bytes 795649 | tf_op jit(solution)/shard_map/jit(_where)/select_n | solution.py:138
  32.3 0.1 reshape.148
  32.4 0.6 %compare_convert_fusion.ov_ref = f32[1,2048]{1,0:T(1,128)} fusion(bf16[1,2048]{1,0:T(2,128)(2,1)S(1)} %convert_element_type.83, pred[]{:T(512)S(6)} %eq.50, bf16[1,1,16,128]{3,2,1,0:T(8,128)(2,1)S(1)} %get-tuple-element.5), kind=kLoop, calls=%fused_computation.15 | loop fusion | flops 6144 | bytes 16385 | tf_op jit(solution)/shard_map/convert_element_type | solution.py:75
  33.0 1.0 %broadcast_in_dim.71.qv_ref = f32[1024,128]{1,0:T(8,128)} broadcast(f32[1024]{0:T(1024)S(1)} %reshape.148), dimensions={0} | broadcast | bytes 528384 | tf_op jit(solution)/shard_map/broadcast_in_dim | solution.py:74
  34.0 3.2 %shard_map.46 = f32[32,64]{1,0:T(8,128)} custom-call(bf16[1024,128]{1,0:T(8,128)(2,1)} %bitcast.35, bf16[2048,128]{1,0:T(8,128)(2,1)} %get-tuple-element.7.o_ref, f32[1024,128]{1,0:T(8,128)} %broadcast_in_dim.71.qv_ref, f32[1,2048]{1,0:T(1,128)} %compare_convert_fusion.ov_ref), custom_call_target="tpu_custom_call" | custom-call | flops 536870912 | bytes 786432 | tf_op jit(solution)/shard_map/pallas_call | solution.py:77
  37.2 0.8 %copy.33 = f32[32,64]{0,1:T(8,128)S(1)} copy(f32[32,64]{1,0:T(8,128)} %shard_map.46) | data formatting | bytes 16384 | tf_op jit(solution)/shard_map/pallas_call | solution.py:77
  38.0 0.2 collective-permute-start.1
  38.2 5.5 %collective-permute-done.2 = bf16[2064,128]{1,0:T(8,128)(2,1)S(1)} collective-permute-done((bf16[2064,128]{1,0:T(8,128)(2,1)S(1)}, bf16[2064,128]{1,0:T(8,128)(2,1)S(1)}, u32[]{:S(2)}, u32[]{:S(2)}) %collective-permute-start.2) | collective-permute-done | bytes 528416 | tf_op jit(solution)/shard_map/ppermute | solution.py:130
  43.6 0.8 %slice.47.o_ref = bf16[2048,128]{1,0:T(8,128)(2,1)} slice(bf16[2064,128]{1,0:T(8,128)(2,1)S(1)} %collective-permute-done.2), slice={[0:2048], [0:128]} | slice | bytes 1048576 | tf_op jit(solution)/shard_map/slice | solution.py:134
  44.5 0.6 %compare_convert_fusion.2 = f32[16,128]{1,0:T(8,128)} fusion(bf16[2064,128]{1,0:T(8,128)(2,1)S(1)} %collective-permute-done.2), kind=kLoop, calls=%fused_computation.28 | loop fusion | flops 4096 | bytes 12288 | tf_op jit(solution)/shard_map/convert_element_type | solution.py:75
  45.1 1.3 %broadcast_in_dim.72.qv_ref = f32[2048,128]{1,0:T(8,128)} broadcast(f32[2048]{0:T(1024)S(1)} %convert_element_type.85), dimensions={0} | broadcast | bytes 1056768 | tf_op jit(solution)/shard_map/broadcast_in_dim | solution.py:74
  46.4 4.6 %shard_map.47 = f32[64,64]{1,0:T(8,128)} custom-call(bf16[2048,128]{1,0:T(8,128)(2,1)} %copy-done.1, bf16[2048,128]{1,0:T(8,128)(2,1)} %slice.47.o_ref, f32[2048,128]{1,0:T(8,128)} %broadcast_in_dim.72.qv_ref, f32[1,2048]{1,0:T(1,128)} %bitcast.39), custom_call_target="tpu_custom_call" | custom-call | flops 1073741824 | bytes 1048576 | tf_op jit(solution)/shard_map/pallas_call | solution.py:77
  51.0 0.8 %copy.37 = f32[64,64]{0,1:T(8,128)S(1)} copy(f32[64,64]{1,0:T(8,128)} %shard_map.47) | data formatting | bytes 32768 | tf_op jit(solution)/shard_map/pallas_call | solution.py:77
  51.8 0.0 collective-permute-start.3
  51.9 0.0 collective-permute-done.1
  51.9 0.1 maximum_select_fusion
  52.0 0.1 copy.36
  52.1 3.7 %collective-permute-done.3 = f32[64,64]{1,0:T(8,128)S(1)} collective-permute-done((f32[64,64]{1,0:T(8,128)S(1)}, f32[64,64]{1,0:T(8,128)S(1)}, u32[]{:S(2)}, u32[]{:S(2)}) %collective-permute-start.3) | collective-permute-done | bytes 16416 | tf_op jit(solution)/shard_map/ppermute | solution.py:153
  55.8 0.8 %broadcast_select_fusion.2 = (f32[64,64]{1,0:T(8,128)S(1)}, f32[64,64]{1,0:T(8,128)S(1)}) fusion(f32[64,64]{1,0:T(8,128)} %shard_map.47, f32[64,64]{1,0:T(8,128)S(1)} %collective-permute-done.3, pred[]{:T(512)S(6)} %eq.58), kind=kLoop, calls=%fused_computation.24 | loop fusion | flops 8192 | bytes 65537 | tf_op jit(solution)/shard_map/jit(_where)/select_n | solution.py:155
  56.5 0.7 %pad_maximum_fusion.1 = f32[64,192]{1,0:T(8,128)} fusion(f32[64,64]{1,0:T(8,128)S(1)} %get-tuple-element.10, f32[64,64]{1,0:T(8,128)S(1)} %get-tuple-element.9, f32[64,64]{1,0:T(8,128)S(1)} %bitcast_select_fusion), kind=kLoop, calls=%fused_computation.12 | loop fusion | flops 24576 | bytes 98304 | tf_op jit(solution)/shard_map/concatenate | solution.py:157
  (10 shorter events, 0.1 us)
Async XLA Ops:
  0.0 1.1 %copy-start = (bf16[256,8,128]{2,1,0:T(8,128)(2,1)S(1)}, bf16[256,8,128]{2,1,0:T(8,128)(2,1)}, u32[]{:S(2)}) copy-start(bf16[256,8,128]{2,1,0:T(8,128)(2,1)} %param.4) | copy-start | bytes 1572868
  1.9 8.2 %copy-start.3 = (s32[64,32]{0,1:T(8,128)S(1)}, s32[64,32]{0,1:T(8,128)}, u32[]{:S(2)}) copy-start(s32[64,32]{0,1:T(8,128)} %param.7) | copy-start | bytes 24580
  1.9 8.2 %copy-start.4 = (s32[64]{0:T(128)S(1)}, s32[64]{0:T(128)}, u32[]{:S(2)}) copy-start(s32[64]{0:T(128)} %param.6) | copy-start | bytes 772
  2.8 23.7 %all-to-all-start = ((bf16[8,32,8,128]{3,2,0,1:T(8,128)(2,1)}), bf16[8,32,8,128]{3,2,0,1:T(8,128)(2,1)S(1)}, u32[]{:S(2)}, u32[]{:S(2)}) async-start(bf16[8,32,8,128]{3,2,0,1:T(8,128)(2,1)} %copy.30), calls=%async_computation | async-start | bytes 1048576 | tf_op jit(solution)/shard_map/all_to_all | solution.py:106
  27.5 1.1 %copy-start.2 = (bf16[64,128]{1,0:T(8,128)(2,1)}, bf16[64,128]{1,0:T(8,128)(2,1)S(1)}, u32[]{:S(2)}) copy-start(bf16[64,128]{1,0:T(8,128)(2,1)S(1)} %slice_bitcast_fusion) | copy-start | bytes 49156
  28.3 3.1 %copy-start.1 = (bf16[2048,128]{1,0:T(8,128)(2,1)}, bf16[2048,128]{1,0:T(8,128)(2,1)S(1)}, u32[]{:S(2)}) copy-start(bf16[2048,128]{1,0:T(8,128)(2,1)S(1)} %fusion.1.q_ref) | copy-start | bytes 1572868
  28.4 2.0 %collective-permute-start = (bf16[2064,128]{1,0:T(8,128)(2,1)S(1)}, bf16[2064,128]{1,0:T(8,128)(2,1)S(1)}, u32[]{:S(2)}, u32[]{:S(2)}) collective-permute-start(bf16[2064,128]{1,0:T(8,128)(2,1)S(1)} %pad_maximum_fusion), channel_id=1, source_target_pairs={{0,1},{1,0},{2,3},{3,2},{4,5},{5,4},{6,7},{7,6},{8,9},{9,8},{10,11... | collective-permute-start | bytes 1585160 | tf_op jit(solution)/shard_map/ppermute | solution.py:131
  28.6 15.1 %collective-permute-start.2 = (bf16[2064,128]{1,0:T(8,128)(2,1)S(1)}, bf16[2064,128]{1,0:T(8,128)(2,1)S(1)}, u32[]{:S(2)}, u32[]{:S(2)}) collective-permute-start(bf16[2064,128]{1,0:T(8,128)(2,1)S(1)} %pad_maximum_fusion), channel_id=1, source_target_pairs={{0,2},{1,5},{2,6},{3,1},{4,0},{5,7},{6,4},{7,3},{8,10},{9,13},{10,... | collective-permute-start | bytes 1585160 | tf_op jit(solution)/shard_map/ppermute | solution.py:130
  30.5 0.9 %slice-start = ((bf16[64,128]{1,0:T(8,128)(2,1)}), bf16[32,128]{1,0:T(8,128)(2,1)S(1)}, s32[]{:S(2)}) async-start(bf16[64,128]{1,0:T(8,128)(2,1)} %copy-done.2), calls=%async_computation.1 | async-start | bytes 16384 | tf_op jit(solution)/shard_map/slice | solution.py:138
  38.0 13.9 %collective-permute-start.1 = (f32[32,64]{0,1:T(8,128)S(1)}, f32[32,64]{0,1:T(8,128)S(1)}, u32[]{:S(2)}, u32[]{:S(2)}) collective-permute-start(f32[32,64]{0,1:T(8,128)S(1)} %copy.33), channel_id=1, source_target_pairs={{0,1},{1,0},{2,3},{3,2},{4,5},{5,4},{6,7},{7,6},{8,9},{9,8},{10,11... | collective-permute-start | bytes 24584 | tf_op jit(solution)/shard_map/ppermute | solution.py:143
  51.8 4.0 %collective-permute-start.3 = (f32[64,64]{1,0:T(8,128)S(1)}, f32[64,64]{1,0:T(8,128)S(1)}, u32[]{:S(2)}, u32[]{:S(2)}) collective-permute-start(f32[64,64]{1,0:T(8,128)S(1)} %bitcast.38), channel_id=1, source_target_pairs={{2,0},{5,1},{6,2},{1,3},{0,4},{7,5},{4,6},{3,7},{10,8},{13,9},{14,... | collective-permute-start | bytes 49160 | tf_op jit(solution)/shard_map/ppermute | solution.py:153

commit v15 on v14

--- a/solution.py
+++ b/solution.py
@@ -35,8 +35,10 @@
     return result.reshape(query_items, other_items)
 
 
-def _chamfer_kernel(tok, nq, no, cw, q_ref, o_ref, qv_ref, ov_ref, out_ref, fm_ref):
+def _chamfer_kernel(tok, nq, no, cw, q_ref, o_ref, qv_ref, out_ref, out_t_ref, fm_ref):
     q = q_ref[...]
+    n_rows = tok * no // 128
+    flags = o_ref[tok * no:tok * no + n_rows, :].astype(jnp.float32)
     acc_b = jnp.zeros((nq, 128), jnp.float32)
     for c in range(tok * no // cw):
         o_c = o_ref[c * cw:(c + 1) * cw, :]
@@ -49,41 +51,34 @@
         else:
             fm_ref[...] = jnp.maximum(fm_ref[...], m)
         mb = jnp.max(d.reshape(tok, nq, cw), axis=0)
-        mbm = jnp.where(ov_ref[:, c * cw:(c + 1) * cw] > 0, mb, 0.0)
-        s = mbm[:, 0:128]
-        for k in range(1, cw // 128):
-            s = s + mbm[:, k * 128:(k + 1) * 128]
-        acc_b = acc_b + s
+        for k in range(cw // 128):
+            row = c * (cw // 128) + k
+            acc_b = acc_b + jnp.where(flags[row:row + 1, :] == 0, mb[:, k * 128:(k + 1) * 128], 0.0)
     fm = fm_ref[...]
     fm = jnp.maximum(fm, pltpu.roll(fm, 64, 1))
     fsum = jnp.sum(jnp.where(qv_ref[...] > 0, fm, 0.0).reshape(tok, nq, 128), axis=0)
     bsum = acc_b + pltpu.roll(acc_b, 64, 1)
-    out_ref[...] = (0.5 * (fsum + bsum))[:, :no]
+    res = 0.5 * (fsum + bsum)
+    out_ref[...] = res[:, :no]
+    out_t_ref[...] = res.T[:no, :]
 
 
-def chamfer_tile(query, query_valid, other, other_valid):
-    tok, nq, width = query.shape
-    no = other.shape[1]
-    if no != 64 or (tok * no) % 512 or nq % 8:
-        return tile_scores(
-            query, jnp.where(query_valid, 0.0, -4.0), other, jnp.where(other_valid, 0.0, -4.0)
-        )
-    tok_nq, tok_no, cw = tok * nq, tok * no, 512
-    q = query.reshape(tok_nq, width)
-    o = other.reshape(tok_no, width)
-    qv = jnp.broadcast_to(query_valid.astype(jnp.float32).reshape(tok_nq, 1), (tok_nq, 128))
-    ov = other_valid.astype(jnp.float32).reshape(1, tok_no)
+def chamfer_tile(query, query_valid, other_packed, tok):
+    tok_nq, width = query.shape
+    nq = tok_nq // tok
+    no = 64
+    cw = 512
     kernel = functools.partial(_chamfer_kernel, tok, nq, no, cw)
     return pl.pallas_call(
         kernel,
-        out_shape=jax.ShapeDtypeStruct((nq, no), jnp.float32),
-        in_specs=[pl.BlockSpec(memory_space=pltpu.VMEM)] * 4,
-        out_specs=pl.BlockSpec(memory_space=pltpu.VMEM),
+        out_shape=(jax.ShapeDtypeStruct((nq, no), jnp.float32), jax.ShapeDtypeStruct((no, nq), jnp.float32)),
+        in_specs=[pl.BlockSpec(memory_space=pltpu.VMEM)] * 3,
+        out_specs=(pl.BlockSpec(memory_space=pltpu.VMEM), pl.BlockSpec(memory_space=pltpu.VMEM)),
         scratch_shapes=[pltpu.VMEM((tok_nq, 128), jnp.float32)],
         cost_estimate=pl.CostEstimate(
-            flops=2 * tok_nq * tok_no * width, transcendentals=0, bytes_accessed=(tok_nq + tok_no) * width * 2
+            flops=2 * tok_nq * tok * no * width, transcendentals=0, bytes_accessed=(tok_nq + tok * no) * width * 2
         ),
-    )(q, o, qv, ov)
+    )(query, other_packed, query_valid)
 
 
 def shards(encoded, slot_items, lengths, token_mask):
@@ -130,16 +125,18 @@
     z_recv = lax.ppermute(packed, "pool", send_pairs)
     c_recv = lax.ppermute(packed, "pool", chip_pairs)
 
-    def unpack(received):
-        return received[:n_tok].reshape(tok, items_dev, width), received[n_tok:].reshape(tok, items_dev)
+    def row_flags(valid_rows):
+        return jnp.broadcast_to(valid_rows.astype(jnp.float32).reshape(-1, 1), (valid_rows.size, 128))
 
     half = items_dev // 2
-    c_blk, c_bias = unpack(c_recv)
-    query = jnp.where(is_a, block[:, :half], c_blk[:, half:])
-    query_bias = jnp.where(is_a, bias[:, :half], c_bias[:, half:])
-    other = jnp.where(is_a, c_blk, block)
-    other_bias = jnp.where(is_a, c_bias, bias)
-    part = chamfer_tile(query, query_bias == 0, other, other_bias == 0)
+    own_flags = row_flags(valid_tm)
+    c_blk = c_recv[:n_tok].reshape(tok, items_dev, width)
+    c_valid = c_recv[n_tok:].reshape(tok, items_dev) == 0
+    query = jnp.where(is_a, block[:, :half], c_blk[:, half:]).reshape(tok * half, width)
+    query_flags = row_flags(jnp.where(is_a, valid_tm[:, :half], c_valid[:, half:]))
+    other_packed = jnp.where(is_a, c_recv, packed)
+    part, _ = chamfer_tile(query, query_flags, other_packed, tok)
+    part, own_flags = lax.optimization_barrier((part, own_flags))
     part_recv = lax.ppermute(part, "pool", chip_pairs)
     joined = jnp.where(
         is_a,
@@ -148,9 +145,8 @@
     )
     tile0 = jnp.where(is_a, joined, joined.T)
 
-    z_blk, z_bias = unpack(z_recv)
-    tile_z = chamfer_tile(block, valid_tm, z_blk, z_bias == 0)
-    tile_back = lax.ppermute(tile_z.T, "pool", back_pairs)
+    tile_z, tile_z_t = chamfer_tile(block.reshape(n_tok, width), own_flags, z_recv, tok)
+    tile_back = lax.ppermute(tile_z_t, "pool", back_pairs)
     via_bit1 = parity == 1
     col1 = jnp.where(via_bit1, tile_z, tile_back)
     col2 = jnp.where(via_bit1, tile_back, tile_z)

time: 57.7 us -> 55 us (0.953)
  local copies, waits for them, and re-layouts: 8.15 us -> 6.6 us
  other arithmetic: 6.43 us -> 5.33 us
    pallas_call x2 -> x0, local copies, waits for them, and re-layouts: 1.63 us -> none  [chamfer_tile(): pl.pallas_call(kernel, out_shape=jax.ShapeDtypeStruct((nq, no), jnp.float...]
    convert_element_type x3 -> x1, other arithmetic: 1.21 us -> 0.01 us  [row_flags(): valid_rows.astype(jnp.float32).reshape(-1, 1)]
    unnamed x11 -> x14, local copies, waits for them, and re-layouts: 0.05 us -> 0.9 us
    slice x3, local copies, waits for them, and re-layouts: 0.83 us -> 0.04 us  [the longest x1 0.03 us: shards(): c_blk = c_recv[:n_tok].reshape(tok, items_dev, width)]
  transfers between devices with their start and end apart: 5 -> 5, of which waited for: 4 -> 4; matrix products, arithmetic and copies ran while one was open for 15% -> 9% of each run, Pallas kernels for 14% -> 15%
where the time goes in v15:
time: 55 us; the launch traced here: 54.7 us
  waiting for transfers between devices  26.9 us (49%)
  Pallas kernels  7.99 us (15%)
  starting transfers between devices  7.6 us (14%)
  local copies, waits for them, and re-layouts  6.6 us (12%)
  other arithmetic  5.33 us (10%)
    all_to_all x1, waiting for transfers between devices, shards(): lax.all_to_all(outgoing, ('enc', 'pool'), split_axis=1, concat_axis=1, ti...  16 us
    pallas_call x2, Pallas kernels, chamfer_tile(): pl.pallas_call(kernel, out_shape=(jax.ShapeDtypeStruct((nq, no), jnp.floa...  7.99 us
    all_to_all x1, starting transfers between devices, shards(): lax.all_to_all(outgoing, ('enc', 'pool'), split_axis=1, concat_axis=1, ti...  7.3 us
    ppermute x1, waiting for transfers between devices, shards(): z_recv = lax.ppermute(packed, 'pool', send_pairs)  5.13 us
    ppermute x1, waiting for transfers between devices, shards(): tile_back = lax.ppermute(tile_z_t, 'pool', back_pairs)  3.94 us
    broadcast_in_dim x3, local copies, waits for them, and re-layouts, row_flags(): jnp.broadcast_to(valid_rows.astype(jnp.float32).reshape(-1, 1), (valid_ro...  2.38 us
    ppermute x1, waiting for transfers between devices, shards(): c_recv = lax.ppermute(packed, 'pool', chip_pairs)  1.79 us
  transfers between devices with their start and end apart: 5, of which 4 were waited for; matrix products, arithmetic and copies ran while one was open for 9% of the time, Pallas kernels for 15%

profile of v15, /device:TPU:0, one launch (start us, length us, event | category | flops | bytes accessed | tf_op | source)
XLA Modules:
  0.0 54.7 jit_solution(8255590538576806875)
XLA Ops:
  0.0 0.0 copy-start
  0.0 0.8 %reshape.79 = s32[32,8,8]{2,1,0:T(8,128)S(1)} reshape(s32[2048]{0:T(1024)} %param.5) | data formatting | bytes 16384 | tf_op jit(solution)/shard_map/reshape | solution.py:97
  0.9 0.1 subtract_reduce_fusion
  0.9 0.1 reshape.87
  1.0 0.0 copy-done
  1.1 0.8 %gather_fusion = bf16[256,8,128]{2,1,0:T(8,128)(2,1)S(1)} fusion(bf16[256,8,128]{2,1,0:T(8,128)(2,1)S(1)} %copy-done, s32[1024]{0:T(1024)S(1)} %pad_clamp_fusion), kind=kCustom, calls=%fused_computation | custom fusion | bytes 1049600 | tf_op jit(solution)/shard_map/jit(_take)/gather | solution.py:99
  1.9 0.0 copy-start.4
  1.9 0.0 copy-start.5
  1.9 0.9 %copy.27 = bf16[8,32,8,128]{3,2,0,1:T(8,128)(2,1)} copy(bf16[8,32,8,128]{3,0,2,1:T(8,128)(2,1)S(1)} %bitcast.26) | data formatting | bytes 1048576 | tf_op jit(solution)/shard_map/transpose | solution.py:100
  2.8 7.3 %all-to-all-start = ((bf16[8,32,8,128]{3,2,0,1:T(8,128)(2,1)}), bf16[8,32,8,128]{3,2,0,1:T(8,128)(2,1)S(1)}, u32[]{:S(2)}, u32[]{:S(2)}) async-start(bf16[8,32,8,128]{3,2,0,1:T(8,128)(2,1)} %copy.27), calls=%async_computation | async-start | bytes 1048576 | tf_op jit(solution)/shard_map/all_to_all | solution.py:101
  10.1 0.0 copy-done.4
  10.1 0.0 copy-done.5
  10.1 0.1 fusion.3
  10.2 0.1 broadcast_in_dim.58
  10.3 0.1 convert_element_type.44
  10.4 16.0 %all-to-all-done = bf16[8,32,8,128]{3,2,0,1:T(8,128)(2,1)S(1)} async-done(((bf16[8,32,8,128]{3,2,0,1:T(8,128)(2,1)}), bf16[8,32,8,128]{3,2,0,1:T(8,128)(2,1)S(1)}, u32[]{:S(2)}, u32[]{:S(2)}) %all-to-all-start) | async-done | bytes 524320 | tf_op jit(solution)/shard_map/all_to_all | solution.py:101
  26.5 0.3 multiply_reduce_fusion
  26.9 0.1 sqrt.17
  27.0 0.1 sqrt.16
  27.1 0.1 copy_convert_fusion
  27.1 0.3 divide_convert_fusion
  27.5 0.0 copy-start.2
  27.5 0.8 %fusion.1.q_ref = bf16[2048,128]{1,0:T(8,128)(2,1)S(1)} fusion(f32[8,32,8,128]{3,2,1,0:T(8,128)S(1)} %copy_convert_fusion, f32[2048]{0:T(1024)S(1)} %sqrt.17, pred[2048]{0:T(1024)(128)(4,1)S(1)} %broadcast_in_dim.58, bf16[64,128]{1,0:T(8,128)(2,1)S(1)} %slice_bitcast_fusion), kind=kLoop, calls=%fused_computation.7 | loop fusion | flops 786432 | bytes 1599488 | tf_op jit(solution)/shard_map/jit(_where)/select_n | solution.py:111
  28.3 0.0 copy-start.1
  28.4 0.1 collective-permute-start
  28.5 0.1 collective-permute-start.2
  28.6 0.0 copy-done.2
  28.6 0.0 slice-start
  28.6 1.8 %collective-permute-done = bf16[2064,128]{1,0:T(8,128)(2,1)S(1)} collective-permute-done((bf16[2064,128]{1,0:T(8,128)(2,1)S(1)}, bf16[2064,128]{1,0:T(8,128)(2,1)S(1)}, u32[]{:S(2)}, u32[]{:S(2)}) %collective-permute-start) | collective-permute-done | bytes 528416 | tf_op jit(solution)/shard_map/ppermute | solution.py:126
  30.4 0.9 %broadcast_select_fusion.o_ref = bf16[2064,128]{1,0:T(8,128)(2,1)} fusion(bf16[2064,128]{1,0:T(8,128)(2,1)S(1)} %collective-permute-done, pred[]{:T(512)S(6)} %eq.32, bf16[16,128]{1,0:T(8,128)(2,1)S(1)} %convert_element_type.44, bf16[2048,128]{1,0:T(8,128)(2,1)S(1)} %fusion.1.q_ref), kind=kLoop, calls=%fused_computation.6 | loop fusion | flops 1320960 | bytes 1585153 | tf_op jit(solution)/shard_map/jit(_where)/select_n | solution.py:137
  31.3 0.0 copy-done.1
  31.3 0.1 eq.39
  31.4 0.1 fusion.4
  31.5 0.1 reshape.84
  31.6 0.0 slice-done
  31.6 0.9 %slice_select_fusion = bf16[32,32,128]{2,1,0:T(8,128)(2,1)} fusion(bf16[32,64,128]{2,1,0:T(8,128)(2,1)S(1)} %bitcast.27, bf16[32,64,128]{2,1,0:T(8,128)(2,1)S(1)} %divide_convert_fusion, pred[32,32]{1,0:T(8,128)(4,1)S(1)} %get-tuple-element.18, pred[]{:T(512)S(6)} %eq.32, bf16[32,128]{1,0:T(8,128)(2,1)S(1)} %slice-done), kind=kLoop, calls=%fused_computation.9 | loop fusion | flops 262144 | bytes 795649 | tf_op jit(solution)/shard_map/jit(_where)/select_n | solution.py:135
  32.5 1.0 %broadcast_in_dim.65.qv_ref = f32[1024,128]{1,0:T(8,128)} broadcast(f32[1024]{0:T(1024)S(1)} %reshape.84), dimensions={0} | broadcast | bytes 528384 | tf_op jit(solution)/shard_map/broadcast_in_dim | solution.py:129
  33.5 3.3 %shard_map.46 = (f32[32,64]{1,0:T(8,128)}, f32[64,32]{1,0:T(8,128)}) custom-call(bf16[1024,128]{1,0:T(8,128)(2,1)} %bitcast.28, bf16[2064,128]{1,0:T(8,128)(2,1)} %broadcast_select_fusion.o_ref, f32[1024,128]{1,0:T(8,128)} %broadcast_in_dim.65.qv_ref), custom_call_target="tpu_custom_call" | custom-call | flops 536870912 | bytes 786432 | tf_op jit(solution)/shard_map/pallas_call | solution.py:72
  36.8 0.0 copy-start.3
  36.8 1.3 %broadcast_in_dim.66.qv_ref = f32[2048,128]{1,0:T(8,128)} broadcast(f32[2048]{0:T(1024)S(1)} %convert_element_type.45), dimensions={0} | broadcast | bytes 1056768 | tf_op jit(solution)/shard_map/broadcast_in_dim | solution.py:129
  38.2 0.0 copy-done.3
  38.2 0.1 copy.30
  38.2 0.2 collective-permute-start.1
  38.4 5.1 %collective-permute-done.2.o_ref = bf16[2064,128]{1,0:T(8,128)(2,1)S(1)} collective-permute-done((bf16[2064,128]{1,0:T(8,128)(2,1)S(1)}, bf16[2064,128]{1,0:T(8,128)(2,1)S(1)}, u32[]{:S(2)}, u32[]{:S(2)}) %collective-permute-start.2) | collective-permute-done | bytes 528416 | tf_op jit(solution)/shard_map/ppermute | solution.py:125
  43.5 0.0 copy-start.6
  43.5 0.8 %copy-done.6 = bf16[2064,128]{1,0:T(8,128)(2,1)} copy-done((bf16[2064,128]{1,0:T(8,128)(2,1)}, bf16[2064,128]{1,0:T(8,128)(2,1)S(1)}, u32[]{:S(2)}) %copy-start.6) | copy-done | bytes 528408
  44.4 4.7 %shard_map.47 = (f32[64,64]{1,0:T(8,128)}, f32[64,64]{1,0:T(8,128)}) custom-call(bf16[2048,128]{1,0:T(8,128)(2,1)} %copy-done.1, bf16[2064,128]{1,0:T(8,128)(2,1)} %copy-done.6, f32[2048,128]{1,0:T(8,128)} %broadcast_in_dim.66.qv_ref), custom_call_target="tpu_custom_call" | custom-call | flops 1073741824 | bytes 1048576 | tf_op jit(solution)/shard_map/pallas_call | solution.py:72
  49.1 0.0 collective-permute-start.3
  49.1 0.0 collective-permute-done.1
  49.1 0.1 maximum_select_fusion
  49.2 0.1 copy.33
  49.2 3.9 %collective-permute-done.3 = f32[64,64]{1,0:T(8,128)S(1)} collective-permute-done((f32[64,64]{1,0:T(8,128)}, f32[64,64]{1,0:T(8,128)S(1)}, u32[]{:S(2)}, u32[]{:S(2)}) %collective-permute-start.3) | collective-permute-done | bytes 16416 | tf_op jit(solution)/shard_map/ppermute | solution.py:149
  53.2 0.8 %broadcast_select_fusion.2 = (f32[64,64]{1,0:T(8,128)S(1)}, f32[64,64]{1,0:T(8,128)S(1)}) fusion(f32[64,64]{1,0:T(8,128)} %get-tuple-element.13, f32[64,64]{1,0:T(8,128)S(1)} %collective-permute-done.3, pred[]{:T(512)S(6)} %eq.40), kind=kLoop, calls=%fused_computation.24 | loop fusion | flops 8192 | bytes 65537 | tf_op jit(solution)/shard_map/jit(_where)/select_n | solution.py:151
  54.0 0.7 %pad_maximum_fusion.1 = f32[64,192]{1,0:T(8,128)} fusion(f32[64,64]{1,0:T(8,128)S(1)} %get-tuple-element.16, f32[64,64]{1,0:T(8,128)S(1)} %get-tuple-element.15, f32[64,64]{1,0:T(8,128)S(1)} %bitcast_select_fusion), kind=kLoop, calls=%fused_computation.12 | loop fusion | flops 24576 | bytes 98304 | tf_op jit(solution)/shard_map/concatenate | solution.py:153
  (11 shorter events, 0.2 us)
Async XLA Ops:
  0.0 1.1 %copy-start = (bf16[256,8,128]{2,1,0:T(8,128)(2,1)S(1)}, bf16[256,8,128]{2,1,0:T(8,128)(2,1)}, u32[]{:S(2)}) copy-start(bf16[256,8,128]{2,1,0:T(8,128)(2,1)} %param.4) | copy-start | bytes 1572868
  1.9 8.2 %copy-start.4 = (s32[64,32]{0,1:T(8,128)S(1)}, s32[64,32]{0,1:T(8,128)}, u32[]{:S(2)}) copy-start(s32[64,32]{0,1:T(8,128)} %param.7) | copy-start | bytes 24580
  1.9 8.2 %copy-start.5 = (s32[64]{0:T(128)S(1)}, s32[64]{0:T(128)}, u32[]{:S(2)}) copy-start(s32[64]{0:T(128)} %param.6) | copy-start | bytes 772
  2.8 23.7 %all-to-all-start = ((bf16[8,32,8,128]{3,2,0,1:T(8,128)(2,1)}), bf16[8,32,8,128]{3,2,0,1:T(8,128)(2,1)S(1)}, u32[]{:S(2)}, u32[]{:S(2)}) async-start(bf16[8,32,8,128]{3,2,0,1:T(8,128)(2,1)} %copy.27), calls=%async_computation | async-start | bytes 1048576 | tf_op jit(solution)/shard_map/all_to_all | solution.py:101
  27.5 1.0 %copy-start.2 = (bf16[64,128]{1,0:T(8,128)(2,1)}, bf16[64,128]{1,0:T(8,128)(2,1)S(1)}, u32[]{:S(2)}) copy-start(bf16[64,128]{1,0:T(8,128)(2,1)S(1)} %slice_bitcast_fusion) | copy-start | bytes 49156
  28.3 3.0 %copy-start.1 = (bf16[2048,128]{1,0:T(8,128)(2,1)}, bf16[2048,128]{1,0:T(8,128)(2,1)S(1)}, u32[]{:S(2)}) copy-start(bf16[2048,128]{1,0:T(8,128)(2,1)S(1)} %fusion.1.q_ref) | copy-start | bytes 1572868
  28.4 2.0 %collective-permute-start = (bf16[2064,128]{1,0:T(8,128)(2,1)S(1)}, bf16[2064,128]{1,0:T(8,128)(2,1)S(1)}, u32[]{:S(2)}, u32[]{:S(2)}) collective-permute-start(bf16[2064,128]{1,0:T(8,128)(2,1)S(1)} %pad_maximum_fusion), channel_id=1, source_target_pairs={{0,1},{1,0},{2,3},{3,2},{4,5},{5,4},{6,7},{7,6},{8,9},{9,8},{10,11... | collective-permute-start | bytes 1585160 | tf_op jit(solution)/shard_map/ppermute | solution.py:126
  28.5 15.0 %collective-permute-start.2 = (bf16[2064,128]{1,0:T(8,128)(2,1)S(1)}, bf16[2064,128]{1,0:T(8,128)(2,1)S(1)}, u32[]{:S(2)}, u32[]{:S(2)}) collective-permute-start(bf16[2064,128]{1,0:T(8,128)(2,1)S(1)} %pad_maximum_fusion), channel_id=1, source_target_pairs={{0,2},{1,5},{2,6},{3,1},{4,0},{5,7},{6,4},{7,3},{8,10},{9,13},{10,... | collective-permute-start | bytes 1585160 | tf_op jit(solution)/shard_map/ppermute | solution.py:125
  28.6 3.0 %slice-start = ((bf16[64,128]{1,0:T(8,128)(2,1)}), bf16[32,128]{1,0:T(8,128)(2,1)S(1)}, s32[]{:S(2)}) async-start(bf16[64,128]{1,0:T(8,128)(2,1)} %copy-done.2), calls=%async_computation.1 | async-start | bytes 16384 | tf_op jit(solution)/shard_map/slice | solution.py:135
  36.8 1.3 %copy-start.3 = (f32[32,64]{1,0:T(8,128)S(1)}, f32[32,64]{1,0:T(8,128)}, u32[]{:S(2)}) copy-start(f32[32,64]{1,0:T(8,128)} %get-tuple-element.11) | copy-start | bytes 24580
  38.2 10.8 %collective-permute-start.1 = (f32[32,64]{0,1:T(8,128)S(1)}, f32[32,64]{0,1:T(8,128)S(1)}, u32[]{:S(2)}, u32[]{:S(2)}) collective-permute-start(f32[32,64]{0,1:T(8,128)S(1)} %copy.30), channel_id=1, source_target_pairs={{0,1},{1,0},{2,3},{3,2},{4,5},{5,4},{6,7},{7,6},{8,9},{9,8},{10,11... | collective-permute-start | bytes 24584 | tf_op jit(solution)/shard_map/ppermute | solution.py:140
  43.5 0.8 %copy-start.6 = (bf16[2064,128]{1,0:T(8,128)(2,1)}, bf16[2064,128]{1,0:T(8,128)(2,1)S(1)}, u32[]{:S(2)}) copy-start(bf16[2064,128]{1,0:T(8,128)(2,1)S(1)} %collective-permute-done.2.o_ref) | copy-start | bytes 1585156
  49.1 4.1 %collective-permute-start.3 = (f32[64,64]{1,0:T(8,128)}, f32[64,64]{1,0:T(8,128)S(1)}, u32[]{:S(2)}, u32[]{:S(2)}) collective-permute-start(f32[64,64]{1,0:T(8,128)} %get-tuple-element.14), channel_id=1, source_target_pairs={{2,0},{5,1},{6,2},{1,3},{0,4},{7,5},{4,6},{3,7},{10,8},{13,9},{14,... | collective-permute-start | bytes 49160 | tf_op jit(solution)/shard_map/ppermute | solution.py:149

commit v16 on v15

--- a/solution.py
+++ b/solution.py
@@ -35,13 +35,25 @@
     return result.reshape(query_items, other_items)
 
 
-def _chamfer_kernel(tok, nq, no, cw, q_ref, o_ref, qv_ref, out_ref, out_t_ref, fm_ref):
+def _chamfer_kernel(tok, nq, no, cw, q_ref, o_hbm, qv_ref, out_ref, out_t_ref, fm_ref, o_buf, f_buf, sems):
+    n_chunks = tok * no // cw
+    n_rows = tok * no // 128
+
+    def chunk_copy(c):
+        return pltpu.make_async_copy(o_hbm.at[pl.ds(c * cw, cw), :], o_buf.at[c % 2], sems.at[c % 2])
+
+    flag_copy = pltpu.make_async_copy(o_hbm.at[pl.ds(tok * no, n_rows), :], f_buf, sems.at[2])
+    flag_copy.start()
+    chunk_copy(0).start()
     q = q_ref[...]
-    n_rows = tok * no // 128
-    flags = o_ref[tok * no:tok * no + n_rows, :].astype(jnp.float32)
+    flag_copy.wait()
+    flags = f_buf[...].astype(jnp.float32)
     acc_b = jnp.zeros((nq, 128), jnp.float32)
-    for c in range(tok * no // cw):
-        o_c = o_ref[c * cw:(c + 1) * cw, :]
+    for c in range(n_chunks):
+        if c + 1 < n_chunks:
+            chunk_copy(c + 1).start()
+        chunk_copy(c).wait()
+        o_c = o_buf[c % 2]
         d = lax.dot_general(q, o_c, (((1,), (1,)), ((), ())), preferred_element_type=jnp.float32)
         m = d[:, 0:128]
         for k in range(1, cw // 128):
@@ -72,9 +84,18 @@
     return pl.pallas_call(
         kernel,
         out_shape=(jax.ShapeDtypeStruct((nq, no), jnp.float32), jax.ShapeDtypeStruct((no, nq), jnp.float32)),
-        in_specs=[pl.BlockSpec(memory_space=pltpu.VMEM)] * 3,
+        in_specs=[
+            pl.BlockSpec(memory_space=pltpu.VMEM),
+            pl.BlockSpec(memory_space=pl.ANY),
+            pl.BlockSpec(memory_space=pltpu.VMEM),
+        ],
         out_specs=(pl.BlockSpec(memory_space=pltpu.VMEM), pl.BlockSpec(memory_space=pltpu.VMEM)),
-        scratch_shapes=[pltpu.VMEM((tok_nq, 128), jnp.float32)],
+        scratch_shapes=[
+            pltpu.VMEM((tok_nq, 128), jnp.float32),
+            pltpu.VMEM((2, cw, width), jnp.bfloat16),
+            pltpu.VMEM((tok * no // 128, width), jnp.bfloat16),
+            pltpu.SemaphoreType.DMA((3,)),
+        ],
         cost_estimate=pl.CostEstimate(
             flops=2 * tok_nq * tok * no * width, transcendentals=0, bytes_accessed=(tok_nq + tok * no) * width * 2
         ),
@@ -144,6 +165,7 @@
         jnp.concatenate([part_recv, part], axis=0),
     )
     tile0 = jnp.where(is_a, joined, joined.T)
+    tile0, z_recv = lax.optimization_barrier((tile0, z_recv))
 
     tile_z, tile_z_t = chamfer_tile(block.reshape(n_tok, width), own_flags, z_recv, tok)
     tile_back = lax.ppermute(tile_z_t, "pool", back_pairs)

time: 55 us -> 56.4 us (1.025)
  Pallas kernels: 7.99 us -> 10.8 us
  waiting for transfers between devices: 26.9 us -> 25.3 us
    pallas_call x2, Pallas kernels: 7.99 us -> 10.8 us  [chamfer_tile(): pl.pallas_call(kernel, out_shape=(jax.ShapeDtypeStruct((nq, no), jnp.floa...]
    ppermute x1, waiting for transfers between devices: 5.13 us -> 2.3 us  [shards(): z_recv = lax.ppermute(packed, 'pool', send_pairs)]
    ppermute x1, waiting for transfers between devices: 0.01 us -> 1.06 us  [shards(): part_recv = lax.ppermute(part, 'pool', chip_pairs)]
  transfers between devices with their start and end apart: 5 -> 5, of which waited for: 4 -> 5; matrix products, arithmetic and copies ran while one was open for 9% -> 9% of each run, Pallas kernels for 15% -> 9%
where the time goes in v16:
time: 56.4 us; the launch traced here: 56 us
  waiting for transfers between devices  25.3 us (45%)
  Pallas kernels  10.8 us (19%)
  starting transfers between devices  7.66 us (14%)
  local copies, waits for them, and re-layouts  6.61 us (12%)
  other arithmetic  5.33 us (9%)
    all_to_all x1, waiting for transfers between devices, shards(): lax.all_to_all(outgoing, ('enc', 'pool'), split_axis=1, concat_axis=1, ti...  16 us
    pallas_call x2, Pallas kernels, chamfer_tile(): pl.pallas_call(kernel, out_shape=(jax.ShapeDtypeStruct((nq, no), jnp.floa...  10.8 us
    all_to_all x1, starting transfers between devices, shards(): lax.all_to_all(outgoing, ('enc', 'pool'), split_axis=1, concat_axis=1, ti...  7.3 us
    ppermute x1, waiting for transfers between devices, shards(): tile_back = lax.ppermute(tile_z_t, 'pool', back_pairs)  4.11 us
    broadcast_in_dim x3, local copies, waits for them, and re-layouts, row_flags(): jnp.broadcast_to(valid_rows.astype(jnp.float32).reshape(-1, 1), (valid_ro...  2.39 us
    ppermute x1, waiting for transfers between devices, shards(): z_recv = lax.ppermute(packed, 'pool', send_pairs)  2.3 us
    ppermute x1, waiting for transfers between devices, shards(): c_recv = lax.ppermute(packed, 'pool', chip_pairs)  1.81 us
  transfers between devices with their start and end apart: 5, of which 5 were waited for; matrix products, arithmetic and copies ran while one was open for 9% of the time, Pallas kernels for 9%

profile of v16, /device:TPU:0, one launch (start us, length us, event | category | flops | bytes accessed | tf_op | source)
XLA Modules:
  0.0 56.0 jit_solution(2940022327331927629)
XLA Ops:
  0.0 0.0 copy-start
  0.0 0.8 %reshape.79 = s32[32,8,8]{2,1,0:T(8,128)S(1)} reshape(s32[2048]{0:T(1024)} %param.5) | data formatting | bytes 16384 | tf_op jit(solution)/shard_map/reshape | solution.py:118
  0.9 0.1 subtract_reduce_fusion
  0.9 0.1 reshape.87
  1.0 0.0 copy-done
  1.1 0.8 %gather_fusion = bf16[256,8,128]{2,1,0:T(8,128)(2,1)S(1)} fusion(bf16[256,8,128]{2,1,0:T(8,128)(2,1)S(1)} %copy-done, s32[1024]{0:T(1024)S(1)} %pad_clamp_fusion), kind=kCustom, calls=%fused_computation | custom fusion | bytes 1049600 | tf_op jit(solution)/shard_map/jit(_take)/gather | solution.py:120
  1.9 0.0 copy-start.4
  1.9 0.0 copy-start.5
  1.9 0.9 %copy.27 = bf16[8,32,8,128]{3,2,0,1:T(8,128)(2,1)} copy(bf16[8,32,8,128]{3,0,2,1:T(8,128)(2,1)S(1)} %bitcast.26) | data formatting | bytes 1048576 | tf_op jit(solution)/shard_map/transpose | solution.py:121
  2.8 7.3 %all-to-all-start = ((bf16[8,32,8,128]{3,2,0,1:T(8,128)(2,1)}), bf16[8,32,8,128]{3,2,0,1:T(8,128)(2,1)S(1)}, u32[]{:S(2)}, u32[]{:S(2)}) async-start(bf16[8,32,8,128]{3,2,0,1:T(8,128)(2,1)} %copy.27), calls=%async_computation | async-start | bytes 1048576 | tf_op jit(solution)/shard_map/all_to_all | solution.py:122
  10.1 0.0 copy-done.4
  10.1 0.0 copy-done.5
  10.1 0.1 fusion.3
  10.2 0.1 broadcast_in_dim.58
  10.3 0.1 convert_element_type.44
  10.4 16.0 %all-to-all-done = bf16[8,32,8,128]{3,2,0,1:T(8,128)(2,1)S(1)} async-done(((bf16[8,32,8,128]{3,2,0,1:T(8,128)(2,1)}), bf16[8,32,8,128]{3,2,0,1:T(8,128)(2,1)S(1)}, u32[]{:S(2)}, u32[]{:S(2)}) %all-to-all-start) | async-done | bytes 524320 | tf_op jit(solution)/shard_map/all_to_all | solution.py:122
  26.5 0.3 multiply_reduce_fusion
  26.9 0.1 sqrt.17
  27.0 0.1 sqrt.16
  27.1 0.1 copy_convert_fusion
  27.1 0.3 divide_convert_fusion
  27.5 0.0 copy-start.2
  27.5 0.8 %fusion.1.q_ref = bf16[2048,128]{1,0:T(8,128)(2,1)S(1)} fusion(f32[8,32,8,128]{3,2,1,0:T(8,128)S(1)} %copy_convert_fusion, f32[2048]{0:T(1024)S(1)} %sqrt.17, pred[2048]{0:T(1024)(128)(4,1)S(1)} %broadcast_in_dim.58, bf16[64,128]{1,0:T(8,128)(2,1)S(1)} %slice_bitcast_fusion), kind=kLoop, calls=%fused_computation.7 | loop fusion | flops 786432 | bytes 1599488 | tf_op jit(solution)/shard_map/jit(_where)/select_n | solution.py:132
  28.3 0.0 copy-start.1
  28.4 0.1 collective-permute-start
  28.5 0.0 copy-done.2
  28.5 0.1 collective-permute-start.2
  28.6 1.8 %collective-permute-done = bf16[2064,128]{1,0:T(8,128)(2,1)S(1)} collective-permute-done((bf16[2064,128]{1,0:T(8,128)(2,1)S(1)}, bf16[2064,128]{1,0:T(8,128)(2,1)S(1)}, u32[]{:S(2)}, u32[]{:S(2)}) %collective-permute-start) | collective-permute-done | bytes 528416 | tf_op jit(solution)/shard_map/ppermute | solution.py:147
  30.4 0.1 eq.39
  30.5 0.1 fusion.4
  30.5 0.1 reshape.84
  30.7 0.0 copy-done.1
  30.7 0.0 slice-start
  30.7 0.9 %broadcast_select_fusion.o_hbm = bf16[2064,128]{1,0:T(8,128)(2,1)} fusion(bf16[2064,128]{1,0:T(8,128)(2,1)S(1)} %collective-permute-done, pred[]{:T(512)S(6)} %eq.32, bf16[16,128]{1,0:T(8,128)(2,1)S(1)} %convert_element_type.44, bf16[2048,128]{1,0:T(8,128)(2,1)S(1)} %fusion.1.q_ref), kind=kLoop, calls=%fused_computation.6 | loop fusion | flops 1320960 | bytes 1585153 | tf_op jit(solution)/shard_map/jit(_where)/select_n | solution.py:158
  31.6 0.0 slice-done
  31.6 0.9 %slice_select_fusion = bf16[32,32,128]{2,1,0:T(8,128)(2,1)} fusion(bf16[32,64,128]{2,1,0:T(8,128)(2,1)S(1)} %bitcast.27, bf16[32,64,128]{2,1,0:T(8,128)(2,1)S(1)} %divide_convert_fusion, pred[32,32]{1,0:T(8,128)(4,1)S(1)} %get-tuple-element.22, pred[]{:T(512)S(6)} %eq.32, bf16[32,128]{1,0:T(8,128)(2,1)S(1)} %slice-done), kind=kLoop, calls=%fused_computation.9 | loop fusion | flops 262144 | bytes 795649 | tf_op jit(solution)/shard_map/jit(_where)/select_n | solution.py:156
  32.5 1.0 %broadcast_in_dim.65.qv_ref = f32[1024,128]{1,0:T(8,128)} broadcast(f32[1024]{0:T(1024)S(1)} %reshape.84), dimensions={0} | broadcast | bytes 528384 | tf_op jit(solution)/shard_map/broadcast_in_dim | solution.py:150
  33.6 4.9 %shard_map.46 = (f32[32,64]{1,0:T(8,128)}, f32[64,32]{1,0:T(8,128)}) custom-call(bf16[1024,128]{1,0:T(8,128)(2,1)} %bitcast.28, bf16[2064,128]{1,0:T(8,128)(2,1)} %broadcast_select_fusion.o_hbm, f32[1024,128]{1,0:T(8,128)} %broadcast_in_dim.65.qv_ref), custom_call_target="tpu_custom_call" | custom-call | flops 536870912 | bytes 786432 | tf_op jit(solution)/shard_map/pallas_call | solution.py:84
  38.4 0.0 copy-start.3
  38.4 1.3 %broadcast_in_dim.66.qv_ref = f32[2048,128]{1,0:T(8,128)} broadcast(f32[2048]{0:T(1024)S(1)} %convert_element_type.45), dimensions={0} | broadcast | bytes 1056768 | tf_op jit(solution)/shard_map/broadcast_in_dim | solution.py:150
  39.7 0.0 copy-done.3
  39.7 0.1 copy.30
  39.8 0.2 collective-permute-start.1
  40.0 1.1 %collective-permute-done.1 = f32[32,64]{0,1:T(8,128)S(1)} collective-permute-done((f32[32,64]{0,1:T(8,128)S(1)}, f32[32,64]{0,1:T(8,128)S(1)}, u32[]{:S(2)}, u32[]{:S(2)}) %collective-permute-start.1) | collective-permute-done | bytes 8224 | tf_op jit(solution)/shard_map/ppermute | solution.py:161
  41.1 0.1 maximum_select_fusion
  41.1 0.1 copy.33
  41.2 2.3 %collective-permute-done.2.o_hbm = bf16[2064,128]{1,0:T(8,128)(2,1)S(1)} collective-permute-done((bf16[2064,128]{1,0:T(8,128)(2,1)S(1)}, bf16[2064,128]{1,0:T(8,128)(2,1)S(1)}, u32[]{:S(2)}, u32[]{:S(2)}) %collective-permute-start.2) | collective-permute-done | bytes 528416 | tf_op jit(solution)/shard_map/ppermute | solution.py:146
  43.5 0.0 copy-start.6
  43.5 0.8 %copy-done.6 = bf16[2064,128]{1,0:T(8,128)(2,1)} copy-done((bf16[2064,128]{1,0:T(8,128)(2,1)}, bf16[2064,128]{1,0:T(8,128)(2,1)S(1)}, u32[]{:S(2)}) %copy-start.6) | copy-done | bytes 528408
  44.4 6.0 %shard_map.47 = (f32[64,64]{1,0:T(8,128)}, f32[64,64]{1,0:T(8,128)}) custom-call(bf16[2048,128]{1,0:T(8,128)(2,1)} %copy-done.1, bf16[2064,128]{1,0:T(8,128)(2,1)} %copy-done.6, f32[2048,128]{1,0:T(8,128)} %broadcast_in_dim.66.qv_ref), custom_call_target="tpu_custom_call" | custom-call | flops 1073741824 | bytes 1048576 | tf_op jit(solution)/shard_map/pallas_call | solution.py:84
  50.4 0.1 collective-permute-start.3
  50.4 4.1 %collective-permute-done.3 = f32[64,64]{1,0:T(8,128)S(1)} collective-permute-done((f32[64,64]{1,0:T(8,128)}, f32[64,64]{1,0:T(8,128)S(1)}, u32[]{:S(2)}, u32[]{:S(2)}) %collective-permute-start.3) | collective-permute-done | bytes 16416 | tf_op jit(solution)/shard_map/ppermute | solution.py:171
  54.5 0.8 %broadcast_select_fusion.2 = (f32[64,64]{1,0:T(8,128)S(1)}, f32[64,64]{1,0:T(8,128)S(1)}) fusion(f32[64,64]{1,0:T(8,128)} %get-tuple-element.17, f32[64,64]{1,0:T(8,128)S(1)} %collective-permute-done.3, pred[]{:T(512)S(6)} %eq.40), kind=kLoop, calls=%fused_computation.24 | loop fusion | flops 8192 | bytes 65537 | tf_op jit(solution)/shard_map/jit(_where)/select_n | solution.py:173
  55.3 0.7 %pad_maximum_fusion.1 = f32[64,192]{1,0:T(8,128)} fusion(f32[64,64]{1,0:T(8,128)S(1)} %get-tuple-element.20, f32[64,64]{1,0:T(8,128)S(1)} %get-tuple-element.19, f32[64,64]{1,0:T(8,128)S(1)} %bitcast_select_fusion), kind=kLoop, calls=%fused_computation.12 | loop fusion | flops 24576 | bytes 98304 | tf_op jit(solution)/shard_map/concatenate | solution.py:175
  (11 shorter events, 0.2 us)
Async XLA Ops:
  0.0 1.1 %copy-start = (bf16[256,8,128]{2,1,0:T(8,128)(2,1)S(1)}, bf16[256,8,128]{2,1,0:T(8,128)(2,1)}, u32[]{:S(2)}) copy-start(bf16[256,8,128]{2,1,0:T(8,128)(2,1)} %param.4) | copy-start | bytes 1572868
  1.9 8.2 %copy-start.4 = (s32[64,32]{0,1:T(8,128)S(1)}, s32[64,32]{0,1:T(8,128)}, u32[]{:S(2)}) copy-start(s32[64,32]{0,1:T(8,128)} %param.7) | copy-start | bytes 24580
  1.9 8.2 %copy-start.5 = (s32[64]{0:T(128)S(1)}, s32[64]{0:T(128)}, u32[]{:S(2)}) copy-start(s32[64]{0:T(128)} %param.6) | copy-start | bytes 772
  2.8 23.7 %all-to-all-start = ((bf16[8,32,8,128]{3,2,0,1:T(8,128)(2,1)}), bf16[8,32,8,128]{3,2,0,1:T(8,128)(2,1)S(1)}, u32[]{:S(2)}, u32[]{:S(2)}) async-start(bf16[8,32,8,128]{3,2,0,1:T(8,128)(2,1)} %copy.27), calls=%async_computation | async-start | bytes 1048576 | tf_op jit(solution)/shard_map/all_to_all | solution.py:122
  27.5 1.0 %copy-start.2 = (bf16[64,128]{1,0:T(8,128)(2,1)}, bf16[64,128]{1,0:T(8,128)(2,1)S(1)}, u32[]{:S(2)}) copy-start(bf16[64,128]{1,0:T(8,128)(2,1)S(1)} %slice_bitcast_fusion) | copy-start | bytes 49156
  28.3 2.3 %copy-start.1 = (bf16[2048,128]{1,0:T(8,128)(2,1)}, bf16[2048,128]{1,0:T(8,128)(2,1)S(1)}, u32[]{:S(2)}) copy-start(bf16[2048,128]{1,0:T(8,128)(2,1)S(1)} %fusion.1.q_ref) | copy-start | bytes 1572868
  28.4 2.0 %collective-permute-start = (bf16[2064,128]{1,0:T(8,128)(2,1)S(1)}, bf16[2064,128]{1,0:T(8,128)(2,1)S(1)}, u32[]{:S(2)}, u32[]{:S(2)}) collective-permute-start(bf16[2064,128]{1,0:T(8,128)(2,1)S(1)} %pad_maximum_fusion), channel_id=1, source_target_pairs={{0,1},{1,0},{2,3},{3,2},{4,5},{5,4},{6,7},{7,6},{8,9},{9,8},{10,11... | collective-permute-start | bytes 1585160 | tf_op jit(solution)/shard_map/ppermute | solution.py:147
  28.5 15.0 %collective-permute-start.2 = (bf16[2064,128]{1,0:T(8,128)(2,1)S(1)}, bf16[2064,128]{1,0:T(8,128)(2,1)S(1)}, u32[]{:S(2)}, u32[]{:S(2)}) collective-permute-start(bf16[2064,128]{1,0:T(8,128)(2,1)S(1)} %pad_maximum_fusion), channel_id=1, source_target_pairs={{0,2},{1,5},{2,6},{3,1},{4,0},{5,7},{6,4},{7,3},{8,10},{9,13},{10,... | collective-permute-start | bytes 1585160 | tf_op jit(solution)/shard_map/ppermute | solution.py:146
  30.7 1.0 %slice-start = ((bf16[64,128]{1,0:T(8,128)(2,1)}), bf16[32,128]{1,0:T(8,128)(2,1)S(1)}, s32[]{:S(2)}) async-start(bf16[64,128]{1,0:T(8,128)(2,1)} %copy-done.2), calls=%async_computation.1 | async-start | bytes 16384 | tf_op jit(solution)/shard_map/slice | solution.py:156
  38.4 1.3 %copy-start.3 = (f32[32,64]{1,0:T(8,128)S(1)}, f32[32,64]{1,0:T(8,128)}, u32[]{:S(2)}) copy-start(f32[32,64]{1,0:T(8,128)} %get-tuple-element.13) | copy-start | bytes 24580
  39.8 1.2 %collective-permute-start.1 = (f32[32,64]{0,1:T(8,128)S(1)}, f32[32,64]{0,1:T(8,128)S(1)}, u32[]{:S(2)}, u32[]{:S(2)}) collective-permute-start(f32[32,64]{0,1:T(8,128)S(1)} %copy.30), channel_id=1, source_target_pairs={{0,1},{1,0},{2,3},{3,2},{4,5},{5,4},{6,7},{7,6},{8,9},{9,8},{10,11... | collective-permute-start | bytes 24584 | tf_op jit(solution)/shard_map/ppermute | solution.py:161
  43.5 0.8 %copy-start.6 = (bf16[2064,128]{1,0:T(8,128)(2,1)}, bf16[2064,128]{1,0:T(8,128)(2,1)S(1)}, u32[]{:S(2)}) copy-start(bf16[2064,128]{1,0:T(8,128)(2,1)S(1)} %collective-permute-done.2.o_hbm) | copy-start | bytes 1585156
  50.4 4.2 %collective-permute-start.3 = (f32[64,64]{1,0:T(8,128)}, f32[64,64]{1,0:T(8,128)S(1)}, u32[]{:S(2)}, u32[]{:S(2)}) collective-permute-start(f32[64,64]{1,0:T(8,128)} %get-tuple-element.18), channel_id=1, source_target_pairs={{2,0},{5,1},{6,2},{1,3},{0,4},{7,5},{4,6},{3,7},{10,8},{13,9},{14,... | collective-permute-start | bytes 49160 | tf_op jit(solution)/shard_map/ppermute | solution.py:171

commit v17 on v15

--- a/solution.py
+++ b/solution.py
@@ -75,6 +75,7 @@
         in_specs=[pl.BlockSpec(memory_space=pltpu.VMEM)] * 3,
         out_specs=(pl.BlockSpec(memory_space=pltpu.VMEM), pl.BlockSpec(memory_space=pltpu.VMEM)),
         scratch_shapes=[pltpu.VMEM((tok_nq, 128), jnp.float32)],
+        compiler_params=pltpu.CompilerParams(vmem_limit_bytes=24 * 1024 * 1024),
         cost_estimate=pl.CostEstimate(
             flops=2 * tok_nq * tok * no * width, transcendentals=0, bytes_accessed=(tok_nq + tok * no) * width * 2
         ),
@@ -147,10 +148,9 @@
 
     tile_z, tile_z_t = chamfer_tile(block.reshape(n_tok, width), own_flags, z_recv, tok)
     tile_back = lax.ppermute(tile_z_t, "pool", back_pairs)
-    via_bit1 = parity == 1
-    col1 = jnp.where(via_bit1, tile_z, tile_back)
-    col2 = jnp.where(via_bit1, tile_back, tile_z)
-    return jnp.concatenate([tile0, col1, col2], axis=1)
+    ready = lax.optimization_barrier(jnp.concatenate([tile0, tile_z, tile_z], axis=1))
+    column = jnp.arange(3 * items_dev, dtype=jnp.int32)[None, :] // items_dev
+    return jnp.where(column == 1 + parity, jnp.tile(tile_back, (1, 3)), ready)
 
 
 def solution(mesh):

time: 55 us -> 52.1 us (0.947)
  waiting for transfers between devices: 26.9 us -> 31.4 us
  Pallas kernels: 7.99 us -> 4.56 us
  local copies, waits for them, and re-layouts: 6.6 us -> 4.12 us
  other arithmetic: 5.33 us -> 3.87 us
    ppermute x1, waiting for transfers between devices: 5.13 us -> 9.7 us  [shards(): z_recv = lax.ppermute(packed, 'pool', send_pairs)]
    pallas_call x2, Pallas kernels: 7.99 us -> 4.56 us  [chamfer_tile(): pl.pallas_call(kernel, out_shape=(jax.ShapeDtypeStruct((nq, no), jnp.floa...]
    broadcast_in_dim x3, local copies, waits for them, and re-layouts: 2.38 us -> 0.59 us  [row_flags(): jnp.broadcast_to(valid_rows.astype(jnp.float32).reshape(-1, 1), (valid_ro...]
    unnamed x14 -> x8, local copies, waits for them, and re-layouts: 0.9 us -> 0.05 us
    concatenate x1, other arithmetic: 0.04 us -> 0.83 us  [shards(): jnp.concatenate([normed.reshape(n_tok, width), bias.reshape(-1, width)],...]
    select_n x1, other arithmetic: 0.94 us -> 0.16 us  [shards(): other_packed = jnp.where(is_a, c_recv, packed)]
    select_n x1, other arithmetic: 0.93 us -> 0.2 us  [shards(): jnp.where(is_a, block[:, :half], c_blk[:, half:]).reshape(tok * half, width)]
    concatenate x1, other arithmetic: 0.72 us -> 0.08 us  [shards(): jnp.concatenate([tile0, tile_z, tile_z], axis=1)]
  transfers between devices with their start and end apart: 5 -> 5, of which waited for: 4 -> 4; matrix products, arithmetic and copies ran while one was open for 9% -> 3% of each run, Pallas kernels for 15% -> 9%
where the time goes in v17:
time: 52.1 us; the launch traced here: 51.8 us
  waiting for transfers between devices  31.4 us (60%)
  starting transfers between devices  7.56 us (15%)
  Pallas kernels  4.56 us (9%)
  local copies, waits for them, and re-layouts  4.12 us (8%)
  other arithmetic  3.87 us (7%)
    all_to_all x1, waiting for transfers between devices, shards(): lax.all_to_all(outgoing, ('enc', 'pool'), split_axis=1, concat_axis=1, ti...  16 us
    ppermute x1, waiting for transfers between devices, shards(): z_recv = lax.ppermute(packed, 'pool', send_pairs)  9.7 us
    all_to_all x1, starting transfers between devices, shards(): lax.all_to_all(outgoing, ('enc', 'pool'), split_axis=1, concat_axis=1, ti...  7.3 us
    pallas_call x2, Pallas kernels, chamfer_tile(): pl.pallas_call(kernel, out_shape=(jax.ShapeDtypeStruct((nq, no), jnp.floa...  4.56 us
    ppermute x1, waiting for transfers between devices, shards(): tile_back = lax.ppermute(tile_z_t, 'pool', back_pairs)  3.61 us
    ppermute x1, waiting for transfers between devices, shards(): c_recv = lax.ppermute(packed, 'pool', chip_pairs)  2.02 us
  transfers between devices with their start and end apart: 5, of which 4 were waited for; matrix products, arithmetic and copies ran while one was open for 3% of the time, Pallas kernels for 9%

profile of v17, /device:TPU:0, one launch (start us, length us, event | category | flops | bytes accessed | tf_op | source)
XLA Modules:
  0.0 51.8 jit_solution(10006402940691303984)
XLA Ops:
  0.0 0.0 copy-start
  0.0 0.8 %reshape.122 = s32[32,8,8]{2,1,0:T(8,128)S(1)} reshape(s32[2048]{0:T(1024)} %param.5) | data formatting | bytes 16384 | tf_op jit(solution)/shard_map/reshape | solution.py:98
  0.9 0.1 subtract_reduce_fusion
  0.9 0.1 reshape.130
  1.0 0.0 copy-done
  1.1 0.8 %gather_fusion = bf16[256,8,128]{2,1,0:T(8,128)(2,1)S(1)} fusion(bf16[256,8,128]{2,1,0:T(8,128)(2,1)S(1)} %copy-done, s32[1024]{0:T(1024)S(1)} %pad_clamp_fusion), kind=kCustom, calls=%fused_computation | custom fusion | bytes 1049600 | tf_op jit(solution)/shard_map/jit(_take)/gather | solution.py:100
  1.9 0.0 copy-start.2
  1.9 0.0 copy-start.3
  1.9 0.9 %copy.31 = bf16[8,32,8,128]{3,2,0,1:T(8,128)(2,1)} copy(bf16[8,32,8,128]{3,0,2,1:T(8,128)(2,1)S(1)} %bitcast.28) | data formatting | bytes 1048576 | tf_op jit(solution)/shard_map/transpose | solution.py:101
  2.8 7.3 %all-to-all-start = ((bf16[8,32,8,128]{3,2,0,1:T(8,128)(2,1)}), bf16[8,32,8,128]{3,2,0,1:T(8,128)(2,1)S(1)}, u32[]{:S(2)}, u32[]{:S(2)}) async-start(bf16[8,32,8,128]{3,2,0,1:T(8,128)(2,1)} %copy.31), calls=%async_computation | async-start | bytes 1048576 | tf_op jit(solution)/shard_map/all_to_all | solution.py:102
  10.1 0.0 copy-done.2
  10.1 0.0 copy-done.3
  10.1 0.1 fusion.3
  10.2 0.1 broadcast_in_dim.64
  10.3 0.1 convert_element_type.44
  10.4 16.0 %all-to-all-done = bf16[8,32,8,128]{3,2,0,1:T(8,128)(2,1)S(1)} async-done(((bf16[8,32,8,128]{3,2,0,1:T(8,128)(2,1)}), bf16[8,32,8,128]{3,2,0,1:T(8,128)(2,1)S(1)}, u32[]{:S(2)}, u32[]{:S(2)}) %all-to-all-start) | async-done | bytes 524320 | tf_op jit(solution)/shard_map/all_to_all | solution.py:102
  26.5 0.3 multiply_reduce_fusion
  26.9 0.1 sqrt.16
  27.0 0.1 sqrt.17
  27.1 0.1 copy_convert_fusion
  27.1 0.3 divide_convert_fusion
  27.5 0.0 copy-start.1
  27.5 0.8 %fusion.1.q_ref = bf16[2048,128]{1,0:T(8,128)(2,1)S(1)} fusion(f32[8,32,8,128]{3,2,1,0:T(8,128)S(1)} %copy_convert_fusion, f32[2048]{0:T(1024)S(1)} %sqrt.16, pred[2048]{0:T(1024)(128)(4,1)S(1)} %broadcast_in_dim.64, bf16[64,128]{1,0:T(8,128)(2,1)S(1)} %slice_bitcast_fusion), kind=kLoop, calls=%fused_computation.7 | loop fusion | flops 786432 | bytes 1599488 | tf_op jit(solution)/shard_map/jit(_where)/select_n | solution.py:112
  28.3 0.8 %pad_maximum_fusion = bf16[2064,128]{1,0:T(8,128)(2,1)} fusion(bf16[16,128]{1,0:T(8,128)(2,1)S(1)} %convert_element_type.44, bf16[2048,128]{1,0:T(8,128)(2,1)S(1)} %fusion.1.q_ref), kind=kLoop, calls=%fused_computation.5 | loop fusion | flops 1056768 | bytes 1056768 | tf_op jit(solution)/shard_map/concatenate | solution.py:113
  29.2 0.0 collective-permute-start.1
  29.2 0.1 collective-permute-start
  29.3 0.0 copy-done.1
  29.3 0.0 slice-start
  29.3 2.0 %collective-permute-done.1 = bf16[2064,128]{1,0:T(8,128)(2,1)S(1)} collective-permute-done((bf16[2064,128]{1,0:T(8,128)(2,1)}, bf16[2064,128]{1,0:T(8,128)(2,1)S(1)}, u32[]{:S(2)}, u32[]{:S(2)}) %collective-permute-start.1) | collective-permute-done | bytes 528416 | tf_op jit(solution)/shard_map/ppermute | solution.py:127
  31.3 0.2 broadcast_select_fusion.o_ref
  31.5 0.1 eq.49
  31.6 0.1 fusion.4
  31.6 0.1 reshape.127
  31.8 0.0 slice-done
  31.8 0.2 slice_select_fusion
  32.0 0.2 broadcast_in_dim.75.qv_ref
  32.2 2.0 %shard_map.46 = (f32[32,64]{1,0:T(8,128)S(1)}, f32[64,32]{1,0:T(8,128)}) custom-call(bf16[1024,128]{1,0:T(8,128)(2,1)S(1)} %bitcast.26, bf16[2064,128]{1,0:T(8,128)(2,1)S(1)} %broadcast_select_fusion.o_ref, f32[1024,128]{1,0:T(8,128)S(1)} %broadcast_in_dim.75.qv_ref), custom_call_target="tpu_custom_call" | custom-call | flops 536870912 | bytes 786432 | tf_op jit(solution)/shard_map/pallas_call | solution.py:72
  34.2 0.3 broadcast_in_dim.76.qv_ref
  34.5 0.1 copy.35
  34.6 0.2 collective-permute-start.3
  34.8 9.7 %collective-permute-done.o_ref = bf16[2064,128]{1,0:T(8,128)(2,1)S(1)} collective-permute-done((bf16[2064,128]{1,0:T(8,128)(2,1)}, bf16[2064,128]{1,0:T(8,128)(2,1)S(1)}, u32[]{:S(2)}, u32[]{:S(2)}) %collective-permute-start) | collective-permute-done | bytes 528416 | tf_op jit(solution)/shard_map/ppermute | solution.py:126
  44.5 2.5 %shard_map.47 = (f32[64,64]{1,0:T(8,128)S(1)}, f32[64,64]{1,0:T(8,128)S(1)}) custom-call(bf16[2048,128]{1,0:T(8,128)(2,1)S(1)} %fusion.1.q_ref, bf16[2064,128]{1,0:T(8,128)(2,1)S(1)} %collective-permute-done.o_ref, f32[2048,128]{1,0:T(8,128)S(1)} %broadcast_in_dim.76.qv_ref), custom_call_target="tpu_custom_call" | custom-call | flops 1073741824 | bytes 1048576 | tf_op jit(solution)/shard_map/pallas_call | solution.py:72
  47.0 0.0 collective-permute-start.2
  47.0 0.0 collective-permute-done.3
  47.1 0.1 maximum_select_fusion
  47.1 0.1 copy.38
  47.2 0.1 pad_maximum_fusion.1
  47.3 3.6 %collective-permute-done.2 = f32[64,64]{1,0:T(8,128)S(1)} collective-permute-done((f32[64,64]{1,0:T(8,128)S(1)}, f32[64,64]{1,0:T(8,128)S(1)}, u32[]{:S(2)}, u32[]{:S(2)}) %collective-permute-start.2) | collective-permute-done | bytes 16416 | tf_op jit(solution)/shard_map/ppermute | solution.py:150
  50.9 0.1 copy.33
  51.0 0.1 copy.39
  51.1 0.6 %broadcast_select_fusion.1 = f32[64,192]{1,0:T(8,128)} fusion(f32[64,192]{1,0:T(8,128)S(1)} %copy.39, f32[64,192]{1,0:T(8,128)S(1)} %pad_maximum_fusion.1, pred[192]{0:T(512)(128)(4,1)S(1)} %fusion.5), kind=kLoop, calls=%fused_computation.15 | loop fusion | flops 12288 | bytes 147648 | tf_op jit(solution)/shard_map/jit(_where)/select_n | solution.py:153
  (12 shorter events, 0.1 us)
Async XLA Ops:
  0.0 1.1 %copy-start = (bf16[256,8,128]{2,1,0:T(8,128)(2,1)S(1)}, bf16[256,8,128]{2,1,0:T(8,128)(2,1)}, u32[]{:S(2)}) copy-start(bf16[256,8,128]{2,1,0:T(8,128)(2,1)} %param.4) | copy-start | bytes 1572868
  1.9 8.2 %copy-start.2 = (s32[64,32]{0,1:T(8,128)S(1)}, s32[64,32]{0,1:T(8,128)}, u32[]{:S(2)}) copy-start(s32[64,32]{0,1:T(8,128)} %param.7) | copy-start | bytes 24580
  1.9 8.2 %copy-start.3 = (s32[64]{0:T(128)S(1)}, s32[64]{0:T(128)}, u32[]{:S(2)}) copy-start(s32[64]{0:T(128)} %param.6) | copy-start | bytes 772
  2.8 23.7 %all-to-all-start = ((bf16[8,32,8,128]{3,2,0,1:T(8,128)(2,1)}), bf16[8,32,8,128]{3,2,0,1:T(8,128)(2,1)S(1)}, u32[]{:S(2)}, u32[]{:S(2)}) async-start(bf16[8,32,8,128]{3,2,0,1:T(8,128)(2,1)} %copy.31), calls=%async_computation | async-start | bytes 1048576 | tf_op jit(solution)/shard_map/all_to_all | solution.py:102
  27.5 1.7 %copy-start.1 = (bf16[64,128]{1,0:T(8,128)(2,1)}, bf16[64,128]{1,0:T(8,128)(2,1)S(1)}, u32[]{:S(2)}) copy-start(bf16[64,128]{1,0:T(8,128)(2,1)S(1)} %slice_bitcast_fusion) | copy-start | bytes 49156
  29.2 2.1 %collective-permute-start.1 = (bf16[2064,128]{1,0:T(8,128)(2,1)}, bf16[2064,128]{1,0:T(8,128)(2,1)S(1)}, u32[]{:S(2)}, u32[]{:S(2)}) collective-permute-start(bf16[2064,128]{1,0:T(8,128)(2,1)} %pad_maximum_fusion), channel_id=1, source_target_pairs={{0,1},{1,0},{2,3},{3,2},{4,5},{5,4},{6,7},{7,6},{8,9},{9,8},{10,11... | collective-permute-start | bytes 1585160 | tf_op jit(solution)/shard_map/ppermute | solution.py:127
  29.2 15.3 %collective-permute-start = (bf16[2064,128]{1,0:T(8,128)(2,1)}, bf16[2064,128]{1,0:T(8,128)(2,1)S(1)}, u32[]{:S(2)}, u32[]{:S(2)}) collective-permute-start(bf16[2064,128]{1,0:T(8,128)(2,1)} %pad_maximum_fusion), channel_id=1, source_target_pairs={{0,2},{1,5},{2,6},{3,1},{4,0},{5,7},{6,4},{7,3},{8,10},{9,13},{10,... | collective-permute-start | bytes 1585160 | tf_op jit(solution)/shard_map/ppermute | solution.py:126
  29.3 2.5 %slice-start = ((bf16[64,128]{1,0:T(8,128)(2,1)}), bf16[32,128]{1,0:T(8,128)(2,1)S(1)}, s32[]{:S(2)}) async-start(bf16[64,128]{1,0:T(8,128)(2,1)} %copy-done.1), calls=%async_computation.1 | async-start | bytes 16384 | tf_op jit(solution)/shard_map/slice | solution.py:136
  34.6 12.4 %collective-permute-start.3 = (f32[32,64]{0,1:T(8,128)S(1)}, f32[32,64]{0,1:T(8,128)S(1)}, u32[]{:S(2)}, u32[]{:S(2)}) collective-permute-start(f32[32,64]{0,1:T(8,128)S(1)} %copy.35), channel_id=1, source_target_pairs={{0,1},{1,0},{2,3},{3,2},{4,5},{5,4},{6,7},{7,6},{8,9},{9,8},{10,11... | collective-permute-start | bytes 24584 | tf_op jit(solution)/shard_map/ppermute | solution.py:141
  47.0 3.9 %collective-permute-start.2 = (f32[64,64]{1,0:T(8,128)S(1)}, f32[64,64]{1,0:T(8,128)S(1)}, u32[]{:S(2)}, u32[]{:S(2)}) collective-permute-start(f32[64,64]{1,0:T(8,128)S(1)} %get-tuple-element.12), channel_id=1, source_target_pairs={{2,0},{5,1},{6,2},{1,3},{0,4},{7,5},{4,6},{3,7},{10,8},{13,9},{14,... | collective-permute-start | bytes 49160 | tf_op jit(solution)/shard_map/ppermute | solution.py:150

commit v18 on v17

--- a/solution.py
+++ b/solution.py
@@ -36,7 +36,7 @@
 
 
 def _chamfer_kernel(tok, nq, no, cw, q_ref, o_ref, qv_ref, out_ref, out_t_ref, fm_ref):
-    q = q_ref[...]
+    q = q_ref[0:tok * nq, :]
     n_rows = tok * no // 128
     flags = o_ref[tok * no:tok * no + n_rows, :].astype(jnp.float32)
     acc_b = jnp.zeros((nq, 128), jnp.float32)
@@ -64,7 +64,7 @@
 
 
 def chamfer_tile(query, query_valid, other_packed, tok):
-    tok_nq, width = query.shape
+    tok_nq, width = query_valid.shape[0], query.shape[1]
     nq = tok_nq // tok
     no = 64
     cw = 512
@@ -146,7 +146,7 @@
     )
     tile0 = jnp.where(is_a, joined, joined.T)
 
-    tile_z, tile_z_t = chamfer_tile(block.reshape(n_tok, width), own_flags, z_recv, tok)
+    tile_z, tile_z_t = chamfer_tile(packed, own_flags, z_recv, tok)
     tile_back = lax.ppermute(tile_z_t, "pool", back_pairs)
     ready = lax.optimization_barrier(jnp.concatenate([tile0, tile_z, tile_z], axis=1))
     column = jnp.arange(3 * items_dev, dtype=jnp.int32)[None, :] // items_dev

time: 52.1 us -> 51.3 us (0.985)
  waiting for transfers between devices: 31.4 us -> 28.6 us
  local copies, waits for them, and re-layouts: 4.12 us -> 5.16 us
  other arithmetic: 3.87 us -> 4.78 us
    ppermute x1, waiting for transfers between devices: 9.7 us -> 6.98 us  [shards(): z_recv = lax.ppermute(packed, 'pool', send_pairs)]
    slice x1, local copies, waits for them, and re-layouts: 0.03 us -> 1.08 us  [shards(): c_blk = c_recv[:n_tok].reshape(tok, items_dev, width)]
    select_n x1, other arithmetic: 0.16 us -> 1.19 us  [shards(): other_packed = jnp.where(is_a, c_recv, packed)]
    concatenate x1, other arithmetic: 0.83 us -> 0.04 us  [shards(): jnp.concatenate([normed.reshape(n_tok, width), bias.reshape(-1, width)],...]
    eq x1, other arithmetic: 0.01 us -> 0.68 us  [shards(): c_valid = c_recv[n_tok:].reshape(tok, items_dev) == 0]
  transfers between devices with their start and end apart: 5 -> 5, of which waited for: 4 -> 4; matrix products, arithmetic and copies ran while one was open for 3% -> 9% of each run, Pallas kernels for 9% -> 9%
where the time goes in v18:
time: 51.3 us; the launch traced here: 50.9 us
  waiting for transfers between devices  28.6 us (56%)
  starting transfers between devices  7.5 us (15%)
  local copies, waits for them, and re-layouts  5.16 us (10%)
  other arithmetic  4.78 us (9%)
  Pallas kernels  4.61 us (9%)
    all_to_all x1, waiting for transfers between devices, shards(): lax.all_to_all(outgoing, ('enc', 'pool'), split_axis=1, concat_axis=1, ti...  16 us
    all_to_all x1, starting transfers between devices, shards(): lax.all_to_all(outgoing, ('enc', 'pool'), split_axis=1, concat_axis=1, ti...  7.29 us
    ppermute x1, waiting for transfers between devices, shards(): z_recv = lax.ppermute(packed, 'pool', send_pairs)  6.98 us
    pallas_call x2, Pallas kernels, chamfer_tile(): pl.pallas_call(kernel, out_shape=(jax.ShapeDtypeStruct((nq, no), jnp.floa...  4.61 us
    ppermute x1, waiting for transfers between devices, shards(): tile_back = lax.ppermute(tile_z_t, 'pool', back_pairs)  3.61 us
    ppermute x1, waiting for transfers between devices, shards(): c_recv = lax.ppermute(packed, 'pool', chip_pairs)  1.91 us
    select_n x1, other arithmetic, shards(): other_packed = jnp.where(is_a, c_recv, packed)  1.19 us
    slice x1, local copies, waits for them, and re-layouts, shards(): c_blk = c_recv[:n_tok].reshape(tok, items_dev, width)  1.08 us
  transfers between devices with their start and end apart: 5, of which 4 were waited for; matrix products, arithmetic and copies ran while one was open for 9% of the time, Pallas kernels for 9%

profile of v18, /device:TPU:0, one launch (start us, length us, event | category | flops | bytes accessed | tf_op | source)
XLA Modules:
  0.0 50.9 jit_solution(4082417704410064211)
XLA Ops:
  0.0 0.0 copy-start
  0.0 0.8 %reshape.122 = s32[32,8,8]{2,1,0:T(8,128)S(1)} reshape(s32[2048]{0:T(1024)} %param.5) | data formatting | bytes 16384 | tf_op jit(solution)/shard_map/reshape | solution.py:98
  0.9 0.1 subtract_reduce_fusion
  0.9 0.1 reshape.130
  1.0 0.0 copy-done
  1.1 0.8 %gather_fusion = bf16[256,8,128]{2,1,0:T(8,128)(2,1)S(1)} fusion(bf16[256,8,128]{2,1,0:T(8,128)(2,1)S(1)} %copy-done, s32[1024]{0:T(1024)S(1)} %pad_clamp_fusion), kind=kCustom, calls=%fused_computation | custom fusion | bytes 1049600 | tf_op jit(solution)/shard_map/jit(_take)/gather | solution.py:100
  1.9 0.0 copy-start.2
  1.9 0.0 copy-start.3
  1.9 0.9 %copy.31 = bf16[8,32,8,128]{3,2,0,1:T(8,128)(2,1)} copy(bf16[8,32,8,128]{3,0,2,1:T(8,128)(2,1)S(1)} %bitcast.28) | data formatting | bytes 1048576 | tf_op jit(solution)/shard_map/transpose | solution.py:101
  2.8 7.3 %all-to-all-start = ((bf16[8,32,8,128]{3,2,0,1:T(8,128)(2,1)}), bf16[8,32,8,128]{3,2,0,1:T(8,128)(2,1)S(1)}, u32[]{:S(2)}, u32[]{:S(2)}) async-start(bf16[8,32,8,128]{3,2,0,1:T(8,128)(2,1)} %copy.31), calls=%async_computation | async-start | bytes 1048576 | tf_op jit(solution)/shard_map/all_to_all | solution.py:102
  10.1 0.0 copy-done.2
  10.1 0.0 copy-done.3
  10.1 0.1 fusion.3
  10.2 0.1 broadcast_in_dim.64
  10.3 0.1 convert_element_type.44
  10.4 16.0 %all-to-all-done = bf16[8,32,8,128]{3,2,0,1:T(8,128)(2,1)S(1)} async-done(((bf16[8,32,8,128]{3,2,0,1:T(8,128)(2,1)}), bf16[8,32,8,128]{3,2,0,1:T(8,128)(2,1)S(1)}, u32[]{:S(2)}, u32[]{:S(2)}) %all-to-all-start) | async-done | bytes 524320 | tf_op jit(solution)/shard_map/all_to_all | solution.py:102
  26.5 0.3 multiply_reduce_fusion
  26.9 0.1 sqrt.16
  27.0 0.1 sqrt.17
  27.1 0.1 copy_convert_fusion
  27.1 0.3 divide_convert_fusion
  27.5 0.0 copy-start.1
  27.5 0.8 %fusion.1 = bf16[2048,128]{1,0:T(8,128)(2,1)S(1)} fusion(f32[8,32,8,128]{3,2,1,0:T(8,128)S(1)} %copy_convert_fusion, f32[2048]{0:T(1024)S(1)} %sqrt.16, pred[2048]{0:T(1024)(128)(4,1)S(1)} %broadcast_in_dim.64, bf16[64,128]{1,0:T(8,128)(2,1)S(1)} %slice_bitcast_fusion), kind=kLoop, calls=%fused_computation.7 | loop fusion | flops 786432 | bytes 1599488 | tf_op jit(solution)/shard_map/jit(_where)/select_n | solution.py:112
  28.4 0.1 collective-permute-start.1
  28.5 0.0 copy-done.1
  28.5 0.0 slice-start
  28.5 0.1 collective-permute-start
  28.6 1.9 %collective-permute-done.1 = bf16[2064,128]{1,0:T(8,128)(2,1)} collective-permute-done((bf16[2064,128]{1,0:T(8,128)(2,1)S(1)}, bf16[2064,128]{1,0:T(8,128)(2,1)}, u32[]{:S(2)}, u32[]{:S(2)}) %collective-permute-start.1) | collective-permute-done | bytes 528416 | tf_op jit(solution)/shard_map/ppermute | solution.py:127
  30.5 1.2 %broadcast_select_fusion.o_ref = bf16[2064,128]{1,0:T(8,128)(2,1)S(1)} fusion(bf16[2064,128]{1,0:T(8,128)(2,1)} %collective-permute-done.1, pred[]{:T(512)S(6)} %eq.46, bf16[16,128]{1,0:T(8,128)(2,1)S(1)} %convert_element_type.44, bf16[2048,128]{1,0:T(8,128)(2,1)S(1)} %fusion.1), kind=kLoop, calls=%fused_computation.6 | loop fusion | flops 1320960 | bytes 1585153 | tf_op jit(solution)/shard_map/jit(_where)/select_n | solution.py:138
  31.7 0.7 %slice_compare_fusion = pred[16,128]{1,0:T(8,128)(4,1)S(1)} fusion(bf16[2064,128]{1,0:T(8,128)(2,1)} %collective-permute-done.1), kind=kLoop, calls=%fused_computation.24 | loop fusion | flops 2048 | bytes 6144 | tf_op jit(solution)/shard_map/eq | solution.py:135
  32.4 0.1 eq.49
  32.4 0.1 fusion.4
  32.5 0.1 reshape.127
  32.6 1.1 %slice.34 = bf16[2048,128]{1,0:T(8,128)(2,1)S(1)} slice(bf16[2064,128]{1,0:T(8,128)(2,1)} %collective-permute-done.1), slice={[0:2048], [0:128]} | slice | bytes 1048576 | tf_op jit(solution)/shard_map/slice | solution.py:134
  33.7 0.0 slice-done
  33.7 0.2 slice_select_fusion
  33.9 0.2 broadcast_in_dim.75.qv_ref
  34.1 2.0 %shard_map.46 = (f32[32,64]{1,0:T(8,128)S(1)}, f32[64,32]{1,0:T(8,128)}) custom-call(bf16[1024,128]{1,0:T(8,128)(2,1)S(1)} %bitcast.26, bf16[2064,128]{1,0:T(8,128)(2,1)S(1)} %broadcast_select_fusion.o_ref, f32[1024,128]{1,0:T(8,128)S(1)} %broadcast_in_dim.75.qv_ref), custom_call_target="tpu_custom_call" | custom-call | flops 536870912 | bytes 786432 | tf_op jit(solution)/shard_map/pallas_call | solution.py:72
  36.1 0.3 broadcast_in_dim.76.qv_ref
  36.5 0.1 copy.35
  36.5 0.0 collective-permute-start.3
  36.6 7.0 %collective-permute-done.o_ref = bf16[2064,128]{1,0:T(8,128)(2,1)S(1)} collective-permute-done((bf16[2064,128]{1,0:T(8,128)(2,1)S(1)}, bf16[2064,128]{1,0:T(8,128)(2,1)S(1)}, u32[]{:S(2)}, u32[]{:S(2)}) %collective-permute-start) | collective-permute-done | bytes 528416 | tf_op jit(solution)/shard_map/ppermute | solution.py:126
  43.6 2.6 %shard_map.47 = (f32[64,64]{1,0:T(8,128)S(1)}, f32[64,64]{1,0:T(8,128)S(1)}) custom-call(bf16[2064,128]{1,0:T(8,128)(2,1)S(1)} %pad_maximum_fusion.q_ref, bf16[2064,128]{1,0:T(8,128)(2,1)S(1)} %collective-permute-done.o_ref, f32[2048,128]{1,0:T(8,128)S(1)} %broadcast_in_dim.76.qv_ref), custom_call_target="tpu_custom_call" | custom-call | flops 1073741824 | bytes 1048576 | tf_op jit(solution)/shard_map/pallas_call | solution.py:72
  46.2 0.0 collective-permute-start.2
  46.2 0.0 collective-permute-done.3
  46.2 0.1 maximum_select_fusion
  46.3 0.1 copy.38
  46.4 0.1 pad_maximum_fusion.1
  46.5 3.6 %collective-permute-done.2 = f32[64,64]{1,0:T(8,128)S(1)} collective-permute-done((f32[64,64]{1,0:T(8,128)S(1)}, f32[64,64]{1,0:T(8,128)S(1)}, u32[]{:S(2)}, u32[]{:S(2)}) %collective-permute-start.2) | collective-permute-done | bytes 16416 | tf_op jit(solution)/shard_map/ppermute | solution.py:150
  50.1 0.1 copy.33
  50.2 0.1 copy.39
  50.3 0.6 %broadcast_select_fusion.1 = f32[64,192]{1,0:T(8,128)} fusion(f32[64,192]{1,0:T(8,128)S(1)} %copy.39, f32[64,192]{1,0:T(8,128)S(1)} %pad_maximum_fusion.1, pred[192]{0:T(512)(128)(4,1)S(1)} %fusion.5), kind=kLoop, calls=%fused_computation.15 | loop fusion | flops 12288 | bytes 147648 | tf_op jit(solution)/shard_map/jit(_where)/select_n | solution.py:153
  (11 shorter events, 0.1 us)
Async XLA Ops:
  0.0 1.1 %copy-start = (bf16[256,8,128]{2,1,0:T(8,128)(2,1)S(1)}, bf16[256,8,128]{2,1,0:T(8,128)(2,1)}, u32[]{:S(2)}) copy-start(bf16[256,8,128]{2,1,0:T(8,128)(2,1)} %param.4) | copy-start | bytes 1572868
  1.9 8.2 %copy-start.2 = (s32[64,32]{0,1:T(8,128)S(1)}, s32[64,32]{0,1:T(8,128)}, u32[]{:S(2)}) copy-start(s32[64,32]{0,1:T(8,128)} %param.7) | copy-start | bytes 24580
  1.9 8.2 %copy-start.3 = (s32[64]{0:T(128)S(1)}, s32[64]{0:T(128)}, u32[]{:S(2)}) copy-start(s32[64]{0:T(128)} %param.6) | copy-start | bytes 772
  2.8 23.7 %all-to-all-start = ((bf16[8,32,8,128]{3,2,0,1:T(8,128)(2,1)}), bf16[8,32,8,128]{3,2,0,1:T(8,128)(2,1)S(1)}, u32[]{:S(2)}, u32[]{:S(2)}) async-start(bf16[8,32,8,128]{3,2,0,1:T(8,128)(2,1)} %copy.31), calls=%async_computation | async-start | bytes 1048576 | tf_op jit(solution)/shard_map/all_to_all | solution.py:102
  27.5 1.0 %copy-start.1 = (bf16[64,128]{1,0:T(8,128)(2,1)}, bf16[64,128]{1,0:T(8,128)(2,1)S(1)}, u32[]{:S(2)}) copy-start(bf16[64,128]{1,0:T(8,128)(2,1)S(1)} %slice_bitcast_fusion) | copy-start | bytes 49156
  28.4 2.1 %collective-permute-start.1 = (bf16[2064,128]{1,0:T(8,128)(2,1)S(1)}, bf16[2064,128]{1,0:T(8,128)(2,1)}, u32[]{:S(2)}, u32[]{:S(2)}) collective-permute-start(bf16[2064,128]{1,0:T(8,128)(2,1)S(1)} %pad_maximum_fusion.q_ref), channel_id=1, source_target_pairs={{0,1},{1,0},{2,3},{3,2},{4,5},{5,4},{6,7},{7,6},{8,9},{9,8},{10,11... | collective-permute-start | bytes 1585160 | tf_op jit(solution)/shard_map/ppermute | solution.py:127
  28.5 5.2 %slice-start = ((bf16[64,128]{1,0:T(8,128)(2,1)}), bf16[32,128]{1,0:T(8,128)(2,1)S(1)}, s32[]{:S(2)}) async-start(bf16[64,128]{1,0:T(8,128)(2,1)} %copy-done.1), calls=%async_computation.1 | async-start | bytes 16384 | tf_op jit(solution)/shard_map/slice | solution.py:136
  28.5 15.1 %collective-permute-start = (bf16[2064,128]{1,0:T(8,128)(2,1)S(1)}, bf16[2064,128]{1,0:T(8,128)(2,1)S(1)}, u32[]{:S(2)}, u32[]{:S(2)}) collective-permute-start(bf16[2064,128]{1,0:T(8,128)(2,1)S(1)} %pad_maximum_fusion.q_ref), channel_id=1, source_target_pairs={{0,2},{1,5},{2,6},{3,1},{4,0},{5,7},{6,4},{7,3},{8,10},{9,13},{10,... | collective-permute-start | bytes 1585160 | tf_op jit(solution)/shard_map/ppermute | solution.py:126
  36.5 9.6 %collective-permute-start.3 = (f32[32,64]{0,1:T(8,128)S(1)}, f32[32,64]{0,1:T(8,128)S(1)}, u32[]{:S(2)}, u32[]{:S(2)}) collective-permute-start(f32[32,64]{0,1:T(8,128)S(1)} %copy.35), channel_id=1, source_target_pairs={{0,1},{1,0},{2,3},{3,2},{4,5},{5,4},{6,7},{7,6},{8,9},{9,8},{10,11... | collective-permute-start | bytes 24584 | tf_op jit(solution)/shard_map/ppermute | solution.py:141
  46.2 3.9 %collective-permute-start.2 = (f32[64,64]{1,0:T(8,128)S(1)}, f32[64,64]{1,0:T(8,128)S(1)}, u32[]{:S(2)}, u32[]{:S(2)}) collective-permute-start(f32[64,64]{1,0:T(8,128)S(1)} %get-tuple-element.12), channel_id=1, source_target_pairs={{2,0},{5,1},{6,2},{1,3},{0,4},{7,5},{4,6},{3,7},{10,8},{13,9},{14,... | collective-permute-start | bytes 49160 | tf_op jit(solution)/shard_map/ppermute | solution.py:150

commit v19 on v18

--- a/solution.py
+++ b/solution.py
@@ -101,15 +101,15 @@
     outgoing = jnp.transpose(outgoing, (2, 0, 1, 3))
     arrived = lax.all_to_all(outgoing, ("enc", "pool"), split_axis=1, concat_axis=1, tiled=True)
     slotted = arrived.reshape(tok, items_dev, width)
+    position = jnp.arange(tok, dtype=jnp.int32)[None, :]
+    valid = (position < lengths[:, None]) & ((position == 0) | (token_mask == 1))
+    valid_tm = jnp.transpose(valid.reshape(items_dev, n_enc, toks), (2, 1, 0)).reshape(tok, items_dev)
+    bias = jnp.where(valid_tm, 0.0, -4.0).astype(jnp.bfloat16)
+    slotted = jnp.where(valid_tm[:, :, None], slotted, slotted[0][None])
     values = slotted.astype(jnp.float32)
     normed = (values / jnp.sqrt(jnp.sum(values * values, axis=-1, keepdims=True) + 1e-06)).astype(
         jnp.bfloat16
     )
-    position = jnp.arange(tok, dtype=jnp.int32)[None, :]
-    valid = (position < lengths[:, None]) & ((position == 0) | (token_mask == 1))
-    valid_tm = jnp.transpose(valid.reshape(items_dev, n_enc, toks), (2, 1, 0)).reshape(tok, items_dev)
-    bias = jnp.where(valid_tm, 0.0, -4.0).astype(jnp.bfloat16)
-    normed = jnp.where(valid_tm[:, :, None], normed, normed[0][None])
     packed = jnp.concatenate([normed.reshape(n_tok, width), bias.reshape(-1, width)], axis=0)
     block = packed[:n_tok].reshape(tok, items_dev, width)
 

time: 51.3 us -> 51.3 us (level)
    select_n x1 -> x0, other arithmetic: 0.8 us -> none  [shards(): normed = jnp.where(valid_tm[:, :, None], normed, normed[0][None])]
  transfers between devices with their start and end apart: 5 -> 5, of which waited for: 4 -> 4; matrix products, arithmetic and copies ran while one was open for 9% -> 10% of each run, Pallas kernels for 9% -> 9%
where the time goes in v19:
time: 51.3 us; the launch traced here: 51 us
  waiting for transfers between devices  28.3 us (55%)
  starting transfers between devices  7.5 us (15%)
  local copies, waits for them, and re-layouts  5.47 us (11%)
  other arithmetic  4.77 us (9%)
  Pallas kernels  4.61 us (9%)
    all_to_all x1, waiting for transfers between devices, shards(): lax.all_to_all(outgoing, ('enc', 'pool'), split_axis=1, concat_axis=1, ti...  15.9 us
    all_to_all x1, starting transfers between devices, shards(): lax.all_to_all(outgoing, ('enc', 'pool'), split_axis=1, concat_axis=1, ti...  7.3 us
    ppermute x1, waiting for transfers between devices, shards(): z_recv = lax.ppermute(packed, 'pool', send_pairs)  6.96 us
    pallas_call x2, Pallas kernels, chamfer_tile(): pl.pallas_call(kernel, out_shape=(jax.ShapeDtypeStruct((nq, no), jnp.floa...  4.61 us
    ppermute x1, waiting for transfers between devices, shards(): tile_back = lax.ppermute(tile_z_t, 'pool', back_pairs)  3.61 us
    ppermute x1, waiting for transfers between devices, shards(): c_recv = lax.ppermute(packed, 'pool', chip_pairs)  1.81 us
    select_n x1, other arithmetic, shards(): other_packed = jnp.where(is_a, c_recv, packed)  1.19 us
    slice x1, local copies, waits for them, and re-layouts, shards(): c_blk = c_recv[:n_tok].reshape(tok, items_dev, width)  1.08 us
  transfers between devices with their start and end apart: 5, of which 4 were waited for; matrix products, arithmetic and copies ran while one was open for 10% of the time, Pallas kernels for 9%

profile of v19, /device:TPU:0, one launch (start us, length us, event | category | flops | bytes accessed | tf_op | source)
XLA Modules:
  0.0 51.0 jit_solution(12228350877411656350)
XLA Ops:
  0.0 0.0 copy-start
  0.0 0.8 %reshape.125 = s32[32,8,8]{2,1,0:T(8,128)S(1)} reshape(s32[2048]{0:T(1024)} %param.5) | data formatting | bytes 16384 | tf_op jit(solution)/shard_map/reshape | solution.py:98
  0.9 0.1 subtract_reduce_fusion
  0.9 0.1 reshape.133
  1.0 0.0 copy-done
  1.1 0.8 %gather_fusion = bf16[256,8,128]{2,1,0:T(8,128)(2,1)S(1)} fusion(bf16[256,8,128]{2,1,0:T(8,128)(2,1)S(1)} %copy-done, s32[1024]{0:T(1024)S(1)} %pad_clamp_fusion), kind=kCustom, calls=%fused_computation | custom fusion | bytes 1049600 | tf_op jit(solution)/shard_map/jit(_take)/gather | solution.py:100
  1.9 0.0 copy-start.2
  1.9 0.0 copy-start.3
  1.9 0.9 %copy.32 = bf16[8,32,8,128]{3,2,0,1:T(8,128)(2,1)} copy(bf16[8,32,8,128]{3,0,2,1:T(8,128)(2,1)S(1)} %bitcast.30) | data formatting | bytes 1048576 | tf_op jit(solution)/shard_map/transpose | solution.py:101
  2.8 7.3 %all-to-all-start = ((bf16[8,32,8,128]{3,2,0,1:T(8,128)(2,1)}), bf16[8,32,8,128]{3,2,0,1:T(8,128)(2,1)S(1)}, u32[]{:S(2)}, u32[]{:S(2)}) async-start(bf16[8,32,8,128]{3,2,0,1:T(8,128)(2,1)} %copy.32), calls=%async_computation | async-start | bytes 1048576 | tf_op jit(solution)/shard_map/all_to_all | solution.py:102
  10.1 0.0 copy-done.2
  10.1 0.0 copy-done.3
  10.1 0.1 fusion.2
  10.2 0.1 broadcast_in_dim.70
  10.3 0.1 broadcast_in_dim.75
  10.5 0.1 convert_element_type.34
  10.5 15.9 %all-to-all-done = bf16[8,32,8,128]{3,2,0,1:T(8,128)(2,1)S(1)} async-done(((bf16[8,32,8,128]{3,2,0,1:T(8,128)(2,1)}), bf16[8,32,8,128]{3,2,0,1:T(8,128)(2,1)S(1)}, u32[]{:S(2)}, u32[]{:S(2)}) %all-to-all-start) | async-done | bytes 524320 | tf_op jit(solution)/shard_map/all_to_all | solution.py:102
  26.5 0.1 copy.33
  26.6 0.0 copy-start.1
  26.6 0.1 broadcast_in_dim.73
  26.7 0.6 %multiply_reduce_fusion = f32[8,32,8]{2,1,0:T(8,128)S(1)} fusion(bf16[8,32,8,128]{3,2,1,0:T(8,128)(2,1)S(1)} %bitcast.29, pred[8,32,8]{2,1,0:T(8,128)(4,1)S(1)} %broadcast_in_dim.75, bf16[8,32,8,128]{3,2,0,1:T(8,128)(2,1)S(1)} %all-to-all-done), kind=kLoop, calls=%fused_computation.2 | loop fusion | flops 1046528 | bytes 1058816 | tf_op jit(solution)/shard_map/reduce_sum | solution.py:110
  27.4 0.1 sqrt.16
  27.5 0.8 %divide_convert_fusion = bf16[2048,128]{1,0:T(8,128)(2,1)S(1)} fusion(bf16[8,32,8,128]{3,2,1,0:T(8,128)(2,1)S(1)} %copy.33, f32[2048]{0:T(1024)S(1)} %sqrt.16, pred[2048]{0:T(1024)(128)(4,1)S(1)} %broadcast_in_dim.70, bf16[64,128]{1,0:T(8,128)(2,1)S(1)} %slice_bitcast_fusion), kind=kLoop, calls=%fused_computation.1 | loop fusion | flops 1048576 | bytes 1075200 | tf_op jit(solution)/shard_map/convert_element_type | solution.py:110
  28.3 0.1 collective-permute-start.1
  28.4 0.0 copy-done.1
  28.5 0.1 sqrt.17
  28.6 0.0 slice-start
  28.6 0.1 collective-permute-start
  28.6 1.8 %collective-permute-done.1 = bf16[2064,128]{1,0:T(8,128)(2,1)} collective-permute-done((bf16[2064,128]{1,0:T(8,128)(2,1)S(1)}, bf16[2064,128]{1,0:T(8,128)(2,1)}, u32[]{:S(2)}, u32[]{:S(2)}) %collective-permute-start.1) | collective-permute-done | bytes 528416 | tf_op jit(solution)/shard_map/ppermute | solution.py:127
  30.4 1.2 %broadcast_select_fusion.o_ref = bf16[2064,128]{1,0:T(8,128)(2,1)S(1)} fusion(bf16[2064,128]{1,0:T(8,128)(2,1)} %collective-permute-done.1, pred[]{:T(512)S(6)} %eq.46, bf16[16,128]{1,0:T(8,128)(2,1)S(1)} %convert_element_type.34, bf16[2048,128]{1,0:T(8,128)(2,1)S(1)} %divide_convert_fusion), kind=kLoop, calls=%fused_computation.4 | loop fusion | flops 1320960 | bytes 1585153 | tf_op jit(solution)/shard_map/jit(_where)/select_n | solution.py:138
  31.6 0.7 %slice_compare_fusion = pred[16,128]{1,0:T(8,128)(4,1)S(1)} fusion(bf16[2064,128]{1,0:T(8,128)(2,1)} %collective-permute-done.1), kind=kLoop, calls=%fused_computation.22 | loop fusion | flops 2048 | bytes 6144 | tf_op jit(solution)/shard_map/eq | solution.py:135
  32.3 0.1 eq.49
  32.4 0.1 fusion.3
  32.5 0.1 reshape.130
  32.5 1.1 %slice.35 = bf16[2048,128]{1,0:T(8,128)(2,1)S(1)} slice(bf16[2064,128]{1,0:T(8,128)(2,1)} %collective-permute-done.1), slice={[0:2048], [0:128]} | slice | bytes 1048576 | tf_op jit(solution)/shard_map/slice | solution.py:134
  33.6 0.0 slice-done
  33.6 0.3 fusion
  34.0 0.2 broadcast_in_dim.84.qv_ref
  34.2 2.0 %shard_map.46 = (f32[32,64]{1,0:T(8,128)S(1)}, f32[64,32]{1,0:T(8,128)}) custom-call(bf16[1024,128]{1,0:T(8,128)(2,1)S(1)} %bitcast.26, bf16[2064,128]{1,0:T(8,128)(2,1)S(1)} %broadcast_select_fusion.o_ref, f32[1024,128]{1,0:T(8,128)S(1)} %broadcast_in_dim.84.qv_ref), custom_call_target="tpu_custom_call" | custom-call | flops 536870912 | bytes 786432 | tf_op jit(solution)/shard_map/pallas_call | solution.py:72
  36.2 0.3 broadcast_in_dim.85.qv_ref
  36.5 0.1 copy.38
  36.6 0.0 collective-permute-start.3
  36.7 7.0 %collective-permute-done.o_ref = bf16[2064,128]{1,0:T(8,128)(2,1)S(1)} collective-permute-done((bf16[2064,128]{1,0:T(8,128)(2,1)S(1)}, bf16[2064,128]{1,0:T(8,128)(2,1)S(1)}, u32[]{:S(2)}, u32[]{:S(2)}) %collective-permute-start) | collective-permute-done | bytes 528416 | tf_op jit(solution)/shard_map/ppermute | solution.py:126
  43.6 2.6 %shard_map.47 = (f32[64,64]{1,0:T(8,128)S(1)}, f32[64,64]{1,0:T(8,128)S(1)}) custom-call(bf16[2064,128]{1,0:T(8,128)(2,1)S(1)} %pad_maximum_fusion.q_ref, bf16[2064,128]{1,0:T(8,128)(2,1)S(1)} %collective-permute-done.o_ref, f32[2048,128]{1,0:T(8,128)S(1)} %broadcast_in_dim.85.qv_ref), custom_call_target="tpu_custom_call" | custom-call | flops 1073741824 | bytes 1048576 | tf_op jit(solution)/shard_map/pallas_call | solution.py:72
  46.2 0.0 collective-permute-start.2
  46.2 0.0 collective-permute-done.3
  46.3 0.1 maximum_select_fusion
  46.3 0.1 copy.41
  46.4 0.1 pad_maximum_fusion.1
  46.5 3.6 %collective-permute-done.2 = f32[64,64]{1,0:T(8,128)S(1)} collective-permute-done((f32[64,64]{1,0:T(8,128)S(1)}, f32[64,64]{1,0:T(8,128)S(1)}, u32[]{:S(2)}, u32[]{:S(2)}) %collective-permute-start.2) | collective-permute-done | bytes 16416 | tf_op jit(solution)/shard_map/ppermute | solution.py:150
  50.1 0.1 copy.36
  50.2 0.1 copy.42
  50.3 0.6 %broadcast_select_fusion.1 = f32[64,192]{1,0:T(8,128)} fusion(f32[64,192]{1,0:T(8,128)S(1)} %copy.42, f32[64,192]{1,0:T(8,128)S(1)} %pad_maximum_fusion.1, pred[192]{0:T(512)(128)(4,1)S(1)} %fusion.4), kind=kLoop, calls=%fused_computation.13 | loop fusion | flops 12288 | bytes 147648 | tf_op jit(solution)/shard_map/jit(_where)/select_n | solution.py:153
  (11 shorter events, 0.1 us)
Async XLA Ops:
  0.0 1.1 %copy-start = (bf16[256,8,128]{2,1,0:T(8,128)(2,1)S(1)}, bf16[256,8,128]{2,1,0:T(8,128)(2,1)}, u32[]{:S(2)}) copy-start(bf16[256,8,128]{2,1,0:T(8,128)(2,1)} %param.4) | copy-start | bytes 1572868
  1.9 8.2 %copy-start.2 = (s32[64,32]{0,1:T(8,128)S(1)}, s32[64,32]{0,1:T(8,128)}, u32[]{:S(2)}) copy-start(s32[64,32]{0,1:T(8,128)} %param.7) | copy-start | bytes 24580
  1.9 8.2 %copy-start.3 = (s32[64]{0:T(128)S(1)}, s32[64]{0:T(128)}, u32[]{:S(2)}) copy-start(s32[64]{0:T(128)} %param.6) | copy-start | bytes 772
  2.8 23.7 %all-to-all-start = ((bf16[8,32,8,128]{3,2,0,1:T(8,128)(2,1)}), bf16[8,32,8,128]{3,2,0,1:T(8,128)(2,1)S(1)}, u32[]{:S(2)}, u32[]{:S(2)}) async-start(bf16[8,32,8,128]{3,2,0,1:T(8,128)(2,1)} %copy.32), calls=%async_computation | async-start | bytes 1048576 | tf_op jit(solution)/shard_map/all_to_all | solution.py:102
  26.6 1.9 %copy-start.1 = (bf16[64,128]{1,0:T(8,128)(2,1)}, bf16[64,128]{1,0:T(8,128)(2,1)S(1)}, u32[]{:S(2)}) copy-start(bf16[64,128]{1,0:T(8,128)(2,1)S(1)} %slice_bitcast_fusion) | copy-start | bytes 49156
  28.3 2.1 %collective-permute-start.1 = (bf16[2064,128]{1,0:T(8,128)(2,1)S(1)}, bf16[2064,128]{1,0:T(8,128)(2,1)}, u32[]{:S(2)}, u32[]{:S(2)}) collective-permute-start(bf16[2064,128]{1,0:T(8,128)(2,1)S(1)} %pad_maximum_fusion.q_ref), channel_id=1, source_target_pairs={{0,1},{1,0},{2,3},{3,2},{4,5},{5,4},{6,7},{7,6},{8,9},{9,8},{10,11... | collective-permute-start | bytes 1585160 | tf_op jit(solution)/shard_map/ppermute | solution.py:127
  28.6 5.1 %slice-start = ((bf16[64,128]{1,0:T(8,128)(2,1)}), bf16[32,128]{1,0:T(8,128)(2,1)S(1)}, s32[]{:S(2)}) async-start(bf16[64,128]{1,0:T(8,128)(2,1)} %copy-done.1), calls=%async_computation.1 | async-start | bytes 16384 | tf_op jit(solution)/shard_map/slice | solution.py:136
  28.6 15.1 %collective-permute-start = (bf16[2064,128]{1,0:T(8,128)(2,1)S(1)}, bf16[2064,128]{1,0:T(8,128)(2,1)S(1)}, u32[]{:S(2)}, u32[]{:S(2)}) collective-permute-start(bf16[2064,128]{1,0:T(8,128)(2,1)S(1)} %pad_maximum_fusion.q_ref), channel_id=1, source_target_pairs={{0,2},{1,5},{2,6},{3,1},{4,0},{5,7},{6,4},{7,3},{8,10},{9,13},{10,... | collective-permute-start | bytes 1585160 | tf_op jit(solution)/shard_map/ppermute | solution.py:126
  36.6 9.6 %collective-permute-start.3 = (f32[32,64]{0,1:T(8,128)S(1)}, f32[32,64]{0,1:T(8,128)S(1)}, u32[]{:S(2)}, u32[]{:S(2)}) collective-permute-start(f32[32,64]{0,1:T(8,128)S(1)} %copy.38), channel_id=1, source_target_pairs={{0,1},{1,0},{2,3},{3,2},{4,5},{5,4},{6,7},{7,6},{8,9},{9,8},{10,11... | collective-permute-start | bytes 24584 | tf_op jit(solution)/shard_map/ppermute | solution.py:141
  46.2 3.9 %collective-permute-start.2 = (f32[64,64]{1,0:T(8,128)S(1)}, f32[64,64]{1,0:T(8,128)S(1)}, u32[]{:S(2)}, u32[]{:S(2)}) collective-permute-start(f32[64,64]{1,0:T(8,128)S(1)} %get-tuple-element.12), channel_id=1, source_target_pairs={{2,0},{5,1},{6,2},{1,3},{0,4},{7,5},{4,6},{3,7},{10,8},{13,9},{14,... | collective-permute-start | bytes 49160 | tf_op jit(solution)/shard_map/ppermute | solution.py:150

commit v20 on v18

--- a/solution.py
+++ b/solution.py
@@ -67,7 +67,7 @@
     tok_nq, width = query_valid.shape[0], query.shape[1]
     nq = tok_nq // tok
     no = 64
-    cw = 512
+    cw = 1024
     kernel = functools.partial(_chamfer_kernel, tok, nq, no, cw)
     return pl.pallas_call(
         kernel,

time: 51.3 us -> 51.4 us (level)
  no operation moved by 1% of the time
where the time goes in v20:
time: 51.4 us; the launch traced here: 51 us
  waiting for transfers between devices  28.5 us (55%)
  starting transfers between devices  7.5 us (15%)
  local copies, waits for them, and re-layouts  5.16 us (10%)
  other arithmetic  4.78 us (9%)
  Pallas kernels  4.75 us (9%)
    all_to_all x1, waiting for transfers between devices, shards(): lax.all_to_all(outgoing, ('enc', 'pool'), split_axis=1, concat_axis=1, ti...  16 us
    all_to_all x1, starting transfers between devices, shards(): lax.all_to_all(outgoing, ('enc', 'pool'), split_axis=1, concat_axis=1, ti...  7.3 us
    ppermute x1, waiting for transfers between devices, shards(): z_recv = lax.ppermute(packed, 'pool', send_pairs)  6.95 us
    pallas_call x2, Pallas kernels, chamfer_tile(): pl.pallas_call(kernel, out_shape=(jax.ShapeDtypeStruct((nq, no), jnp.floa...  4.75 us
    ppermute x1, waiting for transfers between devices, shards(): tile_back = lax.ppermute(tile_z_t, 'pool', back_pairs)  3.61 us
    ppermute x1, waiting for transfers between devices, shards(): c_recv = lax.ppermute(packed, 'pool', chip_pairs)  1.91 us
    select_n x1, other arithmetic, shards(): other_packed = jnp.where(is_a, c_recv, packed)  1.19 us
    slice x1, local copies, waits for them, and re-layouts, shards(): c_blk = c_recv[:n_tok].reshape(tok, items_dev, width)  1.08 us
  transfers between devices with their start and end apart: 5, of which 4 were waited for; matrix products, arithmetic and copies ran while one was open for 9% of the time, Pallas kernels for 9%

profile of v20, /device:TPU:0, one launch (start us, length us, event | category | flops | bytes accessed | tf_op | source)
XLA Modules:
  0.0 51.0 jit_solution(4584695426676372213)
XLA Ops:
  0.0 0.0 copy-start
  0.0 0.8 %reshape.122 = s32[32,8,8]{2,1,0:T(8,128)S(1)} reshape(s32[2048]{0:T(1024)} %param.5) | data formatting | bytes 16384 | tf_op jit(solution)/shard_map/reshape | solution.py:98
  0.9 0.1 subtract_reduce_fusion
  0.9 0.1 reshape.130
  1.0 0.0 copy-done
  1.1 0.8 %gather_fusion = bf16[256,8,128]{2,1,0:T(8,128)(2,1)S(1)} fusion(bf16[256,8,128]{2,1,0:T(8,128)(2,1)S(1)} %copy-done, s32[1024]{0:T(1024)S(1)} %pad_clamp_fusion), kind=kCustom, calls=%fused_computation | custom fusion | bytes 1049600 | tf_op jit(solution)/shard_map/jit(_take)/gather | solution.py:100
  1.9 0.0 copy-start.2
  1.9 0.0 copy-start.3
  1.9 0.9 %copy.31 = bf16[8,32,8,128]{3,2,0,1:T(8,128)(2,1)} copy(bf16[8,32,8,128]{3,0,2,1:T(8,128)(2,1)S(1)} %bitcast.28) | data formatting | bytes 1048576 | tf_op jit(solution)/shard_map/transpose | solution.py:101
  2.8 7.3 %all-to-all-start = ((bf16[8,32,8,128]{3,2,0,1:T(8,128)(2,1)}), bf16[8,32,8,128]{3,2,0,1:T(8,128)(2,1)S(1)}, u32[]{:S(2)}, u32[]{:S(2)}) async-start(bf16[8,32,8,128]{3,2,0,1:T(8,128)(2,1)} %copy.31), calls=%async_computation | async-start | bytes 1048576 | tf_op jit(solution)/shard_map/all_to_all | solution.py:102
  10.1 0.0 copy-done.2
  10.1 0.0 copy-done.3
  10.1 0.1 fusion.3
  10.2 0.1 broadcast_in_dim.64
  10.3 0.1 convert_element_type.44
  10.4 16.0 %all-to-all-done = bf16[8,32,8,128]{3,2,0,1:T(8,128)(2,1)S(1)} async-done(((bf16[8,32,8,128]{3,2,0,1:T(8,128)(2,1)}), bf16[8,32,8,128]{3,2,0,1:T(8,128)(2,1)S(1)}, u32[]{:S(2)}, u32[]{:S(2)}) %all-to-all-start) | async-done | bytes 524320 | tf_op jit(solution)/shard_map/all_to_all | solution.py:102
  26.5 0.3 multiply_reduce_fusion
  26.9 0.1 sqrt.16
  27.0 0.1 sqrt.17
  27.1 0.1 copy_convert_fusion
  27.2 0.3 divide_convert_fusion
  27.5 0.0 copy-start.1
  27.5 0.8 %fusion.1 = bf16[2048,128]{1,0:T(8,128)(2,1)S(1)} fusion(f32[8,32,8,128]{3,2,1,0:T(8,128)S(1)} %copy_convert_fusion, f32[2048]{0:T(1024)S(1)} %sqrt.16, pred[2048]{0:T(1024)(128)(4,1)S(1)} %broadcast_in_dim.64, bf16[64,128]{1,0:T(8,128)(2,1)S(1)} %slice_bitcast_fusion), kind=kLoop, calls=%fused_computation.7 | loop fusion | flops 786432 | bytes 1599488 | tf_op jit(solution)/shard_map/jit(_where)/select_n | solution.py:112
  28.4 0.1 collective-permute-start.1
  28.5 0.0 copy-done.1
  28.5 0.0 slice-start
  28.5 0.1 collective-permute-start
  28.6 1.9 %collective-permute-done.1 = bf16[2064,128]{1,0:T(8,128)(2,1)} collective-permute-done((bf16[2064,128]{1,0:T(8,128)(2,1)S(1)}, bf16[2064,128]{1,0:T(8,128)(2,1)}, u32[]{:S(2)}, u32[]{:S(2)}) %collective-permute-start.1) | collective-permute-done | bytes 528416 | tf_op jit(solution)/shard_map/ppermute | solution.py:127
  30.5 1.2 %broadcast_select_fusion.o_ref = bf16[2064,128]{1,0:T(8,128)(2,1)S(1)} fusion(bf16[2064,128]{1,0:T(8,128)(2,1)} %collective-permute-done.1, pred[]{:T(512)S(6)} %eq.46, bf16[16,128]{1,0:T(8,128)(2,1)S(1)} %convert_element_type.44, bf16[2048,128]{1,0:T(8,128)(2,1)S(1)} %fusion.1), kind=kLoop, calls=%fused_computation.6 | loop fusion | flops 1320960 | bytes 1585153 | tf_op jit(solution)/shard_map/jit(_where)/select_n | solution.py:138
  31.7 0.7 %slice_compare_fusion = pred[16,128]{1,0:T(8,128)(4,1)S(1)} fusion(bf16[2064,128]{1,0:T(8,128)(2,1)} %collective-permute-done.1), kind=kLoop, calls=%fused_computation.24 | loop fusion | flops 2048 | bytes 6144 | tf_op jit(solution)/shard_map/eq | solution.py:135
  32.4 0.1 eq.49
  32.4 0.1 fusion.4
  32.5 0.1 reshape.127
  32.6 1.1 %slice.34 = bf16[2048,128]{1,0:T(8,128)(2,1)S(1)} slice(bf16[2064,128]{1,0:T(8,128)(2,1)} %collective-permute-done.1), slice={[0:2048], [0:128]} | slice | bytes 1048576 | tf_op jit(solution)/shard_map/slice | solution.py:134
  33.7 0.0 slice-done
  33.7 0.2 slice_select_fusion
  33.9 0.2 broadcast_in_dim.75.qv_ref
  34.1 2.1 %shard_map.46 = (f32[32,64]{1,0:T(8,128)S(1)}, f32[64,32]{1,0:T(8,128)}) custom-call(bf16[1024,128]{1,0:T(8,128)(2,1)S(1)} %bitcast.26, bf16[2064,128]{1,0:T(8,128)(2,1)S(1)} %broadcast_select_fusion.o_ref, f32[1024,128]{1,0:T(8,128)S(1)} %broadcast_in_dim.75.qv_ref), custom_call_target="tpu_custom_call" | custom-call | flops 536870912 | bytes 786432 | tf_op jit(solution)/shard_map/pallas_call | solution.py:72
  36.2 0.3 broadcast_in_dim.76.qv_ref
  36.5 0.1 copy.35
  36.6 0.0 collective-permute-start.3
  36.6 6.9 %collective-permute-done.o_ref = bf16[2064,128]{1,0:T(8,128)(2,1)S(1)} collective-permute-done((bf16[2064,128]{1,0:T(8,128)(2,1)S(1)}, bf16[2064,128]{1,0:T(8,128)(2,1)S(1)}, u32[]{:S(2)}, u32[]{:S(2)}) %collective-permute-start) | collective-permute-done | bytes 528416 | tf_op jit(solution)/shard_map/ppermute | solution.py:126
  43.6 2.7 %shard_map.47 = (f32[64,64]{1,0:T(8,128)S(1)}, f32[64,64]{1,0:T(8,128)S(1)}) custom-call(bf16[2064,128]{1,0:T(8,128)(2,1)S(1)} %pad_maximum_fusion.q_ref, bf16[2064,128]{1,0:T(8,128)(2,1)S(1)} %collective-permute-done.o_ref, f32[2048,128]{1,0:T(8,128)S(1)} %broadcast_in_dim.76.qv_ref), custom_call_target="tpu_custom_call" | custom-call | flops 1073741824 | bytes 1048576 | tf_op jit(solution)/shard_map/pallas_call | solution.py:72
  46.3 0.0 collective-permute-start.2
  46.3 0.0 collective-permute-done.3
  46.3 0.1 maximum_select_fusion
  46.4 0.1 copy.38
  46.5 0.1 pad_maximum_fusion.1
  46.6 3.6 %collective-permute-done.2 = f32[64,64]{1,0:T(8,128)S(1)} collective-permute-done((f32[64,64]{1,0:T(8,128)S(1)}, f32[64,64]{1,0:T(8,128)S(1)}, u32[]{:S(2)}, u32[]{:S(2)}) %collective-permute-start.2) | collective-permute-done | bytes 16416 | tf_op jit(solution)/shard_map/ppermute | solution.py:150
  50.2 0.1 copy.33
  50.3 0.1 copy.39
  50.4 0.6 %broadcast_select_fusion.1 = f32[64,192]{1,0:T(8,128)} fusion(f32[64,192]{1,0:T(8,128)S(1)} %copy.39, f32[64,192]{1,0:T(8,128)S(1)} %pad_maximum_fusion.1, pred[192]{0:T(512)(128)(4,1)S(1)} %fusion.5), kind=kLoop, calls=%fused_computation.15 | loop fusion | flops 12288 | bytes 147648 | tf_op jit(solution)/shard_map/jit(_where)/select_n | solution.py:153
  (11 shorter events, 0.1 us)
Async XLA Ops:
  0.0 1.1 %copy-start = (bf16[256,8,128]{2,1,0:T(8,128)(2,1)S(1)}, bf16[256,8,128]{2,1,0:T(8,128)(2,1)}, u32[]{:S(2)}) copy-start(bf16[256,8,128]{2,1,0:T(8,128)(2,1)} %param.4) | copy-start | bytes 1572868
  1.9 8.2 %copy-start.2 = (s32[64,32]{0,1:T(8,128)S(1)}, s32[64,32]{0,1:T(8,128)}, u32[]{:S(2)}) copy-start(s32[64,32]{0,1:T(8,128)} %param.7) | copy-start | bytes 24580
  1.9 8.2 %copy-start.3 = (s32[64]{0:T(128)S(1)}, s32[64]{0:T(128)}, u32[]{:S(2)}) copy-start(s32[64]{0:T(128)} %param.6) | copy-start | bytes 772
  2.8 23.7 %all-to-all-start = ((bf16[8,32,8,128]{3,2,0,1:T(8,128)(2,1)}), bf16[8,32,8,128]{3,2,0,1:T(8,128)(2,1)S(1)}, u32[]{:S(2)}, u32[]{:S(2)}) async-start(bf16[8,32,8,128]{3,2,0,1:T(8,128)(2,1)} %copy.31), calls=%async_computation | async-start | bytes 1048576 | tf_op jit(solution)/shard_map/all_to_all | solution.py:102
  27.5 1.0 %copy-start.1 = (bf16[64,128]{1,0:T(8,128)(2,1)}, bf16[64,128]{1,0:T(8,128)(2,1)S(1)}, u32[]{:S(2)}) copy-start(bf16[64,128]{1,0:T(8,128)(2,1)S(1)} %slice_bitcast_fusion) | copy-start | bytes 49156
  28.4 2.1 %collective-permute-start.1 = (bf16[2064,128]{1,0:T(8,128)(2,1)S(1)}, bf16[2064,128]{1,0:T(8,128)(2,1)}, u32[]{:S(2)}, u32[]{:S(2)}) collective-permute-start(bf16[2064,128]{1,0:T(8,128)(2,1)S(1)} %pad_maximum_fusion.q_ref), channel_id=1, source_target_pairs={{0,1},{1,0},{2,3},{3,2},{4,5},{5,4},{6,7},{7,6},{8,9},{9,8},{10,11... | collective-permute-start | bytes 1585160 | tf_op jit(solution)/shard_map/ppermute | solution.py:127
  28.5 5.2 %slice-start = ((bf16[64,128]{1,0:T(8,128)(2,1)}), bf16[32,128]{1,0:T(8,128)(2,1)S(1)}, s32[]{:S(2)}) async-start(bf16[64,128]{1,0:T(8,128)(2,1)} %copy-done.1), calls=%async_computation.1 | async-start | bytes 16384 | tf_op jit(solution)/shard_map/slice | solution.py:136
  28.5 15.1 %collective-permute-start = (bf16[2064,128]{1,0:T(8,128)(2,1)S(1)}, bf16[2064,128]{1,0:T(8,128)(2,1)S(1)}, u32[]{:S(2)}, u32[]{:S(2)}) collective-permute-start(bf16[2064,128]{1,0:T(8,128)(2,1)S(1)} %pad_maximum_fusion.q_ref), channel_id=1, source_target_pairs={{0,2},{1,5},{2,6},{3,1},{4,0},{5,7},{6,4},{7,3},{8,10},{9,13},{10,... | collective-permute-start | bytes 1585160 | tf_op jit(solution)/shard_map/ppermute | solution.py:126
  36.6 9.7 %collective-permute-start.3 = (f32[32,64]{0,1:T(8,128)S(1)}, f32[32,64]{0,1:T(8,128)S(1)}, u32[]{:S(2)}, u32[]{:S(2)}) collective-permute-start(f32[32,64]{0,1:T(8,128)S(1)} %copy.35), channel_id=1, source_target_pairs={{0,1},{1,0},{2,3},{3,2},{4,5},{5,4},{6,7},{7,6},{8,9},{9,8},{10,11... | collective-permute-start | bytes 24584 | tf_op jit(solution)/shard_map/ppermute | solution.py:141
  46.3 3.9 %collective-permute-start.2 = (f32[64,64]{1,0:T(8,128)S(1)}, f32[64,64]{1,0:T(8,128)S(1)}, u32[]{:S(2)}, u32[]{:S(2)}) collective-permute-start(f32[64,64]{1,0:T(8,128)S(1)} %get-tuple-element.12), channel_id=1, source_target_pairs={{2,0},{5,1},{6,2},{1,3},{0,4},{7,5},{4,6},{3,7},{10,8},{13,9},{14,... | collective-permute-start | bytes 49160 | tf_op jit(solution)/shard_map/ppermute | solution.py:150

commit v21 on v20

--- a/solution.py
+++ b/solution.py
@@ -67,7 +67,7 @@
     tok_nq, width = query_valid.shape[0], query.shape[1]
     nq = tok_nq // tok
     no = 64
-    cw = 1024
+    cw = 256
     kernel = functools.partial(_chamfer_kernel, tok, nq, no, cw)
     return pl.pallas_call(
         kernel,

time: 51.4 us -> 51.3 us (level)
  no operation moved by 1% of the time
where the time goes in v21:
time: 51.3 us; the launch traced here: 50.9 us
  waiting for transfers between devices  28.5 us (56%)
  starting transfers between devices  7.5 us (15%)
  local copies, waits for them, and re-layouts  5.16 us (10%)
  other arithmetic  4.78 us (9%)
  Pallas kernels  4.62 us (9%)
    all_to_all x1, waiting for transfers between devices, shards(): lax.all_to_all(outgoing, ('enc', 'pool'), split_axis=1, concat_axis=1, ti...  16 us
    all_to_all x1, starting transfers between devices, shards(): lax.all_to_all(outgoing, ('enc', 'pool'), split_axis=1, concat_axis=1, ti...  7.3 us
    ppermute x1, waiting for transfers between devices, shards(): z_recv = lax.ppermute(packed, 'pool', send_pairs)  6.98 us
    pallas_call x2, Pallas kernels, chamfer_tile(): pl.pallas_call(kernel, out_shape=(jax.ShapeDtypeStruct((nq, no), jnp.floa...  4.62 us
    ppermute x1, waiting for transfers between devices, shards(): tile_back = lax.ppermute(tile_z_t, 'pool', back_pairs)  3.61 us
    ppermute x1, waiting for transfers between devices, shards(): c_recv = lax.ppermute(packed, 'pool', chip_pairs)  1.91 us
    select_n x1, other arithmetic, shards(): other_packed = jnp.where(is_a, c_recv, packed)  1.19 us
    slice x1, local copies, waits for them, and re-layouts, shards(): c_blk = c_recv[:n_tok].reshape(tok, items_dev, width)  1.08 us
  transfers between devices with their start and end apart: 5, of which 4 were waited for; matrix products, arithmetic and copies ran while one was open for 9% of the time, Pallas kernels for 9%

profile of v21, /device:TPU:0, one launch (start us, length us, event | category | flops | bytes accessed | tf_op | source)
XLA Modules:
  0.0 50.9 jit_solution(1984157638726304584)
XLA Ops:
  0.0 0.0 copy-start
  0.0 0.8 %reshape.122 = s32[32,8,8]{2,1,0:T(8,128)S(1)} reshape(s32[2048]{0:T(1024)} %param.5) | data formatting | bytes 16384 | tf_op jit(solution)/shard_map/reshape | solution.py:98
  0.9 0.1 subtract_reduce_fusion
  0.9 0.1 reshape.130
  1.0 0.0 copy-done
  1.1 0.8 %gather_fusion = bf16[256,8,128]{2,1,0:T(8,128)(2,1)S(1)} fusion(bf16[256,8,128]{2,1,0:T(8,128)(2,1)S(1)} %copy-done, s32[1024]{0:T(1024)S(1)} %pad_clamp_fusion), kind=kCustom, calls=%fused_computation | custom fusion | bytes 1049600 | tf_op jit(solution)/shard_map/jit(_take)/gather | solution.py:100
  1.9 0.0 copy-start.2
  1.9 0.0 copy-start.3
  1.9 0.9 %copy.31 = bf16[8,32,8,128]{3,2,0,1:T(8,128)(2,1)} copy(bf16[8,32,8,128]{3,0,2,1:T(8,128)(2,1)S(1)} %bitcast.28) | data formatting | bytes 1048576 | tf_op jit(solution)/shard_map/transpose | solution.py:101
  2.8 7.3 %all-to-all-start = ((bf16[8,32,8,128]{3,2,0,1:T(8,128)(2,1)}), bf16[8,32,8,128]{3,2,0,1:T(8,128)(2,1)S(1)}, u32[]{:S(2)}, u32[]{:S(2)}) async-start(bf16[8,32,8,128]{3,2,0,1:T(8,128)(2,1)} %copy.31), calls=%async_computation | async-start | bytes 1048576 | tf_op jit(solution)/shard_map/all_to_all | solution.py:102
  10.1 0.0 copy-done.2
  10.1 0.0 copy-done.3
  10.1 0.1 fusion.3
  10.2 0.1 broadcast_in_dim.64
  10.3 0.1 convert_element_type.44
  10.4 16.0 %all-to-all-done = bf16[8,32,8,128]{3,2,0,1:T(8,128)(2,1)S(1)} async-done(((bf16[8,32,8,128]{3,2,0,1:T(8,128)(2,1)}), bf16[8,32,8,128]{3,2,0,1:T(8,128)(2,1)S(1)}, u32[]{:S(2)}, u32[]{:S(2)}) %all-to-all-start) | async-done | bytes 524320 | tf_op jit(solution)/shard_map/all_to_all | solution.py:102
  26.5 0.3 multiply_reduce_fusion
  26.9 0.1 sqrt.16
  27.0 0.1 sqrt.17
  27.1 0.1 copy_convert_fusion
  27.1 0.3 divide_convert_fusion
  27.5 0.0 copy-start.1
  27.5 0.8 %fusion.1 = bf16[2048,128]{1,0:T(8,128)(2,1)S(1)} fusion(f32[8,32,8,128]{3,2,1,0:T(8,128)S(1)} %copy_convert_fusion, f32[2048]{0:T(1024)S(1)} %sqrt.16, pred[2048]{0:T(1024)(128)(4,1)S(1)} %broadcast_in_dim.64, bf16[64,128]{1,0:T(8,128)(2,1)S(1)} %slice_bitcast_fusion), kind=kLoop, calls=%fused_computation.7 | loop fusion | flops 786432 | bytes 1599488 | tf_op jit(solution)/shard_map/jit(_where)/select_n | solution.py:112
  28.4 0.1 collective-permute-start.1
  28.5 0.0 copy-done.1
  28.5 0.0 slice-start
  28.5 0.1 collective-permute-start
  28.6 1.9 %collective-permute-done.1 = bf16[2064,128]{1,0:T(8,128)(2,1)} collective-permute-done((bf16[2064,128]{1,0:T(8,128)(2,1)S(1)}, bf16[2064,128]{1,0:T(8,128)(2,1)}, u32[]{:S(2)}, u32[]{:S(2)}) %collective-permute-start.1) | collective-permute-done | bytes 528416 | tf_op jit(solution)/shard_map/ppermute | solution.py:127
  30.5 1.2 %broadcast_select_fusion.o_ref = bf16[2064,128]{1,0:T(8,128)(2,1)S(1)} fusion(bf16[2064,128]{1,0:T(8,128)(2,1)} %collective-permute-done.1, pred[]{:T(512)S(6)} %eq.46, bf16[16,128]{1,0:T(8,128)(2,1)S(1)} %convert_element_type.44, bf16[2048,128]{1,0:T(8,128)(2,1)S(1)} %fusion.1), kind=kLoop, calls=%fused_computation.6 | loop fusion | flops 1320960 | bytes 1585153 | tf_op jit(solution)/shard_map/jit(_where)/select_n | solution.py:138
  31.7 0.7 %slice_compare_fusion = pred[16,128]{1,0:T(8,128)(4,1)S(1)} fusion(bf16[2064,128]{1,0:T(8,128)(2,1)} %collective-permute-done.1), kind=kLoop, calls=%fused_computation.24 | loop fusion | flops 2048 | bytes 6144 | tf_op jit(solution)/shard_map/eq | solution.py:135
  32.4 0.1 eq.49
  32.4 0.1 fusion.4
  32.5 0.1 reshape.127
  32.6 1.1 %slice.34 = bf16[2048,128]{1,0:T(8,128)(2,1)S(1)} slice(bf16[2064,128]{1,0:T(8,128)(2,1)} %collective-permute-done.1), slice={[0:2048], [0:128]} | slice | bytes 1048576 | tf_op jit(solution)/shard_map/slice | solution.py:134
  33.7 0.0 slice-done
  33.7 0.2 slice_select_fusion
  33.9 0.2 broadcast_in_dim.75.qv_ref
  34.1 2.0 %shard_map.46 = (f32[32,64]{1,0:T(8,128)S(1)}, f32[64,32]{1,0:T(8,128)}) custom-call(bf16[1024,128]{1,0:T(8,128)(2,1)S(1)} %bitcast.26, bf16[2064,128]{1,0:T(8,128)(2,1)S(1)} %broadcast_select_fusion.o_ref, f32[1024,128]{1,0:T(8,128)S(1)} %broadcast_in_dim.75.qv_ref), custom_call_target="tpu_custom_call" | custom-call | flops 536870912 | bytes 786432 | tf_op jit(solution)/shard_map/pallas_call | solution.py:72
  36.1 0.3 broadcast_in_dim.76.qv_ref
  36.5 0.1 copy.35
  36.6 0.0 collective-permute-start.3
  36.6 7.0 %collective-permute-done.o_ref = bf16[2064,128]{1,0:T(8,128)(2,1)S(1)} collective-permute-done((bf16[2064,128]{1,0:T(8,128)(2,1)S(1)}, bf16[2064,128]{1,0:T(8,128)(2,1)S(1)}, u32[]{:S(2)}, u32[]{:S(2)}) %collective-permute-start) | collective-permute-done | bytes 528416 | tf_op jit(solution)/shard_map/ppermute | solution.py:126
  43.6 2.6 %shard_map.47 = (f32[64,64]{1,0:T(8,128)S(1)}, f32[64,64]{1,0:T(8,128)S(1)}) custom-call(bf16[2064,128]{1,0:T(8,128)(2,1)S(1)} %pad_maximum_fusion.q_ref, bf16[2064,128]{1,0:T(8,128)(2,1)S(1)} %collective-permute-done.o_ref, f32[2048,128]{1,0:T(8,128)S(1)} %broadcast_in_dim.76.qv_ref), custom_call_target="tpu_custom_call" | custom-call | flops 1073741824 | bytes 1048576 | tf_op jit(solution)/shard_map/pallas_call | solution.py:72
  46.2 0.0 collective-permute-start.2
  46.2 0.0 collective-permute-done.3
  46.2 0.1 maximum_select_fusion
  46.3 0.1 copy.38
  46.4 0.1 pad_maximum_fusion.1
  46.5 3.6 %collective-permute-done.2 = f32[64,64]{1,0:T(8,128)S(1)} collective-permute-done((f32[64,64]{1,0:T(8,128)S(1)}, f32[64,64]{1,0:T(8,128)S(1)}, u32[]{:S(2)}, u32[]{:S(2)}) %collective-permute-start.2) | collective-permute-done | bytes 16416 | tf_op jit(solution)/shard_map/ppermute | solution.py:150
  50.1 0.1 copy.33
  50.2 0.1 copy.39
  50.3 0.6 %broadcast_select_fusion.1 = f32[64,192]{1,0:T(8,128)} fusion(f32[64,192]{1,0:T(8,128)S(1)} %copy.39, f32[64,192]{1,0:T(8,128)S(1)} %pad_maximum_fusion.1, pred[192]{0:T(512)(128)(4,1)S(1)} %fusion.5), kind=kLoop, calls=%fused_computation.15 | loop fusion | flops 12288 | bytes 147648 | tf_op jit(solution)/shard_map/jit(_where)/select_n | solution.py:153
  (11 shorter events, 0.1 us)
Async XLA Ops:
  0.0 1.1 %copy-start = (bf16[256,8,128]{2,1,0:T(8,128)(2,1)S(1)}, bf16[256,8,128]{2,1,0:T(8,128)(2,1)}, u32[]{:S(2)}) copy-start(bf16[256,8,128]{2,1,0:T(8,128)(2,1)} %param.4) | copy-start | bytes 1572868
  1.9 8.2 %copy-start.2 = (s32[64,32]{0,1:T(8,128)S(1)}, s32[64,32]{0,1:T(8,128)}, u32[]{:S(2)}) copy-start(s32[64,32]{0,1:T(8,128)} %param.7) | copy-start | bytes 24580
  1.9 8.2 %copy-start.3 = (s32[64]{0:T(128)S(1)}, s32[64]{0:T(128)}, u32[]{:S(2)}) copy-start(s32[64]{0:T(128)} %param.6) | copy-start | bytes 772
  2.8 23.7 %all-to-all-start = ((bf16[8,32,8,128]{3,2,0,1:T(8,128)(2,1)}), bf16[8,32,8,128]{3,2,0,1:T(8,128)(2,1)S(1)}, u32[]{:S(2)}, u32[]{:S(2)}) async-start(bf16[8,32,8,128]{3,2,0,1:T(8,128)(2,1)} %copy.31), calls=%async_computation | async-start | bytes 1048576 | tf_op jit(solution)/shard_map/all_to_all | solution.py:102
  27.5 1.0 %copy-start.1 = (bf16[64,128]{1,0:T(8,128)(2,1)}, bf16[64,128]{1,0:T(8,128)(2,1)S(1)}, u32[]{:S(2)}) copy-start(bf16[64,128]{1,0:T(8,128)(2,1)S(1)} %slice_bitcast_fusion) | copy-start | bytes 49156
  28.4 2.1 %collective-permute-start.1 = (bf16[2064,128]{1,0:T(8,128)(2,1)S(1)}, bf16[2064,128]{1,0:T(8,128)(2,1)}, u32[]{:S(2)}, u32[]{:S(2)}) collective-permute-start(bf16[2064,128]{1,0:T(8,128)(2,1)S(1)} %pad_maximum_fusion.q_ref), channel_id=1, source_target_pairs={{0,1},{1,0},{2,3},{3,2},{4,5},{5,4},{6,7},{7,6},{8,9},{9,8},{10,11... | collective-permute-start | bytes 1585160 | tf_op jit(solution)/shard_map/ppermute | solution.py:127
  28.5 5.2 %slice-start = ((bf16[64,128]{1,0:T(8,128)(2,1)}), bf16[32,128]{1,0:T(8,128)(2,1)S(1)}, s32[]{:S(2)}) async-start(bf16[64,128]{1,0:T(8,128)(2,1)} %copy-done.1), calls=%async_computation.1 | async-start | bytes 16384 | tf_op jit(solution)/shard_map/slice | solution.py:136
  28.5 15.1 %collective-permute-start = (bf16[2064,128]{1,0:T(8,128)(2,1)S(1)}, bf16[2064,128]{1,0:T(8,128)(2,1)S(1)}, u32[]{:S(2)}, u32[]{:S(2)}) collective-permute-start(bf16[2064,128]{1,0:T(8,128)(2,1)S(1)} %pad_maximum_fusion.q_ref), channel_id=1, source_target_pairs={{0,2},{1,5},{2,6},{3,1},{4,0},{5,7},{6,4},{7,3},{8,10},{9,13},{10,... | collective-permute-start | bytes 1585160 | tf_op jit(solution)/shard_map/ppermute | solution.py:126
  36.6 9.6 %collective-permute-start.3 = (f32[32,64]{0,1:T(8,128)S(1)}, f32[32,64]{0,1:T(8,128)S(1)}, u32[]{:S(2)}, u32[]{:S(2)}) collective-permute-start(f32[32,64]{0,1:T(8,128)S(1)} %copy.35), channel_id=1, source_target_pairs={{0,1},{1,0},{2,3},{3,2},{4,5},{5,4},{6,7},{7,6},{8,9},{9,8},{10,11... | collective-permute-start | bytes 24584 | tf_op jit(solution)/shard_map/ppermute | solution.py:141
  46.2 3.9 %collective-permute-start.2 = (f32[64,64]{1,0:T(8,128)S(1)}, f32[64,64]{1,0:T(8,128)S(1)}, u32[]{:S(2)}, u32[]{:S(2)}) collective-permute-start(f32[64,64]{1,0:T(8,128)S(1)} %get-tuple-element.12), channel_id=1, source_target_pairs={{2,0},{5,1},{6,2},{1,3},{0,4},{7,5},{4,6},{3,7},{10,8},{13,9},{14,... | collective-permute-start | bytes 49160 | tf_op jit(solution)/shard_map/ppermute | solution.py:150

commit v22 on v18

--- a/solution.py
+++ b/solution.py
@@ -109,6 +109,7 @@
     valid = (position < lengths[:, None]) & ((position == 0) | (token_mask == 1))
     valid_tm = jnp.transpose(valid.reshape(items_dev, n_enc, toks), (2, 1, 0)).reshape(tok, items_dev)
     bias = jnp.where(valid_tm, 0.0, -4.0).astype(jnp.bfloat16)
+    normed = lax.optimization_barrier(normed)
     normed = jnp.where(valid_tm[:, :, None], normed, normed[0][None])
     packed = jnp.concatenate([normed.reshape(n_tok, width), bias.reshape(-1, width)], axis=0)
     block = packed[:n_tok].reshape(tok, items_dev, width)

time: 51.3 us -> 50.8 us (level)
  other arithmetic: 4.78 us -> 4.15 us
where the time goes in v22:
time: 50.8 us; the launch traced here: 50.4 us
  waiting for transfers between devices  28.8 us (57%)
  starting transfers between devices  7.45 us (15%)
  local copies, waits for them, and re-layouts  5.19 us (10%)
  Pallas kernels  4.57 us (9%)
  other arithmetic  4.15 us (8%)
    all_to_all x1, waiting for transfers between devices, shards(): lax.all_to_all(outgoing, ('enc', 'pool'), split_axis=1, concat_axis=1, ti...  16.1 us
    all_to_all x1, starting transfers between devices, shards(): lax.all_to_all(outgoing, ('enc', 'pool'), split_axis=1, concat_axis=1, ti...  7.3 us
    ppermute x1, waiting for transfers between devices, shards(): z_recv = lax.ppermute(packed, 'pool', send_pairs)  7.16 us
    pallas_call x2, Pallas kernels, chamfer_tile(): pl.pallas_call(kernel, out_shape=(jax.ShapeDtypeStruct((nq, no), jnp.floa...  4.57 us
    ppermute x1, waiting for transfers between devices, shards(): tile_back = lax.ppermute(tile_z_t, 'pool', back_pairs)  3.61 us
    ppermute x1, waiting for transfers between devices, shards(): c_recv = lax.ppermute(packed, 'pool', chip_pairs)  1.92 us
    select_n x1, other arithmetic, shards(): other_packed = jnp.where(is_a, c_recv, packed)  1.19 us
    slice x1, local copies, waits for them, and re-layouts, shards(): c_blk = c_recv[:n_tok].reshape(tok, items_dev, width)  1.08 us
  transfers between devices with their start and end apart: 5, of which 4 were waited for; matrix products, arithmetic and copies ran while one was open for 9% of the time, Pallas kernels for 9%

profile of v22, /device:TPU:0, one launch (start us, length us, event | category | flops | bytes accessed | tf_op | source)
XLA Modules:
  0.0 50.4 jit_solution(16790099962769519581)
XLA Ops:
  0.0 0.0 copy-start
  0.0 0.8 %reshape.114 = s32[32,8,8]{2,1,0:T(8,128)S(1)} reshape(s32[2048]{0:T(1024)} %param.5) | data formatting | bytes 16384 | tf_op jit(solution)/shard_map/reshape | solution.py:98
  0.9 0.1 subtract_reduce_fusion
  0.9 0.1 reshape.123
  1.0 0.0 copy-done
  1.1 0.8 %gather_fusion = bf16[256,8,128]{2,1,0:T(8,128)(2,1)S(1)} fusion(bf16[256,8,128]{2,1,0:T(8,128)(2,1)S(1)} %copy-done, s32[1024]{0:T(1024)S(1)} %pad_clamp_fusion), kind=kCustom, calls=%fused_computation | custom fusion | bytes 1049600 | tf_op jit(solution)/shard_map/jit(_take)/gather | solution.py:100
  1.9 0.0 copy-start.1
  1.9 0.0 copy-start.2
  1.9 0.9 %copy.65 = bf16[8,32,8,128]{3,2,0,1:T(8,128)(2,1)} copy(bf16[8,32,8,128]{3,0,2,1:T(8,128)(2,1)S(1)} %bitcast.23) | data formatting | bytes 1048576 | tf_op jit(solution)/shard_map/transpose | solution.py:101
  2.8 7.3 %all-to-all-start = ((bf16[8,32,8,128]{3,2,0,1:T(8,128)(2,1)}), bf16[8,32,8,128]{3,2,0,1:T(8,128)(2,1)S(1)}, u32[]{:S(2)}, u32[]{:S(2)}) async-start(bf16[8,32,8,128]{3,2,0,1:T(8,128)(2,1)} %copy.65), calls=%async_computation | async-start | bytes 1048576 | tf_op jit(solution)/shard_map/all_to_all | solution.py:102
  10.1 0.0 copy-done.1
  10.1 0.0 copy-done.2
  10.1 0.1 fusion.1
  10.2 0.1 convert_element_type.35
  10.3 16.1 %all-to-all-done = bf16[8,32,8,128]{3,2,0,1:T(8,128)(2,1)S(1)} async-done(((bf16[8,32,8,128]{3,2,0,1:T(8,128)(2,1)}), bf16[8,32,8,128]{3,2,0,1:T(8,128)(2,1)S(1)}, u32[]{:S(2)}, u32[]{:S(2)}) %all-to-all-start) | async-done | bytes 524320 | tf_op jit(solution)/shard_map/all_to_all | solution.py:102
  26.5 0.3 multiply_reduce_fusion
  26.8 0.1 copy.68
  26.9 0.1 copy.69
  27.0 0.1 sqrt.12
  27.1 0.1 copy_convert_fusion
  27.2 0.3 divide_convert_fusion
  27.6 0.3 broadcast_select_fusion.1
  28.0 0.1 collective-permute-start.1
  28.0 0.1 reshape.120
  28.1 0.0 collective-permute-start
  28.2 1.9 %collective-permute-done.1 = bf16[2064,128]{1,0:T(8,128)(2,1)} collective-permute-done((bf16[2064,128]{1,0:T(8,128)(2,1)S(1)}, bf16[2064,128]{1,0:T(8,128)(2,1)}, u32[]{:S(2)}, u32[]{:S(2)}) %collective-permute-start.1) | collective-permute-done | bytes 528416 | tf_op jit(solution)/shard_map/ppermute | solution.py:128
  30.1 1.2 %broadcast_select_fusion.o_ref = bf16[2064,128]{1,0:T(8,128)(2,1)S(1)} fusion(bf16[2064,128]{1,0:T(8,128)(2,1)} %collective-permute-done.1, pred[]{:T(512)S(6)} %eq.46, bf16[16,128]{1,0:T(8,128)(2,1)S(1)} %convert_element_type.35, bf16[2048,128]{1,0:T(8,128)(2,1)S(1)} %bitcast.21), kind=kLoop, calls=%fused_computation.4 | loop fusion | flops 1320960 | bytes 1585153 | tf_op jit(solution)/shard_map/jit(_where)/select_n | solution.py:139
  31.3 0.7 %slice_compare_fusion = pred[16,128]{1,0:T(8,128)(4,1)S(1)} fusion(bf16[2064,128]{1,0:T(8,128)(2,1)} %collective-permute-done.1), kind=kLoop, calls=%fused_computation.22 | loop fusion | flops 2048 | bytes 6144 | tf_op jit(solution)/shard_map/eq | solution.py:136
  31.9 0.1 eq.49
  32.0 0.1 fusion.2
  32.1 0.1 reshape.119
  32.2 1.1 %slice.32 = bf16[2048,128]{1,0:T(8,128)(2,1)S(1)} slice(bf16[2064,128]{1,0:T(8,128)(2,1)} %collective-permute-done.1), slice={[0:2048], [0:128]} | slice | bytes 1048576 | tf_op jit(solution)/shard_map/slice | solution.py:135
  33.3 0.2 broadcast_in_dim.66.qv_ref
  33.5 2.0 %shard_map.46 = (f32[32,64]{1,0:T(8,128)S(1)}, f32[64,32]{1,0:T(8,128)}) custom-call(bf16[1024,128]{1,0:T(8,128)(2,1)S(1)} %bitcast.19, bf16[2064,128]{1,0:T(8,128)(2,1)S(1)} %broadcast_select_fusion.o_ref, f32[1024,128]{1,0:T(8,128)S(1)} %broadcast_in_dim.66.qv_ref), custom_call_target="tpu_custom_call" | custom-call | flops 536870912 | bytes 786432 | tf_op jit(solution)/shard_map/pallas_call | solution.py:72
  35.5 0.3 broadcast_in_dim.67.qv_ref
  35.9 0.1 copy.72
  35.9 0.0 collective-permute-start.3
  36.0 7.2 %collective-permute-done.o_ref = bf16[2064,128]{1,0:T(8,128)(2,1)S(1)} collective-permute-done((bf16[2064,128]{1,0:T(8,128)(2,1)S(1)}, bf16[2064,128]{1,0:T(8,128)(2,1)S(1)}, u32[]{:S(2)}, u32[]{:S(2)}) %collective-permute-start) | collective-permute-done | bytes 528416 | tf_op jit(solution)/shard_map/ppermute | solution.py:127
  43.2 2.5 %shard_map.47 = (f32[64,64]{1,0:T(8,128)S(1)}, f32[64,64]{1,0:T(8,128)S(1)}) custom-call(bf16[2064,128]{1,0:T(8,128)(2,1)S(1)} %pad_maximum_fusion.q_ref, bf16[2064,128]{1,0:T(8,128)(2,1)S(1)} %collective-permute-done.o_ref, f32[2048,128]{1,0:T(8,128)S(1)} %broadcast_in_dim.67.qv_ref), custom_call_target="tpu_custom_call" | custom-call | flops 1073741824 | bytes 1048576 | tf_op jit(solution)/shard_map/pallas_call | solution.py:72
  45.7 0.0 collective-permute-start.2
  45.7 0.0 collective-permute-done.3
  45.7 0.1 maximum_select_fusion
  45.8 0.1 copy.75
  45.9 0.1 pad_maximum_fusion.1
  46.0 3.6 %collective-permute-done.2 = f32[64,64]{1,0:T(8,128)S(1)} collective-permute-done((f32[64,64]{1,0:T(8,128)S(1)}, f32[64,64]{1,0:T(8,128)S(1)}, u32[]{:S(2)}, u32[]{:S(2)}) %collective-permute-start.2) | collective-permute-done | bytes 16416 | tf_op jit(solution)/shard_map/ppermute | solution.py:151
  49.6 0.1 copy.70
  49.7 0.1 copy.76
  49.8 0.6 %broadcast_select_fusion.2 = f32[64,192]{1,0:T(8,128)} fusion(f32[64,192]{1,0:T(8,128)S(1)} %copy.76, f32[64,192]{1,0:T(8,128)S(1)} %pad_maximum_fusion.1, pred[192]{0:T(512)(128)(4,1)S(1)} %fusion.3), kind=kLoop, calls=%fused_computation.12 | loop fusion | flops 12288 | bytes 147648 | tf_op jit(solution)/shard_map/jit(_where)/select_n | solution.py:154
  (11 shorter events, 0.2 us)
Async XLA Ops:
  0.0 1.1 %copy-start = (bf16[256,8,128]{2,1,0:T(8,128)(2,1)S(1)}, bf16[256,8,128]{2,1,0:T(8,128)(2,1)}, u32[]{:S(2)}) copy-start(bf16[256,8,128]{2,1,0:T(8,128)(2,1)} %param.4) | copy-start | bytes 1572868
  1.9 8.2 %copy-start.1 = (s32[64,32]{0,1:T(8,128)S(1)}, s32[64,32]{0,1:T(8,128)}, u32[]{:S(2)}) copy-start(s32[64,32]{0,1:T(8,128)} %param.7) | copy-start | bytes 24580
  1.9 8.2 %copy-start.2 = (s32[64]{0:T(128)S(1)}, s32[64]{0:T(128)}, u32[]{:S(2)}) copy-start(s32[64]{0:T(128)} %param.6) | copy-start | bytes 772
  2.8 23.7 %all-to-all-start = ((bf16[8,32,8,128]{3,2,0,1:T(8,128)(2,1)}), bf16[8,32,8,128]{3,2,0,1:T(8,128)(2,1)S(1)}, u32[]{:S(2)}, u32[]{:S(2)}) async-start(bf16[8,32,8,128]{3,2,0,1:T(8,128)(2,1)} %copy.65), calls=%async_computation | async-start | bytes 1048576 | tf_op jit(solution)/shard_map/all_to_all | solution.py:102
  28.0 2.1 %collective-permute-start.1 = (bf16[2064,128]{1,0:T(8,128)(2,1)S(1)}, bf16[2064,128]{1,0:T(8,128)(2,1)}, u32[]{:S(2)}, u32[]{:S(2)}) collective-permute-start(bf16[2064,128]{1,0:T(8,128)(2,1)S(1)} %pad_maximum_fusion.q_ref), channel_id=1, source_target_pairs={{0,1},{1,0},{2,3},{3,2},{4,5},{5,4},{6,7},{7,6},{8,9},{9,8},{10,11... | collective-permute-start | bytes 1585160 | tf_op jit(solution)/shard_map/ppermute | solution.py:128
  28.1 15.0 %collective-permute-start = (bf16[2064,128]{1,0:T(8,128)(2,1)S(1)}, bf16[2064,128]{1,0:T(8,128)(2,1)S(1)}, u32[]{:S(2)}, u32[]{:S(2)}) collective-permute-start(bf16[2064,128]{1,0:T(8,128)(2,1)S(1)} %pad_maximum_fusion.q_ref), channel_id=1, source_target_pairs={{0,2},{1,5},{2,6},{3,1},{4,0},{5,7},{6,4},{7,3},{8,10},{9,13},{10,... | collective-permute-start | bytes 1585160 | tf_op jit(solution)/shard_map/ppermute | solution.py:127
  35.9 9.8 %collective-permute-start.3 = (f32[32,64]{0,1:T(8,128)S(1)}, f32[32,64]{0,1:T(8,128)S(1)}, u32[]{:S(2)}, u32[]{:S(2)}) collective-permute-start(f32[32,64]{0,1:T(8,128)S(1)} %copy.72), channel_id=1, source_target_pairs={{0,1},{1,0},{2,3},{3,2},{4,5},{5,4},{6,7},{7,6},{8,9},{9,8},{10,11... | collective-permute-start | bytes 24584 | tf_op jit(solution)/shard_map/ppermute | solution.py:142
  45.7 3.9 %collective-permute-start.2 = (f32[64,64]{1,0:T(8,128)S(1)}, f32[64,64]{1,0:T(8,128)S(1)}, u32[]{:S(2)}, u32[]{:S(2)}) collective-permute-start(f32[64,64]{1,0:T(8,128)S(1)} %get-tuple-element.12), channel_id=1, source_target_pairs={{2,0},{5,1},{6,2},{1,3},{0,4},{7,5},{4,6},{3,7},{10,8},{13,9},{14,... | collective-permute-start | bytes 49160 | tf_op jit(solution)/shard_map/ppermute | solution.py:151

commit v23 on v22

--- a/solution.py
+++ b/solution.py
@@ -98,9 +98,9 @@
     table = slot_items.reshape(owners, n_pool, per)
     mine = lax.dynamic_index_in_dim(table, pool_index, 1, keepdims=False) - pool_index * group
     outgoing = jnp.take(encoded, mine, axis=0, mode="clip")
-    outgoing = jnp.transpose(outgoing, (2, 0, 1, 3))
-    arrived = lax.all_to_all(outgoing, ("enc", "pool"), split_axis=1, concat_axis=1, tiled=True)
-    slotted = arrived.reshape(tok, items_dev, width)
+    arrived = lax.all_to_all(outgoing, ("enc", "pool"), split_axis=0, concat_axis=0, tiled=True)
+    arrived = arrived.reshape(n_enc, n_pool, per, toks, width)
+    slotted = jnp.transpose(arrived, (3, 0, 1, 2, 4)).reshape(tok, items_dev, width)
     values = slotted.astype(jnp.float32)
     normed = (values / jnp.sqrt(jnp.sum(values * values, axis=-1, keepdims=True) + 1e-06)).astype(
         jnp.bfloat16

time: 50.8 us -> 50.9 us (level)
    transpose x1 -> x0, local copies, waits for them, and re-layouts: 0.89 us -> none  [shards(): outgoing = jnp.transpose(outgoing, (2, 0, 1, 3))]
    gather x1, local copies, waits for them, and re-layouts: 0.82 us -> 1.58 us  [shards(): outgoing = jnp.take(encoded, mine, axis=0, mode='clip')]
where the time goes in v23:
time: 50.9 us; the launch traced here: 50.5 us
  waiting for transfers between devices  28.8 us (57%)
  starting transfers between devices  7.45 us (15%)
  local copies, waits for them, and re-layouts  5.24 us (10%)
  Pallas kernels  4.56 us (9%)
  other arithmetic  4.19 us (8%)
    all_to_all x1, waiting for transfers between devices, shards(): lax.all_to_all(outgoing, ('enc', 'pool'), split_axis=0, concat_axis=0, ti...  16.1 us
    all_to_all x1, starting transfers between devices, shards(): lax.all_to_all(outgoing, ('enc', 'pool'), split_axis=0, concat_axis=0, ti...  7.29 us
    ppermute x1, waiting for transfers between devices, shards(): z_recv = lax.ppermute(packed, 'pool', send_pairs)  7.16 us
    pallas_call x2, Pallas kernels, chamfer_tile(): pl.pallas_call(kernel, out_shape=(jax.ShapeDtypeStruct((nq, no), jnp.floa...  4.56 us
    ppermute x1, waiting for transfers between devices, shards(): tile_back = lax.ppermute(tile_z_t, 'pool', back_pairs)  3.61 us
    ppermute x1, waiting for transfers between devices, shards(): c_recv = lax.ppermute(packed, 'pool', chip_pairs)  1.92 us
    gather x1, local copies, waits for them, and re-layouts, shards(): outgoing = jnp.take(encoded, mine, axis=0, mode='clip')  1.58 us
    select_n x1, other arithmetic, shards(): other_packed = jnp.where(is_a, c_recv, packed)  1.19 us
  transfers between devices with their start and end apart: 5, of which 4 were waited for; matrix products, arithmetic and copies ran while one was open for 9% of the time, Pallas kernels for 9%

profile of v23, /device:TPU:0, one launch (start us, length us, event | category | flops | bytes accessed | tf_op | source)
XLA Modules:
  0.0 50.5 jit_solution(10126526784651394129)
XLA Ops:
  0.0 0.0 copy-start
  0.0 0.8 %reshape.120 = s32[32,8,8]{2,1,0:T(8,128)S(1)} reshape(s32[2048]{0:T(1024)} %param.5) | data formatting | bytes 16384 | tf_op jit(solution)/shard_map/reshape | solution.py:98
  0.9 0.1 subtract_reduce_fusion
  0.9 0.1 reshape.133
  1.0 0.0 copy-done
  1.1 0.0 copy-start.1
  1.1 0.0 copy-start.2
  1.1 1.6 %gather_fusion = bf16[256,8,128]{2,1,0:T(8,128)(2,1)} fusion(bf16[256,8,128]{2,1,0:T(8,128)(2,1)S(1)} %copy-done, s32[1024]{0:T(1024)S(1)} %pad_clamp_fusion), kind=kCustom, calls=%fused_computation | custom fusion | bytes 1049600 | tf_op jit(solution)/shard_map/jit(_take)/gather | solution.py:100
  2.6 7.3 %all-to-all-start = ((bf16[32,8,8,128]{3,2,1,0:T(8,128)(2,1)}), bf16[32,8,8,128]{3,2,1,0:T(8,128)(2,1)S(1)}, u32[]{:S(2)}, u32[]{:S(2)}) async-start(bf16[32,8,8,128]{3,2,1,0:T(8,128)(2,1)} %bitcast.3), calls=%async_computation | async-start | bytes 1048576 | tf_op jit(solution)/shard_map/all_to_all | solution.py:101
  10.0 0.0 copy-done.1
  10.0 0.0 copy-done.2
  10.0 0.1 fusion.1
  10.1 0.1 convert_element_type.45
  10.2 16.1 %all-to-all-done = bf16[32,8,8,128]{3,2,1,0:T(8,128)(2,1)S(1)} async-done(((bf16[32,8,8,128]{3,2,1,0:T(8,128)(2,1)}), bf16[32,8,8,128]{3,2,1,0:T(8,128)(2,1)S(1)}, u32[]{:S(2)}, u32[]{:S(2)}) %all-to-all-start) | async-done | bytes 524320 | tf_op jit(solution)/shard_map/all_to_all | solution.py:101
  26.3 0.1 convert_element_type.51
  26.4 0.2 copy.31
  26.6 0.3 multiply_reduce_fusion
  27.0 0.2 copy.32
  27.2 0.1 sqrt.12
  27.3 0.3 divide_convert_fusion
  27.6 0.3 broadcast_select_fusion.1
  28.0 0.1 collective-permute-start.1
  28.1 0.1 reshape.128
  28.2 0.0 collective-permute-start
  28.2 1.9 %collective-permute-done.1 = bf16[2064,128]{1,0:T(8,128)(2,1)} collective-permute-done((bf16[2064,128]{1,0:T(8,128)(2,1)S(1)}, bf16[2064,128]{1,0:T(8,128)(2,1)}, u32[]{:S(2)}, u32[]{:S(2)}) %collective-permute-start.1) | collective-permute-done | bytes 528416 | tf_op jit(solution)/shard_map/ppermute | solution.py:128
  30.2 1.2 %broadcast_select_fusion.o_ref = bf16[2064,128]{1,0:T(8,128)(2,1)S(1)} fusion(bf16[2064,128]{1,0:T(8,128)(2,1)} %collective-permute-done.1, pred[]{:T(512)S(6)} %eq.46, bf16[16,128]{1,0:T(8,128)(2,1)S(1)} %convert_element_type.45, bf16[2048,128]{1,0:T(8,128)(2,1)S(1)} %bitcast.26), kind=kLoop, calls=%fused_computation.4 | loop fusion | flops 1320960 | bytes 1585153 | tf_op jit(solution)/shard_map/jit(_where)/select_n | solution.py:139
  31.3 0.7 %slice_compare_fusion = pred[16,128]{1,0:T(8,128)(4,1)S(1)} fusion(bf16[2064,128]{1,0:T(8,128)(2,1)} %collective-permute-done.1), kind=kLoop, calls=%fused_computation.21 | loop fusion | flops 2048 | bytes 6144 | tf_op jit(solution)/shard_map/eq | solution.py:136
  32.0 0.1 eq.49
  32.1 0.1 fusion.2
  32.2 0.1 reshape.127
  32.3 1.1 %slice.32 = bf16[2048,128]{1,0:T(8,128)(2,1)S(1)} slice(bf16[2064,128]{1,0:T(8,128)(2,1)} %collective-permute-done.1), slice={[0:2048], [0:128]} | slice | bytes 1048576 | tf_op jit(solution)/shard_map/slice | solution.py:135
  33.4 0.2 broadcast_in_dim.66.qv_ref
  33.6 2.0 %shard_map.46 = (f32[32,64]{1,0:T(8,128)S(1)}, f32[64,32]{1,0:T(8,128)}) custom-call(bf16[1024,128]{1,0:T(8,128)(2,1)S(1)} %bitcast.24, bf16[2064,128]{1,0:T(8,128)(2,1)S(1)} %broadcast_select_fusion.o_ref, f32[1024,128]{1,0:T(8,128)S(1)} %broadcast_in_dim.66.qv_ref), custom_call_target="tpu_custom_call" | custom-call | flops 536870912 | bytes 786432 | tf_op jit(solution)/shard_map/pallas_call | solution.py:72
  35.6 0.3 broadcast_in_dim.67.qv_ref
  35.9 0.1 copy.35
  36.0 0.0 collective-permute-start.3
  36.1 7.2 %collective-permute-done.o_ref = bf16[2064,128]{1,0:T(8,128)(2,1)S(1)} collective-permute-done((bf16[2064,128]{1,0:T(8,128)(2,1)S(1)}, bf16[2064,128]{1,0:T(8,128)(2,1)S(1)}, u32[]{:S(2)}, u32[]{:S(2)}) %collective-permute-start) | collective-permute-done | bytes 528416 | tf_op jit(solution)/shard_map/ppermute | solution.py:127
  43.2 2.5 %shard_map.47 = (f32[64,64]{1,0:T(8,128)S(1)}, f32[64,64]{1,0:T(8,128)S(1)}) custom-call(bf16[2064,128]{1,0:T(8,128)(2,1)S(1)} %pad_maximum_fusion.q_ref, bf16[2064,128]{1,0:T(8,128)(2,1)S(1)} %collective-permute-done.o_ref, f32[2048,128]{1,0:T(8,128)S(1)} %broadcast_in_dim.67.qv_ref), custom_call_target="tpu_custom_call" | custom-call | flops 1073741824 | bytes 1048576 | tf_op jit(solution)/shard_map/pallas_call | solution.py:72
  45.8 0.0 collective-permute-start.2
  45.8 0.0 collective-permute-done.3
  45.8 0.1 maximum_select_fusion
  45.9 0.1 copy.38
  46.0 0.1 pad_maximum_fusion.1
  46.1 3.6 %collective-permute-done.2 = f32[64,64]{1,0:T(8,128)S(1)} collective-permute-done((f32[64,64]{1,0:T(8,128)S(1)}, f32[64,64]{1,0:T(8,128)S(1)}, u32[]{:S(2)}, u32[]{:S(2)}) %collective-permute-start.2) | collective-permute-done | bytes 16416 | tf_op jit(solution)/shard_map/ppermute | solution.py:151
  49.7 0.1 copy.33
  49.8 0.1 copy.39
  49.9 0.6 %broadcast_select_fusion.2 = f32[64,192]{1,0:T(8,128)} fusion(f32[64,192]{1,0:T(8,128)S(1)} %copy.39, f32[64,192]{1,0:T(8,128)S(1)} %pad_maximum_fusion.1, pred[192]{0:T(512)(128)(4,1)S(1)} %fusion.3), kind=kLoop, calls=%fused_computation.11 | loop fusion | flops 12288 | bytes 147648 | tf_op jit(solution)/shard_map/jit(_where)/select_n | solution.py:154
  (11 shorter events, 0.2 us)
Async XLA Ops:
  0.0 1.1 %copy-start = (bf16[256,8,128]{2,1,0:T(8,128)(2,1)S(1)}, bf16[256,8,128]{2,1,0:T(8,128)(2,1)}, u32[]{:S(2)}) copy-start(bf16[256,8,128]{2,1,0:T(8,128)(2,1)} %param.4) | copy-start | bytes 1572868
  1.1 8.9 %copy-start.1 = (s32[64,32]{0,1:T(8,128)S(1)}, s32[64,32]{0,1:T(8,128)}, u32[]{:S(2)}) copy-start(s32[64,32]{0,1:T(8,128)} %param.7) | copy-start | bytes 24580
  1.1 8.9 %copy-start.2 = (s32[64]{0:T(128)S(1)}, s32[64]{0:T(128)}, u32[]{:S(2)}) copy-start(s32[64]{0:T(128)} %param.6) | copy-start | bytes 772
  2.6 23.7 %all-to-all-start = ((bf16[32,8,8,128]{3,2,1,0:T(8,128)(2,1)}), bf16[32,8,8,128]{3,2,1,0:T(8,128)(2,1)S(1)}, u32[]{:S(2)}, u32[]{:S(2)}) async-start(bf16[32,8,8,128]{3,2,1,0:T(8,128)(2,1)} %bitcast.3), calls=%async_computation | async-start | bytes 1048576 | tf_op jit(solution)/shard_map/all_to_all | solution.py:101
  28.0 2.1 %collective-permute-start.1 = (bf16[2064,128]{1,0:T(8,128)(2,1)S(1)}, bf16[2064,128]{1,0:T(8,128)(2,1)}, u32[]{:S(2)}, u32[]{:S(2)}) collective-permute-start(bf16[2064,128]{1,0:T(8,128)(2,1)S(1)} %pad_maximum_fusion.q_ref), channel_id=1, source_target_pairs={{0,1},{1,0},{2,3},{3,2},{4,5},{5,4},{6,7},{7,6},{8,9},{9,8},{10,11... | collective-permute-start | bytes 1585160 | tf_op jit(solution)/shard_map/ppermute | solution.py:128
  28.2 15.0 %collective-permute-start = (bf16[2064,128]{1,0:T(8,128)(2,1)S(1)}, bf16[2064,128]{1,0:T(8,128)(2,1)S(1)}, u32[]{:S(2)}, u32[]{:S(2)}) collective-permute-start(bf16[2064,128]{1,0:T(8,128)(2,1)S(1)} %pad_maximum_fusion.q_ref), channel_id=1, source_target_pairs={{0,2},{1,5},{2,6},{3,1},{4,0},{5,7},{6,4},{7,3},{8,10},{9,13},{10,... | collective-permute-start | bytes 1585160 | tf_op jit(solution)/shard_map/ppermute | solution.py:127
  36.0 9.8 %collective-permute-start.3 = (f32[32,64]{0,1:T(8,128)S(1)}, f32[32,64]{0,1:T(8,128)S(1)}, u32[]{:S(2)}, u32[]{:S(2)}) collective-permute-start(f32[32,64]{0,1:T(8,128)S(1)} %copy.35), channel_id=1, source_target_pairs={{0,1},{1,0},{2,3},{3,2},{4,5},{5,4},{6,7},{7,6},{8,9},{9,8},{10,11... | collective-permute-start | bytes 24584 | tf_op jit(solution)/shard_map/ppermute | solution.py:142
  45.8 3.9 %collective-permute-start.2 = (f32[64,64]{1,0:T(8,128)S(1)}, f32[64,64]{1,0:T(8,128)S(1)}, u32[]{:S(2)}, u32[]{:S(2)}) collective-permute-start(f32[64,64]{1,0:T(8,128)S(1)} %get-tuple-element.12), channel_id=1, source_target_pairs={{2,0},{5,1},{6,2},{1,3},{0,4},{7,5},{4,6},{3,7},{10,8},{13,9},{14,... | collective-permute-start | bytes 49160 | tf_op jit(solution)/shard_map/ppermute | solution.py:151

commit v24 on v22

--- a/solution.py
+++ b/solution.py
@@ -75,7 +75,7 @@
         in_specs=[pl.BlockSpec(memory_space=pltpu.VMEM)] * 3,
         out_specs=(pl.BlockSpec(memory_space=pltpu.VMEM), pl.BlockSpec(memory_space=pltpu.VMEM)),
         scratch_shapes=[pltpu.VMEM((tok_nq, 128), jnp.float32)],
-        compiler_params=pltpu.CompilerParams(vmem_limit_bytes=24 * 1024 * 1024),
+        compiler_params=pltpu.CompilerParams(vmem_limit_bytes=12 * 1024 * 1024),
         cost_estimate=pl.CostEstimate(
             flops=2 * tok_nq * tok * no * width, transcendentals=0, bytes_accessed=(tok_nq + tok * no) * width * 2
         ),

time: 50.8 us -> 50.8 us (level)
  no operation moved by 1% of the time
where the time goes in v24:
time: 50.8 us; the launch traced here: 50.4 us
  waiting for transfers between devices  28.8 us (57%)
  starting transfers between devices  7.45 us (15%)
  local copies, waits for them, and re-layouts  5.2 us (10%)
  Pallas kernels  4.57 us (9%)
  other arithmetic  4.15 us (8%)
    all_to_all x1, waiting for transfers between devices, shards(): lax.all_to_all(outgoing, ('enc', 'pool'), split_axis=1, concat_axis=1, ti...  16.1 us
    all_to_all x1, starting transfers between devices, shards(): lax.all_to_all(outgoing, ('enc', 'pool'), split_axis=1, concat_axis=1, ti...  7.3 us
    ppermute x1, waiting for transfers between devices, shards(): z_recv = lax.ppermute(packed, 'pool', send_pairs)  7.15 us
    pallas_call x2, Pallas kernels, chamfer_tile(): pl.pallas_call(kernel, out_shape=(jax.ShapeDtypeStruct((nq, no), jnp.floa...  4.57 us
    ppermute x1, waiting for transfers between devices, shards(): tile_back = lax.ppermute(tile_z_t, 'pool', back_pairs)  3.61 us
    ppermute x1, waiting for transfers between devices, shards(): c_recv = lax.ppermute(packed, 'pool', chip_pairs)  1.92 us
    select_n x1, other arithmetic, shards(): other_packed = jnp.where(is_a, c_recv, packed)  1.19 us
    slice x1, local copies, waits for them, and re-layouts, shards(): c_blk = c_recv[:n_tok].reshape(tok, items_dev, width)  1.08 us
  transfers between devices with their start and end apart: 5, of which 4 were waited for; matrix products, arithmetic and copies ran while one was open for 9% of the time, Pallas kernels for 9%

profile of v24, /device:TPU:0, one launch (start us, length us, event | category | flops | bytes accessed | tf_op | source)
XLA Modules:
  0.0 50.4 jit_solution(14395514250120587521)
XLA Ops:
  0.0 0.0 copy-start
  0.0 0.8 %reshape.114 = s32[32,8,8]{2,1,0:T(8,128)S(1)} reshape(s32[2048]{0:T(1024)} %param.5) | data formatting | bytes 16384 | tf_op jit(solution)/shard_map/reshape | solution.py:98
  0.9 0.1 subtract_reduce_fusion
  0.9 0.1 reshape.123
  1.0 0.0 copy-done
  1.1 0.8 %gather_fusion = bf16[256,8,128]{2,1,0:T(8,128)(2,1)S(1)} fusion(bf16[256,8,128]{2,1,0:T(8,128)(2,1)S(1)} %copy-done, s32[1024]{0:T(1024)S(1)} %pad_clamp_fusion), kind=kCustom, calls=%fused_computation | custom fusion | bytes 1049600 | tf_op jit(solution)/shard_map/jit(_take)/gather | solution.py:100
  1.9 0.0 copy-start.1
  1.9 0.0 copy-start.2
  1.9 0.9 %copy.65 = bf16[8,32,8,128]{3,2,0,1:T(8,128)(2,1)} copy(bf16[8,32,8,128]{3,0,2,1:T(8,128)(2,1)S(1)} %bitcast.23) | data formatting | bytes 1048576 | tf_op jit(solution)/shard_map/transpose | solution.py:101
  2.8 7.3 %all-to-all-start = ((bf16[8,32,8,128]{3,2,0,1:T(8,128)(2,1)}), bf16[8,32,8,128]{3,2,0,1:T(8,128)(2,1)S(1)}, u32[]{:S(2)}, u32[]{:S(2)}) async-start(bf16[8,32,8,128]{3,2,0,1:T(8,128)(2,1)} %copy.65), calls=%async_computation | async-start | bytes 1048576 | tf_op jit(solution)/shard_map/all_to_all | solution.py:102
  10.1 0.0 copy-done.1
  10.1 0.0 copy-done.2
  10.1 0.1 fusion.1
  10.2 0.1 convert_element_type.35
  10.3 16.1 %all-to-all-done = bf16[8,32,8,128]{3,2,0,1:T(8,128)(2,1)S(1)} async-done(((bf16[8,32,8,128]{3,2,0,1:T(8,128)(2,1)}), bf16[8,32,8,128]{3,2,0,1:T(8,128)(2,1)S(1)}, u32[]{:S(2)}, u32[]{:S(2)}) %all-to-all-start) | async-done | bytes 524320 | tf_op jit(solution)/shard_map/all_to_all | solution.py:102
  26.5 0.3 multiply_reduce_fusion
  26.8 0.1 copy.68
  26.9 0.1 copy.69
  27.0 0.1 sqrt.12
  27.1 0.1 copy_convert_fusion
  27.2 0.3 divide_convert_fusion
  27.6 0.3 broadcast_select_fusion.1
  28.0 0.1 collective-permute-start.1
  28.0 0.1 reshape.120
  28.1 0.0 collective-permute-start
  28.2 1.9 %collective-permute-done.1 = bf16[2064,128]{1,0:T(8,128)(2,1)} collective-permute-done((bf16[2064,128]{1,0:T(8,128)(2,1)S(1)}, bf16[2064,128]{1,0:T(8,128)(2,1)}, u32[]{:S(2)}, u32[]{:S(2)}) %collective-permute-start.1) | collective-permute-done | bytes 528416 | tf_op jit(solution)/shard_map/ppermute | solution.py:128
  30.1 1.2 %broadcast_select_fusion.o_ref = bf16[2064,128]{1,0:T(8,128)(2,1)S(1)} fusion(bf16[2064,128]{1,0:T(8,128)(2,1)} %collective-permute-done.1, pred[]{:T(512)S(6)} %eq.46, bf16[16,128]{1,0:T(8,128)(2,1)S(1)} %convert_element_type.35, bf16[2048,128]{1,0:T(8,128)(2,1)S(1)} %bitcast.21), kind=kLoop, calls=%fused_computation.4 | loop fusion | flops 1320960 | bytes 1585153 | tf_op jit(solution)/shard_map/jit(_where)/select_n | solution.py:139
  31.3 0.7 %slice_compare_fusion = pred[16,128]{1,0:T(8,128)(4,1)S(1)} fusion(bf16[2064,128]{1,0:T(8,128)(2,1)} %collective-permute-done.1), kind=kLoop, calls=%fused_computation.22 | loop fusion | flops 2048 | bytes 6144 | tf_op jit(solution)/shard_map/eq | solution.py:136
  31.9 0.1 eq.49
  32.0 0.1 fusion.2
  32.1 0.1 reshape.119
  32.2 1.1 %slice.32 = bf16[2048,128]{1,0:T(8,128)(2,1)S(1)} slice(bf16[2064,128]{1,0:T(8,128)(2,1)} %collective-permute-done.1), slice={[0:2048], [0:128]} | slice | bytes 1048576 | tf_op jit(solution)/shard_map/slice | solution.py:135
  33.3 0.2 broadcast_in_dim.66.qv_ref
  33.5 2.0 %shard_map.46 = (f32[32,64]{1,0:T(8,128)S(1)}, f32[64,32]{1,0:T(8,128)}) custom-call(bf16[1024,128]{1,0:T(8,128)(2,1)S(1)} %bitcast.19, bf16[2064,128]{1,0:T(8,128)(2,1)S(1)} %broadcast_select_fusion.o_ref, f32[1024,128]{1,0:T(8,128)S(1)} %broadcast_in_dim.66.qv_ref), custom_call_target="tpu_custom_call" | custom-call | flops 536870912 | bytes 786432 | tf_op jit(solution)/shard_map/pallas_call | solution.py:72
  35.5 0.3 broadcast_in_dim.67.qv_ref
  35.9 0.1 copy.72
  36.0 0.0 collective-permute-start.3
  36.0 7.2 %collective-permute-done.o_ref = bf16[2064,128]{1,0:T(8,128)(2,1)S(1)} collective-permute-done((bf16[2064,128]{1,0:T(8,128)(2,1)S(1)}, bf16[2064,128]{1,0:T(8,128)(2,1)S(1)}, u32[]{:S(2)}, u32[]{:S(2)}) %collective-permute-start) | collective-permute-done | bytes 528416 | tf_op jit(solution)/shard_map/ppermute | solution.py:127
  43.2 2.5 %shard_map.47 = (f32[64,64]{1,0:T(8,128)S(1)}, f32[64,64]{1,0:T(8,128)S(1)}) custom-call(bf16[2064,128]{1,0:T(8,128)(2,1)S(1)} %pad_maximum_fusion.q_ref, bf16[2064,128]{1,0:T(8,128)(2,1)S(1)} %collective-permute-done.o_ref, f32[2048,128]{1,0:T(8,128)S(1)} %broadcast_in_dim.67.qv_ref), custom_call_target="tpu_custom_call" | custom-call | flops 1073741824 | bytes 1048576 | tf_op jit(solution)/shard_map/pallas_call | solution.py:72
  45.7 0.0 collective-permute-start.2
  45.7 0.0 collective-permute-done.3
  45.7 0.1 maximum_select_fusion
  45.8 0.1 copy.75
  45.9 0.1 pad_maximum_fusion.1
  46.0 3.6 %collective-permute-done.2 = f32[64,64]{1,0:T(8,128)S(1)} collective-permute-done((f32[64,64]{1,0:T(8,128)S(1)}, f32[64,64]{1,0:T(8,128)S(1)}, u32[]{:S(2)}, u32[]{:S(2)}) %collective-permute-start.2) | collective-permute-done | bytes 16416 | tf_op jit(solution)/shard_map/ppermute | solution.py:151
  49.6 0.1 copy.70
  49.7 0.1 copy.76
  49.8 0.6 %broadcast_select_fusion.2 = f32[64,192]{1,0:T(8,128)} fusion(f32[64,192]{1,0:T(8,128)S(1)} %copy.76, f32[64,192]{1,0:T(8,128)S(1)} %pad_maximum_fusion.1, pred[192]{0:T(512)(128)(4,1)S(1)} %fusion.3), kind=kLoop, calls=%fused_computation.12 | loop fusion | flops 12288 | bytes 147648 | tf_op jit(solution)/shard_map/jit(_where)/select_n | solution.py:154
  (11 shorter events, 0.2 us)
Async XLA Ops:
  0.0 1.1 %copy-start = (bf16[256,8,128]{2,1,0:T(8,128)(2,1)S(1)}, bf16[256,8,128]{2,1,0:T(8,128)(2,1)}, u32[]{:S(2)}) copy-start(bf16[256,8,128]{2,1,0:T(8,128)(2,1)} %param.4) | copy-start | bytes 1572868
  1.9 8.2 %copy-start.1 = (s32[64,32]{0,1:T(8,128)S(1)}, s32[64,32]{0,1:T(8,128)}, u32[]{:S(2)}) copy-start(s32[64,32]{0,1:T(8,128)} %param.7) | copy-start | bytes 24580
  1.9 8.2 %copy-start.2 = (s32[64]{0:T(128)S(1)}, s32[64]{0:T(128)}, u32[]{:S(2)}) copy-start(s32[64]{0:T(128)} %param.6) | copy-start | bytes 772
  2.8 23.7 %all-to-all-start = ((bf16[8,32,8,128]{3,2,0,1:T(8,128)(2,1)}), bf16[8,32,8,128]{3,2,0,1:T(8,128)(2,1)S(1)}, u32[]{:S(2)}, u32[]{:S(2)}) async-start(bf16[8,32,8,128]{3,2,0,1:T(8,128)(2,1)} %copy.65), calls=%async_computation | async-start | bytes 1048576 | tf_op jit(solution)/shard_map/all_to_all | solution.py:102
  28.0 2.1 %collective-permute-start.1 = (bf16[2064,128]{1,0:T(8,128)(2,1)S(1)}, bf16[2064,128]{1,0:T(8,128)(2,1)}, u32[]{:S(2)}, u32[]{:S(2)}) collective-permute-start(bf16[2064,128]{1,0:T(8,128)(2,1)S(1)} %pad_maximum_fusion.q_ref), channel_id=1, source_target_pairs={{0,1},{1,0},{2,3},{3,2},{4,5},{5,4},{6,7},{7,6},{8,9},{9,8},{10,11... | collective-permute-start | bytes 1585160 | tf_op jit(solution)/shard_map/ppermute | solution.py:128
  28.1 15.0 %collective-permute-start = (bf16[2064,128]{1,0:T(8,128)(2,1)S(1)}, bf16[2064,128]{1,0:T(8,128)(2,1)S(1)}, u32[]{:S(2)}, u32[]{:S(2)}) collective-permute-start(bf16[2064,128]{1,0:T(8,128)(2,1)S(1)} %pad_maximum_fusion.q_ref), channel_id=1, source_target_pairs={{0,2},{1,5},{2,6},{3,1},{4,0},{5,7},{6,4},{7,3},{8,10},{9,13},{10,... | collective-permute-start | bytes 1585160 | tf_op jit(solution)/shard_map/ppermute | solution.py:127
  36.0 9.8 %collective-permute-start.3 = (f32[32,64]{0,1:T(8,128)S(1)}, f32[32,64]{0,1:T(8,128)S(1)}, u32[]{:S(2)}, u32[]{:S(2)}) collective-permute-start(f32[32,64]{0,1:T(8,128)S(1)} %copy.72), channel_id=1, source_target_pairs={{0,1},{1,0},{2,3},{3,2},{4,5},{5,4},{6,7},{7,6},{8,9},{9,8},{10,11... | collective-permute-start | bytes 24584 | tf_op jit(solution)/shard_map/ppermute | solution.py:142
  45.7 3.9 %collective-permute-start.2 = (f32[64,64]{1,0:T(8,128)S(1)}, f32[64,64]{1,0:T(8,128)S(1)}, u32[]{:S(2)}, u32[]{:S(2)}) collective-permute-start(f32[64,64]{1,0:T(8,128)S(1)} %get-tuple-element.12), channel_id=1, source_target_pairs={{2,0},{5,1},{6,2},{1,3},{0,4},{7,5},{4,6},{3,7},{10,8},{13,9},{14,... | collective-permute-start | bytes 49160 | tf_op jit(solution)/shard_map/ppermute | solution.py:151

commit v25 on v22

--- a/solution.py
+++ b/solution.py
@@ -148,10 +148,10 @@
     tile0 = jnp.where(is_a, joined, joined.T)
 
     tile_z, tile_z_t = chamfer_tile(packed, own_flags, z_recv, tok)
-    tile_back = lax.ppermute(tile_z_t, "pool", back_pairs)
+    tile_back = lax.ppermute(jnp.tile(tile_z_t, (1, 3)), "pool", back_pairs)
     ready = lax.optimization_barrier(jnp.concatenate([tile0, tile_z, tile_z], axis=1))
     column = jnp.arange(3 * items_dev, dtype=jnp.int32)[None, :] // items_dev
-    return jnp.where(column == 1 + parity, jnp.tile(tile_back, (1, 3)), ready)
+    return jnp.where(column == 1 + parity, tile_back, ready)
 
 
 def solution(mesh):

time: 50.8 us -> 51.2 us (level)
  no operation moved by 1% of the time
where the time goes in v25:
time: 51.2 us; the launch traced here: 50.8 us
  waiting for transfers between devices  29.2 us (57%)
  starting transfers between devices  7.49 us (15%)
  local copies, waits for them, and re-layouts  5.2 us (10%)
  Pallas kernels  4.57 us (9%)
  other arithmetic  4.15 us (8%)
    all_to_all x1, waiting for transfers between devices, shards(): lax.all_to_all(outgoing, ('enc', 'pool'), split_axis=1, concat_axis=1, ti...  16.1 us
    all_to_all x1, starting transfers between devices, shards(): lax.all_to_all(outgoing, ('enc', 'pool'), split_axis=1, concat_axis=1, ti...  7.3 us
    ppermute x1, waiting for transfers between devices, shards(): z_recv = lax.ppermute(packed, 'pool', send_pairs)  7.16 us
    pallas_call x2, Pallas kernels, chamfer_tile(): pl.pallas_call(kernel, out_shape=(jax.ShapeDtypeStruct((nq, no), jnp.floa...  4.57 us
    ppermute x1, waiting for transfers between devices, shards(): tile_back = lax.ppermute(jnp.tile(tile_z_t, (1, 3)), 'pool', back_pairs)  3.97 us
    ppermute x1, waiting for transfers between devices, shards(): c_recv = lax.ppermute(packed, 'pool', chip_pairs)  1.92 us
    select_n x1, other arithmetic, shards(): other_packed = jnp.where(is_a, c_recv, packed)  1.19 us
    slice x1, local copies, waits for them, and re-layouts, shards(): c_blk = c_recv[:n_tok].reshape(tok, items_dev, width)  1.08 us
  transfers between devices with their start and end apart: 5, of which 4 were waited for; matrix products, arithmetic and copies ran while one was open for 9% of the time, Pallas kernels for 9%

profile of v25, /device:TPU:0, one launch (start us, length us, event | category | flops | bytes accessed | tf_op | source)
XLA Modules:
  0.0 50.8 jit_solution(13235337292213202723)
XLA Ops:
  0.0 0.0 copy-start
  0.0 0.8 %reshape.114 = s32[32,8,8]{2,1,0:T(8,128)S(1)} reshape(s32[2048]{0:T(1024)} %param.5) | data formatting | bytes 16384 | tf_op jit(solution)/shard_map/reshape | solution.py:98
  0.9 0.1 subtract_reduce_fusion
  0.9 0.1 reshape.123
  1.0 0.0 copy-done
  1.1 0.8 %gather_fusion = bf16[256,8,128]{2,1,0:T(8,128)(2,1)S(1)} fusion(bf16[256,8,128]{2,1,0:T(8,128)(2,1)S(1)} %copy-done, s32[1024]{0:T(1024)S(1)} %pad_clamp_fusion), kind=kCustom, calls=%fused_computation | custom fusion | bytes 1049600 | tf_op jit(solution)/shard_map/jit(_take)/gather | solution.py:100
  1.9 0.0 copy-start.1
  1.9 0.0 copy-start.2
  1.9 0.9 %copy.65 = bf16[8,32,8,128]{3,2,0,1:T(8,128)(2,1)} copy(bf16[8,32,8,128]{3,0,2,1:T(8,128)(2,1)S(1)} %bitcast.23) | data formatting | bytes 1048576 | tf_op jit(solution)/shard_map/transpose | solution.py:101
  2.8 7.3 %all-to-all-start = ((bf16[8,32,8,128]{3,2,0,1:T(8,128)(2,1)}), bf16[8,32,8,128]{3,2,0,1:T(8,128)(2,1)S(1)}, u32[]{:S(2)}, u32[]{:S(2)}) async-start(bf16[8,32,8,128]{3,2,0,1:T(8,128)(2,1)} %copy.65), calls=%async_computation | async-start | bytes 1048576 | tf_op jit(solution)/shard_map/all_to_all | solution.py:102
  10.1 0.0 copy-done.1
  10.1 0.0 copy-done.2
  10.1 0.1 fusion.1
  10.2 0.1 convert_element_type.35
  10.3 16.1 %all-to-all-done = bf16[8,32,8,128]{3,2,0,1:T(8,128)(2,1)S(1)} async-done(((bf16[8,32,8,128]{3,2,0,1:T(8,128)(2,1)}), bf16[8,32,8,128]{3,2,0,1:T(8,128)(2,1)S(1)}, u32[]{:S(2)}, u32[]{:S(2)}) %all-to-all-start) | async-done | bytes 524320 | tf_op jit(solution)/shard_map/all_to_all | solution.py:102
  26.5 0.3 multiply_reduce_fusion
  26.8 0.1 copy.68
  26.9 0.1 copy.69
  27.0 0.1 sqrt.12
  27.1 0.1 copy_convert_fusion
  27.2 0.3 divide_convert_fusion
  27.6 0.3 broadcast_select_fusion.1
  28.0 0.1 collective-permute-start.1
  28.0 0.1 reshape.120
  28.1 0.0 collective-permute-start
  28.2 1.9 %collective-permute-done.1 = bf16[2064,128]{1,0:T(8,128)(2,1)} collective-permute-done((bf16[2064,128]{1,0:T(8,128)(2,1)S(1)}, bf16[2064,128]{1,0:T(8,128)(2,1)}, u32[]{:S(2)}, u32[]{:S(2)}) %collective-permute-start.1) | collective-permute-done | bytes 528416 | tf_op jit(solution)/shard_map/ppermute | solution.py:128
  30.1 1.2 %broadcast_select_fusion.o_ref = bf16[2064,128]{1,0:T(8,128)(2,1)S(1)} fusion(bf16[2064,128]{1,0:T(8,128)(2,1)} %collective-permute-done.1, pred[]{:T(512)S(6)} %eq.46, bf16[16,128]{1,0:T(8,128)(2,1)S(1)} %convert_element_type.35, bf16[2048,128]{1,0:T(8,128)(2,1)S(1)} %bitcast.21), kind=kLoop, calls=%fused_computation.4 | loop fusion | flops 1320960 | bytes 1585153 | tf_op jit(solution)/shard_map/jit(_where)/select_n | solution.py:139
  31.3 0.7 %slice_compare_fusion = pred[16,128]{1,0:T(8,128)(4,1)S(1)} fusion(bf16[2064,128]{1,0:T(8,128)(2,1)} %collective-permute-done.1), kind=kLoop, calls=%fused_computation.22 | loop fusion | flops 2048 | bytes 6144 | tf_op jit(solution)/shard_map/eq | solution.py:136
  31.9 0.1 eq.49
  32.0 0.1 fusion.2
  32.1 0.1 reshape.119
  32.2 1.1 %slice.32 = bf16[2048,128]{1,0:T(8,128)(2,1)S(1)} slice(bf16[2064,128]{1,0:T(8,128)(2,1)} %collective-permute-done.1), slice={[0:2048], [0:128]} | slice | bytes 1048576 | tf_op jit(solution)/shard_map/slice | solution.py:135
  33.3 0.2 broadcast_in_dim.66.qv_ref
  33.5 2.0 %shard_map.46 = (f32[32,64]{1,0:T(8,128)S(1)}, f32[64,32]{1,0:T(8,128)}) custom-call(bf16[1024,128]{1,0:T(8,128)(2,1)S(1)} %bitcast.19, bf16[2064,128]{1,0:T(8,128)(2,1)S(1)} %broadcast_select_fusion.o_ref, f32[1024,128]{1,0:T(8,128)S(1)} %broadcast_in_dim.66.qv_ref), custom_call_target="tpu_custom_call" | custom-call | flops 536870912 | bytes 786432 | tf_op jit(solution)/shard_map/pallas_call | solution.py:72
  35.5 0.3 broadcast_in_dim.67.qv_ref
  35.9 0.1 copy.73
  35.9 0.0 collective-permute-start.3
  36.0 7.2 %collective-permute-done.o_ref = bf16[2064,128]{1,0:T(8,128)(2,1)S(1)} collective-permute-done((bf16[2064,128]{1,0:T(8,128)(2,1)S(1)}, bf16[2064,128]{1,0:T(8,128)(2,1)S(1)}, u32[]{:S(2)}, u32[]{:S(2)}) %collective-permute-start) | collective-permute-done | bytes 528416 | tf_op jit(solution)/shard_map/ppermute | solution.py:127
  43.2 2.5 %shard_map.47 = (f32[64,64]{1,0:T(8,128)S(1)}, f32[64,64]{1,0:T(8,128)S(1)}) custom-call(bf16[2064,128]{1,0:T(8,128)(2,1)S(1)} %pad_maximum_fusion.q_ref, bf16[2064,128]{1,0:T(8,128)(2,1)S(1)} %collective-permute-done.o_ref, f32[2048,128]{1,0:T(8,128)S(1)} %broadcast_in_dim.67.qv_ref), custom_call_target="tpu_custom_call" | custom-call | flops 1073741824 | bytes 1048576 | tf_op jit(solution)/shard_map/pallas_call | solution.py:72
  45.7 0.1 copy.70
  45.8 0.1 copy.71
  45.9 0.1 collective-permute-start.2
  45.9 0.0 collective-permute-done.3
  46.0 0.1 maximum_select_fusion
  46.0 0.1 copy.76
  46.1 0.1 pad_maximum_fusion.1
  46.2 4.0 %collective-permute-done.2 = f32[64,192]{1,0:T(8,128)S(1)} collective-permute-done((f32[64,192]{1,0:T(8,128)S(1)}, f32[64,192]{1,0:T(8,128)S(1)}, u32[]{:S(2)}, u32[]{:S(2)}) %collective-permute-start.2) | collective-permute-done | bytes 49184 | tf_op jit(solution)/shard_map/ppermute | solution.py:151
  50.2 0.6 %broadcast_select_fusion.2 = f32[64,192]{1,0:T(8,128)} fusion(f32[64,192]{1,0:T(8,128)S(1)} %collective-permute-done.2, f32[64,192]{1,0:T(8,128)S(1)} %pad_maximum_fusion.1, pred[192]{0:T(512)(128)(4,1)S(1)} %fusion.3), kind=kLoop, calls=%fused_computation.12 | loop fusion | flops 12288 | bytes 147648 | tf_op jit(solution)/shard_map/jit(_where)/select_n | solution.py:154
  (11 shorter events, 0.2 us)
Async XLA Ops:
  0.0 1.1 %copy-start = (bf16[256,8,128]{2,1,0:T(8,128)(2,1)S(1)}, bf16[256,8,128]{2,1,0:T(8,128)(2,1)}, u32[]{:S(2)}) copy-start(bf16[256,8,128]{2,1,0:T(8,128)(2,1)} %param.4) | copy-start | bytes 1572868
  1.9 8.2 %copy-start.1 = (s32[64,32]{0,1:T(8,128)S(1)}, s32[64,32]{0,1:T(8,128)}, u32[]{:S(2)}) copy-start(s32[64,32]{0,1:T(8,128)} %param.7) | copy-start | bytes 24580
  1.9 8.2 %copy-start.2 = (s32[64]{0:T(128)S(1)}, s32[64]{0:T(128)}, u32[]{:S(2)}) copy-start(s32[64]{0:T(128)} %param.6) | copy-start | bytes 772
  2.8 23.7 %all-to-all-start = ((bf16[8,32,8,128]{3,2,0,1:T(8,128)(2,1)}), bf16[8,32,8,128]{3,2,0,1:T(8,128)(2,1)S(1)}, u32[]{:S(2)}, u32[]{:S(2)}) async-start(bf16[8,32,8,128]{3,2,0,1:T(8,128)(2,1)} %copy.65), calls=%async_computation | async-start | bytes 1048576 | tf_op jit(solution)/shard_map/all_to_all | solution.py:102
  28.0 2.1 %collective-permute-start.1 = (bf16[2064,128]{1,0:T(8,128)(2,1)S(1)}, bf16[2064,128]{1,0:T(8,128)(2,1)}, u32[]{:S(2)}, u32[]{:S(2)}) collective-permute-start(bf16[2064,128]{1,0:T(8,128)(2,1)S(1)} %pad_maximum_fusion.q_ref), channel_id=1, source_target_pairs={{0,1},{1,0},{2,3},{3,2},{4,5},{5,4},{6,7},{7,6},{8,9},{9,8},{10,11... | collective-permute-start | bytes 1585160 | tf_op jit(solution)/shard_map/ppermute | solution.py:128
  28.1 15.0 %collective-permute-start = (bf16[2064,128]{1,0:T(8,128)(2,1)S(1)}, bf16[2064,128]{1,0:T(8,128)(2,1)S(1)}, u32[]{:S(2)}, u32[]{:S(2)}) collective-permute-start(bf16[2064,128]{1,0:T(8,128)(2,1)S(1)} %pad_maximum_fusion.q_ref), channel_id=1, source_target_pairs={{0,2},{1,5},{2,6},{3,1},{4,0},{5,7},{6,4},{7,3},{8,10},{9,13},{10,... | collective-permute-start | bytes 1585160 | tf_op jit(solution)/shard_map/ppermute | solution.py:127
  35.9 10.0 %collective-permute-start.3 = (f32[32,64]{0,1:T(8,128)S(1)}, f32[32,64]{0,1:T(8,128)S(1)}, u32[]{:S(2)}, u32[]{:S(2)}) collective-permute-start(f32[32,64]{0,1:T(8,128)S(1)} %copy.73), channel_id=1, source_target_pairs={{0,1},{1,0},{2,3},{3,2},{4,5},{5,4},{6,7},{7,6},{8,9},{9,8},{10,11... | collective-permute-start | bytes 24584 | tf_op jit(solution)/shard_map/ppermute | solution.py:142
  45.9 4.3 %collective-permute-start.2 = (f32[64,192]{1,0:T(8,128)S(1)}, f32[64,192]{1,0:T(8,128)S(1)}, u32[]{:S(2)}, u32[]{:S(2)}) collective-permute-start(f32[64,192]{1,0:T(8,128)S(1)} %copy.71), channel_id=1, source_target_pairs={{2,0},{5,1},{6,2},{1,3},{0,4},{7,5},{4,6},{3,7},{10,8},{13,9},{14,... | collective-permute-start | bytes 147464 | tf_op jit(solution)/shard_map/ppermute | solution.py:151
